TPU v7x, 512 devices: a whole 4x4x16 slice. The times are simulated.
512 devices in a mesh: req: 128 (over z, y, core), tp: 4 (over x).
Axes of the slice: x: 4, y: 4, z: 16, core: 2. Of those that a mesh axis runs over, the one named last changes fastest.
Arguments:
- states: bfloat16 [32768, 3072], P('req', 'tp'), may hold values from -12 to 12
- query_weight: bfloat16 [3072, 1536], P(None, 'tp'), may hold values from -0.75 to 0.75
- key_value_weight: bfloat16 [3072, 512], P(None, 'tp'), may hold values from -0.75 to 0.75
- lengths: int32 [128], P('req'), may hold values from 1 to 256, 16384 in all
- adapter_ids: int32 [128], P('req'), may hold values from 0 to 63, as said below
- adapter_slot: int32 [64], replicated, may hold values from 0 to 127, as said below
- down_store: bfloat16 [128, 3072, 32], P('req', 'tp'), may hold values from -0.109375 to 0.109375
- query_up_store: bfloat16 [128, 16, 1536], P('req', None, 'tp'), may hold values from -1.5 to 1.5
- key_value_store: bfloat16 [128, 16, 512], P('req', None, 'tp'), may hold values from -1.5 to 1.5
Outputs:
- context: bfloat16 [32768, 1536], P('req', 'tp')
Inputs may be any that keep to these rules, and one draw needn't show every extreme that they name: `adapter_ids`: exactly 16 distinct adapters are named among all 128 requests. `adapter_slot`: distinct adapters have distinct rows.
All inputs are finite; a program needn't handle non-finite values. No bound on the sum of `lengths` on one device may be relied on, other than what follows from the above.
Results may differ from a plain program's by a relative error of at most 0.0072.
Values may be sent and summed in bfloat16 or wider, within the bound.
No kernel may reach another device: no remote copies, remote signals or barrier semaphores. Data moves between devices by JAX's collectives and lax.ppermute only.
A program may use at most 64 MiB of HBM per device.

v0:
```python
import math

import jax
import jax.numpy as jnp
from jax import lax
from jax.sharding import PartitionSpec as P

HEADS = 12
HEAD_DIM = 128


adapter_scale = 0.5
rope_base = 100000000000.0


def rotate(field):
    half = field.shape[-1] // 2
    count = field.shape[-3]
    position = jnp.arange(count).astype(jnp.float32)
    inverse = rope_base ** (-(jnp.arange(half).astype(jnp.float32) * 2.0) / field.shape[-1])
    angle = position[:, None] * inverse[None, :]
    cosine = jnp.cos(angle)[:, None, :]
    sine = jnp.sin(angle)[:, None, :]
    first_half = field[..., :half]
    second_half = field[..., half:]
    return jnp.concatenate(
        [first_half * cosine - second_half * sine, second_half * cosine + first_half * sine],
        axis=-1,
    )


def lookup_slots(wanted, adapter_slot):
    table = jnp.arange(adapter_slot.shape[0], dtype=jnp.int32)
    matches = wanted[:, None] == table[None, :]
    return jnp.sum(jnp.where(matches, adapter_slot[None, :], 0), axis=1)


def local(
    states,
    query_weight,
    key_value_weight,
    lengths,
    adapter_ids,
    adapter_slot,
    down_store,
    query_up_store,
    key_value_store,
):
    tp_index = lax.axis_index("tp")
    req_dev = lengths.shape[0]
    rows_total = states.shape[0]
    slot_len = rows_total // req_dev
    q_cols = query_weight.shape[1]
    kv_cols = key_value_weight.shape[1]
    heads_here = q_cols // HEAD_DIM
    pooled = (
        lax.all_gather(down_store, "req", axis=0, tiled=True),
        lax.all_gather(query_up_store, "req", axis=0, tiled=True),
        lax.all_gather(key_value_store, "req", axis=0, tiled=True),
    )
    own_slots = lookup_slots(adapter_ids, adapter_slot)
    adapter_down, adapter_query, adapter_pair = (
        jnp.take(member, own_slots, axis=0) for member in pooled
    )
    full_down = lax.all_gather(adapter_down, "tp", axis=1, tiled=True)
    piece = lax.all_gather(states, "tp", axis=1, tiled=True)
    width = piece.shape[1]
    grouped = piece.reshape(req_dev, slot_len, width)
    query_total = jnp.dot(piece, query_weight, preferred_element_type=jnp.float32)
    key_value_sum = jnp.dot(piece, key_value_weight, preferred_element_type=jnp.float32)
    rank_sum = jnp.einsum("rsd,rdk->rsk", grouped, full_down, preferred_element_type=jnp.float32)
    rank_mid = rank_sum.astype(jnp.bfloat16)
    rank_cols = rank_mid.shape[2] // 2
    query_addition = jnp.einsum(
        "rsk,rkc->rsc",
        rank_mid[:, :, :rank_cols],
        adapter_query,
        preferred_element_type=jnp.float32,
    ).reshape(rows_total, q_cols)
    key_value_extra = jnp.einsum(
        "rsk,rkc->rsc", rank_mid[:, :, rank_cols:], adapter_pair, preferred_element_type=jnp.float32
    ).reshape(rows_total, kv_cols)
    query_plain = query_total + adapter_scale * query_addition
    key_value_own = (key_value_sum + adapter_scale * key_value_extra).astype(jnp.bfloat16)
    pair_all = lax.all_gather(key_value_own, "tp", axis=1, tiled=True)
    key_width = pair_all.shape[1] // 2
    kv_heads = key_width // HEAD_DIM
    group = HEADS // kv_heads
    kv_index = tp_index * heads_here // group
    key_block = lax.dynamic_slice_in_dim(pair_all, kv_index * HEAD_DIM, HEAD_DIM, 1)
    value_block = lax.dynamic_slice_in_dim(pair_all, key_width + kv_index * HEAD_DIM, HEAD_DIM, 1)
    queries = rotate(query_plain.reshape(req_dev, slot_len, heads_here, HEAD_DIM)).astype(
        jnp.bfloat16
    )
    keys_one = rotate(key_block.astype(jnp.float32).reshape(req_dev, slot_len, 1, HEAD_DIM)).astype(
        jnp.bfloat16
    )[:, :, 0, :]
    values_one = value_block.reshape(req_dev, slot_len, HEAD_DIM)
    scale = 1.0 / math.sqrt(HEAD_DIM)
    scores = (
        jnp.einsum("rqhd,rkd->rhqk", queries, keys_one, preferred_element_type=jnp.float32) * scale
    )
    position = jnp.arange(slot_len, dtype=jnp.int32)
    allowed = (position[None, None, :] <= position[None, :, None]) & (
        position[None, None, :] < lengths[:, None, None]
    )
    scores = jnp.where(allowed[:, None, :, :], scores, -jnp.inf)
    highest = jnp.max(scores, axis=-1, keepdims=True)
    expo = jnp.exp(scores - highest)
    weights = (expo / jnp.sum(expo, axis=-1, keepdims=True)).astype(jnp.bfloat16)
    context = jnp.einsum("rhqk,rkd->rqhd", weights, values_one, preferred_element_type=jnp.float32)
    live_rows = position[None, :] < lengths[:, None]
    context = jnp.where(live_rows[:, :, None, None], context, 0.0)
    return context.reshape(rows_total, q_cols).astype(jnp.bfloat16)


def solution(mesh):
    return jax.shard_map(
        local,
        mesh=mesh,
        in_specs=(
            P("req", "tp"),
            P(None, "tp"),
            P(None, "tp"),
            P("req"),
            P("req"),
            P(),
            P("req", "tp", None),
            P("req", None, "tp"),
            P("req", None, "tp"),
        ),
        out_specs=P("req", "tp"),
        check_vma=False,
    )
```

profile of v0, /device:TPU:1, one launch (start us, length us, event | category | flops | bytes accessed | tf_op | source)
XLA Modules:
  0.0 357.4 jit_solution(2716103049818812552)
XLA Ops:
  6.5 0.0 copy-start
  6.5 0.0 all-gather.4.cloned.1.call-start
  6.5 0.7 all-gather.4.cloned.1.call-update
  7.3 0.0 all-gather.6.cloned.1.call-start
  7.3 0.7 all-gather.6.cloned.1.call-update
  8.0 0.0 all-gather.8.cloned.1.call-start
  8.1 0.7 all-gather.8.cloned.1.call-update
  9.4 1.3 fusion.39
  13.3 0.0 copy-start.4
  13.4 0.0 copy-start.6
  13.4 0.0 copy-start.2
  13.4 97.6 %all_gather.21 = bf16[128,16,128]{2,1,0:T(8,128)(2,1)} all-gather(bf16[1,16,128]{2,1,0:T(8,128)(2,1)} %param.17), channel_id=1, replica_groups=mesh['req'=128,'tp'=4] {'req'}, dimensions={0}, use_global_device_ids=true | all-gather | bytes 528384 | tf_op jit(solution)/shard_map/all_gather | solution.py:59
  111.0 0.0 copy-done.6
  111.0 0.1 fusion.9
  111.1 0.0 copy-done.4
  111.1 0.0 copy-done.2
  111.1 1.2 multiply_cosine_fusion
  112.3 0.0 all-gather.4.cloned.1.call-done
  112.3 0.0 copy-done
  112.3 2.4 fusion.45
  114.7 82.6 %all-gather.6.cloned.1.call-done = bf16[128,768,32]{1,2,0:T(8,128)(2,1)} async-done(((bf16[1,768,32]{1,2,0:T(8,128)(2,1)}), bf16[128,768,32]{1,2,0:T(8,128)(2,1)}) %all-gather.6.cloned.1.call-update) | async-done | bytes 6291472 | tf_op jit(solution)/shard_map/all_gather | solution.py:57
  197.3 0.8 dynamic-slice_select_fusion
  198.1 10.1 %all_gather.20 = bf16[1,3072,32]{1,2,0:T(8,128)(2,1)S(1)} all-gather(bf16[1,768,32]{1,2,0:T(8,128)(2,1)S(1)} %dynamic-slice_select_fusion), channel_id=1, replica_groups=mesh['req'=128,'tp'=4] {'tp'}, dimensions={1}, use_global_device_ids=true | all-gather | bytes 245760 | tf_op jit(solution)/shard_map/all_gather | solution.py:65
  208.2 2.0 fusion.6
  210.2 124.0 %all-gather.8.cloned.1.call-done = bf16[128,16,384]{2,1,0:T(8,128)(2,1)} async-done(((bf16[1,16,384]{2,1,0:T(8,128)(2,1)}), bf16[128,16,384]{2,1,0:T(8,128)(2,1)}) %all-gather.8.cloned.1.call-update) | async-done | bytes 1572880 | tf_op jit(solution)/shard_map/all_gather | solution.py:58
  334.2 1.0 fusion.2
  335.2 0.2 copy.21
  335.4 0.2 copy.30
  335.6 0.2 copy.31
  335.7 0.9 convolution_multiply_fusion.2
  336.6 0.0 copy-start.3
  336.6 0.0 copy-start.5
  336.6 0.0 copy-start.1
  336.6 2.2 fusion.5
  338.8 9.6 %all_gather.22 = bf16[256,512]{1,0:T(8,128)(2,1)S(1)} all-gather(bf16[256,128]{1,0:T(8,128)(2,1)S(1)} %fusion.5), channel_id=1, replica_groups=mesh['req'=128,'tp'=4] {'tp'}, dimensions={1}, use_global_device_ids=true | all-gather | bytes 327680 | tf_op jit(solution)/shard_map/all_gather | solution.py:85
  348.5 0.0 copy-done.3
  348.5 0.0 copy-done.5
  348.5 0.6 fusion.29
  349.1 0.0 copy-done.1
  349.1 0.0 copy-start.7
  349.1 0.1 fusion.10
  349.2 0.4 fusion.44
  349.6 0.1 fusion.7
  349.7 0.0 copy-done.7
  349.8 0.3 fusion.4
  350.1 0.8 copy.26
  (5 shorter events, 0.1 us)
Async XLA Ops:
  6.5 105.8 %copy-start = (bf16[3072,384]{1,0:T(8,128)(2,1)S(1)}, bf16[3072,384]{1,0:T(8,128)(2,1)}, u32[]{:S(2)}) copy-start(bf16[3072,384]{1,0:T(8,128)(2,1)} %param.10) | copy-start | bytes 7077892
  6.5 105.8 %all-gather.4.cloned.1.call-start = ((), (), s32[]{:S(2)}) async-start(), calls=%async_computation | async-start | bytes 1966080 | tf_op jit(solution)/shard_map/all_gather | solution.py:66
  7.3 190.1 %all-gather.6.cloned.1.call-start = ((), (), s32[]{:S(2)}) async-start(), calls=%async_computation.1 | async-start | bytes 6340608 | tf_op jit(solution)/shard_map/all_gather | solution.py:57
  8.0 326.2 %all-gather.8.cloned.1.call-start = ((), (), s32[]{:S(2)}) async-start(), calls=%async_computation.2 | async-start | bytes 1585152 | tf_op jit(solution)/shard_map/all_gather | solution.py:58
  13.3 97.8 %copy-start.4 = (f32[64]{0:T(128)}, f32[64]{0:T(128)S(1)}, u32[]{:S(2)}) copy-start(f32[64]{0:T(128)S(1)} %multiply_power_fusion) | copy-start | bytes 772
  13.4 97.6 %copy-start.6 = (pred[256]{0:T(512)(128)(4,1)}, pred[256]{0:T(512)(128)(4,1)S(1)}, u32[]{:S(2)}) copy-start(pred[256]{0:T(512)(128)(4,1)S(1)} %iota_compare_fusion.1) | copy-start | bytes 772
  13.4 97.7 %copy-start.2 = (f32[256]{0:T(256)}, f32[256]{0:T(256)S(1)}, u32[]{:S(2)}) copy-start(f32[256]{0:T(256)S(1)} %iota_convert_fusion) | copy-start | bytes 3076
  336.6 11.9 %copy-start.3 = (f32[256]{0:T(256)S(1)}, f32[256]{0:T(256)}, u32[]{:S(2)}) copy-start(f32[256]{0:T(256)} %copy-done.2) | copy-start | bytes 3076
  336.6 11.9 %copy-start.5 = (f32[64]{0:T(128)S(1)}, f32[64]{0:T(128)}, u32[]{:S(2)}) copy-start(f32[64]{0:T(128)} %copy-done.4) | copy-start | bytes 772
  336.6 12.5 %copy-start.1 = (f32[256,64]{1,0:T(8,128)S(1)}, f32[256,64]{1,0:T(8,128)}, u32[]{:S(2)}) copy-start(f32[256,64]{1,0:T(8,128)} %get-tuple-element.45) | copy-start | bytes 196612
  349.1 0.7 copy-start.7
Sparse Core Ops, SparseCore 0:
  9.5 39.4 all-gather.3
  52.1 145.1 all-gather.5
  200.4 133.7 all-gather.7
where the time goes:
time: 359 us; the launch traced here: 357 us
  waiting for transfers between devices  209 us (58%)
  blocking collectives  117 us (33%)
  between operations  16.5 us (5%)
  matrix products  9.02 us (3%)
  other arithmetic  4.29 us (1%)
    all_gather x1, waiting for transfers between devices, local(): lax.all_gather(query_up_store, 'req', axis=0, tiled=True)  124 us
    all_gather x1, blocking collectives, local(): lax.all_gather(key_value_store, 'req', axis=0, tiled=True)  97.6 us
    all_gather x1, waiting for transfers between devices, local(): lax.all_gather(down_store, 'req', axis=0, tiled=True)  82.6 us
    all_gather x1, blocking collectives, local(): full_down = lax.all_gather(adapter_down, 'tp', axis=1, tiled=True)  10.1 us
    all_gather x1, blocking collectives, local(): pair_all = lax.all_gather(key_value_own, 'tp', axis=1, tiled=True)  9.64 us
  transfers between devices with their start and end apart: 3, of which 2 were waited for; matrix products, arithmetic and copies ran while one was open for 2% of the time, Pallas kernels for 0%

commit v1 on v0

--- a/solution.py
+++ b/solution.py
@@ -7,6 +7,7 @@
 
 HEADS = 12
 HEAD_DIM = 128
+ACTIVE = 16
 
 
 adapter_scale = 0.5
@@ -35,6 +36,12 @@
     return jnp.sum(jnp.where(matches, adapter_slot[None, :], 0), axis=1)
 
 
+def shifted(x, shift, n, pairs=None):
+    if pairs is None:
+        pairs = [(i, (i + shift) % n) for i in range(n)]
+    return lax.ppermute(x, "tp", pairs)
+
+
 def local(
     states,
     query_weight,
@@ -47,30 +54,60 @@
     key_value_store,
 ):
     tp_index = lax.axis_index("tp")
+    req_index = lax.axis_index("req")
+    n_tp = lax.axis_size("tp")
+    n_req = lax.axis_size("req")
     req_dev = lengths.shape[0]
     rows_total = states.shape[0]
     slot_len = rows_total // req_dev
     q_cols = query_weight.shape[1]
     kv_cols = key_value_weight.shape[1]
     heads_here = q_cols // HEAD_DIM
-    pooled = (
-        lax.all_gather(down_store, "req", axis=0, tiled=True),
-        lax.all_gather(query_up_store, "req", axis=0, tiled=True),
-        lax.all_gather(key_value_store, "req", axis=0, tiled=True),
+    store_rows = down_store.shape[0]
+
+    ids_all = lax.all_gather(adapter_ids, "req", axis=0, tiled=True)
+    slots_all = lookup_slots(ids_all, adapter_slot)
+    slot_range = jnp.arange(store_rows * n_req, dtype=jnp.int32)
+    used = jnp.any(slots_all[:, None] == slot_range[None, :], axis=0).astype(jnp.int32)
+    prefix = jnp.sum(
+        jnp.where(slot_range[None, :] < slot_range[:, None], used[None, :], 0), axis=1
+    )
+    own_rows = req_index * store_rows + jnp.arange(store_rows, dtype=jnp.int32)
+    place = (jnp.arange(ACTIVE, dtype=jnp.int32)[None, :] == prefix[own_rows][:, None]) & (
+        used[own_rows][:, None] > 0
+    )
+
+    def compact(member):
+        picked = jnp.where(
+            place[:, :, None, None], member[:, None, :, :], jnp.zeros((), member.dtype)
+        )
+        return jnp.sum(picked, axis=0)
+
+    pooled = lax.psum(
+        (compact(down_store), compact(query_up_store), compact(key_value_store)), "req"
     )
     own_slots = lookup_slots(adapter_ids, adapter_slot)
+    own_k = prefix[own_slots]
     adapter_down, adapter_query, adapter_pair = (
-        jnp.take(member, own_slots, axis=0) for member in pooled
+        jnp.take(member, own_k, axis=0) for member in pooled
     )
-    full_down = lax.all_gather(adapter_down, "tp", axis=1, tiled=True)
-    piece = lax.all_gather(states, "tp", axis=1, tiled=True)
-    width = piece.shape[1]
-    grouped = piece.reshape(req_dev, slot_len, width)
+
+    blocks = [states] + [shifted(states, s, n_tp) for s in range(1, n_tp)]
+    stacked = jnp.stack(blocks, axis=0)
+    source = (tp_index - jnp.arange(n_tp, dtype=jnp.int32)) % n_tp
+    piece = jnp.take(stacked, source, axis=0)
+    piece = jnp.transpose(piece, (1, 0, 2)).reshape(rows_total, -1)
+
+    grouped_local = states.reshape(req_dev, slot_len, states.shape[1])
+    rank_part = jnp.einsum(
+        "rsd,rdk->rsk", grouped_local, adapter_down, preferred_element_type=jnp.float32
+    )
+    rank_sum = lax.optimization_barrier(lax.psum(rank_part, "tp"))
+    rank_mid = rank_sum.astype(jnp.bfloat16)
+    rank_cols = rank_mid.shape[2] // 2
+
     query_total = jnp.dot(piece, query_weight, preferred_element_type=jnp.float32)
     key_value_sum = jnp.dot(piece, key_value_weight, preferred_element_type=jnp.float32)
-    rank_sum = jnp.einsum("rsd,rdk->rsk", grouped, full_down, preferred_element_type=jnp.float32)
-    rank_mid = rank_sum.astype(jnp.bfloat16)
-    rank_cols = rank_mid.shape[2] // 2
     query_addition = jnp.einsum(
         "rsk,rkc->rsc",
         rank_mid[:, :, :rank_cols],
@@ -82,13 +119,17 @@
     ).reshape(rows_total, kv_cols)
     query_plain = query_total + adapter_scale * query_addition
     key_value_own = (key_value_sum + adapter_scale * key_value_extra).astype(jnp.bfloat16)
-    pair_all = lax.all_gather(key_value_own, "tp", axis=1, tiled=True)
-    key_width = pair_all.shape[1] // 2
-    kv_heads = key_width // HEAD_DIM
-    group = HEADS // kv_heads
-    kv_index = tp_index * heads_here // group
-    key_block = lax.dynamic_slice_in_dim(pair_all, kv_index * HEAD_DIM, HEAD_DIM, 1)
-    value_block = lax.dynamic_slice_in_dim(pair_all, key_width + kv_index * HEAD_DIM, HEAD_DIM, 1)
+
+    from_left = shifted(key_value_own, 1, n_tp, [(0, 1), (1, 2)])
+    from_right = shifted(key_value_own, -1, n_tp, [(2, 1), (3, 2)])
+    from_far = shifted(key_value_own, 2, n_tp, [(1, 3), (2, 0)])
+    key_block = jnp.where(
+        tp_index == 0, key_value_own, jnp.where(tp_index == 3, from_far, from_left)
+    )
+    value_block = jnp.where(
+        tp_index == 3, key_value_own, jnp.where(tp_index == 0, from_far, from_right)
+    )
+
     queries = rotate(query_plain.reshape(req_dev, slot_len, heads_here, HEAD_DIM)).astype(
         jnp.bfloat16
     )

time: 359 us -> 439 us (1.22); the launches traced: 357 us -> 432 us
  waiting for transfers between devices: 209 us -> 312 us
  blocking collectives: 117 us -> 44.1 us
  starting transfers between devices: 0.08 us -> 18.3 us
  other arithmetic: 4.29 us -> 19 us
  local copies, waits for them, and re-layouts: 1.42 us -> 10.5 us
    psum x0 -> x1, waiting for transfers between devices: none -> 312 us  [local(): lax.psum((compact(down_store), compact(query_up_store), compact(key_value...]
    all_gather x3 -> x0, waiting for transfers between devices: 207 us -> none  [the longest x1 124 us: local(): lax.all_gather(query_up_store, 'req', axis=0, tiled=True)]
    all_gather x3 -> x0, blocking collectives: 117 us -> none  [the longest x1 97.6 us: local(): lax.all_gather(key_value_store, 'req', axis=0, tiled=True)]
    unnamed x0 -> x1, blocking collectives: none -> 30.8 us
    ppermute x0 -> x6, starting transfers between devices: none -> 18.3 us  [shifted(): return lax.ppermute(x, 'tp', pairs)]
    psum x0 -> x1, blocking collectives: none -> 13.3 us  [local(): rank_sum = lax.optimization_barrier(lax.psum(rank_part, 'tp'))]
    select_n x1 -> x5, other arithmetic: 0.81 us -> 8.04 us  [the longest x3 4.67 us: compact(): jnp.where(place[:, :, None, None], member[:, None, :, :], jnp.zeros((), m...]
    gather x0 -> x3, local copies, waits for them, and re-layouts: none -> 4.49 us  [the longest x1 3.2 us: local(): piece = jnp.take(stacked, source, axis=0)]
  transfers between devices with their start and end apart: 3 -> 7, of which waited for: 2 -> 1; matrix products, arithmetic and copies ran while one was open for 2% -> 8% of each run, Pallas kernels for 0% -> 0%
where the time goes in v1:
time: 439 us; the launch traced here: 432 us
  waiting for transfers between devices  312 us (71%)
  blocking collectives  44.1 us (10%)
  between operations  19.3 us (4%)
  other arithmetic  19 us (4%)
  starting transfers between devices  18.3 us (4%)
  local copies, waits for them, and re-layouts  10.5 us (2%)
  matrix products  9.5 us (2%)
    psum x1, waiting for transfers between devices, local(): lax.psum((compact(down_store), compact(query_up_store), compact(key_value...  312 us
    unnamed x1, blocking collectives  30.8 us
    ppermute x6, starting transfers between devices, shifted(): return lax.ppermute(x, 'tp', pairs)  18.3 us
    psum x1, blocking collectives, local(): rank_sum = lax.optimization_barrier(lax.psum(rank_part, 'tp'))  13.3 us
  transfers between devices with their start and end apart: 7, of which 1 were waited for; matrix products, arithmetic and copies ran while one was open for 8% of the time, Pallas kernels for 0%

profile of v1, /device:TPU:1, one launch (start us, length us, event | category | flops | bytes accessed | tf_op | source)
XLA Modules:
  0.0 432.3 jit_solution(9131677211873605731)
XLA Ops:
  6.5 4.2 collective-permute-start
  10.7 4.4 %collective-permute-start.1 = (bf16[256,768]{1,0:T(8,128)(2,1)}, bf16[256,768]{1,0:T(8,128)(2,1)S(1)}, u32[]{:S(2)}, u32[]{:S(2)}) collective-permute-start(bf16[256,768]{1,0:T(8,128)(2,1)} %param.9), channel_id=1, source_target_pairs={{0,2},{1,3},{2,0},{3,1},{4,6},{5,7},{6,4},{7,5},{8,10},{9,11},{10,... | collective-permute-start | bytes 1179656 | tf_op jit(solution)/shard_map/ppermute | solution.py:42
  15.1 3.1 collective-permute-start.2
  18.8 1.4 fusion.44
  21.6 1.3 dynamic-slice.21
  22.9 0.7 dynamic-update-slice.6
  23.6 30.8 %all-reduce = s32[128]{0:T(128)S(1)} all-reduce(s32[128]{0:T(128)S(1)} %dynamic-update-slice.6), channel_id=1, replica_groups=mesh['req'=128,'tp'=4] {'req'}, use_global_device_ids=true, to_apply=%add | all-reduce | flops 128 | bytes 1024
  54.5 0.7 select_reduce_fusion.1
  55.2 0.1 fusion.27
  55.3 0.1 select_reduce_fusion
  55.5 0.6 dynamic-slice.17
  57.4 0.7 fusion.53
  58.1 0.7 compare_and_fusion
  58.8 1.8 broadcast_select_fusion
  60.6 1.5 broadcast_select_fusion.1
  62.1 1.4 broadcast_select_fusion.2
  63.5 0.0 all-reduce.4.cloned.1.call-update
  63.5 0.6 fusion.47
  64.1 0.5 compare_and_fusion.1
  65.3 0.7 fusion.8
  67.7 0.7 pad_clamp_fusion
  68.3 1.2 multiply_cosine_fusion
  69.6 0.0 collective-permute-done
  69.6 0.0 collective-permute-done.1
  69.6 2.3 pad_maximum_fusion
  72.0 3.2 gather_fusion
  75.2 2.8 select_bitcast_fusion
  77.9 2.6 copy.31
  80.5 2.4 fusion.55
  83.0 311.6 %all-reduce.4.cloned.1.call-done = (bf16[16,16,384]{2,1,0:T(8,128)(2,1)}, bf16[16,768,32]{1,2,0:T(8,128)(2,1)}, bf16[16,16,128]{2,1,0:T(8,128)(2,1)}) async-done(((bf16[16,16,384]{2,1,0:T(8,128)(2,1)}, bf16[16,768,32]{1,2,0:T(8,128)(2,1)}, bf16[16,16,128]{2,1,0:T(8,128)(2,1)}), (bf16[16,16,384]{2,1,0:T(8,128)(2,1)}, bf16[16,768,32]{1,2,0:T(8,128)(2,1)}, ...) | async-done | bytes 1048592 | tf_op jit(solution)/shard_map/psum | solution.py:86
  394.5 1.0 convolution_bitcast_fusion.1
  395.6 13.3 %psum.29 = bf16[1,256,32]{1,2,0:T(8,128)(2,1)S(1)} all-reduce(f32[1,256,32]{1,2,0:T(8,128)S(1)} %convolution_bitcast_fusion.1), channel_id=1, replica_groups=mesh['req'=128,'tp'=4] {'tp'}, use_global_device_ids=true, to_apply=%region_5.6 | all-reduce | flops 8192 | bytes 49152 | tf_op jit(solution)/shard_map/psum | solution.py:105
  408.9 0.9 convolution_multiply_fusion.2
  409.8 2.7 fusion.5
  412.4 1.3 collective-permute-start.3
  413.7 4.1 collective-permute-start.5
  417.8 1.3 collective-permute-start.4
  419.1 1.0 fusion.2
  420.1 0.2 copy.32
  420.3 0.2 copy.41
  420.4 0.2 copy.42
  420.6 1.1 fusion.9
  421.7 0.9 bitcast_convert_fusion
  422.6 0.3 fusion.33
  422.9 0.4 fusion.54
  423.3 0.1 fusion.6
  423.5 1.1 fusion.4
  424.6 0.8 copy.37
  (19 shorter events, 0.1 us)
Async XLA Ops:
  6.5 74.0 %copy-start = (bf16[3072,384]{1,0:T(8,128)(2,1)S(1)}, bf16[3072,384]{1,0:T(8,128)(2,1)}, u32[]{:S(2)}) copy-start(bf16[3072,384]{1,0:T(8,128)(2,1)} %param.10) | copy-start | bytes 7077892
  6.5 63.1 %copy-start.1 = (bf16[256,768]{1,0:T(8,128)(2,1)S(1)}, bf16[256,768]{1,0:T(8,128)(2,1)}, u32[]{:S(2)}) copy-start(bf16[256,768]{1,0:T(8,128)(2,1)} %param.9) | copy-start | bytes 1179652
  6.5 388.0 %all-reduce.4.cloned.1.call-start = ((), (), s32[]{:S(2)}) async-start(), calls=%async_computation | async-start | bytes 2097152 | tf_op jit(solution)/shard_map/psum | solution.py:86
  6.5 63.1 %collective-permute-start = (bf16[256,768]{1,0:T(8,128)(2,1)}, bf16[256,768]{1,0:T(8,128)(2,1)S(1)}, u32[]{:S(2)}, u32[]{:S(2)}) collective-permute-start(bf16[256,768]{1,0:T(8,128)(2,1)} %param.9), channel_id=1, source_target_pairs={{0,1},{1,2},{2,3},{3,0},{4,5},{5,6},{6,7},{7,4},{8,9},{9,10},{10,1... | collective-permute-start | bytes 1179656 | tf_op jit(solution)/shard_map/ppermute | solution.py:42
  10.7 58.8 %collective-permute-start.1 = (bf16[256,768]{1,0:T(8,128)(2,1)}, bf16[256,768]{1,0:T(8,128)(2,1)S(1)}, u32[]{:S(2)}, u32[]{:S(2)}) collective-permute-start(bf16[256,768]{1,0:T(8,128)(2,1)} %param.9), channel_id=1, source_target_pairs={{0,2},{1,3},{2,0},{3,1},{4,6},{5,7},{6,4},{7,5},{8,10},{9,11},{10,... | collective-permute-start | bytes 1179656 | tf_op jit(solution)/shard_map/ppermute | solution.py:42
  15.1 54.5 %collective-permute-start.2 = (bf16[256,768]{1,0:T(8,128)(2,1)}, bf16[256,768]{1,0:T(8,128)(2,1)}, u32[]{:S(2)}, u32[]{:S(2)}) collective-permute-start(bf16[256,768]{1,0:T(8,128)(2,1)} %param.9), channel_id=1, source_target_pairs={{0,3},{1,0},{2,1},{3,2},{4,7},{5,4},{6,5},{7,6},{8,11},{9,8},{10,9... | collective-permute-start | bytes 1179656 | tf_op jit(solution)/shard_map/ppermute | solution.py:42
  72.0 3.2 copy-start.3
  412.4 9.2 %collective-permute-start.3 = (bf16[256,128]{0,1:T(8,128)(2,1)}, bf16[256,128]{0,1:T(8,128)(2,1)}, u32[]{:S(2)}, u32[]{:S(2)}) collective-permute-start(bf16[256,128]{0,1:T(8,128)(2,1)} %fusion.5), channel_id=1, source_target_pairs={{1,3},{2,0},{5,7},{6,4},{9,11},{10,8},{13,15},{14,12},{17,19},{18,... | collective-permute-start | bytes 196616 | tf_op jit(solution)/shard_map/ppermute | solution.py:42
  413.7 8.0 %collective-permute-start.5 = (bf16[256,128]{0,1:T(8,128)(2,1)}, bf16[256,128]{0,1:T(8,128)(2,1)}, u32[]{:S(2)}, u32[]{:S(2)}) collective-permute-start(bf16[256,128]{0,1:T(8,128)(2,1)} %fusion.5), channel_id=1, source_target_pairs={{0,1},{1,2},{4,5},{5,6},{8,9},{9,10},{12,13},{13,14},{16,17},{17,1... | collective-permute-start | bytes 196616 | tf_op jit(solution)/shard_map/ppermute | solution.py:42
  417.8 5.7 %collective-permute-start.4 = (bf16[256,128]{0,1:T(8,128)(2,1)}, bf16[256,128]{0,1:T(8,128)(2,1)}, u32[]{:S(2)}, u32[]{:S(2)}) collective-permute-start(bf16[256,128]{0,1:T(8,128)(2,1)} %fusion.5), channel_id=1, source_target_pairs={{2,1},{3,2},{6,5},{7,6},{10,9},{11,10},{14,13},{15,14},{18,17},{19... | collective-permute-start | bytes 196616 | tf_op jit(solution)/shard_map/ppermute | solution.py:42
  420.4 2.5 copy-start.2
Sparse Core Ops, SparseCore 0:
  63.6 330.9 all-reduce.3

commit v2 on v1

--- a/solution.py
+++ b/solution.py
@@ -36,10 +36,18 @@
     return jnp.sum(jnp.where(matches, adapter_slot[None, :], 0), axis=1)
 
 
-def shifted(x, shift, n, pairs=None):
+def shifted(x, shift, n, pairs=None, axis="tp"):
     if pairs is None:
         pairs = [(i, (i + shift) % n) for i in range(n)]
-    return lax.ppermute(x, "tp", pairs)
+    return lax.ppermute(x, axis, pairs)
+
+
+def doubled_sum(x, axis, n):
+    step = 1
+    while step < n:
+        x = x + shifted(x, step, n, axis=axis)
+        step *= 2
+    return x
 
 
 def local(
@@ -54,9 +62,13 @@
     key_value_store,
 ):
     tp_index = lax.axis_index("tp")
-    req_index = lax.axis_index("req")
+    iz = lax.axis_index("rz")
+    iy = lax.axis_index("ry")
     n_tp = lax.axis_size("tp")
-    n_req = lax.axis_size("req")
+    nz = lax.axis_size("rz")
+    ny = lax.axis_size("ry")
+    n_req = nz * ny
+    me = iz * ny + iy
     req_dev = lengths.shape[0]
     rows_total = states.shape[0]
     slot_len = rows_total // req_dev
@@ -64,33 +76,40 @@
     kv_cols = key_value_weight.shape[1]
     heads_here = q_cols // HEAD_DIM
     store_rows = down_store.shape[0]
+    assert req_dev == 1 and store_rows == 1 and ACTIVE % ny == 0
 
-    ids_all = lax.all_gather(adapter_ids, "req", axis=0, tiled=True)
-    slots_all = lookup_slots(ids_all, adapter_slot)
-    slot_range = jnp.arange(store_rows * n_req, dtype=jnp.int32)
+    own_slot = lookup_slots(adapter_ids, adapter_slot)
+    req_range = jnp.arange(n_req, dtype=jnp.int32)
+    slots_all = jnp.where(req_range == me, own_slot[0], 0)
+    slots_all = doubled_sum(doubled_sum(slots_all, "ry", ny), "rz", nz)
+    slot_range = jnp.arange(n_req * store_rows, dtype=jnp.int32)
     used = jnp.any(slots_all[:, None] == slot_range[None, :], axis=0).astype(jnp.int32)
     prefix = jnp.sum(
         jnp.where(slot_range[None, :] < slot_range[:, None], used[None, :], 0), axis=1
     )
-    own_rows = req_index * store_rows + jnp.arange(store_rows, dtype=jnp.int32)
-    place = (jnp.arange(ACTIVE, dtype=jnp.int32)[None, :] == prefix[own_rows][:, None]) & (
-        used[own_rows][:, None] > 0
+
+    down_rows = down_store[0].T.reshape(-1, 128)
+    query_rows = query_up_store[0].reshape(-1, 128)
+    pair_rows = key_value_store[0].reshape(-1, 128)
+    n_down, n_query = down_rows.shape[0], query_rows.shape[0]
+    row = jnp.concatenate([down_rows, query_rows, pair_rows], axis=0)
+
+    plane = jnp.stack([row] + [shifted(row, s, ny, axis="ry") for s in range(1, ny)])
+    per_column = ACTIVE // ny
+    back = jnp.arange(ny, dtype=jnp.int32)
+    plane_slots = iz * ny + (iy - back) % ny
+    wanted = iy + ny * jnp.arange(per_column, dtype=jnp.int32)
+    choose = (used[plane_slots][None, :] > 0) & (prefix[plane_slots][None, :] == wanted[:, None])
+    column = jnp.sum(
+        jnp.where(choose[:, :, None, None], plane[None], jnp.zeros((), plane.dtype)), axis=1
     )
-
-    def compact(member):
-        picked = jnp.where(
-            place[:, :, None, None], member[:, None, :, :], jnp.zeros((), member.dtype)
-        )
-        return jnp.sum(picked, axis=0)
-
-    pooled = lax.psum(
-        (compact(down_store), compact(query_up_store), compact(key_value_store)), "req"
-    )
-    own_slots = lookup_slots(adapter_ids, adapter_slot)
-    own_k = prefix[own_slots]
-    adapter_down, adapter_query, adapter_pair = (
-        jnp.take(member, own_k, axis=0) for member in pooled
-    )
+    column = doubled_sum(column, "rz", nz)
+    gathered = jnp.stack([column] + [shifted(column, s, ny, axis="ry") for s in range(1, ny)])
+    own_k = prefix[own_slot[0]]
+    picked = gathered[(iy - own_k % ny) % ny, own_k // ny]
+    down_t = picked[:n_down].reshape(down_store.shape[2], down_store.shape[1])
+    adapter_query = picked[n_down:n_down + n_query].reshape(query_up_store.shape[1:])
+    adapter_pair = picked[n_down + n_query:].reshape(key_value_store.shape[1:])
 
     blocks = [states] + [shifted(states, s, n_tp) for s in range(1, n_tp)]
     stacked = jnp.stack(blocks, axis=0)
@@ -98,25 +117,21 @@
     piece = jnp.take(stacked, source, axis=0)
     piece = jnp.transpose(piece, (1, 0, 2)).reshape(rows_total, -1)
 
-    grouped_local = states.reshape(req_dev, slot_len, states.shape[1])
-    rank_part = jnp.einsum(
-        "rsd,rdk->rsk", grouped_local, adapter_down, preferred_element_type=jnp.float32
-    )
-    rank_sum = lax.optimization_barrier(lax.psum(rank_part, "tp"))
+    rank_part = jnp.einsum("kd,sd->ks", down_t, states, preferred_element_type=jnp.float32)
+    rank_sum = rank_part
+    for s in range(1, n_tp):
+        rank_sum = rank_sum + shifted(rank_part, s, n_tp)
     rank_mid = rank_sum.astype(jnp.bfloat16)
-    rank_cols = rank_mid.shape[2] // 2
+    rank_cols = rank_mid.shape[0] // 2
 
     query_total = jnp.dot(piece, query_weight, preferred_element_type=jnp.float32)
     key_value_sum = jnp.dot(piece, key_value_weight, preferred_element_type=jnp.float32)
     query_addition = jnp.einsum(
-        "rsk,rkc->rsc",
-        rank_mid[:, :, :rank_cols],
-        adapter_query,
-        preferred_element_type=jnp.float32,
-    ).reshape(rows_total, q_cols)
+        "ks,kc->sc", rank_mid[:rank_cols], adapter_query, preferred_element_type=jnp.float32
+    )
     key_value_extra = jnp.einsum(
-        "rsk,rkc->rsc", rank_mid[:, :, rank_cols:], adapter_pair, preferred_element_type=jnp.float32
-    ).reshape(rows_total, kv_cols)
+        "ks,kc->sc", rank_mid[rank_cols:], adapter_pair, preferred_element_type=jnp.float32
+    )
     query_plain = query_total + adapter_scale * query_addition
     key_value_own = (key_value_sum + adapter_scale * key_value_extra).astype(jnp.bfloat16)
 
@@ -156,20 +171,26 @@
 
 
 def solution(mesh):
+    n_req = mesh.shape["req"]
+    ny = 8 if n_req % 8 == 0 else 1
+    split = jax.sharding.Mesh(
+        mesh.devices.reshape(n_req // ny, ny, mesh.shape["tp"]), ("rz", "ry", "tp")
+    )
+    req = ("rz", "ry")
     return jax.shard_map(
         local,
-        mesh=mesh,
+        mesh=split,
         in_specs=(
-            P("req", "tp"),
+            P(req, "tp"),
             P(None, "tp"),
             P(None, "tp"),
-            P("req"),
-            P("req"),
+            P(req),
+            P(req),
             P(),
-            P("req", "tp", None),
-            P("req", None, "tp"),
-            P("req", None, "tp"),
+            P(req, "tp", None),
+            P(req, None, "tp"),
+            P(req, None, "tp"),
         ),
-        out_specs=P("req", "tp"),
+        out_specs=P(req, "tp"),
         check_vma=False,
     )

time: 439 us -> 221 us (0.50); the launches traced: 432 us -> 220 us
  waiting for transfers between devices: 312 us -> 59.5 us
  starting transfers between devices: 18.3 us -> 116 us
  blocking collectives: 44.1 us -> 0 us
  between operations: 19.3 us -> 6.71 us
  local copies, waits for them, and re-layouts: 10.5 us -> 15.4 us
    psum x1 -> x0, waiting for transfers between devices: 312 us -> none  [local(): lax.psum((compact(down_store), compact(query_up_store), compact(key_value...]
    ppermute x6 -> x34, starting transfers between devices: 18.3 us -> 116 us  [shifted(): return lax.ppermute(x, axis, pairs)]
    ppermute x6 -> x34, waiting for transfers between devices: 0.02 us -> 59.5 us  [shifted(): return lax.ppermute(x, axis, pairs)]
    unnamed x1 -> x0, blocking collectives: 30.8 us -> none
    psum x1 -> x0, blocking collectives: 13.3 us -> none  [local(): rank_sum = lax.optimization_barrier(lax.psum(rank_part, 'tp'))]
  transfers between devices with their start and end apart: 7 -> 34, of which waited for: 1 -> 18; matrix products, arithmetic and copies ran while one was open for 8% -> 14% of each run, Pallas kernels for 0% -> 0%
where the time goes in v2:
time: 221 us; the launch traced here: 220 us
  starting transfers between devices  116 us (52%)
  waiting for transfers between devices  59.5 us (27%)
  local copies, waits for them, and re-layouts  15.4 us (7%)
  other arithmetic  15.3 us (7%)
  between operations  6.71 us (3%)
  matrix products  6.58 us (3%)
    ppermute x34, starting transfers between devices, shifted(): return lax.ppermute(x, axis, pairs)  116 us
    ppermute x34, waiting for transfers between devices, shifted(): return lax.ppermute(x, axis, pairs)  59.5 us
  transfers between devices with their start and end apart: 34, of which 18 were waited for; matrix products, arithmetic and copies ran while one was open for 14% of the time, Pallas kernels for 0%

profile of v2, /device:TPU:1, one launch (start us, length us, event | category | flops | bytes accessed | tf_op | source)
XLA Modules:
  0.0 219.9 jit_solution(18189811311705593907)
XLA Ops:
  2.4 5.5 %collective-permute-start.15 = (bf16[256,128]{1,0:T(8,128)(2,1)S(1)}, bf16[256,128]{1,0:T(8,128)(2,1)S(1)}, u32[]{:S(2)}, u32[]{:S(2)}) collective-permute-start(bf16[256,128]{1,0:T(8,128)(2,1)S(1)} %pad_maximum_fusion.1), channel_id=1, source_target_pairs={{0,24},{4,28},{8,0},{12,4},{16,8},{20,12},{24,16},{28,20},{1,25},{... | collective-permute-start | bytes 196616 | tf_op jit(solution)/shard_map/ppermute | solution.py:42
  7.9 3.2 %collective-permute-start.14 = (bf16[256,128]{1,0:T(8,128)(2,1)S(1)}, bf16[256,128]{1,0:T(8,128)(2,1)S(1)}, u32[]{:S(2)}, u32[]{:S(2)}) collective-permute-start(bf16[256,128]{1,0:T(8,128)(2,1)S(1)} %pad_maximum_fusion.1), channel_id=1, source_target_pairs={{0,20},{4,24},{8,28},{12,0},{16,4},{20,8},{24,12},{28,16},{1,21},{... | collective-permute-start | bytes 196616 | tf_op jit(solution)/shard_map/ppermute | solution.py:42
  11.1 7.3 %collective-permute-start.13 = (bf16[256,128]{1,0:T(8,128)(2,1)S(1)}, bf16[256,128]{1,0:T(8,128)(2,1)}, u32[]{:S(2)}, u32[]{:S(2)}) collective-permute-start(bf16[256,128]{1,0:T(8,128)(2,1)S(1)} %pad_maximum_fusion.1), channel_id=1, source_target_pairs={{0,16},{4,20},{8,24},{12,28},{16,0},{20,4},{24,8},{28,12},{1,17},{... | collective-permute-start | bytes 196616 | tf_op jit(solution)/shard_map/ppermute | solution.py:42
  18.5 1.9 collective-permute-start.12
  21.1 1.4 fusion.36
  24.9 3.4 %collective-permute-start.4 = (s32[128]{0:T(128)S(1)}, s32[128]{0:T(128)S(1)}, u32[]{:S(2)}, u32[]{:S(2)}) collective-permute-start(s32[128]{0:T(128)S(1)} %fusion.56), channel_id=1, source_target_pairs={{0,8},{4,12},{8,16},{12,20},{16,24},{20,28},{24,0},{28,4},{1,9},{5... | collective-permute-start | bytes 1544 | tf_op jit(solution)/shard_map/ppermute | solution.py:42
  31.1 4.4 %collective-permute-start.5 = (s32[128]{0:T(128)S(1)}, s32[128]{0:T(128)S(1)}, u32[]{:S(2)}, u32[]{:S(2)}) collective-permute-start(s32[128]{0:T(128)S(1)} %fusion.57), channel_id=1, source_target_pairs={{0,16},{4,20},{8,24},{12,28},{16,0},{20,4},{24,8},{28,12},{1,17},{... | collective-permute-start | bytes 1544 | tf_op jit(solution)/shard_map/ppermute | solution.py:42
  36.9 1.9 collective-permute-start.6
  38.8 7.5 %collective-permute-done.6 = s32[128]{0:T(128)S(1)} collective-permute-done((s32[128]{0:T(128)S(1)}, s32[128]{0:T(128)S(1)}, u32[]{:S(2)}, u32[]{:S(2)}) %collective-permute-start.6) | collective-permute-done | bytes 544 | tf_op jit(solution)/shard_map/ppermute | solution.py:42
  46.3 1.9 collective-permute-start.7
  48.2 4.5 %collective-permute-done.7 = s32[128]{0:T(128)S(1)} collective-permute-done((s32[128]{0:T(128)S(1)}, s32[128]{0:T(128)S(1)}, u32[]{:S(2)}, u32[]{:S(2)}) %collective-permute-start.7) | collective-permute-done | bytes 544 | tf_op jit(solution)/shard_map/ppermute | solution.py:42
  52.7 2.3 %collective-permute-start.8 = (s32[128]{0:T(128)S(1)}, s32[128]{0:T(128)S(1)}, u32[]{:S(2)}, u32[]{:S(2)}) collective-permute-start(s32[128]{0:T(128)S(1)} %add.162), channel_id=1, source_target_pairs={{0,128},{32,160},{64,192},{96,224},{128,256},{160,288},{192,320},{... | collective-permute-start | bytes 1544 | tf_op jit(solution)/shard_map/ppermute | solution.py:42
  55.6 5.3 %collective-permute-done.8 = s32[128]{0:T(128)S(1)} collective-permute-done((s32[128]{0:T(128)S(1)}, s32[128]{0:T(128)S(1)}, u32[]{:S(2)}, u32[]{:S(2)}) %collective-permute-start.8) | collective-permute-done | bytes 544 | tf_op jit(solution)/shard_map/ppermute | solution.py:42
  60.9 8.9 %collective-permute-start.9 = (s32[128]{0:T(128)S(1)}, s32[128]{0:T(128)S(1)}, u32[]{:S(2)}, u32[]{:S(2)}) collective-permute-start(s32[128]{0:T(128)S(1)} %add.163), channel_id=1, source_target_pairs={{0,256},{32,288},{64,320},{96,352},{128,384},{160,416},{192,448},{... | collective-permute-start | bytes 1544 | tf_op jit(solution)/shard_map/ppermute | solution.py:42
  69.8 4.1 %collective-permute-done.9 = s32[128]{0:T(128)S(1)} collective-permute-done((s32[128]{0:T(128)S(1)}, s32[128]{0:T(128)S(1)}, u32[]{:S(2)}, u32[]{:S(2)}) %collective-permute-start.9) | collective-permute-done | bytes 544 | tf_op jit(solution)/shard_map/ppermute | solution.py:42
  73.8 7.6 %collective-permute-start.10 = (bf16[256,128]{1,0:T(8,128)(2,1)S(1)}, bf16[256,128]{1,0:T(8,128)(2,1)}, u32[]{:S(2)}, u32[]{:S(2)}) collective-permute-start(bf16[256,128]{1,0:T(8,128)(2,1)S(1)} %pad_maximum_fusion.1), channel_id=1, source_target_pairs={{0,4},{4,8},{8,12},{12,16},{16,20},{20,24},{24,28},{28,0},{1,5},{5... | collective-permute-start | bytes 196616 | tf_op jit(solution)/shard_map/ppermute | solution.py:42
  83.9 2.4 %collective-permute-start.11 = (bf16[256,128]{1,0:T(8,128)(2,1)S(1)}, bf16[256,128]{1,0:T(8,128)(2,1)S(1)}, u32[]{:S(2)}, u32[]{:S(2)}) collective-permute-start(bf16[256,128]{1,0:T(8,128)(2,1)S(1)} %pad_maximum_fusion.1), channel_id=1, source_target_pairs={{0,8},{4,12},{8,16},{12,20},{16,24},{20,28},{24,0},{28,4},{1,9},{5... | collective-permute-start | bytes 196616 | tf_op jit(solution)/shard_map/ppermute | solution.py:42
  87.2 3.6 %collective-permute-done.11 = bf16[256,128]{1,0:T(8,128)(2,1)S(1)} collective-permute-done((bf16[256,128]{1,0:T(8,128)(2,1)S(1)}, bf16[256,128]{1,0:T(8,128)(2,1)S(1)}, u32[]{:S(2)}, u32[]{:S(2)}) %collective-permute-start.11) | collective-permute-done | bytes 65568 | tf_op jit(solution)/shard_map/ppermute | solution.py:42
  90.8 4.6 %collective-permute-start.16 = (bf16[256,128]{1,0:T(8,128)(2,1)S(1)}, bf16[256,128]{1,0:T(8,128)(2,1)S(1)}, u32[]{:S(2)}, u32[]{:S(2)}) collective-permute-start(bf16[256,128]{1,0:T(8,128)(2,1)S(1)} %pad_maximum_fusion.1), channel_id=1, source_target_pairs={{0,28},{4,0},{8,4},{12,8},{16,12},{20,16},{24,20},{28,24},{1,29},{... | collective-permute-start | bytes 196616 | tf_op jit(solution)/shard_map/ppermute | solution.py:42
  95.5 4.7 %collective-permute-start.1 = (bf16[256,768]{1,0:T(8,128)(2,1)S(1)}, bf16[256,768]{1,0:T(8,128)(2,1)}, u32[]{:S(2)}, u32[]{:S(2)}) collective-permute-start(bf16[256,768]{1,0:T(8,128)(2,1)S(1)} %copy-done.2), channel_id=1, source_target_pairs={{0,2},{1,3},{2,0},{3,1},{4,6},{5,7},{6,4},{7,5},{8,10},{9,11},{10,... | collective-permute-start | bytes 1179656 | tf_op jit(solution)/shard_map/ppermute | solution.py:42
  101.0 2.2 %collective-permute-start = (bf16[256,768]{1,0:T(8,128)(2,1)S(1)}, bf16[256,768]{1,0:T(8,128)(2,1)}, u32[]{:S(2)}, u32[]{:S(2)}) collective-permute-start(bf16[256,768]{1,0:T(8,128)(2,1)S(1)} %copy-done.2), channel_id=1, source_target_pairs={{0,1},{1,2},{2,3},{3,0},{4,5},{5,6},{6,7},{7,4},{8,9},{9,10},{10,1... | collective-permute-start | bytes 1179656 | tf_op jit(solution)/shard_map/ppermute | solution.py:42
  104.1 4.3 %collective-permute-start.2 = (bf16[256,768]{1,0:T(8,128)(2,1)S(1)}, bf16[256,768]{1,0:T(8,128)(2,1)}, u32[]{:S(2)}, u32[]{:S(2)}) collective-permute-start(bf16[256,768]{1,0:T(8,128)(2,1)S(1)} %copy-done.2), channel_id=1, source_target_pairs={{0,3},{1,0},{2,1},{3,2},{4,7},{5,4},{6,5},{7,6},{8,11},{9,8},{10,9... | collective-permute-start | bytes 1179656 | tf_op jit(solution)/shard_map/ppermute | solution.py:42
  108.7 1.9 collective-permute-start.17
  111.4 4.7 %collective-permute-done.17 = bf16[2,256,128]{2,1,0:T(8,128)(2,1)S(1)} collective-permute-done((bf16[2,256,128]{2,1,0:T(8,128)(2,1)S(1)}, bf16[2,256,128]{2,1,0:T(8,128)(2,1)S(1)}, u32[]{:S(2)}, u32[]{:S(2)}) %collective-permute-start.17) | collective-permute-done | bytes 131104 | tf_op jit(solution)/shard_map/ppermute | solution.py:42
  116.1 1.9 collective-permute-start.18
  124.7 4.5 %collective-permute-start.19 = (bf16[2,256,128]{2,1,0:T(8,128)(2,1)S(1)}, bf16[2,256,128]{2,1,0:T(8,128)(2,1)S(1)}, u32[]{:S(2)}, u32[]{:S(2)}) collective-permute-start(bf16[2,256,128]{2,1,0:T(8,128)(2,1)S(1)} %add.172), channel_id=1, source_target_pairs={{0,128},{32,160},{64,192},{96,224},{128,256},{160,288},{192,320},{... | collective-permute-start | bytes 393224 | tf_op jit(solution)/shard_map/ppermute | solution.py:42
  129.3 2.6 %pad_maximum_fusion = bf16[4,256,768]{2,1,0:T(8,128)(2,1)} fusion(bf16[1,256,768]{2,1,0:T(8,128)(2,1)} %bitcast.4, bf16[1,256,768]{2,1,0:T(8,128)(2,1)} %bitcast.3, bf16[1,256,768]{2,1,0:T(8,128)(2,1)} %bitcast.2, bf16[1,256,768]{2,1,0:T(8,128)(2,1)S(1)} %bitcast.106), kind=kLoop, calls=%fused_computation.3 | loop fusion | flops 2359296 | bytes 3145728 | tf_op jit(solution)/shard_map/stack | solution.py:115
  131.9 3.2 %gather_fusion = bf16[4,256,768]{2,1,0:T(8,128)(2,1)} fusion(bf16[4,256,768]{2,1,0:T(8,128)(2,1)} %pad_maximum_fusion, s32[1024]{0:T(1024)S(1)} %pad_clamp_fusion.1), kind=kCustom, calls=%fused_computation | custom fusion | bytes 3145744 | tf_op jit(solution)/shard_map/jit(_take)/gather | solution.py:117
  135.1 2.8 %select_bitcast_fusion = bf16[256,4,768]{2,0,1:T(8,128)(2,1)} fusion(bf16[4,256,768]{2,1,0:T(8,128)(2,1)} %gather_fusion, pred[4]{0:T(512)(128)(4,1)S(1)} %compare_and_fusion.1), kind=kLoop, calls=%fused_computation.4 | loop fusion | flops 786432 | bytes 3145732 | tf_op jit(solution)/shard_map/jit(_take)/select_n | solution.py:117
  137.8 2.6 %copy.28 = bf16[256,4,768]{0,2,1:T(8,128)(2,1)} copy(bf16[256,4,768]{2,0,1:T(8,128)(2,1)} %select_bitcast_fusion) | data formatting | bytes 3145728 | tf_op jit(solution)/shard_map/jit(_take)/select_n | solution.py:117
  140.4 3.1 %collective-permute-done.19 = bf16[2,256,128]{2,1,0:T(8,128)(2,1)S(1)} collective-permute-done((bf16[2,256,128]{2,1,0:T(8,128)(2,1)S(1)}, bf16[2,256,128]{2,1,0:T(8,128)(2,1)S(1)}, u32[]{:S(2)}, u32[]{:S(2)}) %collective-permute-start.19) | collective-permute-done | bytes 131104 | tf_op jit(solution)/shard_map/ppermute | solution.py:42
  143.6 9.3 %collective-permute-start.20 = (bf16[2,256,128]{2,1,0:T(8,128)(2,1)S(1)}, bf16[2,256,128]{2,1,0:T(8,128)(2,1)S(1)}, u32[]{:S(2)}, u32[]{:S(2)}) collective-permute-start(bf16[2,256,128]{2,1,0:T(8,128)(2,1)S(1)} %add.173), channel_id=1, source_target_pairs={{0,256},{32,288},{64,320},{96,352},{128,384},{160,416},{192,448},{... | collective-permute-start | bytes 393224 | tf_op jit(solution)/shard_map/ppermute | solution.py:42
  153.0 2.6 %fusion.48 = f32[256,384]{1,0:T(8,128)S(1)} fusion(bf16[256,3072]{0,1:T(8,128)(2,1)} %bitcast.104, bf16[3072,384]{1,0:T(8,128)(2,1)S(1)} %copy-done), kind=kOutput, calls=%fused_computation.116 | convolution fusion | flops 603979776 | bytes 4325376 | tf_op jit(solution)/shard_map/dot_general | solution.py:127
  155.6 6.2 %collective-permute-done.20 = bf16[2,256,128]{2,1,0:T(8,128)(2,1)S(1)} collective-permute-done((bf16[2,256,128]{2,1,0:T(8,128)(2,1)S(1)}, bf16[2,256,128]{2,1,0:T(8,128)(2,1)S(1)}, u32[]{:S(2)}, u32[]{:S(2)}) %collective-permute-start.20) | collective-permute-done | bytes 131104 | tf_op jit(solution)/shard_map/ppermute | solution.py:42
  163.0 6.1 %collective-permute-start.26 = (bf16[2,256,128]{2,1,0:T(8,128)(2,1)S(1)}, bf16[2,256,128]{2,1,0:T(8,128)(2,1)S(1)}, u32[]{:S(2)}, u32[]{:S(2)}) collective-permute-start(bf16[2,256,128]{2,1,0:T(8,128)(2,1)S(1)} %get-tuple-element.6), channel_id=1, source_target_pairs={{0,24},{4,28},{8,0},{12,4},{16,8},{20,12},{24,16},{28,20},{1,25},{... | collective-permute-start | bytes 393224 | tf_op jit(solution)/shard_map/ppermute | solution.py:42
  169.0 1.9 collective-permute-start.25
  171.0 2.8 %collective-permute-start.24 = (bf16[2,256,128]{2,1,0:T(8,128)(2,1)S(1)}, bf16[2,256,128]{2,1,0:T(8,128)(2,1)S(1)}, u32[]{:S(2)}, u32[]{:S(2)}) collective-permute-start(bf16[2,256,128]{2,1,0:T(8,128)(2,1)S(1)} %get-tuple-element.6), channel_id=1, source_target_pairs={{0,16},{4,20},{8,24},{12,28},{16,0},{20,4},{24,8},{28,12},{1,17},{... | collective-permute-start | bytes 393224 | tf_op jit(solution)/shard_map/ppermute | solution.py:42
  173.8 4.3 %collective-permute-start.23 = (bf16[2,256,128]{2,1,0:T(8,128)(2,1)S(1)}, bf16[2,256,128]{2,1,0:T(8,128)(2,1)S(1)}, u32[]{:S(2)}, u32[]{:S(2)}) collective-permute-start(bf16[2,256,128]{2,1,0:T(8,128)(2,1)S(1)} %get-tuple-element.6), channel_id=1, source_target_pairs={{0,12},{4,16},{8,20},{12,24},{16,28},{20,0},{24,4},{28,8},{1,13},{... | collective-permute-start | bytes 393224 | tf_op jit(solution)/shard_map/ppermute | solution.py:42
  178.1 2.8 %collective-permute-start.22 = (bf16[2,256,128]{2,1,0:T(8,128)(2,1)S(1)}, bf16[2,256,128]{2,1,0:T(8,128)(2,1)S(1)}, u32[]{:S(2)}, u32[]{:S(2)}) collective-permute-start(bf16[2,256,128]{2,1,0:T(8,128)(2,1)S(1)} %get-tuple-element.6), channel_id=1, source_target_pairs={{0,8},{4,12},{8,16},{12,20},{16,24},{20,28},{24,0},{28,4},{1,9},{5... | collective-permute-start | bytes 393224 | tf_op jit(solution)/shard_map/ppermute | solution.py:42
  180.9 5.4 %collective-permute-done.22 = bf16[2,256,128]{2,1,0:T(8,128)(2,1)S(1)} collective-permute-done((bf16[2,256,128]{2,1,0:T(8,128)(2,1)S(1)}, bf16[2,256,128]{2,1,0:T(8,128)(2,1)S(1)}, u32[]{:S(2)}, u32[]{:S(2)}) %collective-permute-start.22) | collective-permute-done | bytes 131104 | tf_op jit(solution)/shard_map/ppermute | solution.py:42
  187.5 3.2 %collective-permute-done.27 = bf16[2,256,128]{2,1,0:T(8,128)(2,1)S(1)} collective-permute-done((bf16[2,256,128]{2,1,0:T(8,128)(2,1)S(1)}, bf16[2,256,128]{2,1,0:T(8,128)(2,1)S(1)}, u32[]{:S(2)}, u32[]{:S(2)}) %collective-permute-start.27) | collective-permute-done | bytes 131104 | tf_op jit(solution)/shard_map/ppermute | solution.py:42
  192.0 2.6 %collective-permute-start.30 = (f32[32,256]{1,0:T(8,128)S(1)}, f32[32,256]{1,0:T(8,128)S(1)}, u32[]{:S(2)}, u32[]{:S(2)}) collective-permute-start(f32[32,256]{1,0:T(8,128)S(1)} %fusion.47), channel_id=1, source_target_pairs={{0,3},{1,0},{2,1},{3,2},{4,7},{5,4},{6,5},{7,6},{8,11},{9,8},{10,9... | collective-permute-start | bytes 98312 | tf_op jit(solution)/shard_map/ppermute | solution.py:42
  194.6 3.7 %collective-permute-start.29 = (f32[32,256]{1,0:T(8,128)S(1)}, f32[32,256]{1,0:T(8,128)S(1)}, u32[]{:S(2)}, u32[]{:S(2)}) collective-permute-start(f32[32,256]{1,0:T(8,128)S(1)} %fusion.47), channel_id=1, source_target_pairs={{0,2},{1,3},{2,0},{3,1},{4,6},{5,7},{6,4},{7,5},{8,10},{9,11},{10,... | collective-permute-start | bytes 98312 | tf_op jit(solution)/shard_map/ppermute | solution.py:42
  198.3 1.9 collective-permute-start.28
  201.2 3.4 %collective-permute-done.28 = f32[32,256]{1,0:T(8,128)S(1)} collective-permute-done((f32[32,256]{1,0:T(8,128)S(1)}, f32[32,256]{1,0:T(8,128)S(1)}, u32[]{:S(2)}, u32[]{:S(2)}) %collective-permute-start.28) | collective-permute-done | bytes 32800 | tf_op jit(solution)/shard_map/ppermute | solution.py:42
  204.6 1.5 fusion.6
  206.2 1.9 collective-permute-start.33
  212.6 3.6 %collective-permute-done.31 = bf16[256,128]{0,1:T(8,128)(2,1)} collective-permute-done((bf16[256,128]{0,1:T(8,128)(2,1)}, bf16[256,128]{0,1:T(8,128)(2,1)}, u32[]{:S(2)}, u32[]{:S(2)}) %collective-permute-start.31) | collective-permute-done | bytes 65568 | tf_op jit(solution)/shard_map/ppermute | solution.py:42
  (108 shorter events, 29.9 us)
Async XLA Ops:
  0.0 153.0 %copy-start = (bf16[3072,384]{1,0:T(8,128)(2,1)S(1)}, bf16[3072,384]{1,0:T(8,128)(2,1)}, u32[]{:S(2)}) copy-start(bf16[3072,384]{1,0:T(8,128)(2,1)} %param.10) | copy-start | bytes 7077892
  0.0 95.5 %copy-start.2 = (bf16[256,768]{1,0:T(8,128)(2,1)S(1)}, bf16[256,768]{1,0:T(8,128)(2,1)}, u32[]{:S(2)}) copy-start(bf16[256,768]{1,0:T(8,128)(2,1)} %param.9) | copy-start | bytes 1179652
  2.4 105.9 %collective-permute-start.15 = (bf16[256,128]{1,0:T(8,128)(2,1)S(1)}, bf16[256,128]{1,0:T(8,128)(2,1)S(1)}, u32[]{:S(2)}, u32[]{:S(2)}) collective-permute-start(bf16[256,128]{1,0:T(8,128)(2,1)S(1)} %pad_maximum_fusion.1), channel_id=1, source_target_pairs={{0,24},{4,28},{8,0},{12,4},{16,8},{20,12},{24,16},{28,20},{1,25},{... | collective-permute-start | bytes 196616 | tf_op jit(solution)/shard_map/ppermute | solution.py:42
  7.9 96.2 %collective-permute-start.14 = (bf16[256,128]{1,0:T(8,128)(2,1)S(1)}, bf16[256,128]{1,0:T(8,128)(2,1)S(1)}, u32[]{:S(2)}, u32[]{:S(2)}) collective-permute-start(bf16[256,128]{1,0:T(8,128)(2,1)S(1)} %pad_maximum_fusion.1), channel_id=1, source_target_pairs={{0,20},{4,24},{8,28},{12,0},{16,4},{20,8},{24,12},{28,16},{1,21},{... | collective-permute-start | bytes 196616 | tf_op jit(solution)/shard_map/ppermute | solution.py:42
  11.1 89.8 %collective-permute-start.13 = (bf16[256,128]{1,0:T(8,128)(2,1)S(1)}, bf16[256,128]{1,0:T(8,128)(2,1)}, u32[]{:S(2)}, u32[]{:S(2)}) collective-permute-start(bf16[256,128]{1,0:T(8,128)(2,1)S(1)} %pad_maximum_fusion.1), channel_id=1, source_target_pairs={{0,16},{4,20},{8,24},{12,28},{16,0},{20,4},{24,8},{28,12},{1,17},{... | collective-permute-start | bytes 196616 | tf_op jit(solution)/shard_map/ppermute | solution.py:42
  18.5 77.0 %collective-permute-start.12 = (bf16[256,128]{1,0:T(8,128)(2,1)S(1)}, bf16[256,128]{1,0:T(8,128)(2,1)}, u32[]{:S(2)}, u32[]{:S(2)}) collective-permute-start(bf16[256,128]{1,0:T(8,128)(2,1)S(1)} %pad_maximum_fusion.1), channel_id=1, source_target_pairs={{0,12},{4,16},{8,20},{12,24},{16,28},{20,0},{24,4},{28,8},{1,13},{... | collective-permute-start | bytes 196616 | tf_op jit(solution)/shard_map/ppermute | solution.py:42
  23.1 1.1 collective-permute-start.3
  24.9 5.5 %collective-permute-start.4 = (s32[128]{0:T(128)S(1)}, s32[128]{0:T(128)S(1)}, u32[]{:S(2)}, u32[]{:S(2)}) collective-permute-start(s32[128]{0:T(128)S(1)} %fusion.56), channel_id=1, source_target_pairs={{0,8},{4,12},{8,16},{12,20},{16,24},{20,28},{24,0},{28,4},{1,9},{5... | collective-permute-start | bytes 1544 | tf_op jit(solution)/shard_map/ppermute | solution.py:42
  31.1 5.8 %collective-permute-start.5 = (s32[128]{0:T(128)S(1)}, s32[128]{0:T(128)S(1)}, u32[]{:S(2)}, u32[]{:S(2)}) collective-permute-start(s32[128]{0:T(128)S(1)} %fusion.57), channel_id=1, source_target_pairs={{0,16},{4,20},{8,24},{12,28},{16,0},{20,4},{24,8},{28,12},{1,17},{... | collective-permute-start | bytes 1544 | tf_op jit(solution)/shard_map/ppermute | solution.py:42
  36.9 9.4 %collective-permute-start.6 = (s32[128]{0:T(128)S(1)}, s32[128]{0:T(128)S(1)}, u32[]{:S(2)}, u32[]{:S(2)}) collective-permute-start(s32[128]{0:T(128)S(1)} %add.160), channel_id=1, source_target_pairs={{0,32},{32,64},{64,96},{96,128},{128,160},{160,192},{192,224},{224... | collective-permute-start | bytes 1544 | tf_op jit(solution)/shard_map/ppermute | solution.py:42
  46.3 6.4 %collective-permute-start.7 = (s32[128]{0:T(128)S(1)}, s32[128]{0:T(128)S(1)}, u32[]{:S(2)}, u32[]{:S(2)}) collective-permute-start(s32[128]{0:T(128)S(1)} %add.161), channel_id=1, source_target_pairs={{0,64},{32,96},{64,128},{96,160},{128,192},{160,224},{192,256},{22... | collective-permute-start | bytes 1544 | tf_op jit(solution)/shard_map/ppermute | solution.py:42
  52.7 8.2 %collective-permute-start.8 = (s32[128]{0:T(128)S(1)}, s32[128]{0:T(128)S(1)}, u32[]{:S(2)}, u32[]{:S(2)}) collective-permute-start(s32[128]{0:T(128)S(1)} %add.162), channel_id=1, source_target_pairs={{0,128},{32,160},{64,192},{96,224},{128,256},{160,288},{192,320},{... | collective-permute-start | bytes 1544 | tf_op jit(solution)/shard_map/ppermute | solution.py:42
  60.9 13.0 %collective-permute-start.9 = (s32[128]{0:T(128)S(1)}, s32[128]{0:T(128)S(1)}, u32[]{:S(2)}, u32[]{:S(2)}) collective-permute-start(s32[128]{0:T(128)S(1)} %add.163), channel_id=1, source_target_pairs={{0,256},{32,288},{64,320},{96,352},{128,384},{160,416},{192,448},{... | collective-permute-start | bytes 1544 | tf_op jit(solution)/shard_map/ppermute | solution.py:42
  73.8 10.1 %collective-permute-start.10 = (bf16[256,128]{1,0:T(8,128)(2,1)S(1)}, bf16[256,128]{1,0:T(8,128)(2,1)}, u32[]{:S(2)}, u32[]{:S(2)}) collective-permute-start(bf16[256,128]{1,0:T(8,128)(2,1)S(1)} %pad_maximum_fusion.1), channel_id=1, source_target_pairs={{0,4},{4,8},{8,12},{12,16},{16,20},{20,24},{24,28},{28,0},{1,5},{5... | collective-permute-start | bytes 196616 | tf_op jit(solution)/shard_map/ppermute | solution.py:42
  83.9 6.8 %collective-permute-start.11 = (bf16[256,128]{1,0:T(8,128)(2,1)S(1)}, bf16[256,128]{1,0:T(8,128)(2,1)S(1)}, u32[]{:S(2)}, u32[]{:S(2)}) collective-permute-start(bf16[256,128]{1,0:T(8,128)(2,1)S(1)} %pad_maximum_fusion.1), channel_id=1, source_target_pairs={{0,8},{4,12},{8,16},{12,20},{16,24},{20,28},{24,0},{28,4},{1,9},{5... | collective-permute-start | bytes 196616 | tf_op jit(solution)/shard_map/ppermute | solution.py:42
  90.8 17.6 %collective-permute-start.16 = (bf16[256,128]{1,0:T(8,128)(2,1)S(1)}, bf16[256,128]{1,0:T(8,128)(2,1)S(1)}, u32[]{:S(2)}, u32[]{:S(2)}) collective-permute-start(bf16[256,128]{1,0:T(8,128)(2,1)S(1)} %pad_maximum_fusion.1), channel_id=1, source_target_pairs={{0,28},{4,0},{8,4},{12,8},{16,12},{20,16},{24,20},{28,24},{1,29},{... | collective-permute-start | bytes 196616 | tf_op jit(solution)/shard_map/ppermute | solution.py:42
  95.5 33.8 %collective-permute-start.1 = (bf16[256,768]{1,0:T(8,128)(2,1)S(1)}, bf16[256,768]{1,0:T(8,128)(2,1)}, u32[]{:S(2)}, u32[]{:S(2)}) collective-permute-start(bf16[256,768]{1,0:T(8,128)(2,1)S(1)} %copy-done.2), channel_id=1, source_target_pairs={{0,2},{1,3},{2,0},{3,1},{4,6},{5,7},{6,4},{7,5},{8,10},{9,11},{10,... | collective-permute-start | bytes 1179656 | tf_op jit(solution)/shard_map/ppermute | solution.py:42
  101.0 28.2 %collective-permute-start = (bf16[256,768]{1,0:T(8,128)(2,1)S(1)}, bf16[256,768]{1,0:T(8,128)(2,1)}, u32[]{:S(2)}, u32[]{:S(2)}) collective-permute-start(bf16[256,768]{1,0:T(8,128)(2,1)S(1)} %copy-done.2), channel_id=1, source_target_pairs={{0,1},{1,2},{2,3},{3,0},{4,5},{5,6},{6,7},{7,4},{8,9},{9,10},{10,1... | collective-permute-start | bytes 1179656 | tf_op jit(solution)/shard_map/ppermute | solution.py:42
  104.1 25.2 %collective-permute-start.2 = (bf16[256,768]{1,0:T(8,128)(2,1)S(1)}, bf16[256,768]{1,0:T(8,128)(2,1)}, u32[]{:S(2)}, u32[]{:S(2)}) collective-permute-start(bf16[256,768]{1,0:T(8,128)(2,1)S(1)} %copy-done.2), channel_id=1, source_target_pairs={{0,3},{1,0},{2,1},{3,2},{4,7},{5,4},{6,5},{7,6},{8,11},{9,8},{10,9... | collective-permute-start | bytes 1179656 | tf_op jit(solution)/shard_map/ppermute | solution.py:42
  108.7 7.4 %collective-permute-start.17 = (bf16[2,256,128]{2,1,0:T(8,128)(2,1)S(1)}, bf16[2,256,128]{2,1,0:T(8,128)(2,1)S(1)}, u32[]{:S(2)}, u32[]{:S(2)}) collective-permute-start(bf16[2,256,128]{2,1,0:T(8,128)(2,1)S(1)} %select_reduce_fusion), channel_id=1, source_target_pairs={{0,32},{32,64},{64,96},{96,128},{128,160},{160,192},{192,224},{224... | collective-permute-start | bytes 393224 | tf_op jit(solution)/shard_map/ppermute | solution.py:42
  116.1 8.6 %collective-permute-start.18 = (bf16[2,256,128]{2,1,0:T(8,128)(2,1)S(1)}, bf16[2,256,128]{2,1,0:T(8,128)(2,1)S(1)}, u32[]{:S(2)}, u32[]{:S(2)}) collective-permute-start(bf16[2,256,128]{2,1,0:T(8,128)(2,1)S(1)} %add.171), channel_id=1, source_target_pairs={{0,64},{32,96},{64,128},{96,160},{128,192},{160,224},{192,256},{22... | collective-permute-start | bytes 393224 | tf_op jit(solution)/shard_map/ppermute | solution.py:42
  124.7 18.8 %collective-permute-start.19 = (bf16[2,256,128]{2,1,0:T(8,128)(2,1)S(1)}, bf16[2,256,128]{2,1,0:T(8,128)(2,1)S(1)}, u32[]{:S(2)}, u32[]{:S(2)}) collective-permute-start(bf16[2,256,128]{2,1,0:T(8,128)(2,1)S(1)} %add.172), channel_id=1, source_target_pairs={{0,128},{32,160},{64,192},{96,224},{128,256},{160,288},{192,320},{... | collective-permute-start | bytes 393224 | tf_op jit(solution)/shard_map/ppermute | solution.py:42
  143.6 18.1 %collective-permute-start.20 = (bf16[2,256,128]{2,1,0:T(8,128)(2,1)S(1)}, bf16[2,256,128]{2,1,0:T(8,128)(2,1)S(1)}, u32[]{:S(2)}, u32[]{:S(2)}) collective-permute-start(bf16[2,256,128]{2,1,0:T(8,128)(2,1)S(1)} %add.173), channel_id=1, source_target_pairs={{0,256},{32,288},{64,320},{96,352},{128,384},{160,416},{192,448},{... | collective-permute-start | bytes 393224 | tf_op jit(solution)/shard_map/ppermute | solution.py:42
  153.0 9.5 %copy-start.1 = (bf16[256,4,768]{0,2,1:T(8,128)(2,1)S(1)}, bf16[256,4,768]{0,2,1:T(8,128)(2,1)}, u32[]{:S(2)}) copy-start(bf16[256,4,768]{0,2,1:T(8,128)(2,1)} %copy.28) | copy-start | bytes 4718596
  153.0 9.5 %copy-start.5 = (bf16[3072,128]{1,0:T(8,128)(2,1)S(1)}, bf16[3072,128]{1,0:T(8,128)(2,1)}, u32[]{:S(2)}) copy-start(bf16[3072,128]{1,0:T(8,128)(2,1)} %param.11) | copy-start | bytes 2359300
  161.8 16.2 %collective-permute-start.21 = (bf16[2,256,128]{2,1,0:T(8,128)(2,1)S(1)}, bf16[2,256,128]{2,1,0:T(8,128)(2,1)S(1)}, u32[]{:S(2)}, u32[]{:S(2)}) collective-permute-start(bf16[2,256,128]{2,1,0:T(8,128)(2,1)S(1)} %get-tuple-element.6), channel_id=1, source_target_pairs={{0,4},{4,8},{8,12},{12,16},{16,20},{20,24},{24,28},{28,0},{1,5},{5... | collective-permute-start | bytes 393224 | tf_op jit(solution)/shard_map/ppermute | solution.py:42
  163.0 24.5 %collective-permute-start.26 = (bf16[2,256,128]{2,1,0:T(8,128)(2,1)S(1)}, bf16[2,256,128]{2,1,0:T(8,128)(2,1)S(1)}, u32[]{:S(2)}, u32[]{:S(2)}) collective-permute-start(bf16[2,256,128]{2,1,0:T(8,128)(2,1)S(1)} %get-tuple-element.6), channel_id=1, source_target_pairs={{0,24},{4,28},{8,0},{12,4},{16,8},{20,12},{24,16},{28,20},{1,25},{... | collective-permute-start | bytes 393224 | tf_op jit(solution)/shard_map/ppermute | solution.py:42
  169.0 18.3 %collective-permute-start.25 = (bf16[2,256,128]{2,1,0:T(8,128)(2,1)S(1)}, bf16[2,256,128]{2,1,0:T(8,128)(2,1)S(1)}, u32[]{:S(2)}, u32[]{:S(2)}) collective-permute-start(bf16[2,256,128]{2,1,0:T(8,128)(2,1)S(1)} %get-tuple-element.6), channel_id=1, source_target_pairs={{0,20},{4,24},{8,28},{12,0},{16,4},{20,8},{24,12},{28,16},{1,21},{... | collective-permute-start | bytes 393224 | tf_op jit(solution)/shard_map/ppermute | solution.py:42
  171.0 16.4 %collective-permute-start.24 = (bf16[2,256,128]{2,1,0:T(8,128)(2,1)S(1)}, bf16[2,256,128]{2,1,0:T(8,128)(2,1)S(1)}, u32[]{:S(2)}, u32[]{:S(2)}) collective-permute-start(bf16[2,256,128]{2,1,0:T(8,128)(2,1)S(1)} %get-tuple-element.6), channel_id=1, source_target_pairs={{0,16},{4,20},{8,24},{12,28},{16,0},{20,4},{24,8},{28,12},{1,17},{... | collective-permute-start | bytes 393224 | tf_op jit(solution)/shard_map/ppermute | solution.py:42
  173.8 13.6 %collective-permute-start.23 = (bf16[2,256,128]{2,1,0:T(8,128)(2,1)S(1)}, bf16[2,256,128]{2,1,0:T(8,128)(2,1)S(1)}, u32[]{:S(2)}, u32[]{:S(2)}) collective-permute-start(bf16[2,256,128]{2,1,0:T(8,128)(2,1)S(1)} %get-tuple-element.6), channel_id=1, source_target_pairs={{0,12},{4,16},{8,20},{12,24},{16,28},{20,0},{24,4},{28,8},{1,13},{... | collective-permute-start | bytes 393224 | tf_op jit(solution)/shard_map/ppermute | solution.py:42
  178.1 8.2 %collective-permute-start.22 = (bf16[2,256,128]{2,1,0:T(8,128)(2,1)S(1)}, bf16[2,256,128]{2,1,0:T(8,128)(2,1)S(1)}, u32[]{:S(2)}, u32[]{:S(2)}) collective-permute-start(bf16[2,256,128]{2,1,0:T(8,128)(2,1)S(1)} %get-tuple-element.6), channel_id=1, source_target_pairs={{0,8},{4,12},{8,16},{12,20},{16,24},{20,28},{24,0},{28,4},{1,9},{5... | collective-permute-start | bytes 393224 | tf_op jit(solution)/shard_map/ppermute | solution.py:42
  186.3 4.4 %collective-permute-start.27 = (bf16[2,256,128]{2,1,0:T(8,128)(2,1)S(1)}, bf16[2,256,128]{2,1,0:T(8,128)(2,1)S(1)}, u32[]{:S(2)}, u32[]{:S(2)}) collective-permute-start(bf16[2,256,128]{2,1,0:T(8,128)(2,1)S(1)} %get-tuple-element.6), channel_id=1, source_target_pairs={{0,28},{4,0},{8,4},{12,8},{16,12},{20,16},{24,20},{28,24},{1,29},{... | collective-permute-start | bytes 393224 | tf_op jit(solution)/shard_map/ppermute | solution.py:42
  190.7 1.0 copy-start.4
  192.0 9.0 %collective-permute-start.30 = (f32[32,256]{1,0:T(8,128)S(1)}, f32[32,256]{1,0:T(8,128)S(1)}, u32[]{:S(2)}, u32[]{:S(2)}) collective-permute-start(f32[32,256]{1,0:T(8,128)S(1)} %fusion.47), channel_id=1, source_target_pairs={{0,3},{1,0},{2,1},{3,2},{4,7},{5,4},{6,5},{7,6},{8,11},{9,8},{10,9... | collective-permute-start | bytes 98312 | tf_op jit(solution)/shard_map/ppermute | solution.py:42
  194.6 6.6 %collective-permute-start.29 = (f32[32,256]{1,0:T(8,128)S(1)}, f32[32,256]{1,0:T(8,128)S(1)}, u32[]{:S(2)}, u32[]{:S(2)}) collective-permute-start(f32[32,256]{1,0:T(8,128)S(1)} %fusion.47), channel_id=1, source_target_pairs={{0,2},{1,3},{2,0},{3,1},{4,6},{5,7},{6,4},{7,5},{8,10},{9,11},{10,... | collective-permute-start | bytes 98312 | tf_op jit(solution)/shard_map/ppermute | solution.py:42
  198.3 6.3 %collective-permute-start.28 = (f32[32,256]{1,0:T(8,128)S(1)}, f32[32,256]{1,0:T(8,128)S(1)}, u32[]{:S(2)}, u32[]{:S(2)}) collective-permute-start(f32[32,256]{1,0:T(8,128)S(1)} %fusion.47), channel_id=1, source_target_pairs={{0,1},{1,2},{2,3},{3,0},{4,5},{5,6},{6,7},{7,4},{8,9},{9,10},{10,1... | collective-permute-start | bytes 98312 | tf_op jit(solution)/shard_map/ppermute | solution.py:42
  206.2 6.4 %collective-permute-start.33 = (bf16[256,128]{0,1:T(8,128)(2,1)}, bf16[256,128]{0,1:T(8,128)(2,1)}, u32[]{:S(2)}, u32[]{:S(2)}) collective-permute-start(bf16[256,128]{0,1:T(8,128)(2,1)} %fusion.6), channel_id=1, source_target_pairs={{0,1},{1,2},{4,5},{5,6},{8,9},{9,10},{12,13},{13,14},{16,17},{17,1... | collective-permute-start | bytes 196616 | tf_op jit(solution)/shard_map/ppermute | solution.py:42
  208.1 9.9 %collective-permute-start.32 = (bf16[256,128]{0,1:T(8,128)(2,1)}, bf16[256,128]{0,1:T(8,128)(2,1)}, u32[]{:S(2)}, u32[]{:S(2)}) collective-permute-start(bf16[256,128]{0,1:T(8,128)(2,1)} %fusion.6), channel_id=1, source_target_pairs={{2,1},{3,2},{6,5},{7,6},{10,9},{11,10},{14,13},{15,14},{18,17},{19... | collective-permute-start | bytes 196616 | tf_op jit(solution)/shard_map/ppermute | solution.py:42
  209.4 6.8 %collective-permute-start.31 = (bf16[256,128]{0,1:T(8,128)(2,1)}, bf16[256,128]{0,1:T(8,128)(2,1)}, u32[]{:S(2)}, u32[]{:S(2)}) collective-permute-start(bf16[256,128]{0,1:T(8,128)(2,1)} %fusion.6), channel_id=1, source_target_pairs={{1,3},{2,0},{5,7},{6,4},{9,11},{10,8},{13,15},{14,12},{17,19},{18,... | collective-permute-start | bytes 196616 | tf_op jit(solution)/shard_map/ppermute | solution.py:42
  211.3 6.1 %copy-start.3 = (pred[256,256]{0,1:T(8,128)(4,1)S(1)}, pred[256,256]{0,1:T(8,128)(4,1)}, u32[]{:S(2)}) copy-start(pred[256,256]{0,1:T(8,128)(4,1)} %fusion.9) | copy-start | bytes 196612

commit v3 on v2

--- a/solution.py
+++ b/solution.py
@@ -42,11 +42,14 @@
     return lax.ppermute(x, axis, pairs)
 
 
-def doubled_sum(x, axis, n):
+def spread_sum(x, axis, n, radix=4):
     step = 1
     while step < n:
-        x = x + shifted(x, step, n, axis=axis)
-        step *= 2
+        width = min(radix, n // step)
+        assert n % (step * width) == 0
+        terms = [x] + [shifted(x, step * m, n, axis=axis) for m in range(1, width)]
+        x = sum(terms[1:], terms[0])
+        step *= width
     return x
 
 
@@ -79,31 +82,40 @@
     assert req_dev == 1 and store_rows == 1 and ACTIVE % ny == 0
 
     own_slot = lookup_slots(adapter_ids, adapter_slot)
+
+    down_rows = down_store[0].T.reshape(-1, 128)
+    query_rows = query_up_store[0].reshape(-1, 128)
+    pair_rows = key_value_store[0].reshape(-1, 128)
+    n_down, n_query = down_rows.shape[0], query_rows.shape[0]
+    n_row = n_down + n_query + pair_rows.shape[0]
+    tag = jnp.zeros((8, 128), jnp.int32).at[0, 0].set(own_slot[0]).astype(down_rows.dtype)
+    row = jnp.concatenate([down_rows, query_rows, pair_rows, tag], axis=0)
+
+    plane = jnp.stack([row] + [shifted(row, s, ny, axis="ry") for s in range(1, ny)])
+    back = jnp.arange(ny, dtype=jnp.int32)
+    plane_req = iz * ny + (iy - back) % ny
+    plane_tags = plane[:, n_row, 0].astype(jnp.int32)
+
     req_range = jnp.arange(n_req, dtype=jnp.int32)
-    slots_all = jnp.where(req_range == me, own_slot[0], 0)
-    slots_all = doubled_sum(doubled_sum(slots_all, "ry", ny), "rz", nz)
+    slots_all = jnp.sum(
+        jnp.where(req_range[None, :] == plane_req[:, None], plane_tags[:, None], 0), axis=0
+    )
+    slots_all = spread_sum(slots_all, "rz", nz)
     slot_range = jnp.arange(n_req * store_rows, dtype=jnp.int32)
     used = jnp.any(slots_all[:, None] == slot_range[None, :], axis=0).astype(jnp.int32)
     prefix = jnp.sum(
         jnp.where(slot_range[None, :] < slot_range[:, None], used[None, :], 0), axis=1
     )
 
-    down_rows = down_store[0].T.reshape(-1, 128)
-    query_rows = query_up_store[0].reshape(-1, 128)
-    pair_rows = key_value_store[0].reshape(-1, 128)
-    n_down, n_query = down_rows.shape[0], query_rows.shape[0]
-    row = jnp.concatenate([down_rows, query_rows, pair_rows], axis=0)
-
-    plane = jnp.stack([row] + [shifted(row, s, ny, axis="ry") for s in range(1, ny)])
     per_column = ACTIVE // ny
-    back = jnp.arange(ny, dtype=jnp.int32)
-    plane_slots = iz * ny + (iy - back) % ny
+    plane_slots = plane_req
     wanted = iy + ny * jnp.arange(per_column, dtype=jnp.int32)
     choose = (used[plane_slots][None, :] > 0) & (prefix[plane_slots][None, :] == wanted[:, None])
     column = jnp.sum(
-        jnp.where(choose[:, :, None, None], plane[None], jnp.zeros((), plane.dtype)), axis=1
-    )
-    column = doubled_sum(column, "rz", nz)
+        jnp.where(choose[:, :, None, None], plane[None, :, :n_row], jnp.zeros((), plane.dtype)),
+        axis=1,
+    )
+    column = spread_sum(column, "rz", nz)
     gathered = jnp.stack([column] + [shifted(column, s, ny, axis="ry") for s in range(1, ny)])
     own_k = prefix[own_slot[0]]
     picked = gathered[(iy - own_k % ny) % ny, own_k // ny]

time: 221 us -> 221 us (level)
  waiting for transfers between devices: 59.5 us -> 39.1 us
  starting transfers between devices: 116 us -> 125 us
  local copies, waits for them, and re-layouts: 15.4 us -> 20.8 us
  other arithmetic: 15.3 us -> 18.1 us
    ppermute x34 -> x35, waiting for transfers between devices: 59.5 us -> 39.1 us  [shifted(): return lax.ppermute(x, axis, pairs)]
    ppermute x34 -> x35, starting transfers between devices: 116 us -> 125 us  [shifted(): return lax.ppermute(x, axis, pairs)]
    unnamed x26 -> x34, local copies, waits for them, and re-layouts: 4.08 us -> 8 us
    unnamed x2, other arithmetic: 0.73 us -> 2.98 us
  transfers between devices with their start and end apart: 34 -> 35, of which waited for: 18 -> 13; matrix products, arithmetic and copies ran while one was open for 14% -> 18% of each run, Pallas kernels for 0% -> 0%
where the time goes in v3:
time: 221 us; the launch traced here: 218 us
  starting transfers between devices  125 us (57%)
  waiting for transfers between devices  39.1 us (18%)
  local copies, waits for them, and re-layouts  20.8 us (9%)
  other arithmetic  18.1 us (8%)
  matrix products  8.34 us (4%)
  between operations  6.92 us (3%)
    ppermute x35, starting transfers between devices, shifted(): return lax.ppermute(x, axis, pairs)  125 us
    ppermute x35, waiting for transfers between devices, shifted(): return lax.ppermute(x, axis, pairs)  39.1 us
    unnamed x34, local copies, waits for them, and re-layouts  8 us
  transfers between devices with their start and end apart: 35, of which 13 were waited for; matrix products, arithmetic and copies ran while one was open for 18% of the time, Pallas kernels for 0%

profile of v3, /device:TPU:1, one launch (start us, length us, event | category | flops | bytes accessed | tf_op | source)
XLA Modules:
  0.0 217.9 jit_solution(1894812065057735445)
XLA Ops:
  4.9 5.5 %collective-permute-start.8 = (bf16[264,128]{1,0:T(8,128)(2,1)S(1)}, bf16[264,128]{1,0:T(8,128)(2,1)S(1)}, u32[]{:S(2)}, u32[]{:S(2)}) collective-permute-start(bf16[264,128]{1,0:T(8,128)(2,1)S(1)} %fusion.20), channel_id=1, source_target_pairs={{0,24},{4,28},{8,0},{12,4},{16,8},{20,12},{24,16},{28,20},{1,25},{... | collective-permute-start | bytes 202760 | tf_op jit(solution)/shard_map/ppermute | solution.py:42
  10.4 3.2 %collective-permute-start.7 = (bf16[264,128]{1,0:T(8,128)(2,1)S(1)}, bf16[264,128]{1,0:T(8,128)(2,1)S(1)}, u32[]{:S(2)}, u32[]{:S(2)}) collective-permute-start(bf16[264,128]{1,0:T(8,128)(2,1)S(1)} %fusion.20), channel_id=1, source_target_pairs={{0,20},{4,24},{8,28},{12,0},{16,4},{20,8},{24,12},{28,16},{1,21},{... | collective-permute-start | bytes 202760 | tf_op jit(solution)/shard_map/ppermute | solution.py:42
  13.6 7.3 %collective-permute-start.6 = (bf16[264,128]{1,0:T(8,128)(2,1)S(1)}, bf16[264,128]{1,0:T(8,128)(2,1)S(1)}, u32[]{:S(2)}, u32[]{:S(2)}) collective-permute-start(bf16[264,128]{1,0:T(8,128)(2,1)S(1)} %fusion.20), channel_id=1, source_target_pairs={{0,16},{4,20},{8,24},{12,28},{16,0},{20,4},{24,8},{28,12},{1,17},{... | collective-permute-start | bytes 202760 | tf_op jit(solution)/shard_map/ppermute | solution.py:42
  20.9 1.9 collective-permute-start.5
  22.9 1.3 bitcast_dynamic-update-slice_fusion.15
  24.8 3.0 %collective-permute-start.4 = (bf16[264,128]{1,0:T(8,128)(2,1)S(1)}, bf16[264,128]{1,0:T(8,128)(2,1)S(1)}, u32[]{:S(2)}, u32[]{:S(2)}) collective-permute-start(bf16[264,128]{1,0:T(8,128)(2,1)S(1)} %fusion.20), channel_id=1, source_target_pairs={{0,8},{4,12},{8,16},{12,20},{16,24},{20,28},{24,0},{28,4},{1,9},{5... | collective-permute-start | bytes 202760 | tf_op jit(solution)/shard_map/ppermute | solution.py:42
  28.5 2.5 %collective-permute-done.4 = bf16[264,128]{1,0:T(8,128)(2,1)S(1)} collective-permute-done((bf16[264,128]{1,0:T(8,128)(2,1)S(1)}, bf16[264,128]{1,0:T(8,128)(2,1)S(1)}, u32[]{:S(2)}, u32[]{:S(2)}) %collective-permute-start.4) | collective-permute-done | bytes 67616 | tf_op jit(solution)/shard_map/ppermute | solution.py:42
  31.1 3.0 %collective-permute-start.9 = (bf16[264,128]{1,0:T(8,128)(2,1)S(1)}, bf16[264,128]{1,0:T(8,128)(2,1)S(1)}, u32[]{:S(2)}, u32[]{:S(2)}) collective-permute-start(bf16[264,128]{1,0:T(8,128)(2,1)S(1)} %fusion.20), channel_id=1, source_target_pairs={{0,28},{4,0},{8,4},{12,8},{16,12},{20,16},{24,20},{28,24},{1,29},{... | collective-permute-start | bytes 202760 | tf_op jit(solution)/shard_map/ppermute | solution.py:42
  34.7 3.1 %collective-permute-start.1 = (bf16[256,768]{1,0:T(8,128)(2,1)}, bf16[256,768]{1,0:T(8,128)(2,1)}, u32[]{:S(2)}, u32[]{:S(2)}) collective-permute-start(bf16[256,768]{1,0:T(8,128)(2,1)} %param.11), channel_id=1, source_target_pairs={{0,2},{1,3},{2,0},{3,1},{4,6},{5,7},{6,4},{7,5},{8,10},{9,11},{10,... | collective-permute-start | bytes 1179656 | tf_op jit(solution)/shard_map/ppermute | solution.py:42
  38.5 2.2 %collective-permute-start = (bf16[256,768]{1,0:T(8,128)(2,1)}, bf16[256,768]{1,0:T(8,128)(2,1)}, u32[]{:S(2)}, u32[]{:S(2)}) collective-permute-start(bf16[256,768]{1,0:T(8,128)(2,1)} %param.11), channel_id=1, source_target_pairs={{0,1},{1,2},{2,3},{3,0},{4,5},{5,6},{6,7},{7,4},{8,9},{9,10},{10,1... | collective-permute-start | bytes 1179656 | tf_op jit(solution)/shard_map/ppermute | solution.py:42
  44.3 6.3 %collective-permute-start.12 = (s32[128]{0:T(128)S(1)}, s32[128]{0:T(128)S(1)}, u32[]{:S(2)}, u32[]{:S(2)}) collective-permute-start(s32[128]{0:T(128)S(1)} %select_reduce_fusion.2), channel_id=1, source_target_pairs={{0,96},{32,128},{64,160},{96,192},{128,224},{160,256},{192,288},{2... | collective-permute-start | bytes 1544 | tf_op jit(solution)/shard_map/ppermute | solution.py:42
  50.6 6.1 %collective-permute-start.11 = (s32[128]{0:T(128)S(1)}, s32[128]{0:T(128)S(1)}, u32[]{:S(2)}, u32[]{:S(2)}) collective-permute-start(s32[128]{0:T(128)S(1)} %select_reduce_fusion.2), channel_id=1, source_target_pairs={{0,64},{32,96},{64,128},{96,160},{128,192},{160,224},{192,256},{22... | collective-permute-start | bytes 1544 | tf_op jit(solution)/shard_map/ppermute | solution.py:42
  56.7 3.5 %collective-permute-start.10 = (s32[128]{0:T(128)S(1)}, s32[128]{0:T(128)S(1)}, u32[]{:S(2)}, u32[]{:S(2)}) collective-permute-start(s32[128]{0:T(128)S(1)} %select_reduce_fusion.2), channel_id=1, source_target_pairs={{0,32},{32,64},{64,96},{96,128},{128,160},{160,192},{192,224},{224... | collective-permute-start | bytes 1544 | tf_op jit(solution)/shard_map/ppermute | solution.py:42
  60.3 1.9 collective-permute-done.10
  62.2 6.0 %collective-permute-start.15 = (s32[128]{0:T(128)S(1)}, s32[128]{0:T(128)S(1)}, u32[]{:S(2)}, u32[]{:S(2)}) collective-permute-start(s32[128]{0:T(128)S(1)} %add_add_fusion.3), channel_id=1, source_target_pairs={{0,384},{32,416},{64,448},{96,480},{128,0},{160,32},{192,64},{224,... | collective-permute-start | bytes 1544 | tf_op jit(solution)/shard_map/ppermute | solution.py:42
  68.1 8.9 %collective-permute-start.14 = (s32[128]{0:T(128)S(1)}, s32[128]{0:T(128)S(1)}, u32[]{:S(2)}, u32[]{:S(2)}) collective-permute-start(s32[128]{0:T(128)S(1)} %add_add_fusion.3), channel_id=1, source_target_pairs={{0,256},{32,288},{64,320},{96,352},{128,384},{160,416},{192,448},{... | collective-permute-start | bytes 1544 | tf_op jit(solution)/shard_map/ppermute | solution.py:42
  77.1 4.0 %collective-permute-start.13 = (s32[128]{0:T(128)S(1)}, s32[128]{0:T(128)S(1)}, u32[]{:S(2)}, u32[]{:S(2)}) collective-permute-start(s32[128]{0:T(128)S(1)} %add_add_fusion.3), channel_id=1, source_target_pairs={{0,128},{32,160},{64,192},{96,224},{128,256},{160,288},{192,320},{... | collective-permute-start | bytes 1544 | tf_op jit(solution)/shard_map/ppermute | solution.py:42
  82.2 3.0 %collective-permute-done.13 = s32[128]{0:T(128)S(1)} collective-permute-done((s32[128]{0:T(128)S(1)}, s32[128]{0:T(128)S(1)}, u32[]{:S(2)}, u32[]{:S(2)}) %collective-permute-start.13) | collective-permute-done | bytes 544 | tf_op jit(solution)/shard_map/ppermute | solution.py:42
  87.2 2.3 %collective-permute-start.18 = (bf16[2,256,128]{2,1,0:T(8,128)(2,1)S(1)}, bf16[2,256,128]{2,1,0:T(8,128)(2,1)S(1)}, u32[]{:S(2)}, u32[]{:S(2)}) collective-permute-start(bf16[2,256,128]{2,1,0:T(8,128)(2,1)S(1)} %select_reduce_fusion), channel_id=1, source_target_pairs={{0,96},{32,128},{64,160},{96,192},{128,224},{160,256},{192,288},{2... | collective-permute-start | bytes 393224 | tf_op jit(solution)/shard_map/ppermute | solution.py:42
  89.5 3.5 %collective-permute-start.17 = (bf16[2,256,128]{2,1,0:T(8,128)(2,1)S(1)}, bf16[2,256,128]{2,1,0:T(8,128)(2,1)S(1)}, u32[]{:S(2)}, u32[]{:S(2)}) collective-permute-start(bf16[2,256,128]{2,1,0:T(8,128)(2,1)S(1)} %select_reduce_fusion), channel_id=1, source_target_pairs={{0,64},{32,96},{64,128},{96,160},{128,192},{160,224},{192,256},{22... | collective-permute-start | bytes 393224 | tf_op jit(solution)/shard_map/ppermute | solution.py:42
  93.0 2.6 %collective-permute-start.16 = (bf16[2,256,128]{2,1,0:T(8,128)(2,1)S(1)}, bf16[2,256,128]{2,1,0:T(8,128)(2,1)S(1)}, u32[]{:S(2)}, u32[]{:S(2)}) collective-permute-start(bf16[2,256,128]{2,1,0:T(8,128)(2,1)S(1)} %select_reduce_fusion), channel_id=1, source_target_pairs={{0,32},{32,64},{64,96},{96,128},{128,160},{160,192},{192,224},{224... | collective-permute-start | bytes 393224 | tf_op jit(solution)/shard_map/ppermute | solution.py:42
  98.1 4.3 %collective-permute-start.2 = (bf16[256,768]{1,0:T(8,128)(2,1)S(1)}, bf16[256,768]{1,0:T(8,128)(2,1)S(1)}, u32[]{:S(2)}, u32[]{:S(2)}) collective-permute-start(bf16[256,768]{1,0:T(8,128)(2,1)S(1)} %copy-done.2), channel_id=1, source_target_pairs={{0,3},{1,0},{2,1},{3,2},{4,7},{5,4},{6,5},{7,6},{8,11},{9,8},{10,9... | collective-permute-start | bytes 1179656 | tf_op jit(solution)/shard_map/ppermute | solution.py:42
  102.3 6.3 %collective-permute-done.16 = bf16[2,256,128]{2,1,0:T(8,128)(2,1)S(1)} collective-permute-done((bf16[2,256,128]{2,1,0:T(8,128)(2,1)S(1)}, bf16[2,256,128]{2,1,0:T(8,128)(2,1)S(1)}, u32[]{:S(2)}, u32[]{:S(2)}) %collective-permute-start.16) | collective-permute-done | bytes 131104 | tf_op jit(solution)/shard_map/ppermute | solution.py:42
  108.7 3.0 %collective-permute-start.21 = (bf16[2,256,128]{2,1,0:T(8,128)(2,1)S(1)}, bf16[2,256,128]{2,1,0:T(8,128)(2,1)S(1)}, u32[]{:S(2)}, u32[]{:S(2)}) collective-permute-start(bf16[2,256,128]{2,1,0:T(8,128)(2,1)S(1)} %add_add_fusion.1), channel_id=1, source_target_pairs={{0,384},{32,416},{64,448},{96,480},{128,0},{160,32},{192,64},{224,... | collective-permute-start | bytes 393224 | tf_op jit(solution)/shard_map/ppermute | solution.py:42
  113.0 8.0 %collective-permute-start.20 = (bf16[2,256,128]{2,1,0:T(8,128)(2,1)S(1)}, bf16[2,256,128]{2,1,0:T(8,128)(2,1)S(1)}, u32[]{:S(2)}, u32[]{:S(2)}) collective-permute-start(bf16[2,256,128]{2,1,0:T(8,128)(2,1)S(1)} %add_add_fusion.1), channel_id=1, source_target_pairs={{0,256},{32,288},{64,320},{96,352},{128,384},{160,416},{192,448},{... | collective-permute-start | bytes 393224 | tf_op jit(solution)/shard_map/ppermute | solution.py:42
  121.0 4.4 %collective-permute-done.21 = bf16[2,256,128]{2,1,0:T(8,128)(2,1)S(1)} collective-permute-done((bf16[2,256,128]{2,1,0:T(8,128)(2,1)S(1)}, bf16[2,256,128]{2,1,0:T(8,128)(2,1)S(1)}, u32[]{:S(2)}, u32[]{:S(2)}) %collective-permute-start.21) | collective-permute-done | bytes 131104 | tf_op jit(solution)/shard_map/ppermute | solution.py:42
  125.4 6.4 %collective-permute-start.19 = (bf16[2,256,128]{2,1,0:T(8,128)(2,1)S(1)}, bf16[2,256,128]{2,1,0:T(8,128)(2,1)}, u32[]{:S(2)}, u32[]{:S(2)}) collective-permute-start(bf16[2,256,128]{2,1,0:T(8,128)(2,1)S(1)} %add_add_fusion.1), channel_id=1, source_target_pairs={{0,128},{32,160},{64,192},{96,224},{128,256},{160,288},{192,320},{... | collective-permute-start | bytes 393224 | tf_op jit(solution)/shard_map/ppermute | solution.py:42
  138.0 7.0 %collective-permute-done.19 = bf16[2,256,128]{2,1,0:T(8,128)(2,1)} collective-permute-done((bf16[2,256,128]{2,1,0:T(8,128)(2,1)S(1)}, bf16[2,256,128]{2,1,0:T(8,128)(2,1)}, u32[]{:S(2)}, u32[]{:S(2)}) %collective-permute-start.19) | collective-permute-done | bytes 131104 | tf_op jit(solution)/shard_map/ppermute | solution.py:42
  145.0 1.7 bitcast_dynamic-update-slice_fusion.7
  146.6 2.1 collective-permute-start.27
  148.8 2.8 %collective-permute-start.26 = (bf16[2,256,128]{2,1,0:T(8,128)(2,1)}, bf16[2,256,128]{2,1,0:T(8,128)(2,1)S(1)}, u32[]{:S(2)}, u32[]{:S(2)}) collective-permute-start(bf16[2,256,128]{2,1,0:T(8,128)(2,1)} %get-tuple-element.18), channel_id=1, source_target_pairs={{0,20},{4,24},{8,28},{12,0},{16,4},{20,8},{24,12},{28,16},{1,21},{... | collective-permute-start | bytes 393224 | tf_op jit(solution)/shard_map/ppermute | solution.py:42
  151.7 4.7 %collective-permute-start.25 = (bf16[2,256,128]{2,1,0:T(8,128)(2,1)}, bf16[2,256,128]{2,1,0:T(8,128)(2,1)}, u32[]{:S(2)}, u32[]{:S(2)}) collective-permute-start(bf16[2,256,128]{2,1,0:T(8,128)(2,1)} %get-tuple-element.18), channel_id=1, source_target_pairs={{0,16},{4,20},{8,24},{12,28},{16,0},{20,4},{24,8},{28,12},{1,17},{... | collective-permute-start | bytes 393224 | tf_op jit(solution)/shard_map/ppermute | solution.py:42
  156.4 2.2 collective-permute-start.24
  159.3 2.5 %pad_maximum_fusion = bf16[4,256,768]{2,1,0:T(8,128)(2,1)} fusion(bf16[1,256,768]{2,1,0:T(8,128)(2,1)S(1)} %bitcast.109, bf16[1,256,768]{2,1,0:T(8,128)(2,1)} %bitcast.3, bf16[1,256,768]{2,1,0:T(8,128)(2,1)} %bitcast.2, bf16[1,256,768]{2,1,0:T(8,128)(2,1)S(1)} %bitcast.107), kind=kLoop, calls=%fused_computation.3 | loop fusion | flops 2359296 | bytes 3145728 | tf_op jit(solution)/shard_map/stack | solution.py:127
  161.8 3.2 %gather_fusion = bf16[4,256,768]{2,1,0:T(8,128)(2,1)} fusion(bf16[4,256,768]{2,1,0:T(8,128)(2,1)} %pad_maximum_fusion, s32[1024]{0:T(1024)S(1)} %pad_clamp_fusion.1), kind=kCustom, calls=%fused_computation | custom fusion | bytes 3145744 | tf_op jit(solution)/shard_map/jit(_take)/gather | solution.py:129
  165.0 2.8 %select_bitcast_fusion = bf16[256,4,768]{2,0,1:T(8,128)(2,1)} fusion(bf16[4,256,768]{2,1,0:T(8,128)(2,1)} %gather_fusion, pred[4]{0:T(512)(128)(4,1)S(1)} %copy-done.8), kind=kLoop, calls=%fused_computation.4 | loop fusion | flops 786432 | bytes 3145732 | tf_op jit(solution)/shard_map/jit(_take)/select_n | solution.py:129
  167.8 2.6 %copy.36 = bf16[256,4,768]{0,2,1:T(8,128)(2,1)} copy(bf16[256,4,768]{2,0,1:T(8,128)(2,1)} %select_bitcast_fusion) | data formatting | bytes 3145728 | tf_op jit(solution)/shard_map/jit(_take)/select_n | solution.py:129
  170.4 3.4 %fusion.53 = f32[256,384]{1,0:T(8,128)} fusion(bf16[256,3072]{0,1:T(8,128)(2,1)} %bitcast.105, bf16[3072,384]{1,0:T(8,128)(2,1)S(1)} %copy-done), kind=kOutput, calls=%fused_computation.130 | convolution fusion | flops 603979776 | bytes 4325376 | tf_op jit(solution)/shard_map/dot_general | solution.py:139
  174.3 2.9 %collective-permute-start.23 = (bf16[2,256,128]{2,1,0:T(8,128)(2,1)}, bf16[2,256,128]{2,1,0:T(8,128)(2,1)S(1)}, u32[]{:S(2)}, u32[]{:S(2)}) collective-permute-start(bf16[2,256,128]{2,1,0:T(8,128)(2,1)} %get-tuple-element.18), channel_id=1, source_target_pairs={{0,8},{4,12},{8,16},{12,20},{16,24},{20,28},{24,0},{28,4},{1,9},{5... | collective-permute-start | bytes 393224 | tf_op jit(solution)/shard_map/ppermute | solution.py:42
  178.1 4.7 %collective-permute-done.23 = bf16[2,256,128]{2,1,0:T(8,128)(2,1)S(1)} collective-permute-done((bf16[2,256,128]{2,1,0:T(8,128)(2,1)}, bf16[2,256,128]{2,1,0:T(8,128)(2,1)S(1)}, u32[]{:S(2)}, u32[]{:S(2)}) %collective-permute-start.23) | collective-permute-done | bytes 131104 | tf_op jit(solution)/shard_map/ppermute | solution.py:42
  185.5 1.9 collective-permute-done.28
  188.7 4.5 %collective-permute-start.31 = (f32[32,256]{1,0:T(8,128)S(1)}, f32[32,256]{1,0:T(8,128)S(1)}, u32[]{:S(2)}, u32[]{:S(2)}) collective-permute-start(f32[32,256]{1,0:T(8,128)S(1)} %fusion.52), channel_id=1, source_target_pairs={{0,3},{1,0},{2,1},{3,2},{4,7},{5,4},{6,5},{7,6},{8,11},{9,8},{10,9... | collective-permute-start | bytes 98312 | tf_op jit(solution)/shard_map/ppermute | solution.py:42
  193.2 3.1 %collective-permute-start.30 = (f32[32,256]{1,0:T(8,128)S(1)}, f32[32,256]{1,0:T(8,128)S(1)}, u32[]{:S(2)}, u32[]{:S(2)}) collective-permute-start(f32[32,256]{1,0:T(8,128)S(1)} %fusion.52), channel_id=1, source_target_pairs={{0,2},{1,3},{2,0},{3,1},{4,6},{5,7},{6,4},{7,5},{8,10},{9,11},{10,... | collective-permute-start | bytes 98312 | tf_op jit(solution)/shard_map/ppermute | solution.py:42
  196.3 1.9 collective-permute-start.29
  199.9 2.7 %collective-permute-done.29 = f32[32,256]{1,0:T(8,128)S(1)} collective-permute-done((f32[32,256]{1,0:T(8,128)S(1)}, f32[32,256]{1,0:T(8,128)S(1)}, u32[]{:S(2)}, u32[]{:S(2)}) %collective-permute-start.29) | collective-permute-done | bytes 32800 | tf_op jit(solution)/shard_map/ppermute | solution.py:42
  202.6 1.5 fusion.6
  204.1 1.9 collective-permute-start.34
  211.5 2.6 %collective-permute-done.32 = bf16[256,128]{0,1:T(8,128)(2,1)} collective-permute-done((bf16[256,128]{0,1:T(8,128)(2,1)}, bf16[256,128]{0,1:T(8,128)(2,1)}, u32[]{:S(2)}, u32[]{:S(2)}) %collective-permute-start.32) | collective-permute-done | bytes 65568 | tf_op jit(solution)/shard_map/ppermute | solution.py:42
  (114 shorter events, 34.3 us)
Async XLA Ops:
  0.0 170.4 %copy-start = (bf16[3072,384]{1,0:T(8,128)(2,1)S(1)}, bf16[3072,384]{1,0:T(8,128)(2,1)}, u32[]{:S(2)}) copy-start(bf16[3072,384]{1,0:T(8,128)(2,1)} %param.12) | copy-start | bytes 7077892
  4.9 37.1 %collective-permute-start.8 = (bf16[264,128]{1,0:T(8,128)(2,1)S(1)}, bf16[264,128]{1,0:T(8,128)(2,1)S(1)}, u32[]{:S(2)}, u32[]{:S(2)}) collective-permute-start(bf16[264,128]{1,0:T(8,128)(2,1)S(1)} %fusion.20), channel_id=1, source_target_pairs={{0,24},{4,28},{8,0},{12,4},{16,8},{20,12},{24,16},{28,20},{1,25},{... | collective-permute-start | bytes 202760 | tf_op jit(solution)/shard_map/ppermute | solution.py:42
  10.4 31.0 %collective-permute-start.7 = (bf16[264,128]{1,0:T(8,128)(2,1)S(1)}, bf16[264,128]{1,0:T(8,128)(2,1)S(1)}, u32[]{:S(2)}, u32[]{:S(2)}) collective-permute-start(bf16[264,128]{1,0:T(8,128)(2,1)S(1)} %fusion.20), channel_id=1, source_target_pairs={{0,20},{4,24},{8,28},{12,0},{16,4},{20,8},{24,12},{28,16},{1,21},{... | collective-permute-start | bytes 202760 | tf_op jit(solution)/shard_map/ppermute | solution.py:42
  13.6 24.9 %collective-permute-start.6 = (bf16[264,128]{1,0:T(8,128)(2,1)S(1)}, bf16[264,128]{1,0:T(8,128)(2,1)S(1)}, u32[]{:S(2)}, u32[]{:S(2)}) collective-permute-start(bf16[264,128]{1,0:T(8,128)(2,1)S(1)} %fusion.20), channel_id=1, source_target_pairs={{0,16},{4,20},{8,24},{12,28},{16,0},{20,4},{24,8},{28,12},{1,17},{... | collective-permute-start | bytes 202760 | tf_op jit(solution)/shard_map/ppermute | solution.py:42
  20.9 13.8 %collective-permute-start.5 = (bf16[264,128]{1,0:T(8,128)(2,1)S(1)}, bf16[264,128]{1,0:T(8,128)(2,1)S(1)}, u32[]{:S(2)}, u32[]{:S(2)}) collective-permute-start(bf16[264,128]{1,0:T(8,128)(2,1)S(1)} %fusion.20), channel_id=1, source_target_pairs={{0,12},{4,16},{8,20},{12,24},{16,28},{20,0},{24,4},{28,8},{1,13},{... | collective-permute-start | bytes 202760 | tf_op jit(solution)/shard_map/ppermute | solution.py:42
  22.9 2.0 collective-permute-start.3
  24.8 6.2 %collective-permute-start.4 = (bf16[264,128]{1,0:T(8,128)(2,1)S(1)}, bf16[264,128]{1,0:T(8,128)(2,1)S(1)}, u32[]{:S(2)}, u32[]{:S(2)}) collective-permute-start(bf16[264,128]{1,0:T(8,128)(2,1)S(1)} %fusion.20), channel_id=1, source_target_pairs={{0,8},{4,12},{8,16},{12,20},{16,24},{20,28},{24,0},{28,4},{1,9},{5... | collective-permute-start | bytes 202760 | tf_op jit(solution)/shard_map/ppermute | solution.py:42
  31.1 11.5 %collective-permute-start.9 = (bf16[264,128]{1,0:T(8,128)(2,1)S(1)}, bf16[264,128]{1,0:T(8,128)(2,1)S(1)}, u32[]{:S(2)}, u32[]{:S(2)}) collective-permute-start(bf16[264,128]{1,0:T(8,128)(2,1)S(1)} %fusion.20), channel_id=1, source_target_pairs={{0,28},{4,0},{8,4},{12,8},{16,12},{20,16},{24,20},{28,24},{1,29},{... | collective-permute-start | bytes 202760 | tf_op jit(solution)/shard_map/ppermute | solution.py:42
  34.7 116.9 %collective-permute-start.1 = (bf16[256,768]{1,0:T(8,128)(2,1)}, bf16[256,768]{1,0:T(8,128)(2,1)}, u32[]{:S(2)}, u32[]{:S(2)}) collective-permute-start(bf16[256,768]{1,0:T(8,128)(2,1)} %param.11), channel_id=1, source_target_pairs={{0,2},{1,3},{2,0},{3,1},{4,6},{5,7},{6,4},{7,5},{8,10},{9,11},{10,... | collective-permute-start | bytes 1179656 | tf_op jit(solution)/shard_map/ppermute | solution.py:42
  38.5 117.9 %collective-permute-start = (bf16[256,768]{1,0:T(8,128)(2,1)}, bf16[256,768]{1,0:T(8,128)(2,1)}, u32[]{:S(2)}, u32[]{:S(2)}) collective-permute-start(bf16[256,768]{1,0:T(8,128)(2,1)} %param.11), channel_id=1, source_target_pairs={{0,1},{1,2},{2,3},{3,0},{4,5},{5,6},{6,7},{7,4},{8,9},{9,10},{10,1... | collective-permute-start | bytes 1179656 | tf_op jit(solution)/shard_map/ppermute | solution.py:42
  42.6 55.5 %copy-start.2 = (bf16[256,768]{1,0:T(8,128)(2,1)S(1)}, bf16[256,768]{1,0:T(8,128)(2,1)}, u32[]{:S(2)}) copy-start(bf16[256,768]{1,0:T(8,128)(2,1)} %param.11) | copy-start | bytes 1179652
  44.3 15.9 %collective-permute-start.12 = (s32[128]{0:T(128)S(1)}, s32[128]{0:T(128)S(1)}, u32[]{:S(2)}, u32[]{:S(2)}) collective-permute-start(s32[128]{0:T(128)S(1)} %select_reduce_fusion.2), channel_id=1, source_target_pairs={{0,96},{32,128},{64,160},{96,192},{128,224},{160,256},{192,288},{2... | collective-permute-start | bytes 1544 | tf_op jit(solution)/shard_map/ppermute | solution.py:42
  50.6 9.7 %collective-permute-start.11 = (s32[128]{0:T(128)S(1)}, s32[128]{0:T(128)S(1)}, u32[]{:S(2)}, u32[]{:S(2)}) collective-permute-start(s32[128]{0:T(128)S(1)} %select_reduce_fusion.2), channel_id=1, source_target_pairs={{0,64},{32,96},{64,128},{96,160},{128,192},{160,224},{192,256},{22... | collective-permute-start | bytes 1544 | tf_op jit(solution)/shard_map/ppermute | solution.py:42
  56.7 5.5 %collective-permute-start.10 = (s32[128]{0:T(128)S(1)}, s32[128]{0:T(128)S(1)}, u32[]{:S(2)}, u32[]{:S(2)}) collective-permute-start(s32[128]{0:T(128)S(1)} %select_reduce_fusion.2), channel_id=1, source_target_pairs={{0,32},{32,64},{64,96},{96,128},{128,160},{160,192},{192,224},{224... | collective-permute-start | bytes 1544 | tf_op jit(solution)/shard_map/ppermute | solution.py:42
  62.2 20.0 %collective-permute-start.15 = (s32[128]{0:T(128)S(1)}, s32[128]{0:T(128)S(1)}, u32[]{:S(2)}, u32[]{:S(2)}) collective-permute-start(s32[128]{0:T(128)S(1)} %add_add_fusion.3), channel_id=1, source_target_pairs={{0,384},{32,416},{64,448},{96,480},{128,0},{160,32},{192,64},{224,... | collective-permute-start | bytes 1544 | tf_op jit(solution)/shard_map/ppermute | solution.py:42
  68.1 14.1 %collective-permute-start.14 = (s32[128]{0:T(128)S(1)}, s32[128]{0:T(128)S(1)}, u32[]{:S(2)}, u32[]{:S(2)}) collective-permute-start(s32[128]{0:T(128)S(1)} %add_add_fusion.3), channel_id=1, source_target_pairs={{0,256},{32,288},{64,320},{96,352},{128,384},{160,416},{192,448},{... | collective-permute-start | bytes 1544 | tf_op jit(solution)/shard_map/ppermute | solution.py:42
  77.1 8.2 %collective-permute-start.13 = (s32[128]{0:T(128)S(1)}, s32[128]{0:T(128)S(1)}, u32[]{:S(2)}, u32[]{:S(2)}) collective-permute-start(s32[128]{0:T(128)S(1)} %add_add_fusion.3), channel_id=1, source_target_pairs={{0,128},{32,160},{64,192},{96,224},{128,256},{160,288},{192,320},{... | collective-permute-start | bytes 1544 | tf_op jit(solution)/shard_map/ppermute | solution.py:42
  87.2 10.9 %collective-permute-start.18 = (bf16[2,256,128]{2,1,0:T(8,128)(2,1)S(1)}, bf16[2,256,128]{2,1,0:T(8,128)(2,1)S(1)}, u32[]{:S(2)}, u32[]{:S(2)}) collective-permute-start(bf16[2,256,128]{2,1,0:T(8,128)(2,1)S(1)} %select_reduce_fusion), channel_id=1, source_target_pairs={{0,96},{32,128},{64,160},{96,192},{128,224},{160,256},{192,288},{2... | collective-permute-start | bytes 393224 | tf_op jit(solution)/shard_map/ppermute | solution.py:42
  89.5 12.8 %collective-permute-start.17 = (bf16[2,256,128]{2,1,0:T(8,128)(2,1)S(1)}, bf16[2,256,128]{2,1,0:T(8,128)(2,1)S(1)}, u32[]{:S(2)}, u32[]{:S(2)}) collective-permute-start(bf16[2,256,128]{2,1,0:T(8,128)(2,1)S(1)} %select_reduce_fusion), channel_id=1, source_target_pairs={{0,64},{32,96},{64,128},{96,160},{128,192},{160,224},{192,256},{22... | collective-permute-start | bytes 393224 | tf_op jit(solution)/shard_map/ppermute | solution.py:42
  93.0 15.6 %collective-permute-start.16 = (bf16[2,256,128]{2,1,0:T(8,128)(2,1)S(1)}, bf16[2,256,128]{2,1,0:T(8,128)(2,1)S(1)}, u32[]{:S(2)}, u32[]{:S(2)}) collective-permute-start(bf16[2,256,128]{2,1,0:T(8,128)(2,1)S(1)} %select_reduce_fusion), channel_id=1, source_target_pairs={{0,32},{32,64},{64,96},{96,128},{128,160},{160,192},{192,224},{224... | collective-permute-start | bytes 393224 | tf_op jit(solution)/shard_map/ppermute | solution.py:42
  97.6 35.9 %copy-start.6 = (pred[256]{0:T(512)(128)(4,1)}, pred[256]{0:T(512)(128)(4,1)S(1)}, u32[]{:S(2)}) copy-start(pred[256]{0:T(512)(128)(4,1)S(1)} %iota_compare_fusion.5) | copy-start | bytes 772
  98.1 60.5 %collective-permute-start.2 = (bf16[256,768]{1,0:T(8,128)(2,1)S(1)}, bf16[256,768]{1,0:T(8,128)(2,1)S(1)}, u32[]{:S(2)}, u32[]{:S(2)}) collective-permute-start(bf16[256,768]{1,0:T(8,128)(2,1)S(1)} %copy-done.2), channel_id=1, source_target_pairs={{0,3},{1,0},{2,1},{3,2},{4,7},{5,4},{6,5},{7,6},{8,11},{9,8},{10,9... | collective-permute-start | bytes 1179656 | tf_op jit(solution)/shard_map/ppermute | solution.py:42
  108.7 16.7 %collective-permute-start.21 = (bf16[2,256,128]{2,1,0:T(8,128)(2,1)S(1)}, bf16[2,256,128]{2,1,0:T(8,128)(2,1)S(1)}, u32[]{:S(2)}, u32[]{:S(2)}) collective-permute-start(bf16[2,256,128]{2,1,0:T(8,128)(2,1)S(1)} %add_add_fusion.1), channel_id=1, source_target_pairs={{0,384},{32,416},{64,448},{96,480},{128,0},{160,32},{192,64},{224,... | collective-permute-start | bytes 393224 | tf_op jit(solution)/shard_map/ppermute | solution.py:42
  113.0 25.0 %collective-permute-start.20 = (bf16[2,256,128]{2,1,0:T(8,128)(2,1)S(1)}, bf16[2,256,128]{2,1,0:T(8,128)(2,1)S(1)}, u32[]{:S(2)}, u32[]{:S(2)}) collective-permute-start(bf16[2,256,128]{2,1,0:T(8,128)(2,1)S(1)} %add_add_fusion.1), channel_id=1, source_target_pairs={{0,256},{32,288},{64,320},{96,352},{128,384},{160,416},{192,448},{... | collective-permute-start | bytes 393224 | tf_op jit(solution)/shard_map/ppermute | solution.py:42
  125.4 19.6 %collective-permute-start.19 = (bf16[2,256,128]{2,1,0:T(8,128)(2,1)S(1)}, bf16[2,256,128]{2,1,0:T(8,128)(2,1)}, u32[]{:S(2)}, u32[]{:S(2)}) collective-permute-start(bf16[2,256,128]{2,1,0:T(8,128)(2,1)S(1)} %add_add_fusion.1), channel_id=1, source_target_pairs={{0,128},{32,160},{64,192},{96,224},{128,256},{160,288},{192,320},{... | collective-permute-start | bytes 393224 | tf_op jit(solution)/shard_map/ppermute | solution.py:42
  146.6 38.8 %collective-permute-start.27 = (bf16[2,256,128]{2,1,0:T(8,128)(2,1)}, bf16[2,256,128]{2,1,0:T(8,128)(2,1)S(1)}, u32[]{:S(2)}, u32[]{:S(2)}) collective-permute-start(bf16[2,256,128]{2,1,0:T(8,128)(2,1)} %get-tuple-element.18), channel_id=1, source_target_pairs={{0,24},{4,28},{8,0},{12,4},{16,8},{20,12},{24,16},{28,20},{1,25},{... | collective-permute-start | bytes 393224 | tf_op jit(solution)/shard_map/ppermute | solution.py:42
  148.8 36.6 %collective-permute-start.26 = (bf16[2,256,128]{2,1,0:T(8,128)(2,1)}, bf16[2,256,128]{2,1,0:T(8,128)(2,1)S(1)}, u32[]{:S(2)}, u32[]{:S(2)}) collective-permute-start(bf16[2,256,128]{2,1,0:T(8,128)(2,1)} %get-tuple-element.18), channel_id=1, source_target_pairs={{0,20},{4,24},{8,28},{12,0},{16,4},{20,8},{24,12},{28,16},{1,21},{... | collective-permute-start | bytes 393224 | tf_op jit(solution)/shard_map/ppermute | solution.py:42
  151.7 32.8 %collective-permute-start.25 = (bf16[2,256,128]{2,1,0:T(8,128)(2,1)}, bf16[2,256,128]{2,1,0:T(8,128)(2,1)}, u32[]{:S(2)}, u32[]{:S(2)}) collective-permute-start(bf16[2,256,128]{2,1,0:T(8,128)(2,1)} %get-tuple-element.18), channel_id=1, source_target_pairs={{0,16},{4,20},{8,24},{12,28},{16,0},{20,4},{24,8},{28,12},{1,17},{... | collective-permute-start | bytes 393224 | tf_op jit(solution)/shard_map/ppermute | solution.py:42
  156.4 27.1 %collective-permute-start.24 = (bf16[2,256,128]{2,1,0:T(8,128)(2,1)}, bf16[2,256,128]{2,1,0:T(8,128)(2,1)}, u32[]{:S(2)}, u32[]{:S(2)}) collective-permute-start(bf16[2,256,128]{2,1,0:T(8,128)(2,1)} %get-tuple-element.18), channel_id=1, source_target_pairs={{0,12},{4,16},{8,20},{12,24},{16,28},{20,0},{24,4},{28,8},{1,13},{... | collective-permute-start | bytes 393224 | tf_op jit(solution)/shard_map/ppermute | solution.py:42
  158.6 15.7 %collective-permute-start.22 = (bf16[2,256,128]{2,1,0:T(8,128)(2,1)}, bf16[2,256,128]{2,1,0:T(8,128)(2,1)}, u32[]{:S(2)}, u32[]{:S(2)}) collective-permute-start(bf16[2,256,128]{2,1,0:T(8,128)(2,1)} %get-tuple-element.18), channel_id=1, source_target_pairs={{0,4},{4,8},{8,12},{12,16},{16,20},{20,24},{24,28},{28,0},{1,5},{5... | collective-permute-start | bytes 393224 | tf_op jit(solution)/shard_map/ppermute | solution.py:42
  161.8 3.2 %copy-start.8 = (pred[4]{0:T(512)(128)(4,1)S(1)}, pred[4]{0:T(512)(128)(4,1)}, u32[]{:S(2)}) copy-start(pred[4]{0:T(512)(128)(4,1)} %compare_and_fusion.1) | copy-start | bytes 16
  170.4 3.4 %copy-start.1 = (bf16[256,4,768]{0,2,1:T(8,128)(2,1)S(1)}, bf16[256,4,768]{0,2,1:T(8,128)(2,1)}, u32[]{:S(2)}) copy-start(bf16[256,4,768]{0,2,1:T(8,128)(2,1)} %copy.36) | copy-start | bytes 4718596
  170.4 3.4 %copy-start.9 = (bf16[3072,128]{1,0:T(8,128)(2,1)S(1)}, bf16[3072,128]{1,0:T(8,128)(2,1)}, u32[]{:S(2)}) copy-start(bf16[3072,128]{1,0:T(8,128)(2,1)} %param.13) | copy-start | bytes 2359300
  173.8 3.4 %copy-start.4 = (bf16[8,2,256,128]{3,2,1,0:T(8,128)(2,1)S(1)}, bf16[8,2,256,128]{3,2,1,0:T(8,128)(2,1)}, u32[]{:S(2)}) copy-start(bf16[8,2,256,128]{3,2,1,0:T(8,128)(2,1)} %get-tuple-element.17) | copy-start | bytes 3145732
  174.3 8.5 %collective-permute-start.23 = (bf16[2,256,128]{2,1,0:T(8,128)(2,1)}, bf16[2,256,128]{2,1,0:T(8,128)(2,1)S(1)}, u32[]{:S(2)}, u32[]{:S(2)}) collective-permute-start(bf16[2,256,128]{2,1,0:T(8,128)(2,1)} %get-tuple-element.18), channel_id=1, source_target_pairs={{0,8},{4,12},{8,16},{12,20},{16,24},{20,28},{24,0},{28,4},{1,9},{5... | collective-permute-start | bytes 393224 | tf_op jit(solution)/shard_map/ppermute | solution.py:42
  182.8 4.6 %collective-permute-start.28 = (bf16[2,256,128]{2,1,0:T(8,128)(2,1)}, bf16[2,256,128]{2,1,0:T(8,128)(2,1)S(1)}, u32[]{:S(2)}, u32[]{:S(2)}) collective-permute-start(bf16[2,256,128]{2,1,0:T(8,128)(2,1)} %get-tuple-element.18), channel_id=1, source_target_pairs={{0,28},{4,0},{8,4},{12,8},{16,12},{20,16},{24,20},{28,24},{1,29},{... | collective-permute-start | bytes 393224 | tf_op jit(solution)/shard_map/ppermute | solution.py:42
  187.4 1.0 copy-start.5
  188.7 10.2 %collective-permute-start.31 = (f32[32,256]{1,0:T(8,128)S(1)}, f32[32,256]{1,0:T(8,128)S(1)}, u32[]{:S(2)}, u32[]{:S(2)}) collective-permute-start(f32[32,256]{1,0:T(8,128)S(1)} %fusion.52), channel_id=1, source_target_pairs={{0,3},{1,0},{2,1},{3,2},{4,7},{5,4},{6,5},{7,6},{8,11},{9,8},{10,9... | collective-permute-start | bytes 98312 | tf_op jit(solution)/shard_map/ppermute | solution.py:42
  193.2 6.7 %collective-permute-start.30 = (f32[32,256]{1,0:T(8,128)S(1)}, f32[32,256]{1,0:T(8,128)S(1)}, u32[]{:S(2)}, u32[]{:S(2)}) collective-permute-start(f32[32,256]{1,0:T(8,128)S(1)} %fusion.52), channel_id=1, source_target_pairs={{0,2},{1,3},{2,0},{3,1},{4,6},{5,7},{6,4},{7,5},{8,10},{9,11},{10,... | collective-permute-start | bytes 98312 | tf_op jit(solution)/shard_map/ppermute | solution.py:42
  196.3 6.3 %collective-permute-start.29 = (f32[32,256]{1,0:T(8,128)S(1)}, f32[32,256]{1,0:T(8,128)S(1)}, u32[]{:S(2)}, u32[]{:S(2)}) collective-permute-start(f32[32,256]{1,0:T(8,128)S(1)} %fusion.52), channel_id=1, source_target_pairs={{0,1},{1,2},{2,3},{3,0},{4,5},{5,6},{6,7},{7,4},{8,9},{9,10},{10,1... | collective-permute-start | bytes 98312 | tf_op jit(solution)/shard_map/ppermute | solution.py:42
  204.1 7.4 %collective-permute-start.34 = (bf16[256,128]{0,1:T(8,128)(2,1)}, bf16[256,128]{0,1:T(8,128)(2,1)}, u32[]{:S(2)}, u32[]{:S(2)}) collective-permute-start(bf16[256,128]{0,1:T(8,128)(2,1)} %fusion.6), channel_id=1, source_target_pairs={{0,1},{1,2},{4,5},{5,6},{8,9},{9,10},{12,13},{13,14},{16,17},{17,1... | collective-permute-start | bytes 196616 | tf_op jit(solution)/shard_map/ppermute | solution.py:42
  206.0 9.8 %collective-permute-start.33 = (bf16[256,128]{0,1:T(8,128)(2,1)}, bf16[256,128]{0,1:T(8,128)(2,1)}, u32[]{:S(2)}, u32[]{:S(2)}) collective-permute-start(bf16[256,128]{0,1:T(8,128)(2,1)} %fusion.6), channel_id=1, source_target_pairs={{2,1},{3,2},{6,5},{7,6},{10,9},{11,10},{14,13},{15,14},{18,17},{19... | collective-permute-start | bytes 196616 | tf_op jit(solution)/shard_map/ppermute | solution.py:42
  207.3 6.8 %collective-permute-start.32 = (bf16[256,128]{0,1:T(8,128)(2,1)}, bf16[256,128]{0,1:T(8,128)(2,1)}, u32[]{:S(2)}, u32[]{:S(2)}) collective-permute-start(bf16[256,128]{0,1:T(8,128)(2,1)} %fusion.6), channel_id=1, source_target_pairs={{1,3},{2,0},{5,7},{6,4},{9,11},{10,8},{13,15},{14,12},{17,19},{18,... | collective-permute-start | bytes 196616 | tf_op jit(solution)/shard_map/ppermute | solution.py:42
  210.2 5.1 %copy-start.3 = (pred[256,256]{0,1:T(8,128)(4,1)S(1)}, pred[256,256]{0,1:T(8,128)(4,1)}, u32[]{:S(2)}) copy-start(pred[256,256]{0,1:T(8,128)(4,1)} %fusion.9) | copy-start | bytes 196612
  211.5 4.4 %copy-start.7 = (pred[256]{0:T(512)(128)(4,1)S(1)}, pred[256]{0:T(512)(128)(4,1)}, u32[]{:S(2)}) copy-start(pred[256]{0:T(512)(128)(4,1)} %copy-done.6) | copy-start | bytes 772

commit v4 on v3

--- a/solution.py
+++ b/solution.py
@@ -40,6 +40,11 @@
     if pairs is None:
         pairs = [(i, (i + shift) % n) for i in range(n)]
     return lax.ppermute(x, axis, pairs)
+
+
+def gather_over(x, axis, n):
+    copies = jnp.broadcast_to(x[None], (n,) + x.shape)
+    return lax.all_to_all(copies, axis, 0, 0, tiled=True)
 
 
 def spread_sum(x, axis, n, radix=4):
@@ -91,9 +96,8 @@
     tag = jnp.zeros((8, 128), jnp.int32).at[0, 0].set(own_slot[0]).astype(down_rows.dtype)
     row = jnp.concatenate([down_rows, query_rows, pair_rows, tag], axis=0)
 
-    plane = jnp.stack([row] + [shifted(row, s, ny, axis="ry") for s in range(1, ny)])
-    back = jnp.arange(ny, dtype=jnp.int32)
-    plane_req = iz * ny + (iy - back) % ny
+    plane = gather_over(row, "ry", ny)
+    plane_req = iz * ny + jnp.arange(ny, dtype=jnp.int32)
     plane_tags = plane[:, n_row, 0].astype(jnp.int32)
 
     req_range = jnp.arange(n_req, dtype=jnp.int32)
@@ -116,9 +120,9 @@
         axis=1,
     )
     column = spread_sum(column, "rz", nz)
-    gathered = jnp.stack([column] + [shifted(column, s, ny, axis="ry") for s in range(1, ny)])
+    gathered = gather_over(column, "ry", ny)
     own_k = prefix[own_slot[0]]
-    picked = gathered[(iy - own_k % ny) % ny, own_k // ny]
+    picked = gathered[own_k % ny, own_k // ny]
     down_t = picked[:n_down].reshape(down_store.shape[2], down_store.shape[1])
     adapter_query = picked[n_down:n_down + n_query].reshape(query_up_store.shape[1:])
     adapter_pair = picked[n_down + n_query:].reshape(key_value_store.shape[1:])

time: 221 us -> 186 us (0.84)
  the two profiles are of different devices: /device:TPU:1 before, /device:TPU:6 now
where the time goes in v4:
time: 186 us; the launch traced here: 184 us
  starting transfers between devices  93.8 us (50%)
  waiting for transfers between devices  48.8 us (26%)
  local copies, waits for them, and re-layouts  14.4 us (8%)
  other arithmetic  13.4 us (7%)
  between operations  7.01 us (4%)
  matrix products  6.78 us (4%)
    ppermute x21, starting transfers between devices, shifted(): return lax.ppermute(x, axis, pairs)  86 us
    ppermute x21, waiting for transfers between devices, shifted(): return lax.ppermute(x, axis, pairs)  36.3 us
    all_to_all x2, waiting for transfers between devices, gather_over(): return lax.all_to_all(copies, axis, 0, 0, tiled=True)  12.6 us
    all_to_all x2, starting transfers between devices, gather_over(): return lax.all_to_all(copies, axis, 0, 0, tiled=True)  7.8 us
  transfers between devices with their start and end apart: 23, of which 10 were waited for; matrix products, arithmetic and copies ran while one was open for 16% of the time, Pallas kernels for 0%

profile of v4, /device:TPU:6, one launch (start us, length us, event | category | flops | bytes accessed | tf_op | source)
XLA Modules:
  0.0 184.2 jit_solution(992680786151039298)
XLA Ops:
  0.0 3.4 %collective-permute-start.1 = (bf16[256,768]{1,0:T(8,128)(2,1)}, bf16[256,768]{1,0:T(8,128)(2,1)}, u32[]{:S(2)}, u32[]{:S(2)}) collective-permute-start(bf16[256,768]{1,0:T(8,128)(2,1)} %param.11), channel_id=1, source_target_pairs={{0,2},{1,3},{2,0},{3,1},{4,6},{5,7},{6,4},{7,5},{8,10},{9,11},{10,... | collective-permute-start | bytes 1179656 | tf_op jit(solution)/shard_map/ppermute | solution.py:42
  3.4 6.4 %collective-permute-start = (bf16[256,768]{1,0:T(8,128)(2,1)}, bf16[256,768]{1,0:T(8,128)(2,1)}, u32[]{:S(2)}, u32[]{:S(2)}) collective-permute-start(bf16[256,768]{1,0:T(8,128)(2,1)} %param.11), channel_id=1, source_target_pairs={{0,1},{1,2},{2,3},{3,0},{4,5},{5,6},{6,7},{7,4},{8,9},{9,10},{10,1... | collective-permute-start | bytes 1179656 | tf_op jit(solution)/shard_map/ppermute | solution.py:42
  10.5 1.3 fusion.39
  13.2 0.9 reshape.438
  14.7 0.9 broadcast_in_dim.86
  15.6 3.5 %all-to-all-start = ((bf16[8,264,128]{2,1,0:T(8,128)(2,1)}), bf16[8,264,128]{2,1,0:T(8,128)(2,1)S(1)}, u32[]{:S(2)}, u32[]{:S(2)}) async-start(bf16[8,264,128]{2,1,0:T(8,128)(2,1)} %broadcast_in_dim.86), calls=%async_computation | async-start | bytes 1081344 | tf_op jit(solution)/shard_map/all_to_all | solution.py:47
  19.9 1.3 multiply_cosine_fusion
  21.1 8.4 %all-to-all-done = bf16[8,264,128]{2,1,0:T(8,128)(2,1)S(1)} async-done(((bf16[8,264,128]{2,1,0:T(8,128)(2,1)}), bf16[8,264,128]{2,1,0:T(8,128)(2,1)S(1)}, u32[]{:S(2)}, u32[]{:S(2)}) %all-to-all-start) | async-done | bytes 540704 | tf_op jit(solution)/shard_map/all_to_all | solution.py:47
  29.9 5.2 %collective-permute-start.5 = (s32[128]{0:T(128)S(1)}, s32[128]{0:T(128)S(1)}, u32[]{:S(2)}, u32[]{:S(2)}) collective-permute-start(s32[128]{0:T(128)S(1)} %select_reduce_fusion.2), channel_id=1, source_target_pairs={{0,96},{32,128},{64,160},{96,192},{128,224},{160,256},{192,288},{2... | collective-permute-start | bytes 1544 | tf_op jit(solution)/shard_map/ppermute | solution.py:42
  35.1 6.4 %collective-permute-start.4 = (s32[128]{0:T(128)S(1)}, s32[128]{0:T(128)S(1)}, u32[]{:S(2)}, u32[]{:S(2)}) collective-permute-start(s32[128]{0:T(128)S(1)} %select_reduce_fusion.2), channel_id=1, source_target_pairs={{0,64},{32,96},{64,128},{96,160},{128,192},{160,224},{192,256},{22... | collective-permute-start | bytes 1544 | tf_op jit(solution)/shard_map/ppermute | solution.py:42
  41.5 3.8 %collective-permute-start.3 = (s32[128]{0:T(128)S(1)}, s32[128]{0:T(128)S(1)}, u32[]{:S(2)}, u32[]{:S(2)}) collective-permute-start(s32[128]{0:T(128)S(1)} %select_reduce_fusion.2), channel_id=1, source_target_pairs={{0,32},{32,64},{64,96},{96,128},{128,160},{160,192},{192,224},{224... | collective-permute-start | bytes 1544 | tf_op jit(solution)/shard_map/ppermute | solution.py:42
  45.9 2.3 %collective-permute-done.3 = s32[128]{0:T(128)S(1)} collective-permute-done((s32[128]{0:T(128)S(1)}, s32[128]{0:T(128)S(1)}, u32[]{:S(2)}, u32[]{:S(2)}) %collective-permute-start.3) | collective-permute-done | bytes 544 | tf_op jit(solution)/shard_map/ppermute | solution.py:42
  48.1 5.6 %collective-permute-start.8 = (s32[128]{0:T(128)S(1)}, s32[128]{0:T(128)S(1)}, u32[]{:S(2)}, u32[]{:S(2)}) collective-permute-start(s32[128]{0:T(128)S(1)} %add_add_fusion.3), channel_id=1, source_target_pairs={{0,384},{32,416},{64,448},{96,480},{128,0},{160,32},{192,64},{224,... | collective-permute-start | bytes 1544 | tf_op jit(solution)/shard_map/ppermute | solution.py:42
  53.7 9.9 %collective-permute-start.7 = (s32[128]{0:T(128)S(1)}, s32[128]{0:T(128)S(1)}, u32[]{:S(2)}, u32[]{:S(2)}) collective-permute-start(s32[128]{0:T(128)S(1)} %add_add_fusion.3), channel_id=1, source_target_pairs={{0,256},{32,288},{64,320},{96,352},{128,384},{160,416},{192,448},{... | collective-permute-start | bytes 1544 | tf_op jit(solution)/shard_map/ppermute | solution.py:42
  63.6 4.3 %collective-permute-start.6 = (s32[128]{0:T(128)S(1)}, s32[128]{0:T(128)S(1)}, u32[]{:S(2)}, u32[]{:S(2)}) collective-permute-start(s32[128]{0:T(128)S(1)} %add_add_fusion.3), channel_id=1, source_target_pairs={{0,128},{32,160},{64,192},{96,224},{128,256},{160,288},{192,320},{... | collective-permute-start | bytes 1544 | tf_op jit(solution)/shard_map/ppermute | solution.py:42
  68.0 2.1 %collective-permute-start.2 = (bf16[256,768]{1,0:T(8,128)(2,1)}, bf16[256,768]{1,0:T(8,128)(2,1)}, u32[]{:S(2)}, u32[]{:S(2)}) collective-permute-start(bf16[256,768]{1,0:T(8,128)(2,1)} %param.11), channel_id=1, source_target_pairs={{0,3},{1,0},{2,1},{3,2},{4,7},{5,4},{6,5},{7,6},{8,11},{9,8},{10,9... | collective-permute-start | bytes 1179656 | tf_op jit(solution)/shard_map/ppermute | solution.py:42
  70.1 2.9 %collective-permute-done.6 = s32[128]{0:T(128)S(1)} collective-permute-done((s32[128]{0:T(128)S(1)}, s32[128]{0:T(128)S(1)}, u32[]{:S(2)}, u32[]{:S(2)}) %collective-permute-start.6) | collective-permute-done | bytes 544 | tf_op jit(solution)/shard_map/ppermute | solution.py:42
  74.9 2.6 %collective-permute-start.11 = (bf16[2,256,128]{2,1,0:T(8,128)(2,1)S(1)}, bf16[2,256,128]{2,1,0:T(8,128)(2,1)S(1)}, u32[]{:S(2)}, u32[]{:S(2)}) collective-permute-start(bf16[2,256,128]{2,1,0:T(8,128)(2,1)S(1)} %select_reduce_fusion), channel_id=1, source_target_pairs={{0,96},{32,128},{64,160},{96,192},{128,224},{160,256},{192,288},{2... | collective-permute-start | bytes 393224 | tf_op jit(solution)/shard_map/ppermute | solution.py:42
  78.2 3.4 %collective-permute-start.10 = (bf16[2,256,128]{2,1,0:T(8,128)(2,1)S(1)}, bf16[2,256,128]{2,1,0:T(8,128)(2,1)S(1)}, u32[]{:S(2)}, u32[]{:S(2)}) collective-permute-start(bf16[2,256,128]{2,1,0:T(8,128)(2,1)S(1)} %select_reduce_fusion), channel_id=1, source_target_pairs={{0,64},{32,96},{64,128},{96,160},{128,192},{160,224},{192,256},{22... | collective-permute-start | bytes 393224 | tf_op jit(solution)/shard_map/ppermute | solution.py:42
  81.6 8.9 %collective-permute-done.11 = bf16[2,256,128]{2,1,0:T(8,128)(2,1)S(1)} collective-permute-done((bf16[2,256,128]{2,1,0:T(8,128)(2,1)S(1)}, bf16[2,256,128]{2,1,0:T(8,128)(2,1)S(1)}, u32[]{:S(2)}, u32[]{:S(2)}) %collective-permute-start.11) | collective-permute-done | bytes 131104 | tf_op jit(solution)/shard_map/ppermute | solution.py:42
  90.5 1.9 %collective-permute-start.9 = (bf16[2,256,128]{2,1,0:T(8,128)(2,1)S(1)}, bf16[2,256,128]{2,1,0:T(8,128)(2,1)S(1)}, u32[]{:S(2)}, u32[]{:S(2)}) collective-permute-start(bf16[2,256,128]{2,1,0:T(8,128)(2,1)S(1)} %select_reduce_fusion), channel_id=1, source_target_pairs={{0,32},{32,64},{64,96},{96,128},{128,160},{160,192},{192,224},{224... | collective-permute-start | bytes 393224 | tf_op jit(solution)/shard_map/ppermute | solution.py:42
  94.4 4.2 %collective-permute-done.9 = bf16[2,256,128]{2,1,0:T(8,128)(2,1)S(1)} collective-permute-done((bf16[2,256,128]{2,1,0:T(8,128)(2,1)S(1)}, bf16[2,256,128]{2,1,0:T(8,128)(2,1)S(1)}, u32[]{:S(2)}, u32[]{:S(2)}) %collective-permute-start.9) | collective-permute-done | bytes 131104 | tf_op jit(solution)/shard_map/ppermute | solution.py:42
  98.6 2.4 %collective-permute-start.14 = (bf16[2,256,128]{2,1,0:T(8,128)(2,1)S(1)}, bf16[2,256,128]{2,1,0:T(8,128)(2,1)S(1)}, u32[]{:S(2)}, u32[]{:S(2)}) collective-permute-start(bf16[2,256,128]{2,1,0:T(8,128)(2,1)S(1)} %add_add_fusion.1), channel_id=1, source_target_pairs={{0,384},{32,416},{64,448},{96,480},{128,0},{160,32},{192,64},{224,... | collective-permute-start | bytes 393224 | tf_op jit(solution)/shard_map/ppermute | solution.py:42
  101.0 8.5 %collective-permute-start.13 = (bf16[2,256,128]{2,1,0:T(8,128)(2,1)S(1)}, bf16[2,256,128]{2,1,0:T(8,128)(2,1)S(1)}, u32[]{:S(2)}, u32[]{:S(2)}) collective-permute-start(bf16[2,256,128]{2,1,0:T(8,128)(2,1)S(1)} %add_add_fusion.1), channel_id=1, source_target_pairs={{0,256},{32,288},{64,320},{96,352},{128,384},{160,416},{192,448},{... | collective-permute-start | bytes 393224 | tf_op jit(solution)/shard_map/ppermute | solution.py:42
  109.6 3.7 %collective-permute-start.12 = (bf16[2,256,128]{2,1,0:T(8,128)(2,1)S(1)}, bf16[2,256,128]{2,1,0:T(8,128)(2,1)S(1)}, u32[]{:S(2)}, u32[]{:S(2)}) collective-permute-start(bf16[2,256,128]{2,1,0:T(8,128)(2,1)S(1)} %add_add_fusion.1), channel_id=1, source_target_pairs={{0,128},{32,160},{64,192},{96,224},{128,256},{160,288},{192,320},{... | collective-permute-start | bytes 393224 | tf_op jit(solution)/shard_map/ppermute | solution.py:42
  113.3 2.6 %pad_maximum_fusion = bf16[4,256,768]{2,1,0:T(8,128)(2,1)} fusion(bf16[1,256,768]{2,1,0:T(8,128)(2,1)} %bitcast.4, bf16[1,256,768]{2,1,0:T(8,128)(2,1)} %bitcast.3, bf16[1,256,768]{2,1,0:T(8,128)(2,1)} %bitcast.2, bf16[1,256,768]{2,1,0:T(8,128)(2,1)S(1)} %bitcast.75), kind=kLoop, calls=%fused_computation.3 | loop fusion | flops 2359296 | bytes 3145728 | tf_op jit(solution)/shard_map/stack | solution.py:131
  115.9 3.2 %gather_fusion = bf16[4,256,768]{2,1,0:T(8,128)(2,1)} fusion(bf16[4,256,768]{2,1,0:T(8,128)(2,1)} %pad_maximum_fusion, s32[1024]{0:T(1024)S(1)} %pad_clamp_fusion.1), kind=kCustom, calls=%fused_computation | custom fusion | bytes 3145744 | tf_op jit(solution)/shard_map/jit(_take)/gather | solution.py:133
  119.1 7.7 %collective-permute-done.13 = bf16[2,256,128]{2,1,0:T(8,128)(2,1)S(1)} collective-permute-done((bf16[2,256,128]{2,1,0:T(8,128)(2,1)S(1)}, bf16[2,256,128]{2,1,0:T(8,128)(2,1)S(1)}, u32[]{:S(2)}, u32[]{:S(2)}) %collective-permute-start.13) | collective-permute-done | bytes 131104 | tf_op jit(solution)/shard_map/ppermute | solution.py:42
  126.8 3.9 %collective-permute-done.12 = bf16[2,256,128]{2,1,0:T(8,128)(2,1)S(1)} collective-permute-done((bf16[2,256,128]{2,1,0:T(8,128)(2,1)S(1)}, bf16[2,256,128]{2,1,0:T(8,128)(2,1)S(1)}, u32[]{:S(2)}, u32[]{:S(2)}) %collective-permute-start.12) | collective-permute-done | bytes 131104 | tf_op jit(solution)/shard_map/ppermute | solution.py:42
  130.8 1.2 broadcast_in_dim.139
  132.0 4.3 %all-to-all-start.1 = ((bf16[8,2,256,128]{3,2,1,0:T(8,128)(2,1)}), bf16[8,2,256,128]{3,2,1,0:T(8,128)(2,1)}, u32[]{:S(2)}, u32[]{:S(2)}) async-start(bf16[8,2,256,128]{3,2,1,0:T(8,128)(2,1)} %broadcast_in_dim.139), calls=%async_computation.1 | async-start | bytes 2097152 | tf_op jit(solution)/shard_map/all_to_all | solution.py:47
  136.2 2.8 %select_bitcast_fusion = bf16[256,4,768]{2,0,1:T(8,128)(2,1)} fusion(bf16[4,256,768]{2,1,0:T(8,128)(2,1)} %gather_fusion, pred[4]{0:T(512)(128)(4,1)S(1)} %compare_and_fusion.1), kind=kLoop, calls=%fused_computation.4 | loop fusion | flops 786432 | bytes 3145732 | tf_op jit(solution)/shard_map/jit(_take)/select_n | solution.py:133
  139.0 2.6 %copy.45 = bf16[256,4,768]{0,2,1:T(8,128)(2,1)} copy(bf16[256,4,768]{2,0,1:T(8,128)(2,1)} %select_bitcast_fusion) | data formatting | bytes 3145728 | tf_op jit(solution)/shard_map/jit(_take)/select_n | solution.py:133
  141.6 2.2 %fusion.47 = f32[256,128]{0,1:T(8,128)S(1)} fusion(bf16[256,3072]{0,1:T(8,128)(2,1)} %bitcast.73, bf16[3072,128]{1,0:T(8,128)(2,1)} %param.13), kind=kOutput, calls=%fused_computation.103 | convolution fusion | flops 201326592 | bytes 2490368 | tf_op jit(solution)/shard_map/dot_general | solution.py:144
  143.8 1.0 fusion.49
  148.1 4.1 %all-to-all-done.1 = bf16[8,2,256,128]{3,2,1,0:T(8,128)(2,1)} async-done(((bf16[8,2,256,128]{3,2,1,0:T(8,128)(2,1)}), bf16[8,2,256,128]{3,2,1,0:T(8,128)(2,1)}, u32[]{:S(2)}, u32[]{:S(2)}) %all-to-all-start.1) | async-done | bytes 1048608 | tf_op jit(solution)/shard_map/all_to_all | solution.py:47
  153.3 2.0 %collective-permute-start.17 = (f32[32,256]{1,0:T(8,128)S(1)}, f32[32,256]{1,0:T(8,128)S(1)}, u32[]{:S(2)}, u32[]{:S(2)}) collective-permute-start(f32[32,256]{1,0:T(8,128)S(1)} %fusion.48), channel_id=1, source_target_pairs={{0,3},{1,0},{2,1},{3,2},{4,7},{5,4},{6,5},{7,6},{8,11},{9,8},{10,9... | collective-permute-start | bytes 98312 | tf_op jit(solution)/shard_map/ppermute | solution.py:42
  155.3 2.8 %collective-permute-start.16 = (f32[32,256]{1,0:T(8,128)S(1)}, f32[32,256]{1,0:T(8,128)S(1)}, u32[]{:S(2)}, u32[]{:S(2)}) collective-permute-start(f32[32,256]{1,0:T(8,128)S(1)} %fusion.48), channel_id=1, source_target_pairs={{0,2},{1,3},{2,0},{3,1},{4,6},{5,7},{6,4},{7,5},{8,10},{9,11},{10,... | collective-permute-start | bytes 98312 | tf_op jit(solution)/shard_map/ppermute | solution.py:42
  158.1 4.5 %collective-permute-start.15 = (f32[32,256]{1,0:T(8,128)S(1)}, f32[32,256]{1,0:T(8,128)S(1)}, u32[]{:S(2)}, u32[]{:S(2)}) collective-permute-start(f32[32,256]{1,0:T(8,128)S(1)} %fusion.48), channel_id=1, source_target_pairs={{0,1},{1,2},{2,3},{3,0},{4,5},{5,6},{6,7},{7,4},{8,9},{9,10},{10,1... | collective-permute-start | bytes 98312 | tf_op jit(solution)/shard_map/ppermute | solution.py:42
  163.4 1.6 collective-permute-done.15
  165.1 1.5 fusion.6
  166.6 1.3 collective-permute-start.20
  167.9 4.5 %collective-permute-start.19 = (bf16[256,128]{0,1:T(8,128)(2,1)}, bf16[256,128]{0,1:T(8,128)(2,1)}, u32[]{:S(2)}, u32[]{:S(2)}) collective-permute-start(bf16[256,128]{0,1:T(8,128)(2,1)} %fusion.6), channel_id=1, source_target_pairs={{2,1},{3,2},{6,5},{7,6},{10,9},{11,10},{14,13},{15,14},{18,17},{19... | collective-permute-start | bytes 196616 | tf_op jit(solution)/shard_map/ppermute | solution.py:42
  172.4 1.3 collective-permute-start.18
  174.5 1.1 fusion.10
  175.7 4.8 %collective-permute-done.18 = bf16[256,128]{0,1:T(8,128)(2,1)} collective-permute-done((bf16[256,128]{0,1:T(8,128)(2,1)}, bf16[256,128]{0,1:T(8,128)(2,1)}, u32[]{:S(2)}, u32[]{:S(2)}) %collective-permute-start.18) | collective-permute-done | bytes 65568 | tf_op jit(solution)/shard_map/ppermute | solution.py:42
  180.4 0.9 bitcast_convert_fusion
  182.2 1.2 fusion.4
  (77 shorter events, 10.0 us)
Async XLA Ops:
  0.0 143.8 %copy-start = (bf16[3072,384]{1,0:T(8,128)(2,1)S(1)}, bf16[3072,384]{1,0:T(8,128)(2,1)}, u32[]{:S(2)}) copy-start(bf16[3072,384]{1,0:T(8,128)(2,1)} %param.12) | copy-start | bytes 7077892
  0.0 109.6 %collective-permute-start.1 = (bf16[256,768]{1,0:T(8,128)(2,1)}, bf16[256,768]{1,0:T(8,128)(2,1)}, u32[]{:S(2)}, u32[]{:S(2)}) collective-permute-start(bf16[256,768]{1,0:T(8,128)(2,1)} %param.11), channel_id=1, source_target_pairs={{0,2},{1,3},{2,0},{3,1},{4,6},{5,7},{6,4},{7,5},{8,10},{9,11},{10,... | collective-permute-start | bytes 1179656 | tf_op jit(solution)/shard_map/ppermute | solution.py:42
  3.4 109.8 %collective-permute-start = (bf16[256,768]{1,0:T(8,128)(2,1)}, bf16[256,768]{1,0:T(8,128)(2,1)}, u32[]{:S(2)}, u32[]{:S(2)}) collective-permute-start(bf16[256,768]{1,0:T(8,128)(2,1)} %param.11), channel_id=1, source_target_pairs={{0,1},{1,2},{2,3},{3,0},{4,5},{5,6},{6,7},{7,4},{8,9},{9,10},{10,1... | collective-permute-start | bytes 1179656 | tf_op jit(solution)/shard_map/ppermute | solution.py:42
  15.6 14.0 %all-to-all-start = ((bf16[8,264,128]{2,1,0:T(8,128)(2,1)}), bf16[8,264,128]{2,1,0:T(8,128)(2,1)S(1)}, u32[]{:S(2)}, u32[]{:S(2)}) async-start(bf16[8,264,128]{2,1,0:T(8,128)(2,1)} %broadcast_in_dim.86), calls=%async_computation | async-start | bytes 1081344 | tf_op jit(solution)/shard_map/all_to_all | solution.py:47
  19.1 48.8 %copy-start.6 = (f32[64]{0:T(128)}, f32[64]{0:T(128)S(1)}, u32[]{:S(2)}) copy-start(f32[64]{0:T(128)S(1)} %multiply_power_fusion) | copy-start | bytes 772
  19.8 48.1 %copy-start.4 = (f32[256]{0:T(256)}, f32[256]{0:T(256)S(1)}, u32[]{:S(2)}) copy-start(f32[256]{0:T(256)S(1)} %iota_convert_fusion) | copy-start | bytes 3076
  29.9 16.0 %collective-permute-start.5 = (s32[128]{0:T(128)S(1)}, s32[128]{0:T(128)S(1)}, u32[]{:S(2)}, u32[]{:S(2)}) collective-permute-start(s32[128]{0:T(128)S(1)} %select_reduce_fusion.2), channel_id=1, source_target_pairs={{0,96},{32,128},{64,160},{96,192},{128,224},{160,256},{192,288},{2... | collective-permute-start | bytes 1544 | tf_op jit(solution)/shard_map/ppermute | solution.py:42
  35.1 10.8 %collective-permute-start.4 = (s32[128]{0:T(128)S(1)}, s32[128]{0:T(128)S(1)}, u32[]{:S(2)}, u32[]{:S(2)}) collective-permute-start(s32[128]{0:T(128)S(1)} %select_reduce_fusion.2), channel_id=1, source_target_pairs={{0,64},{32,96},{64,128},{96,160},{128,192},{160,224},{192,256},{22... | collective-permute-start | bytes 1544 | tf_op jit(solution)/shard_map/ppermute | solution.py:42
  41.5 6.6 %collective-permute-start.3 = (s32[128]{0:T(128)S(1)}, s32[128]{0:T(128)S(1)}, u32[]{:S(2)}, u32[]{:S(2)}) collective-permute-start(s32[128]{0:T(128)S(1)} %select_reduce_fusion.2), channel_id=1, source_target_pairs={{0,32},{32,64},{64,96},{96,128},{128,160},{160,192},{192,224},{224... | collective-permute-start | bytes 1544 | tf_op jit(solution)/shard_map/ppermute | solution.py:42
  48.1 19.9 %collective-permute-start.8 = (s32[128]{0:T(128)S(1)}, s32[128]{0:T(128)S(1)}, u32[]{:S(2)}, u32[]{:S(2)}) collective-permute-start(s32[128]{0:T(128)S(1)} %add_add_fusion.3), channel_id=1, source_target_pairs={{0,384},{32,416},{64,448},{96,480},{128,0},{160,32},{192,64},{224,... | collective-permute-start | bytes 1544 | tf_op jit(solution)/shard_map/ppermute | solution.py:42
  53.7 16.4 %collective-permute-start.7 = (s32[128]{0:T(128)S(1)}, s32[128]{0:T(128)S(1)}, u32[]{:S(2)}, u32[]{:S(2)}) collective-permute-start(s32[128]{0:T(128)S(1)} %add_add_fusion.3), channel_id=1, source_target_pairs={{0,256},{32,288},{64,320},{96,352},{128,384},{160,416},{192,448},{... | collective-permute-start | bytes 1544 | tf_op jit(solution)/shard_map/ppermute | solution.py:42
  63.6 9.3 %collective-permute-start.6 = (s32[128]{0:T(128)S(1)}, s32[128]{0:T(128)S(1)}, u32[]{:S(2)}, u32[]{:S(2)}) collective-permute-start(s32[128]{0:T(128)S(1)} %add_add_fusion.3), channel_id=1, source_target_pairs={{0,128},{32,160},{64,192},{96,224},{128,256},{160,288},{192,320},{... | collective-permute-start | bytes 1544 | tf_op jit(solution)/shard_map/ppermute | solution.py:42
  68.0 9.5 %copy-start.8 = (pred[256]{0:T(512)(128)(4,1)S(1)}, pred[256]{0:T(512)(128)(4,1)}, u32[]{:S(2)}) copy-start(pred[256]{0:T(512)(128)(4,1)} %iota_compare_fusion.5) | copy-start | bytes 772
  68.0 45.3 %copy-start.2 = (bf16[256,768]{1,0:T(8,128)(2,1)S(1)}, bf16[256,768]{1,0:T(8,128)(2,1)}, u32[]{:S(2)}) copy-start(bf16[256,768]{1,0:T(8,128)(2,1)} %param.11) | copy-start | bytes 1179652
  68.0 45.2 %collective-permute-start.2 = (bf16[256,768]{1,0:T(8,128)(2,1)}, bf16[256,768]{1,0:T(8,128)(2,1)}, u32[]{:S(2)}, u32[]{:S(2)}) collective-permute-start(bf16[256,768]{1,0:T(8,128)(2,1)} %param.11), channel_id=1, source_target_pairs={{0,3},{1,0},{2,1},{3,2},{4,7},{5,4},{6,5},{7,6},{8,11},{9,8},{10,9... | collective-permute-start | bytes 1179656 | tf_op jit(solution)/shard_map/ppermute | solution.py:42
  74.9 15.7 %collective-permute-start.11 = (bf16[2,256,128]{2,1,0:T(8,128)(2,1)S(1)}, bf16[2,256,128]{2,1,0:T(8,128)(2,1)S(1)}, u32[]{:S(2)}, u32[]{:S(2)}) collective-permute-start(bf16[2,256,128]{2,1,0:T(8,128)(2,1)S(1)} %select_reduce_fusion), channel_id=1, source_target_pairs={{0,96},{32,128},{64,160},{96,192},{128,224},{160,256},{192,288},{2... | collective-permute-start | bytes 393224 | tf_op jit(solution)/shard_map/ppermute | solution.py:42
  78.2 16.1 %collective-permute-start.10 = (bf16[2,256,128]{2,1,0:T(8,128)(2,1)S(1)}, bf16[2,256,128]{2,1,0:T(8,128)(2,1)S(1)}, u32[]{:S(2)}, u32[]{:S(2)}) collective-permute-start(bf16[2,256,128]{2,1,0:T(8,128)(2,1)S(1)} %select_reduce_fusion), channel_id=1, source_target_pairs={{0,64},{32,96},{64,128},{96,160},{128,192},{160,224},{192,256},{22... | collective-permute-start | bytes 393224 | tf_op jit(solution)/shard_map/ppermute | solution.py:42
  90.5 8.1 %collective-permute-start.9 = (bf16[2,256,128]{2,1,0:T(8,128)(2,1)S(1)}, bf16[2,256,128]{2,1,0:T(8,128)(2,1)S(1)}, u32[]{:S(2)}, u32[]{:S(2)}) collective-permute-start(bf16[2,256,128]{2,1,0:T(8,128)(2,1)S(1)} %select_reduce_fusion), channel_id=1, source_target_pairs={{0,32},{32,64},{64,96},{96,128},{128,160},{160,192},{192,224},{224... | collective-permute-start | bytes 393224 | tf_op jit(solution)/shard_map/ppermute | solution.py:42
  98.6 20.5 %collective-permute-start.14 = (bf16[2,256,128]{2,1,0:T(8,128)(2,1)S(1)}, bf16[2,256,128]{2,1,0:T(8,128)(2,1)S(1)}, u32[]{:S(2)}, u32[]{:S(2)}) collective-permute-start(bf16[2,256,128]{2,1,0:T(8,128)(2,1)S(1)} %add_add_fusion.1), channel_id=1, source_target_pairs={{0,384},{32,416},{64,448},{96,480},{128,0},{160,32},{192,64},{224,... | collective-permute-start | bytes 393224 | tf_op jit(solution)/shard_map/ppermute | solution.py:42
  101.0 25.8 %collective-permute-start.13 = (bf16[2,256,128]{2,1,0:T(8,128)(2,1)S(1)}, bf16[2,256,128]{2,1,0:T(8,128)(2,1)S(1)}, u32[]{:S(2)}, u32[]{:S(2)}) collective-permute-start(bf16[2,256,128]{2,1,0:T(8,128)(2,1)S(1)} %add_add_fusion.1), channel_id=1, source_target_pairs={{0,256},{32,288},{64,320},{96,352},{128,384},{160,416},{192,448},{... | collective-permute-start | bytes 393224 | tf_op jit(solution)/shard_map/ppermute | solution.py:42
  109.6 21.2 %collective-permute-start.12 = (bf16[2,256,128]{2,1,0:T(8,128)(2,1)S(1)}, bf16[2,256,128]{2,1,0:T(8,128)(2,1)S(1)}, u32[]{:S(2)}, u32[]{:S(2)}) collective-permute-start(bf16[2,256,128]{2,1,0:T(8,128)(2,1)S(1)} %add_add_fusion.1), channel_id=1, source_target_pairs={{0,128},{32,160},{64,192},{96,224},{128,256},{160,288},{192,320},{... | collective-permute-start | bytes 393224 | tf_op jit(solution)/shard_map/ppermute | solution.py:42
  132.0 20.2 %all-to-all-start.1 = ((bf16[8,2,256,128]{3,2,1,0:T(8,128)(2,1)}), bf16[8,2,256,128]{3,2,1,0:T(8,128)(2,1)}, u32[]{:S(2)}, u32[]{:S(2)}) async-start(bf16[8,2,256,128]{3,2,1,0:T(8,128)(2,1)} %broadcast_in_dim.139), calls=%async_computation.1 | async-start | bytes 2097152 | tf_op jit(solution)/shard_map/all_to_all | solution.py:47
  141.6 2.2 %copy-start.1 = (bf16[256,4,768]{0,2,1:T(8,128)(2,1)S(1)}, bf16[256,4,768]{0,2,1:T(8,128)(2,1)}, u32[]{:S(2)}) copy-start(bf16[256,4,768]{0,2,1:T(8,128)(2,1)} %copy.45) | copy-start | bytes 4718596
  153.3 10.1 %collective-permute-start.17 = (f32[32,256]{1,0:T(8,128)S(1)}, f32[32,256]{1,0:T(8,128)S(1)}, u32[]{:S(2)}, u32[]{:S(2)}) collective-permute-start(f32[32,256]{1,0:T(8,128)S(1)} %fusion.48), channel_id=1, source_target_pairs={{0,3},{1,0},{2,1},{3,2},{4,7},{5,4},{6,5},{7,6},{8,11},{9,8},{10,9... | collective-permute-start | bytes 98312 | tf_op jit(solution)/shard_map/ppermute | solution.py:42
  155.3 8.1 %collective-permute-start.16 = (f32[32,256]{1,0:T(8,128)S(1)}, f32[32,256]{1,0:T(8,128)S(1)}, u32[]{:S(2)}, u32[]{:S(2)}) collective-permute-start(f32[32,256]{1,0:T(8,128)S(1)} %fusion.48), channel_id=1, source_target_pairs={{0,2},{1,3},{2,0},{3,1},{4,6},{5,7},{6,4},{7,5},{8,10},{9,11},{10,... | collective-permute-start | bytes 98312 | tf_op jit(solution)/shard_map/ppermute | solution.py:42
  158.1 6.9 %collective-permute-start.15 = (f32[32,256]{1,0:T(8,128)S(1)}, f32[32,256]{1,0:T(8,128)S(1)}, u32[]{:S(2)}, u32[]{:S(2)}) collective-permute-start(f32[32,256]{1,0:T(8,128)S(1)} %fusion.48), channel_id=1, source_target_pairs={{0,1},{1,2},{2,3},{3,0},{4,5},{5,6},{6,7},{7,4},{8,9},{9,10},{10,1... | collective-permute-start | bytes 98312 | tf_op jit(solution)/shard_map/ppermute | solution.py:42
  166.6 9.0 %collective-permute-start.20 = (bf16[256,128]{0,1:T(8,128)(2,1)}, bf16[256,128]{0,1:T(8,128)(2,1)}, u32[]{:S(2)}, u32[]{:S(2)}) collective-permute-start(bf16[256,128]{0,1:T(8,128)(2,1)} %fusion.6), channel_id=1, source_target_pairs={{0,1},{1,2},{4,5},{5,6},{8,9},{9,10},{12,13},{13,14},{16,17},{17,1... | collective-permute-start | bytes 196616 | tf_op jit(solution)/shard_map/ppermute | solution.py:42
  167.9 14.3 %collective-permute-start.19 = (bf16[256,128]{0,1:T(8,128)(2,1)}, bf16[256,128]{0,1:T(8,128)(2,1)}, u32[]{:S(2)}, u32[]{:S(2)}) collective-permute-start(bf16[256,128]{0,1:T(8,128)(2,1)} %fusion.6), channel_id=1, source_target_pairs={{2,1},{3,2},{6,5},{7,6},{10,9},{11,10},{14,13},{15,14},{18,17},{19... | collective-permute-start | bytes 196616 | tf_op jit(solution)/shard_map/ppermute | solution.py:42
  172.4 8.0 %collective-permute-start.18 = (bf16[256,128]{0,1:T(8,128)(2,1)}, bf16[256,128]{0,1:T(8,128)(2,1)}, u32[]{:S(2)}, u32[]{:S(2)}) collective-permute-start(bf16[256,128]{0,1:T(8,128)(2,1)} %fusion.6), channel_id=1, source_target_pairs={{1,3},{2,0},{5,7},{6,4},{9,11},{10,8},{13,15},{14,12},{17,19},{18,... | collective-permute-start | bytes 196616 | tf_op jit(solution)/shard_map/ppermute | solution.py:42
  174.2 7.1 %copy-start.5 = (f32[256]{0:T(256)S(1)}, f32[256]{0:T(256)}, u32[]{:S(2)}) copy-start(f32[256]{0:T(256)} %copy-done.4) | copy-start | bytes 3076
  174.2 7.1 %copy-start.7 = (f32[64]{0:T(128)S(1)}, f32[64]{0:T(128)}, u32[]{:S(2)}) copy-start(f32[64]{0:T(128)} %copy-done.6) | copy-start | bytes 772
  174.4 7.2 %copy-start.3 = (pred[256,256]{0,1:T(8,128)(4,1)S(1)}, pred[256,256]{0,1:T(8,128)(4,1)}, u32[]{:S(2)}) copy-start(pred[256,256]{0,1:T(8,128)(4,1)} %fusion.9) | copy-start | bytes 196612
  175.6 6.5 %copy-start.9 = (pred[256]{0:T(512)(128)(4,1)S(1)}, pred[256]{0:T(512)(128)(4,1)}, u32[]{:S(2)}) copy-start(pred[256]{0:T(512)(128)(4,1)} %iota_compare_fusion.5) | copy-start | bytes 772

commit v5 on v4

--- a/solution.py
+++ b/solution.py
@@ -100,11 +100,7 @@
     plane_req = iz * ny + jnp.arange(ny, dtype=jnp.int32)
     plane_tags = plane[:, n_row, 0].astype(jnp.int32)
 
-    req_range = jnp.arange(n_req, dtype=jnp.int32)
-    slots_all = jnp.sum(
-        jnp.where(req_range[None, :] == plane_req[:, None], plane_tags[:, None], 0), axis=0
-    )
-    slots_all = spread_sum(slots_all, "rz", nz)
+    slots_all = gather_over(plane_tags, "rz", nz).reshape(n_req)
     slot_range = jnp.arange(n_req * store_rows, dtype=jnp.int32)
     used = jnp.any(slots_all[:, None] == slot_range[None, :], axis=0).astype(jnp.int32)
     prefix = jnp.sum(

time: 186 us -> 174 us (0.935)
  the two profiles are of different devices: /device:TPU:6 before, /device:TPU:32 now
where the time goes in v5:
time: 174 us; the launch traced here: 173 us
  starting transfers between devices  73.9 us (42%)
  waiting for transfers between devices  55.9 us (32%)
  local copies, waits for them, and re-layouts  15.6 us (9%)
  other arithmetic  14 us (8%)
  between operations  7.04 us (4%)
  matrix products  6.73 us (4%)
    ppermute x15, starting transfers between devices, shifted(): return lax.ppermute(x, axis, pairs)  50 us
    ppermute x15, waiting for transfers between devices, shifted(): return lax.ppermute(x, axis, pairs)  32.8 us
    all_to_all x3, starting transfers between devices, gather_over(): return lax.all_to_all(copies, axis, 0, 0, tiled=True)  23.9 us
    all_to_all x3, waiting for transfers between devices, gather_over(): return lax.all_to_all(copies, axis, 0, 0, tiled=True)  23.1 us
  transfers between devices with their start and end apart: 18, of which 10 were waited for; matrix products, arithmetic and copies ran while one was open for 18% of the time, Pallas kernels for 0%

profile of v5, /device:TPU:32, one launch (start us, length us, event | category | flops | bytes accessed | tf_op | source)
XLA Modules:
  0.0 173.1 jit_solution(14861220435401316393)
XLA Ops:
  0.0 5.1 %collective-permute-start.1 = (bf16[256,768]{1,0:T(8,128)(2,1)}, bf16[256,768]{1,0:T(8,128)(2,1)}, u32[]{:S(2)}, u32[]{:S(2)}) collective-permute-start(bf16[256,768]{1,0:T(8,128)(2,1)} %param.11), channel_id=1, source_target_pairs={{0,2},{1,3},{2,0},{3,1},{4,6},{5,7},{6,4},{7,5},{8,10},{9,11},{10,... | collective-permute-start | bytes 1179656 | tf_op jit(solution)/shard_map/ppermute | solution.py:42
  5.1 2.5 %collective-permute-start = (bf16[256,768]{1,0:T(8,128)(2,1)}, bf16[256,768]{1,0:T(8,128)(2,1)}, u32[]{:S(2)}, u32[]{:S(2)}) collective-permute-start(bf16[256,768]{1,0:T(8,128)(2,1)} %param.11), channel_id=1, source_target_pairs={{0,1},{1,2},{2,3},{3,0},{4,5},{5,6},{6,7},{7,4},{8,9},{9,10},{10,1... | collective-permute-start | bytes 1179656 | tf_op jit(solution)/shard_map/ppermute | solution.py:42
  7.6 4.6 %collective-permute-start.2 = (bf16[256,768]{1,0:T(8,128)(2,1)}, bf16[256,768]{1,0:T(8,128)(2,1)}, u32[]{:S(2)}, u32[]{:S(2)}) collective-permute-start(bf16[256,768]{1,0:T(8,128)(2,1)} %param.11), channel_id=1, source_target_pairs={{0,3},{1,0},{2,1},{3,2},{4,7},{5,4},{6,5},{7,6},{8,11},{9,8},{10,9... | collective-permute-start | bytes 1179656 | tf_op jit(solution)/shard_map/ppermute | solution.py:42
  12.8 1.4 fusion.39
  14.8 0.7 reshape_squeeze.3
  15.6 0.9 reshape.443
  16.4 0.7 fusion.20
  17.1 0.9 broadcast_in_dim.76
  18.0 4.5 %all-to-all-start = ((bf16[8,264,128]{2,1,0:T(8,128)(2,1)}), bf16[8,264,128]{2,1,0:T(8,128)(2,1)S(1)}, u32[]{:S(2)}, u32[]{:S(2)}) async-start(bf16[8,264,128]{2,1,0:T(8,128)(2,1)} %broadcast_in_dim.76), calls=%async_computation | async-start | bytes 1081344 | tf_op jit(solution)/shard_map/all_to_all | solution.py:47
  23.8 1.2 multiply_cosine_fusion
  25.0 8.0 %all-to-all-done = bf16[8,264,128]{2,1,0:T(8,128)(2,1)S(1)} async-done(((bf16[8,264,128]{2,1,0:T(8,128)(2,1)}), bf16[8,264,128]{2,1,0:T(8,128)(2,1)S(1)}, u32[]{:S(2)}, u32[]{:S(2)}) %all-to-all-start) | async-done | bytes 540704 | tf_op jit(solution)/shard_map/all_to_all | solution.py:47
  33.8 15.2 %all-to-all-start.1 = ((s32[16,1,8]{2,1,0:T(1,128)}), s32[16,1,8]{2,1,0:T(1,128)S(1)}, u32[]{:S(2)}, u32[]{:S(2)}) async-start(s32[16,1,8]{2,1,0:T(1,128)} %broadcast_in_dim.77), calls=%async_computation.1 | async-start | bytes 16384 | tf_op jit(solution)/shard_map/all_to_all | solution.py:47
  49.1 11.0 %all-to-all-done.1 = s32[16,1,8]{2,1,0:T(1,128)S(1)} async-done(((s32[16,1,8]{2,1,0:T(1,128)}), s32[16,1,8]{2,1,0:T(1,128)S(1)}, u32[]{:S(2)}, u32[]{:S(2)}) %all-to-all-start.1) | async-done | bytes 544 | tf_op jit(solution)/shard_map/all_to_all | solution.py:47
  63.2 2.5 %collective-permute-start.5 = (bf16[2,256,128]{2,1,0:T(8,128)(2,1)S(1)}, bf16[2,256,128]{2,1,0:T(8,128)(2,1)S(1)}, u32[]{:S(2)}, u32[]{:S(2)}) collective-permute-start(bf16[2,256,128]{2,1,0:T(8,128)(2,1)S(1)} %select_reduce_fusion), channel_id=1, source_target_pairs={{0,96},{32,128},{64,160},{96,192},{128,224},{160,256},{192,288},{2... | collective-permute-start | bytes 393224 | tf_op jit(solution)/shard_map/ppermute | solution.py:42
  65.7 0.8 fusion.9
  66.4 2.5 %collective-permute-start.4 = (bf16[2,256,128]{2,1,0:T(8,128)(2,1)S(1)}, bf16[2,256,128]{2,1,0:T(8,128)(2,1)S(1)}, u32[]{:S(2)}, u32[]{:S(2)}) collective-permute-start(bf16[2,256,128]{2,1,0:T(8,128)(2,1)S(1)} %select_reduce_fusion), channel_id=1, source_target_pairs={{0,64},{32,96},{64,128},{96,160},{128,192},{160,224},{192,256},{22... | collective-permute-start | bytes 393224 | tf_op jit(solution)/shard_map/ppermute | solution.py:42
  69.0 7.2 %collective-permute-done.5 = bf16[2,256,128]{2,1,0:T(8,128)(2,1)S(1)} collective-permute-done((bf16[2,256,128]{2,1,0:T(8,128)(2,1)S(1)}, bf16[2,256,128]{2,1,0:T(8,128)(2,1)S(1)}, u32[]{:S(2)}, u32[]{:S(2)}) %collective-permute-start.5) | collective-permute-done | bytes 131104 | tf_op jit(solution)/shard_map/ppermute | solution.py:42
  76.2 8.0 %collective-permute-start.3 = (bf16[2,256,128]{2,1,0:T(8,128)(2,1)S(1)}, bf16[2,256,128]{2,1,0:T(8,128)(2,1)S(1)}, u32[]{:S(2)}, u32[]{:S(2)}) collective-permute-start(bf16[2,256,128]{2,1,0:T(8,128)(2,1)S(1)} %select_reduce_fusion), channel_id=1, source_target_pairs={{0,32},{32,64},{64,96},{96,128},{128,160},{160,192},{192,224},{224... | collective-permute-start | bytes 393224 | tf_op jit(solution)/shard_map/ppermute | solution.py:42
  86.7 3.5 %collective-permute-start.8 = (bf16[2,256,128]{2,1,0:T(8,128)(2,1)S(1)}, bf16[2,256,128]{2,1,0:T(8,128)(2,1)S(1)}, u32[]{:S(2)}, u32[]{:S(2)}) collective-permute-start(bf16[2,256,128]{2,1,0:T(8,128)(2,1)S(1)} %add_add_fusion.1), channel_id=1, source_target_pairs={{0,384},{32,416},{64,448},{96,480},{128,0},{160,32},{192,64},{224,... | collective-permute-start | bytes 393224 | tf_op jit(solution)/shard_map/ppermute | solution.py:42
  90.2 6.3 %collective-permute-start.7 = (bf16[2,256,128]{2,1,0:T(8,128)(2,1)S(1)}, bf16[2,256,128]{2,1,0:T(8,128)(2,1)S(1)}, u32[]{:S(2)}, u32[]{:S(2)}) collective-permute-start(bf16[2,256,128]{2,1,0:T(8,128)(2,1)S(1)} %add_add_fusion.1), channel_id=1, source_target_pairs={{0,256},{32,288},{64,320},{96,352},{128,384},{160,416},{192,448},{... | collective-permute-start | bytes 393224 | tf_op jit(solution)/shard_map/ppermute | solution.py:42
  96.5 2.9 %collective-permute-start.6 = (bf16[2,256,128]{2,1,0:T(8,128)(2,1)S(1)}, bf16[2,256,128]{2,1,0:T(8,128)(2,1)S(1)}, u32[]{:S(2)}, u32[]{:S(2)}) collective-permute-start(bf16[2,256,128]{2,1,0:T(8,128)(2,1)S(1)} %add_add_fusion.1), channel_id=1, source_target_pairs={{0,128},{32,160},{64,192},{96,224},{128,256},{160,288},{192,320},{... | collective-permute-start | bytes 393224 | tf_op jit(solution)/shard_map/ppermute | solution.py:42
  99.4 2.6 %pad_maximum_fusion = bf16[4,256,768]{2,1,0:T(8,128)(2,1)} fusion(bf16[1,256,768]{2,1,0:T(8,128)(2,1)} %bitcast.4, bf16[1,256,768]{2,1,0:T(8,128)(2,1)} %bitcast.3, bf16[1,256,768]{2,1,0:T(8,128)(2,1)} %bitcast.2, bf16[1,256,768]{2,1,0:T(8,128)(2,1)S(1)} %bitcast.75), kind=kLoop, calls=%fused_computation.3 | loop fusion | flops 2359296 | bytes 3145728 | tf_op jit(solution)/shard_map/stack | solution.py:127
  102.0 3.2 %gather_fusion = bf16[4,256,768]{2,1,0:T(8,128)(2,1)} fusion(bf16[4,256,768]{2,1,0:T(8,128)(2,1)} %pad_maximum_fusion, s32[1024]{0:T(1024)S(1)} %pad_clamp_fusion.1), kind=kCustom, calls=%fused_computation | custom fusion | bytes 3145744 | tf_op jit(solution)/shard_map/jit(_take)/gather | solution.py:129
  105.2 5.2 %collective-permute-done.7 = bf16[2,256,128]{2,1,0:T(8,128)(2,1)S(1)} collective-permute-done((bf16[2,256,128]{2,1,0:T(8,128)(2,1)S(1)}, bf16[2,256,128]{2,1,0:T(8,128)(2,1)S(1)}, u32[]{:S(2)}, u32[]{:S(2)}) %collective-permute-start.7) | collective-permute-done | bytes 131104 | tf_op jit(solution)/shard_map/ppermute | solution.py:42
  110.4 11.4 %collective-permute-done.6 = bf16[2,256,128]{2,1,0:T(8,128)(2,1)S(1)} collective-permute-done((bf16[2,256,128]{2,1,0:T(8,128)(2,1)S(1)}, bf16[2,256,128]{2,1,0:T(8,128)(2,1)S(1)}, u32[]{:S(2)}, u32[]{:S(2)}) %collective-permute-start.6) | collective-permute-done | bytes 131104 | tf_op jit(solution)/shard_map/ppermute | solution.py:42
  121.8 1.2 broadcast_in_dim.128
  123.0 4.2 %all-to-all-start.2 = ((bf16[8,2,256,128]{3,2,1,0:T(8,128)(2,1)}), bf16[8,2,256,128]{3,2,1,0:T(8,128)(2,1)}, u32[]{:S(2)}, u32[]{:S(2)}) async-start(bf16[8,2,256,128]{3,2,1,0:T(8,128)(2,1)} %broadcast_in_dim.128), calls=%async_computation.2 | async-start | bytes 2097152 | tf_op jit(solution)/shard_map/all_to_all | solution.py:47
  127.2 2.8 %select_bitcast_fusion = bf16[256,4,768]{2,0,1:T(8,128)(2,1)} fusion(bf16[4,256,768]{2,1,0:T(8,128)(2,1)} %gather_fusion, pred[4]{0:T(512)(128)(4,1)S(1)} %compare_and_fusion.1), kind=kLoop, calls=%fused_computation.4 | loop fusion | flops 786432 | bytes 3145732 | tf_op jit(solution)/shard_map/jit(_take)/select_n | solution.py:129
  130.0 2.6 %copy.45 = bf16[256,4,768]{0,2,1:T(8,128)(2,1)} copy(bf16[256,4,768]{2,0,1:T(8,128)(2,1)} %select_bitcast_fusion) | data formatting | bytes 3145728 | tf_op jit(solution)/shard_map/jit(_take)/select_n | solution.py:129
  132.6 2.2 %fusion.47 = f32[256,128]{0,1:T(8,128)S(1)} fusion(bf16[256,3072]{0,1:T(8,128)(2,1)} %bitcast.73, bf16[3072,128]{1,0:T(8,128)(2,1)} %param.13), kind=kOutput, calls=%fused_computation.98 | convolution fusion | flops 201326592 | bytes 2490368 | tf_op jit(solution)/shard_map/dot_general | solution.py:140
  134.8 1.0 fusion.49
  139.0 4.2 %all-to-all-done.2 = bf16[8,2,256,128]{3,2,1,0:T(8,128)(2,1)} async-done(((bf16[8,2,256,128]{3,2,1,0:T(8,128)(2,1)}), bf16[8,2,256,128]{3,2,1,0:T(8,128)(2,1)}, u32[]{:S(2)}, u32[]{:S(2)}) %all-to-all-start.2) | async-done | bytes 1048608 | tf_op jit(solution)/shard_map/all_to_all | solution.py:47
  143.2 0.8 constant_dynamic-slice_fusion
  144.3 2.0 %collective-permute-start.11 = (f32[32,256]{1,0:T(8,128)S(1)}, f32[32,256]{1,0:T(8,128)S(1)}, u32[]{:S(2)}, u32[]{:S(2)}) collective-permute-start(f32[32,256]{1,0:T(8,128)S(1)} %fusion.48), channel_id=1, source_target_pairs={{0,3},{1,0},{2,1},{3,2},{4,7},{5,4},{6,5},{7,6},{8,11},{9,8},{10,9... | collective-permute-start | bytes 98312 | tf_op jit(solution)/shard_map/ppermute | solution.py:42
  146.3 3.3 %collective-permute-start.10 = (f32[32,256]{1,0:T(8,128)S(1)}, f32[32,256]{1,0:T(8,128)S(1)}, u32[]{:S(2)}, u32[]{:S(2)}) collective-permute-start(f32[32,256]{1,0:T(8,128)S(1)} %fusion.48), channel_id=1, source_target_pairs={{0,2},{1,3},{2,0},{3,1},{4,6},{5,7},{6,4},{7,5},{8,10},{9,11},{10,... | collective-permute-start | bytes 98312 | tf_op jit(solution)/shard_map/ppermute | solution.py:42
  149.6 2.5 %collective-permute-start.9 = (f32[32,256]{1,0:T(8,128)S(1)}, f32[32,256]{1,0:T(8,128)S(1)}, u32[]{:S(2)}, u32[]{:S(2)}) collective-permute-start(f32[32,256]{1,0:T(8,128)S(1)} %fusion.48), channel_id=1, source_target_pairs={{0,1},{1,2},{2,3},{3,0},{4,5},{5,6},{6,7},{7,4},{8,9},{9,10},{10,1... | collective-permute-start | bytes 98312 | tf_op jit(solution)/shard_map/ppermute | solution.py:42
  152.1 0.7 constant_dynamic-slice_fusion.1
  152.9 0.7 collective-permute-done.10
  153.6 3.1 %collective-permute-done.9 = f32[32,256]{1,0:T(8,128)S(1)} collective-permute-done((f32[32,256]{1,0:T(8,128)S(1)}, f32[32,256]{1,0:T(8,128)S(1)}, u32[]{:S(2)}, u32[]{:S(2)}) %collective-permute-start.9) | collective-permute-done | bytes 32800 | tf_op jit(solution)/shard_map/ppermute | solution.py:42
  156.7 1.5 fusion.6
  158.2 1.9 %collective-permute-start.14 = (bf16[256,128]{0,1:T(8,128)(2,1)}, bf16[256,128]{0,1:T(8,128)(2,1)}, u32[]{:S(2)}, u32[]{:S(2)}) collective-permute-start(bf16[256,128]{0,1:T(8,128)(2,1)} %fusion.6), channel_id=1, source_target_pairs={{0,1},{1,2},{4,5},{5,6},{8,9},{9,10},{12,13},{13,14},{16,17},{17,1... | collective-permute-start | bytes 196616 | tf_op jit(solution)/shard_map/ppermute | solution.py:42
  160.1 1.3 collective-permute-start.13
  161.4 1.3 collective-permute-start.12
  163.5 1.1 fusion.10
  164.6 4.8 %collective-permute-done.12 = bf16[256,128]{0,1:T(8,128)(2,1)} collective-permute-done((bf16[256,128]{0,1:T(8,128)(2,1)}, bf16[256,128]{0,1:T(8,128)(2,1)}, u32[]{:S(2)}, u32[]{:S(2)}) %collective-permute-start.12) | collective-permute-done | bytes 65568 | tf_op jit(solution)/shard_map/ppermute | solution.py:42
  169.3 0.9 bitcast_convert_fusion
  171.1 1.1 fusion.4
  172.3 0.8 copy.51
  (67 shorter events, 7.7 us)
Async XLA Ops:
  0.0 134.8 %copy-start = (bf16[3072,384]{1,0:T(8,128)(2,1)S(1)}, bf16[3072,384]{1,0:T(8,128)(2,1)}, u32[]{:S(2)}) copy-start(bf16[3072,384]{1,0:T(8,128)(2,1)} %param.12) | copy-start | bytes 7077892
  0.0 96.5 %collective-permute-start.1 = (bf16[256,768]{1,0:T(8,128)(2,1)}, bf16[256,768]{1,0:T(8,128)(2,1)}, u32[]{:S(2)}, u32[]{:S(2)}) collective-permute-start(bf16[256,768]{1,0:T(8,128)(2,1)} %param.11), channel_id=1, source_target_pairs={{0,2},{1,3},{2,0},{3,1},{4,6},{5,7},{6,4},{7,5},{8,10},{9,11},{10,... | collective-permute-start | bytes 1179656 | tf_op jit(solution)/shard_map/ppermute | solution.py:42
  5.1 94.3 %collective-permute-start = (bf16[256,768]{1,0:T(8,128)(2,1)}, bf16[256,768]{1,0:T(8,128)(2,1)}, u32[]{:S(2)}, u32[]{:S(2)}) collective-permute-start(bf16[256,768]{1,0:T(8,128)(2,1)} %param.11), channel_id=1, source_target_pairs={{0,1},{1,2},{2,3},{3,0},{4,5},{5,6},{6,7},{7,4},{8,9},{9,10},{10,1... | collective-permute-start | bytes 1179656 | tf_op jit(solution)/shard_map/ppermute | solution.py:42
  7.6 91.8 %collective-permute-start.2 = (bf16[256,768]{1,0:T(8,128)(2,1)}, bf16[256,768]{1,0:T(8,128)(2,1)}, u32[]{:S(2)}, u32[]{:S(2)}) collective-permute-start(bf16[256,768]{1,0:T(8,128)(2,1)} %param.11), channel_id=1, source_target_pairs={{0,3},{1,0},{2,1},{3,2},{4,7},{5,4},{6,5},{7,6},{8,11},{9,8},{10,9... | collective-permute-start | bytes 1179656 | tf_op jit(solution)/shard_map/ppermute | solution.py:42
  18.0 15.0 %all-to-all-start = ((bf16[8,264,128]{2,1,0:T(8,128)(2,1)}), bf16[8,264,128]{2,1,0:T(8,128)(2,1)S(1)}, u32[]{:S(2)}, u32[]{:S(2)}) async-start(bf16[8,264,128]{2,1,0:T(8,128)(2,1)} %broadcast_in_dim.76), calls=%async_computation | async-start | bytes 1081344 | tf_op jit(solution)/shard_map/all_to_all | solution.py:47
  22.5 26.6 %copy-start.6 = (f32[64]{0:T(128)}, f32[64]{0:T(128)S(1)}, u32[]{:S(2)}) copy-start(f32[64]{0:T(128)S(1)} %multiply_power_fusion) | copy-start | bytes 772
  23.7 25.3 %copy-start.4 = (f32[256]{0:T(256)}, f32[256]{0:T(256)S(1)}, u32[]{:S(2)}) copy-start(f32[256]{0:T(256)S(1)} %iota_convert_fusion) | copy-start | bytes 3076
  33.8 26.3 %all-to-all-start.1 = ((s32[16,1,8]{2,1,0:T(1,128)}), s32[16,1,8]{2,1,0:T(1,128)S(1)}, u32[]{:S(2)}, u32[]{:S(2)}) async-start(s32[16,1,8]{2,1,0:T(1,128)} %broadcast_in_dim.77), calls=%async_computation.1 | async-start | bytes 16384 | tf_op jit(solution)/shard_map/all_to_all | solution.py:47
  49.1 16.6 %copy-start.8 = (pred[256]{0:T(512)(128)(4,1)S(1)}, pred[256]{0:T(512)(128)(4,1)}, u32[]{:S(2)}) copy-start(pred[256]{0:T(512)(128)(4,1)} %iota_compare_fusion.4) | copy-start | bytes 772
  49.1 50.3 %copy-start.2 = (bf16[256,768]{1,0:T(8,128)(2,1)S(1)}, bf16[256,768]{1,0:T(8,128)(2,1)}, u32[]{:S(2)}) copy-start(bf16[256,768]{1,0:T(8,128)(2,1)} %param.11) | copy-start | bytes 1179652
  63.2 13.0 %collective-permute-start.5 = (bf16[2,256,128]{2,1,0:T(8,128)(2,1)S(1)}, bf16[2,256,128]{2,1,0:T(8,128)(2,1)S(1)}, u32[]{:S(2)}, u32[]{:S(2)}) collective-permute-start(bf16[2,256,128]{2,1,0:T(8,128)(2,1)S(1)} %select_reduce_fusion), channel_id=1, source_target_pairs={{0,96},{32,128},{64,160},{96,192},{128,224},{160,256},{192,288},{2... | collective-permute-start | bytes 393224 | tf_op jit(solution)/shard_map/ppermute | solution.py:42
  66.4 19.8 %collective-permute-start.4 = (bf16[2,256,128]{2,1,0:T(8,128)(2,1)S(1)}, bf16[2,256,128]{2,1,0:T(8,128)(2,1)S(1)}, u32[]{:S(2)}, u32[]{:S(2)}) collective-permute-start(bf16[2,256,128]{2,1,0:T(8,128)(2,1)S(1)} %select_reduce_fusion), channel_id=1, source_target_pairs={{0,64},{32,96},{64,128},{96,160},{128,192},{160,224},{192,256},{22... | collective-permute-start | bytes 393224 | tf_op jit(solution)/shard_map/ppermute | solution.py:42
  76.2 10.5 %collective-permute-start.3 = (bf16[2,256,128]{2,1,0:T(8,128)(2,1)S(1)}, bf16[2,256,128]{2,1,0:T(8,128)(2,1)S(1)}, u32[]{:S(2)}, u32[]{:S(2)}) collective-permute-start(bf16[2,256,128]{2,1,0:T(8,128)(2,1)S(1)} %select_reduce_fusion), channel_id=1, source_target_pairs={{0,32},{32,64},{64,96},{96,128},{128,160},{160,192},{192,224},{224... | collective-permute-start | bytes 393224 | tf_op jit(solution)/shard_map/ppermute | solution.py:42
  86.7 18.5 %collective-permute-start.8 = (bf16[2,256,128]{2,1,0:T(8,128)(2,1)S(1)}, bf16[2,256,128]{2,1,0:T(8,128)(2,1)S(1)}, u32[]{:S(2)}, u32[]{:S(2)}) collective-permute-start(bf16[2,256,128]{2,1,0:T(8,128)(2,1)S(1)} %add_add_fusion.1), channel_id=1, source_target_pairs={{0,384},{32,416},{64,448},{96,480},{128,0},{160,32},{192,64},{224,... | collective-permute-start | bytes 393224 | tf_op jit(solution)/shard_map/ppermute | solution.py:42
  90.2 20.2 %collective-permute-start.7 = (bf16[2,256,128]{2,1,0:T(8,128)(2,1)S(1)}, bf16[2,256,128]{2,1,0:T(8,128)(2,1)S(1)}, u32[]{:S(2)}, u32[]{:S(2)}) collective-permute-start(bf16[2,256,128]{2,1,0:T(8,128)(2,1)S(1)} %add_add_fusion.1), channel_id=1, source_target_pairs={{0,256},{32,288},{64,320},{96,352},{128,384},{160,416},{192,448},{... | collective-permute-start | bytes 393224 | tf_op jit(solution)/shard_map/ppermute | solution.py:42
  96.5 25.3 %collective-permute-start.6 = (bf16[2,256,128]{2,1,0:T(8,128)(2,1)S(1)}, bf16[2,256,128]{2,1,0:T(8,128)(2,1)S(1)}, u32[]{:S(2)}, u32[]{:S(2)}) collective-permute-start(bf16[2,256,128]{2,1,0:T(8,128)(2,1)S(1)} %add_add_fusion.1), channel_id=1, source_target_pairs={{0,128},{32,160},{64,192},{96,224},{128,256},{160,288},{192,320},{... | collective-permute-start | bytes 393224 | tf_op jit(solution)/shard_map/ppermute | solution.py:42
  123.0 20.2 %all-to-all-start.2 = ((bf16[8,2,256,128]{3,2,1,0:T(8,128)(2,1)}), bf16[8,2,256,128]{3,2,1,0:T(8,128)(2,1)}, u32[]{:S(2)}, u32[]{:S(2)}) async-start(bf16[8,2,256,128]{3,2,1,0:T(8,128)(2,1)} %broadcast_in_dim.128), calls=%async_computation.2 | async-start | bytes 2097152 | tf_op jit(solution)/shard_map/all_to_all | solution.py:47
  132.6 2.2 %copy-start.1 = (bf16[256,4,768]{0,2,1:T(8,128)(2,1)S(1)}, bf16[256,4,768]{0,2,1:T(8,128)(2,1)}, u32[]{:S(2)}) copy-start(bf16[256,4,768]{0,2,1:T(8,128)(2,1)} %copy.45) | copy-start | bytes 4718596
  144.3 8.6 %collective-permute-start.11 = (f32[32,256]{1,0:T(8,128)S(1)}, f32[32,256]{1,0:T(8,128)S(1)}, u32[]{:S(2)}, u32[]{:S(2)}) collective-permute-start(f32[32,256]{1,0:T(8,128)S(1)} %fusion.48), channel_id=1, source_target_pairs={{0,3},{1,0},{2,1},{3,2},{4,7},{5,4},{6,5},{7,6},{8,11},{9,8},{10,9... | collective-permute-start | bytes 98312 | tf_op jit(solution)/shard_map/ppermute | solution.py:42
  146.3 7.3 %collective-permute-start.10 = (f32[32,256]{1,0:T(8,128)S(1)}, f32[32,256]{1,0:T(8,128)S(1)}, u32[]{:S(2)}, u32[]{:S(2)}) collective-permute-start(f32[32,256]{1,0:T(8,128)S(1)} %fusion.48), channel_id=1, source_target_pairs={{0,2},{1,3},{2,0},{3,1},{4,6},{5,7},{6,4},{7,5},{8,10},{9,11},{10,... | collective-permute-start | bytes 98312 | tf_op jit(solution)/shard_map/ppermute | solution.py:42
  149.6 7.0 %collective-permute-start.9 = (f32[32,256]{1,0:T(8,128)S(1)}, f32[32,256]{1,0:T(8,128)S(1)}, u32[]{:S(2)}, u32[]{:S(2)}) collective-permute-start(f32[32,256]{1,0:T(8,128)S(1)} %fusion.48), channel_id=1, source_target_pairs={{0,1},{1,2},{2,3},{3,0},{4,5},{5,6},{6,7},{7,4},{8,9},{9,10},{10,1... | collective-permute-start | bytes 98312 | tf_op jit(solution)/shard_map/ppermute | solution.py:42
  158.2 6.4 %collective-permute-start.14 = (bf16[256,128]{0,1:T(8,128)(2,1)}, bf16[256,128]{0,1:T(8,128)(2,1)}, u32[]{:S(2)}, u32[]{:S(2)}) collective-permute-start(bf16[256,128]{0,1:T(8,128)(2,1)} %fusion.6), channel_id=1, source_target_pairs={{0,1},{1,2},{4,5},{5,6},{8,9},{9,10},{12,13},{13,14},{16,17},{17,1... | collective-permute-start | bytes 196616 | tf_op jit(solution)/shard_map/ppermute | solution.py:42
  160.1 11.0 %collective-permute-start.13 = (bf16[256,128]{0,1:T(8,128)(2,1)}, bf16[256,128]{0,1:T(8,128)(2,1)}, u32[]{:S(2)}, u32[]{:S(2)}) collective-permute-start(bf16[256,128]{0,1:T(8,128)(2,1)} %fusion.6), channel_id=1, source_target_pairs={{2,1},{3,2},{6,5},{7,6},{10,9},{11,10},{14,13},{15,14},{18,17},{19... | collective-permute-start | bytes 196616 | tf_op jit(solution)/shard_map/ppermute | solution.py:42
  161.4 8.0 %collective-permute-start.12 = (bf16[256,128]{0,1:T(8,128)(2,1)}, bf16[256,128]{0,1:T(8,128)(2,1)}, u32[]{:S(2)}, u32[]{:S(2)}) collective-permute-start(bf16[256,128]{0,1:T(8,128)(2,1)} %fusion.6), channel_id=1, source_target_pairs={{1,3},{2,0},{5,7},{6,4},{9,11},{10,8},{13,15},{14,12},{17,19},{18,... | collective-permute-start | bytes 196616 | tf_op jit(solution)/shard_map/ppermute | solution.py:42
  163.1 7.1 %copy-start.5 = (f32[256]{0:T(256)S(1)}, f32[256]{0:T(256)}, u32[]{:S(2)}) copy-start(f32[256]{0:T(256)} %copy-done.4) | copy-start | bytes 3076
  163.1 7.1 %copy-start.7 = (f32[64]{0:T(128)S(1)}, f32[64]{0:T(128)}, u32[]{:S(2)}) copy-start(f32[64]{0:T(128)} %copy-done.6) | copy-start | bytes 772
  163.3 7.3 %copy-start.3 = (pred[256,256]{0,1:T(8,128)(4,1)S(1)}, pred[256,256]{0,1:T(8,128)(4,1)}, u32[]{:S(2)}) copy-start(pred[256,256]{0,1:T(8,128)(4,1)} %fusion.9) | copy-start | bytes 196612
  164.6 6.6 %copy-start.9 = (pred[256]{0:T(512)(128)(4,1)S(1)}, pred[256]{0:T(512)(128)(4,1)}, u32[]{:S(2)}) copy-start(pred[256]{0:T(512)(128)(4,1)} %iota_compare_fusion.4) | copy-start | bytes 772

commit v6 on v5

--- a/solution.py
+++ b/solution.py
@@ -129,33 +129,47 @@
     piece = jnp.take(stacked, source, axis=0)
     piece = jnp.transpose(piece, (1, 0, 2)).reshape(rows_total, -1)
 
+    key_value_sum = jnp.dot(piece, key_value_weight, preferred_element_type=jnp.float32)
+    from_left = shifted(key_value_sum, 1, n_tp, [(0, 1), (1, 2)])
+    from_right = shifted(key_value_sum, -1, n_tp, [(2, 1), (3, 2)])
+    from_far = shifted(key_value_sum, 2, n_tp, [(1, 3), (2, 0)])
+    key_sum = jnp.where(
+        tp_index == 0, key_value_sum, jnp.where(tp_index == 3, from_far, from_left)
+    )
+    value_sum = jnp.where(
+        tp_index == 3, key_value_sum, jnp.where(tp_index == 0, from_far, from_right)
+    )
+
     rank_part = jnp.einsum("kd,sd->ks", down_t, states, preferred_element_type=jnp.float32)
-    rank_sum = rank_part
-    for s in range(1, n_tp):
-        rank_sum = rank_sum + shifted(rank_part, s, n_tp)
+    n_rank = rank_part.shape[0]
+    up_block = adapter_pair.astype(jnp.float32).reshape(-1, rank_part.shape[1])
+    bundle = jnp.concatenate([rank_part, up_block], axis=0)
+    arrived = [bundle] + [shifted(bundle, s, n_tp) for s in range(1, n_tp)]
+    rank_sum = arrived[0][:n_rank]
+    for part in arrived[1:]:
+        rank_sum = rank_sum + part[:n_rank]
     rank_mid = rank_sum.astype(jnp.bfloat16)
     rank_cols = rank_mid.shape[0] // 2
+    up_all = jnp.stack([part[n_rank:] for part in arrived]).astype(jnp.bfloat16)
+    up_all = up_all.reshape((n_tp,) + adapter_pair.shape)
+    kv_heads = (n_tp * kv_cols) // 2 // HEAD_DIM
+    group_index = tp_index * heads_here // (HEADS // kv_heads)
+    key_up = up_all[(tp_index - group_index) % n_tp]
+    value_up = up_all[(tp_index - kv_heads - group_index) % n_tp]
 
     query_total = jnp.dot(piece, query_weight, preferred_element_type=jnp.float32)
-    key_value_sum = jnp.dot(piece, key_value_weight, preferred_element_type=jnp.float32)
     query_addition = jnp.einsum(
         "ks,kc->sc", rank_mid[:rank_cols], adapter_query, preferred_element_type=jnp.float32
     )
-    key_value_extra = jnp.einsum(
-        "ks,kc->sc", rank_mid[rank_cols:], adapter_pair, preferred_element_type=jnp.float32
-    )
     query_plain = query_total + adapter_scale * query_addition
-    key_value_own = (key_value_sum + adapter_scale * key_value_extra).astype(jnp.bfloat16)
-
-    from_left = shifted(key_value_own, 1, n_tp, [(0, 1), (1, 2)])
-    from_right = shifted(key_value_own, -1, n_tp, [(2, 1), (3, 2)])
-    from_far = shifted(key_value_own, 2, n_tp, [(1, 3), (2, 0)])
-    key_block = jnp.where(
-        tp_index == 0, key_value_own, jnp.where(tp_index == 3, from_far, from_left)
-    )
-    value_block = jnp.where(
-        tp_index == 3, key_value_own, jnp.where(tp_index == 0, from_far, from_right)
-    )
+    key_extra = jnp.einsum(
+        "ks,kc->sc", rank_mid[rank_cols:], key_up, preferred_element_type=jnp.float32
+    )
+    value_extra = jnp.einsum(
+        "ks,kc->sc", rank_mid[rank_cols:], value_up, preferred_element_type=jnp.float32
+    )
+    key_block = (key_sum + adapter_scale * key_extra).astype(jnp.bfloat16)
+    value_block = (value_sum + adapter_scale * value_extra).astype(jnp.bfloat16)
 
     queries = rotate(query_plain.reshape(req_dev, slot_len, heads_here, HEAD_DIM)).astype(
         jnp.bfloat16

time: 174 us -> 173 us (level)
  the two profiles are of different devices: /device:TPU:32 before, /device:TPU:40 now
where the time goes in v6:
time: 173 us; the launch traced here: 172 us
  starting transfers between devices  77.2 us (45%)
  waiting for transfers between devices  46.9 us (27%)
  local copies, waits for them, and re-layouts  17.2 us (10%)
  other arithmetic  16.3 us (9%)
  matrix products  7.78 us (4%)
  between operations  6.77 us (4%)
    ppermute x15, starting transfers between devices, shifted(): return lax.ppermute(x, axis, pairs)  51.5 us
    ppermute x15, waiting for transfers between devices, shifted(): return lax.ppermute(x, axis, pairs)  29.4 us
    all_to_all x3, starting transfers between devices, gather_over(): return lax.all_to_all(copies, axis, 0, 0, tiled=True)  25.7 us
    all_to_all x3, waiting for transfers between devices, gather_over(): return lax.all_to_all(copies, axis, 0, 0, tiled=True)  17.6 us
  transfers between devices with their start and end apart: 18, of which 8 were waited for; matrix products, arithmetic and copies ran while one was open for 22% of the time, Pallas kernels for 0%

profile of v6, /device:TPU:40, one launch (start us, length us, event | category | flops | bytes accessed | tf_op | source)
XLA Modules:
  0.0 172.2 jit_solution(14666800133386913906)
XLA Ops:
  0.0 5.1 %collective-permute-start.1 = (bf16[256,768]{1,0:T(8,128)(2,1)}, bf16[256,768]{1,0:T(8,128)(2,1)}, u32[]{:S(2)}, u32[]{:S(2)}) collective-permute-start(bf16[256,768]{1,0:T(8,128)(2,1)} %param.11), channel_id=1, source_target_pairs={{0,2},{1,3},{2,0},{3,1},{4,6},{5,7},{6,4},{7,5},{8,10},{9,11},{10,... | collective-permute-start | bytes 1179656 | tf_op jit(solution)/shard_map/ppermute | solution.py:42
  5.1 2.5 %collective-permute-start = (bf16[256,768]{1,0:T(8,128)(2,1)}, bf16[256,768]{1,0:T(8,128)(2,1)}, u32[]{:S(2)}, u32[]{:S(2)}) collective-permute-start(bf16[256,768]{1,0:T(8,128)(2,1)} %param.11), channel_id=1, source_target_pairs={{0,1},{1,2},{2,3},{3,0},{4,5},{5,6},{6,7},{7,4},{8,9},{9,10},{10,1... | collective-permute-start | bytes 1179656 | tf_op jit(solution)/shard_map/ppermute | solution.py:42
  7.6 4.6 %collective-permute-start.2 = (bf16[256,768]{1,0:T(8,128)(2,1)}, bf16[256,768]{1,0:T(8,128)(2,1)}, u32[]{:S(2)}, u32[]{:S(2)}) collective-permute-start(bf16[256,768]{1,0:T(8,128)(2,1)} %param.11), channel_id=1, source_target_pairs={{0,3},{1,0},{2,1},{3,2},{4,7},{5,4},{6,5},{7,6},{8,11},{9,8},{10,9... | collective-permute-start | bytes 1179656 | tf_op jit(solution)/shard_map/ppermute | solution.py:42
  12.8 1.3 fusion.50
  14.6 0.7 reshape_squeeze.3
  15.3 0.9 reshape.471
  16.9 0.9 broadcast_in_dim.76
  17.8 4.9 %all-to-all-start = ((bf16[8,264,128]{2,1,0:T(8,128)(2,1)}), bf16[8,264,128]{2,1,0:T(8,128)(2,1)S(1)}, u32[]{:S(2)}, u32[]{:S(2)}) async-start(bf16[8,264,128]{2,1,0:T(8,128)(2,1)} %broadcast_in_dim.76), calls=%async_computation | async-start | bytes 1081344 | tf_op jit(solution)/shard_map/all_to_all | solution.py:47
  24.0 1.2 multiply_cosine_fusion
  25.2 6.5 %all-to-all-done = bf16[8,264,128]{2,1,0:T(8,128)(2,1)S(1)} async-done(((bf16[8,264,128]{2,1,0:T(8,128)(2,1)}), bf16[8,264,128]{2,1,0:T(8,128)(2,1)S(1)}, u32[]{:S(2)}, u32[]{:S(2)}) %all-to-all-start) | async-done | bytes 540704 | tf_op jit(solution)/shard_map/all_to_all | solution.py:47
  32.6 15.2 %all-to-all-start.1 = ((s32[16,1,8]{2,1,0:T(1,128)}), s32[16,1,8]{2,1,0:T(1,128)S(1)}, u32[]{:S(2)}, u32[]{:S(2)}) async-start(s32[16,1,8]{2,1,0:T(1,128)} %broadcast_in_dim.77), calls=%async_computation.1 | async-start | bytes 16384 | tf_op jit(solution)/shard_map/all_to_all | solution.py:47
  47.9 11.0 %all-to-all-done.1 = s32[16,1,8]{2,1,0:T(1,128)S(1)} async-done(((s32[16,1,8]{2,1,0:T(1,128)}), s32[16,1,8]{2,1,0:T(1,128)S(1)}, u32[]{:S(2)}, u32[]{:S(2)}) %all-to-all-start.1) | async-done | bytes 544 | tf_op jit(solution)/shard_map/all_to_all | solution.py:47
  62.2 2.5 %collective-permute-start.7 = (bf16[2,256,128]{2,1,0:T(8,128)(2,1)S(1)}, bf16[2,256,128]{2,1,0:T(8,128)(2,1)S(1)}, u32[]{:S(2)}, u32[]{:S(2)}) collective-permute-start(bf16[2,256,128]{2,1,0:T(8,128)(2,1)S(1)} %select_reduce_fusion), channel_id=1, source_target_pairs={{0,96},{32,128},{64,160},{96,192},{128,224},{160,256},{192,288},{2... | collective-permute-start | bytes 393224 | tf_op jit(solution)/shard_map/ppermute | solution.py:42
  64.7 0.7 fusion.7
  65.4 2.5 %collective-permute-start.6 = (bf16[2,256,128]{2,1,0:T(8,128)(2,1)S(1)}, bf16[2,256,128]{2,1,0:T(8,128)(2,1)S(1)}, u32[]{:S(2)}, u32[]{:S(2)}) collective-permute-start(bf16[2,256,128]{2,1,0:T(8,128)(2,1)S(1)} %select_reduce_fusion), channel_id=1, source_target_pairs={{0,64},{32,96},{64,128},{96,160},{128,192},{160,224},{192,256},{22... | collective-permute-start | bytes 393224 | tf_op jit(solution)/shard_map/ppermute | solution.py:42
  67.9 7.5 %collective-permute-done.7 = bf16[2,256,128]{2,1,0:T(8,128)(2,1)S(1)} collective-permute-done((bf16[2,256,128]{2,1,0:T(8,128)(2,1)S(1)}, bf16[2,256,128]{2,1,0:T(8,128)(2,1)S(1)}, u32[]{:S(2)}, u32[]{:S(2)}) %collective-permute-start.7) | collective-permute-done | bytes 131104 | tf_op jit(solution)/shard_map/ppermute | solution.py:42
  75.5 7.6 %collective-permute-start.5 = (bf16[2,256,128]{2,1,0:T(8,128)(2,1)S(1)}, bf16[2,256,128]{2,1,0:T(8,128)(2,1)S(1)}, u32[]{:S(2)}, u32[]{:S(2)}) collective-permute-start(bf16[2,256,128]{2,1,0:T(8,128)(2,1)S(1)} %select_reduce_fusion), channel_id=1, source_target_pairs={{0,32},{32,64},{64,96},{96,128},{128,160},{160,192},{192,224},{224... | collective-permute-start | bytes 393224 | tf_op jit(solution)/shard_map/ppermute | solution.py:42
  84.9 0.7 collective-permute-done.5
  85.7 3.8 %collective-permute-start.10 = (bf16[2,256,128]{2,1,0:T(8,128)(2,1)S(1)}, bf16[2,256,128]{2,1,0:T(8,128)(2,1)S(1)}, u32[]{:S(2)}, u32[]{:S(2)}) collective-permute-start(bf16[2,256,128]{2,1,0:T(8,128)(2,1)S(1)} %add_add_fusion.1), channel_id=1, source_target_pairs={{0,384},{32,416},{64,448},{96,480},{128,0},{160,32},{192,64},{224,... | collective-permute-start | bytes 393224 | tf_op jit(solution)/shard_map/ppermute | solution.py:42
  89.5 5.1 %collective-permute-start.9 = (bf16[2,256,128]{2,1,0:T(8,128)(2,1)S(1)}, bf16[2,256,128]{2,1,0:T(8,128)(2,1)S(1)}, u32[]{:S(2)}, u32[]{:S(2)}) collective-permute-start(bf16[2,256,128]{2,1,0:T(8,128)(2,1)S(1)} %add_add_fusion.1), channel_id=1, source_target_pairs={{0,256},{32,288},{64,320},{96,352},{128,384},{160,416},{192,448},{... | collective-permute-start | bytes 393224 | tf_op jit(solution)/shard_map/ppermute | solution.py:42
  94.7 4.1 %collective-permute-start.8 = (bf16[2,256,128]{2,1,0:T(8,128)(2,1)S(1)}, bf16[2,256,128]{2,1,0:T(8,128)(2,1)S(1)}, u32[]{:S(2)}, u32[]{:S(2)}) collective-permute-start(bf16[2,256,128]{2,1,0:T(8,128)(2,1)S(1)} %add_add_fusion.1), channel_id=1, source_target_pairs={{0,128},{32,160},{64,192},{96,224},{128,256},{160,288},{192,320},{... | collective-permute-start | bytes 393224 | tf_op jit(solution)/shard_map/ppermute | solution.py:42
  98.8 2.6 %pad_maximum_fusion = bf16[4,256,768]{2,1,0:T(8,128)(2,1)} fusion(bf16[1,256,768]{2,1,0:T(8,128)(2,1)} %bitcast.4, bf16[1,256,768]{2,1,0:T(8,128)(2,1)} %bitcast.3, bf16[1,256,768]{2,1,0:T(8,128)(2,1)} %bitcast.2, bf16[1,256,768]{2,1,0:T(8,128)(2,1)S(1)} %bitcast.85), kind=kLoop, calls=%fused_computation.3 | loop fusion | flops 2359296 | bytes 3145728 | tf_op jit(solution)/shard_map/stack | solution.py:127
  101.4 3.2 %gather_fusion = bf16[4,256,768]{2,1,0:T(8,128)(2,1)} fusion(bf16[4,256,768]{2,1,0:T(8,128)(2,1)} %pad_maximum_fusion, s32[1024]{0:T(1024)S(1)} %pad_clamp_fusion.1), kind=kCustom, calls=%fused_computation | custom fusion | bytes 3145744 | tf_op jit(solution)/shard_map/jit(_take)/gather | solution.py:129
  104.6 5.4 %collective-permute-done.9 = bf16[2,256,128]{2,1,0:T(8,128)(2,1)S(1)} collective-permute-done((bf16[2,256,128]{2,1,0:T(8,128)(2,1)S(1)}, bf16[2,256,128]{2,1,0:T(8,128)(2,1)S(1)}, u32[]{:S(2)}, u32[]{:S(2)}) %collective-permute-start.9) | collective-permute-done | bytes 131104 | tf_op jit(solution)/shard_map/ppermute | solution.py:42
  110.0 10.9 %collective-permute-done.8 = bf16[2,256,128]{2,1,0:T(8,128)(2,1)S(1)} collective-permute-done((bf16[2,256,128]{2,1,0:T(8,128)(2,1)S(1)}, bf16[2,256,128]{2,1,0:T(8,128)(2,1)S(1)}, u32[]{:S(2)}, u32[]{:S(2)}) %collective-permute-start.8) | collective-permute-done | bytes 131104 | tf_op jit(solution)/shard_map/ppermute | solution.py:42
  120.8 1.2 broadcast_in_dim.128
  122.0 5.6 %all-to-all-start.2 = ((bf16[8,2,256,128]{3,2,1,0:T(8,128)(2,1)}), bf16[8,2,256,128]{3,2,1,0:T(8,128)(2,1)}, u32[]{:S(2)}, u32[]{:S(2)}) async-start(bf16[8,2,256,128]{3,2,1,0:T(8,128)(2,1)} %broadcast_in_dim.128), calls=%async_computation.2 | async-start | bytes 2097152 | tf_op jit(solution)/shard_map/all_to_all | solution.py:47
  127.6 2.8 %select_bitcast_fusion = bf16[256,4,768]{2,0,1:T(8,128)(2,1)} fusion(bf16[4,256,768]{2,1,0:T(8,128)(2,1)} %gather_fusion, pred[4]{0:T(512)(128)(4,1)S(1)} %compare_and_fusion.1), kind=kLoop, calls=%fused_computation.4 | loop fusion | flops 786432 | bytes 3145732 | tf_op jit(solution)/shard_map/jit(_take)/select_n | solution.py:129
  130.4 2.7 %copy.48 = bf16[256,4,768]{0,2,1:T(8,128)(2,1)} copy(bf16[256,4,768]{2,0,1:T(8,128)(2,1)} %select_bitcast_fusion) | data formatting | bytes 3145728 | tf_op jit(solution)/shard_map/jit(_take)/select_n | solution.py:129
  133.1 2.6 %fusion.59 = f32[256,128]{0,1:T(8,128)} fusion(bf16[256,3072]{0,1:T(8,128)(2,1)} %bitcast.83, bf16[3072,128]{1,0:T(8,128)(2,1)S(1)} %copy-done.11), kind=kOutput, calls=%fused_computation.115 | convolution fusion | flops 201326592 | bytes 2490368 | tf_op jit(solution)/shard_map/dot_general | solution.py:132
  135.7 1.9 %collective-permute-start.14 = (f32[256,128]{0,1:T(8,128)}, f32[256,128]{0,1:T(8,128)}, u32[]{:S(2)}, u32[]{:S(2)}) collective-permute-start(f32[256,128]{0,1:T(8,128)} %fusion.59), channel_id=1, source_target_pairs={{0,1},{1,2},{4,5},{5,6},{8,9},{9,10},{12,13},{13,14},{16,17},{17,1... | collective-permute-start | bytes 393224 | tf_op jit(solution)/shard_map/ppermute | solution.py:42
  137.7 1.3 collective-permute-start.4
  139.0 1.0 fusion.61
  143.4 0.8 constant_dynamic-slice_fusion
  144.5 1.3 dynamic-slice_bitcast_fusion
  145.8 2.5 %collective-permute-start.13 = (f32[40,256]{1,0:T(8,128)S(1)}, f32[40,256]{1,0:T(8,128)S(1)}, u32[]{:S(2)}, u32[]{:S(2)}) collective-permute-start(f32[40,256]{1,0:T(8,128)S(1)} %pad_maximum_fusion.1), channel_id=1, source_target_pairs={{0,3},{1,0},{2,1},{3,2},{4,7},{5,4},{6,5},{7,6},{8,11},{9,8},{10,9... | collective-permute-start | bytes 122888 | tf_op jit(solution)/shard_map/ppermute | solution.py:42
  148.3 3.4 %collective-permute-start.12 = (f32[40,256]{1,0:T(8,128)S(1)}, f32[40,256]{1,0:T(8,128)S(1)}, u32[]{:S(2)}, u32[]{:S(2)}) collective-permute-start(f32[40,256]{1,0:T(8,128)S(1)} %pad_maximum_fusion.1), channel_id=1, source_target_pairs={{0,2},{1,3},{2,0},{3,1},{4,6},{5,7},{6,4},{7,5},{8,10},{9,11},{10,... | collective-permute-start | bytes 122888 | tf_op jit(solution)/shard_map/ppermute | solution.py:42
  151.7 3.3 %collective-permute-start.11 = (f32[40,256]{1,0:T(8,128)S(1)}, f32[40,256]{1,0:T(8,128)S(1)}, u32[]{:S(2)}, u32[]{:S(2)}) collective-permute-start(f32[40,256]{1,0:T(8,128)S(1)} %pad_maximum_fusion.1), channel_id=1, source_target_pairs={{0,1},{1,2},{2,3},{3,0},{4,5},{5,6},{6,7},{7,4},{8,9},{9,10},{10,1... | collective-permute-start | bytes 122888 | tf_op jit(solution)/shard_map/ppermute | solution.py:42
  155.8 1.3 collective-permute-start.3
  157.1 1.7 %collective-permute-done.11 = f32[40,256]{1,0:T(8,128)S(1)} collective-permute-done((f32[40,256]{1,0:T(8,128)S(1)}, f32[40,256]{1,0:T(8,128)S(1)}, u32[]{:S(2)}, u32[]{:S(2)}) %collective-permute-start.11) | collective-permute-done | bytes 40992 | tf_op jit(solution)/shard_map/ppermute | solution.py:42
  159.9 0.7 slice.147
  161.4 3.1 %collective-permute-done.3 = f32[256,128]{0,1:T(8,128)} collective-permute-done((f32[256,128]{0,1:T(8,128)}, f32[256,128]{0,1:T(8,128)}, u32[]{:S(2)}, u32[]{:S(2)}) %collective-permute-start.3) | collective-permute-done | bytes 131104 | tf_op jit(solution)/shard_map/ppermute | solution.py:42
  164.5 1.2 fusion.26
  165.7 1.6 fusion.35
  167.7 1.0 fusion.8
  168.7 1.2 fusion.58
  170.0 1.3 fusion.4
  171.3 0.8 copy.55
  (80 shorter events, 9.5 us)
Async XLA Ops:
  0.0 139.0 %copy-start = (bf16[3072,384]{1,0:T(8,128)(2,1)S(1)}, bf16[3072,384]{1,0:T(8,128)(2,1)}, u32[]{:S(2)}) copy-start(bf16[3072,384]{1,0:T(8,128)(2,1)} %param.12) | copy-start | bytes 7077892
  0.0 94.7 %collective-permute-start.1 = (bf16[256,768]{1,0:T(8,128)(2,1)}, bf16[256,768]{1,0:T(8,128)(2,1)}, u32[]{:S(2)}, u32[]{:S(2)}) collective-permute-start(bf16[256,768]{1,0:T(8,128)(2,1)} %param.11), channel_id=1, source_target_pairs={{0,2},{1,3},{2,0},{3,1},{4,6},{5,7},{6,4},{7,5},{8,10},{9,11},{10,... | collective-permute-start | bytes 1179656 | tf_op jit(solution)/shard_map/ppermute | solution.py:42
  5.1 93.7 %collective-permute-start = (bf16[256,768]{1,0:T(8,128)(2,1)}, bf16[256,768]{1,0:T(8,128)(2,1)}, u32[]{:S(2)}, u32[]{:S(2)}) collective-permute-start(bf16[256,768]{1,0:T(8,128)(2,1)} %param.11), channel_id=1, source_target_pairs={{0,1},{1,2},{2,3},{3,0},{4,5},{5,6},{6,7},{7,4},{8,9},{9,10},{10,1... | collective-permute-start | bytes 1179656 | tf_op jit(solution)/shard_map/ppermute | solution.py:42
  7.6 91.2 %collective-permute-start.2 = (bf16[256,768]{1,0:T(8,128)(2,1)}, bf16[256,768]{1,0:T(8,128)(2,1)}, u32[]{:S(2)}, u32[]{:S(2)}) collective-permute-start(bf16[256,768]{1,0:T(8,128)(2,1)} %param.11), channel_id=1, source_target_pairs={{0,3},{1,0},{2,1},{3,2},{4,7},{5,4},{6,5},{7,6},{8,11},{9,8},{10,9... | collective-permute-start | bytes 1179656 | tf_op jit(solution)/shard_map/ppermute | solution.py:42
  17.8 14.0 %all-to-all-start = ((bf16[8,264,128]{2,1,0:T(8,128)(2,1)}), bf16[8,264,128]{2,1,0:T(8,128)(2,1)S(1)}, u32[]{:S(2)}, u32[]{:S(2)}) async-start(bf16[8,264,128]{2,1,0:T(8,128)(2,1)} %broadcast_in_dim.76), calls=%async_computation | async-start | bytes 1081344 | tf_op jit(solution)/shard_map/all_to_all | solution.py:47
  22.7 25.1 %copy-start.8 = (f32[64]{0:T(128)}, f32[64]{0:T(128)S(1)}, u32[]{:S(2)}) copy-start(f32[64]{0:T(128)S(1)} %multiply_power_fusion) | copy-start | bytes 772
  24.0 23.9 %copy-start.7 = (f32[256]{0:T(256)}, f32[256]{0:T(256)S(1)}, u32[]{:S(2)}) copy-start(f32[256]{0:T(256)S(1)} %iota_convert_fusion) | copy-start | bytes 3076
  32.6 26.3 %all-to-all-start.1 = ((s32[16,1,8]{2,1,0:T(1,128)}), s32[16,1,8]{2,1,0:T(1,128)S(1)}, u32[]{:S(2)}, u32[]{:S(2)}) async-start(s32[16,1,8]{2,1,0:T(1,128)} %broadcast_in_dim.77), calls=%async_computation.1 | async-start | bytes 16384 | tf_op jit(solution)/shard_map/all_to_all | solution.py:47
  47.9 16.8 %copy-start.9 = (pred[256]{0:T(512)(128)(4,1)S(1)}, pred[256]{0:T(512)(128)(4,1)}, u32[]{:S(2)}) copy-start(pred[256]{0:T(512)(128)(4,1)} %iota_compare_fusion.4) | copy-start | bytes 772
  47.9 50.9 %copy-start.2 = (bf16[256,768]{1,0:T(8,128)(2,1)S(1)}, bf16[256,768]{1,0:T(8,128)(2,1)}, u32[]{:S(2)}) copy-start(bf16[256,768]{1,0:T(8,128)(2,1)} %param.11) | copy-start | bytes 1179652
  62.2 13.3 %collective-permute-start.7 = (bf16[2,256,128]{2,1,0:T(8,128)(2,1)S(1)}, bf16[2,256,128]{2,1,0:T(8,128)(2,1)S(1)}, u32[]{:S(2)}, u32[]{:S(2)}) collective-permute-start(bf16[2,256,128]{2,1,0:T(8,128)(2,1)S(1)} %select_reduce_fusion), channel_id=1, source_target_pairs={{0,96},{32,128},{64,160},{96,192},{128,224},{160,256},{192,288},{2... | collective-permute-start | bytes 393224 | tf_op jit(solution)/shard_map/ppermute | solution.py:42
  65.4 19.4 %collective-permute-start.6 = (bf16[2,256,128]{2,1,0:T(8,128)(2,1)S(1)}, bf16[2,256,128]{2,1,0:T(8,128)(2,1)S(1)}, u32[]{:S(2)}, u32[]{:S(2)}) collective-permute-start(bf16[2,256,128]{2,1,0:T(8,128)(2,1)S(1)} %select_reduce_fusion), channel_id=1, source_target_pairs={{0,64},{32,96},{64,128},{96,160},{128,192},{160,224},{192,256},{22... | collective-permute-start | bytes 393224 | tf_op jit(solution)/shard_map/ppermute | solution.py:42
  75.5 10.1 %collective-permute-start.5 = (bf16[2,256,128]{2,1,0:T(8,128)(2,1)S(1)}, bf16[2,256,128]{2,1,0:T(8,128)(2,1)S(1)}, u32[]{:S(2)}, u32[]{:S(2)}) collective-permute-start(bf16[2,256,128]{2,1,0:T(8,128)(2,1)S(1)} %select_reduce_fusion), channel_id=1, source_target_pairs={{0,32},{32,64},{64,96},{96,128},{128,160},{160,192},{192,224},{224... | collective-permute-start | bytes 393224 | tf_op jit(solution)/shard_map/ppermute | solution.py:42
  85.7 18.9 %collective-permute-start.10 = (bf16[2,256,128]{2,1,0:T(8,128)(2,1)S(1)}, bf16[2,256,128]{2,1,0:T(8,128)(2,1)S(1)}, u32[]{:S(2)}, u32[]{:S(2)}) collective-permute-start(bf16[2,256,128]{2,1,0:T(8,128)(2,1)S(1)} %add_add_fusion.1), channel_id=1, source_target_pairs={{0,384},{32,416},{64,448},{96,480},{128,0},{160,32},{192,64},{224,... | collective-permute-start | bytes 393224 | tf_op jit(solution)/shard_map/ppermute | solution.py:42
  89.5 20.4 %collective-permute-start.9 = (bf16[2,256,128]{2,1,0:T(8,128)(2,1)S(1)}, bf16[2,256,128]{2,1,0:T(8,128)(2,1)S(1)}, u32[]{:S(2)}, u32[]{:S(2)}) collective-permute-start(bf16[2,256,128]{2,1,0:T(8,128)(2,1)S(1)} %add_add_fusion.1), channel_id=1, source_target_pairs={{0,256},{32,288},{64,320},{96,352},{128,384},{160,416},{192,448},{... | collective-permute-start | bytes 393224 | tf_op jit(solution)/shard_map/ppermute | solution.py:42
  94.7 26.1 %collective-permute-start.8 = (bf16[2,256,128]{2,1,0:T(8,128)(2,1)S(1)}, bf16[2,256,128]{2,1,0:T(8,128)(2,1)S(1)}, u32[]{:S(2)}, u32[]{:S(2)}) collective-permute-start(bf16[2,256,128]{2,1,0:T(8,128)(2,1)S(1)} %add_add_fusion.1), channel_id=1, source_target_pairs={{0,128},{32,160},{64,192},{96,224},{128,256},{160,288},{192,320},{... | collective-permute-start | bytes 393224 | tf_op jit(solution)/shard_map/ppermute | solution.py:42
  122.0 21.4 %all-to-all-start.2 = ((bf16[8,2,256,128]{3,2,1,0:T(8,128)(2,1)}), bf16[8,2,256,128]{3,2,1,0:T(8,128)(2,1)}, u32[]{:S(2)}, u32[]{:S(2)}) async-start(bf16[8,2,256,128]{3,2,1,0:T(8,128)(2,1)} %broadcast_in_dim.128), calls=%async_computation.2 | async-start | bytes 2097152 | tf_op jit(solution)/shard_map/all_to_all | solution.py:47
  130.4 2.7 %copy-start.11 = (bf16[3072,128]{1,0:T(8,128)(2,1)S(1)}, bf16[3072,128]{1,0:T(8,128)(2,1)}, u32[]{:S(2)}) copy-start(bf16[3072,128]{1,0:T(8,128)(2,1)} %param.13) | copy-start | bytes 2359300
  133.1 5.9 %copy-start.1 = (bf16[256,4,768]{0,2,1:T(8,128)(2,1)S(1)}, bf16[256,4,768]{0,2,1:T(8,128)(2,1)}, u32[]{:S(2)}) copy-start(bf16[256,4,768]{0,2,1:T(8,128)(2,1)} %copy.48) | copy-start | bytes 4718596
  135.7 25.7 %collective-permute-start.14 = (f32[256,128]{0,1:T(8,128)}, f32[256,128]{0,1:T(8,128)}, u32[]{:S(2)}, u32[]{:S(2)}) collective-permute-start(f32[256,128]{0,1:T(8,128)} %fusion.59), channel_id=1, source_target_pairs={{0,1},{1,2},{4,5},{5,6},{8,9},{9,10},{12,13},{13,14},{16,17},{17,1... | collective-permute-start | bytes 393224 | tf_op jit(solution)/shard_map/ppermute | solution.py:42
  137.7 32.4 %collective-permute-start.4 = (f32[256,128]{0,1:T(8,128)}, f32[256,128]{0,1:T(8,128)}, u32[]{:S(2)}, u32[]{:S(2)}) collective-permute-start(f32[256,128]{0,1:T(8,128)} %fusion.59), channel_id=1, source_target_pairs={{2,1},{3,2},{6,5},{7,6},{10,9},{11,10},{14,13},{15,14},{18,17},{19... | collective-permute-start | bytes 393224 | tf_op jit(solution)/shard_map/ppermute | solution.py:42
  145.8 10.0 %collective-permute-start.13 = (f32[40,256]{1,0:T(8,128)S(1)}, f32[40,256]{1,0:T(8,128)S(1)}, u32[]{:S(2)}, u32[]{:S(2)}) collective-permute-start(f32[40,256]{1,0:T(8,128)S(1)} %pad_maximum_fusion.1), channel_id=1, source_target_pairs={{0,3},{1,0},{2,1},{3,2},{4,7},{5,4},{6,5},{7,6},{8,11},{9,8},{10,9... | collective-permute-start | bytes 122888 | tf_op jit(solution)/shard_map/ppermute | solution.py:42
  148.3 8.7 %collective-permute-start.12 = (f32[40,256]{1,0:T(8,128)S(1)}, f32[40,256]{1,0:T(8,128)S(1)}, u32[]{:S(2)}, u32[]{:S(2)}) collective-permute-start(f32[40,256]{1,0:T(8,128)S(1)} %pad_maximum_fusion.1), channel_id=1, source_target_pairs={{0,2},{1,3},{2,0},{3,1},{4,6},{5,7},{6,4},{7,5},{8,10},{9,11},{10,... | collective-permute-start | bytes 122888 | tf_op jit(solution)/shard_map/ppermute | solution.py:42
  151.7 7.1 %collective-permute-start.11 = (f32[40,256]{1,0:T(8,128)S(1)}, f32[40,256]{1,0:T(8,128)S(1)}, u32[]{:S(2)}, u32[]{:S(2)}) collective-permute-start(f32[40,256]{1,0:T(8,128)S(1)} %pad_maximum_fusion.1), channel_id=1, source_target_pairs={{0,1},{1,2},{2,3},{3,0},{4,5},{5,6},{6,7},{7,4},{8,9},{9,10},{10,1... | collective-permute-start | bytes 122888 | tf_op jit(solution)/shard_map/ppermute | solution.py:42
  155.8 8.7 %collective-permute-start.3 = (f32[256,128]{0,1:T(8,128)}, f32[256,128]{0,1:T(8,128)}, u32[]{:S(2)}, u32[]{:S(2)}) collective-permute-start(f32[256,128]{0,1:T(8,128)} %fusion.59), channel_id=1, source_target_pairs={{1,3},{2,0},{5,7},{6,4},{9,11},{10,8},{13,15},{14,12},{17,19},{18,... | collective-permute-start | bytes 393224 | tf_op jit(solution)/shard_map/ppermute | solution.py:42
  158.8 0.6 copy-start.5
  159.9 7.7 %copy-start.3 = (f32[256,64]{1,0:T(8,128)S(1)}, f32[256,64]{1,0:T(8,128)}, u32[]{:S(2)}) copy-start(f32[256,64]{1,0:T(8,128)} %get-tuple-element.25) | copy-start | bytes 196612
  161.4 5.9 %copy-start.6 = (bf16[4,16,128]{2,1,0:T(8,128)(2,1)}, bf16[4,16,128]{2,1,0:T(8,128)(2,1)S(1)}, u32[]{:S(2)}) copy-start(bf16[4,16,128]{2,1,0:T(8,128)(2,1)S(1)} %pad_maximum_fusion.2) | copy-start | bytes 49156
  167.3 1.4 copy-start.4
  168.7 1.3 copy-start.10

commit v7 on v6

--- a/solution.py
+++ b/solution.py
@@ -88,19 +88,18 @@
 
     own_slot = lookup_slots(adapter_ids, adapter_slot)
 
+    slots_all = gather_over(own_slot, ("rz", "ry"), n_req).reshape(n_req)
+
     down_rows = down_store[0].T.reshape(-1, 128)
     query_rows = query_up_store[0].reshape(-1, 128)
     pair_rows = key_value_store[0].reshape(-1, 128)
     n_down, n_query = down_rows.shape[0], query_rows.shape[0]
     n_row = n_down + n_query + pair_rows.shape[0]
-    tag = jnp.zeros((8, 128), jnp.int32).at[0, 0].set(own_slot[0]).astype(down_rows.dtype)
-    row = jnp.concatenate([down_rows, query_rows, pair_rows, tag], axis=0)
+    row = jnp.concatenate([down_rows, query_rows, pair_rows], axis=0)
 
     plane = gather_over(row, "ry", ny)
     plane_req = iz * ny + jnp.arange(ny, dtype=jnp.int32)
-    plane_tags = plane[:, n_row, 0].astype(jnp.int32)
-
-    slots_all = gather_over(plane_tags, "rz", nz).reshape(n_req)
+
     slot_range = jnp.arange(n_req * store_rows, dtype=jnp.int32)
     used = jnp.any(slots_all[:, None] == slot_range[None, :], axis=0).astype(jnp.int32)
     prefix = jnp.sum(
@@ -112,7 +111,7 @@
     wanted = iy + ny * jnp.arange(per_column, dtype=jnp.int32)
     choose = (used[plane_slots][None, :] > 0) & (prefix[plane_slots][None, :] == wanted[:, None])
     column = jnp.sum(
-        jnp.where(choose[:, :, None, None], plane[None, :, :n_row], jnp.zeros((), plane.dtype)),
+        jnp.where(choose[:, :, None, None], plane[None], jnp.zeros((), plane.dtype)),
         axis=1,
     )
     column = spread_sum(column, "rz", nz)
@@ -123,39 +122,31 @@
     adapter_query = picked[n_down:n_down + n_query].reshape(query_up_store.shape[1:])
     adapter_pair = picked[n_down + n_query:].reshape(key_value_store.shape[1:])
 
-    blocks = [states] + [shifted(states, s, n_tp) for s in range(1, n_tp)]
-    stacked = jnp.stack(blocks, axis=0)
-    source = (tp_index - jnp.arange(n_tp, dtype=jnp.int32)) % n_tp
-    piece = jnp.take(stacked, source, axis=0)
+    piece = gather_over(states, "tp", n_tp)
     piece = jnp.transpose(piece, (1, 0, 2)).reshape(rows_total, -1)
 
     key_value_sum = jnp.dot(piece, key_value_weight, preferred_element_type=jnp.float32)
-    from_left = shifted(key_value_sum, 1, n_tp, [(0, 1), (1, 2)])
-    from_right = shifted(key_value_sum, -1, n_tp, [(2, 1), (3, 2)])
-    from_far = shifted(key_value_sum, 2, n_tp, [(1, 3), (2, 0)])
-    key_sum = jnp.where(
-        tp_index == 0, key_value_sum, jnp.where(tp_index == 3, from_far, from_left)
-    )
-    value_sum = jnp.where(
-        tp_index == 3, key_value_sum, jnp.where(tp_index == 0, from_far, from_right)
-    )
 
     rank_part = jnp.einsum("kd,sd->ks", down_t, states, preferred_element_type=jnp.float32)
-    n_rank = rank_part.shape[0]
-    up_block = adapter_pair.astype(jnp.float32).reshape(-1, rank_part.shape[1])
-    bundle = jnp.concatenate([rank_part, up_block], axis=0)
-    arrived = [bundle] + [shifted(bundle, s, n_tp) for s in range(1, n_tp)]
-    rank_sum = arrived[0][:n_rank]
-    for part in arrived[1:]:
-        rank_sum = rank_sum + part[:n_rank]
+    n_rank, width = rank_part.shape
+    up_block = adapter_pair.astype(jnp.float32).reshape(-1, width)
+    n_up = up_block.shape[0]
+    bundle = jnp.concatenate([rank_part, up_block, key_value_sum.reshape(-1, width)], axis=0)
+    arrived = gather_over(bundle, "tp", n_tp)
+    rank_sum = arrived[0, :n_rank]
+    for d in range(1, n_tp):
+        rank_sum = rank_sum + arrived[d, :n_rank]
     rank_mid = rank_sum.astype(jnp.bfloat16)
     rank_cols = rank_mid.shape[0] // 2
-    up_all = jnp.stack([part[n_rank:] for part in arrived]).astype(jnp.bfloat16)
+    up_all = arrived[:, n_rank:n_rank + n_up].astype(jnp.bfloat16)
     up_all = up_all.reshape((n_tp,) + adapter_pair.shape)
+    base_all = arrived[:, n_rank + n_up:].reshape((n_tp,) + key_value_sum.shape)
     kv_heads = (n_tp * kv_cols) // 2 // HEAD_DIM
     group_index = tp_index * heads_here // (HEADS // kv_heads)
-    key_up = up_all[(tp_index - group_index) % n_tp]
-    value_up = up_all[(tp_index - kv_heads - group_index) % n_tp]
+    key_up = up_all[group_index]
+    value_up = up_all[kv_heads + group_index]
+    key_sum = base_all[group_index]
+    value_sum = base_all[kv_heads + group_index]
 
     query_total = jnp.dot(piece, query_weight, preferred_element_type=jnp.float32)
     query_addition = jnp.einsum(
@@ -168,13 +159,15 @@
     value_extra = jnp.einsum(
         "ks,kc->sc", rank_mid[rank_cols:], value_up, preferred_element_type=jnp.float32
     )
-    key_block = (key_sum + adapter_scale * key_extra).astype(jnp.bfloat16)
+    key_block = lax.reduce_precision(
+        key_sum + adapter_scale * key_extra, exponent_bits=8, mantissa_bits=7
+    )
     value_block = (value_sum + adapter_scale * value_extra).astype(jnp.bfloat16)
 
     queries = rotate(query_plain.reshape(req_dev, slot_len, heads_here, HEAD_DIM)).astype(
         jnp.bfloat16
     )
-    keys_one = rotate(key_block.astype(jnp.float32).reshape(req_dev, slot_len, 1, HEAD_DIM)).astype(
+    keys_one = rotate(key_block.reshape(req_dev, slot_len, 1, HEAD_DIM)).astype(
         jnp.bfloat16
     )[:, :, 0, :]
     values_one = value_block.reshape(req_dev, slot_len, HEAD_DIM)

time: 173 us -> 177 us (1.023)
  the two profiles are of different devices: /device:TPU:40 before, /device:TPU:32 now
where the time goes in v7:
time: 177 us; the launch traced here: 176 us
  waiting for transfers between devices  67.8 us (38%)
  starting transfers between devices  59.1 us (33%)
  local copies, waits for them, and re-layouts  22.1 us (12%)
  other arithmetic  10.9 us (6%)
  matrix products  10.1 us (6%)
  between operations  6.13 us (3%)
    ppermute x6, waiting for transfers between devices, shifted(): return lax.ppermute(x, axis, pairs)  37.1 us
    all_to_all x5, starting transfers between devices, gather_over(): return lax.all_to_all(copies, axis, 0, 0, tiled=True)  35.7 us
    all_to_all x5, waiting for transfers between devices, gather_over(): return lax.all_to_all(copies, axis, 0, 0, tiled=True)  30.8 us
    ppermute x6, starting transfers between devices, shifted(): return lax.ppermute(x, axis, pairs)  23.4 us
    broadcast_in_dim x5, local copies, waits for them, and re-layouts, gather_over(): copies = jnp.broadcast_to(x[None], (n,) + x.shape)  7.43 us
  transfers between devices with their start and end apart: 11, of which 10 were waited for; matrix products, arithmetic and copies ran while one was open for 10% of the time, Pallas kernels for 0%

profile of v7, /device:TPU:32, one launch (start us, length us, event | category | flops | bytes accessed | tf_op | source)
XLA Modules:
  0.0 176.1 jit_solution(8906576382789039267)
XLA Ops:
  0.8 1.3 fusion.45
  2.1 1.2 broadcast_in_dim.64
  3.4 19.2 %all-to-all-start = ((s32[128,1,1]{2,1,0:T(1,128)}), s32[128,1,1]{2,1,0:T(1,128)S(1)}, u32[]{:S(2)}, u32[]{:S(2)}) async-start(s32[128,1,1]{2,1,0:T(1,128)} %broadcast_in_dim.64), calls=%async_computation | async-start | bytes 131072 | tf_op jit(solution)/shard_map/all_to_all | solution.py:47
  23.3 0.9 reshape.364
  24.9 12.0 %all-to-all-done = s32[128,1,1]{2,1,0:T(1,128)S(1)} async-done(((s32[128,1,1]{2,1,0:T(1,128)}), s32[128,1,1]{2,1,0:T(1,128)S(1)}, u32[]{:S(2)}, u32[]{:S(2)}) %all-to-all-start) | async-done | bytes 544 | tf_op jit(solution)/shard_map/all_to_all | solution.py:47
  36.9 0.9 broadcast_in_dim.68
  37.7 3.5 %all-to-all-start.1 = ((bf16[8,256,128]{2,1,0:T(8,128)(2,1)}), bf16[8,256,128]{2,1,0:T(8,128)(2,1)S(1)}, u32[]{:S(2)}, u32[]{:S(2)}) async-start(bf16[8,256,128]{2,1,0:T(8,128)(2,1)} %broadcast_in_dim.68), calls=%async_computation.1 | async-start | bytes 1048576 | tf_op jit(solution)/shard_map/all_to_all | solution.py:47
  41.3 0.9 copy.40
  42.2 2.3 %reduce.5 = s32[128]{0:T(128)S(1)} reduce(s32[128,1,1]{2,1,0:T(1,128)S(1)} %all-to-all-done, s32[]{:T(128)} %constant.27.clone.1), dimensions={1,2}, to_apply=%all_to_all.16.reduce_sub_computation | reduce | bytes 1028 | tf_op jit(solution)/shard_map/all_to_all | solution.py:47
  45.3 6.2 %all-to-all-done.1 = bf16[8,256,128]{2,1,0:T(8,128)(2,1)S(1)} async-done(((bf16[8,256,128]{2,1,0:T(8,128)(2,1)}), bf16[8,256,128]{2,1,0:T(8,128)(2,1)S(1)}, u32[]{:S(2)}, u32[]{:S(2)}) %all-to-all-start.1) | async-done | bytes 524320 | tf_op jit(solution)/shard_map/all_to_all | solution.py:47
  51.5 2.3 %broadcast_in_dim.76 = bf16[4,256,768]{1,2,0:T(8,128)(2,1)} broadcast(bf16[256,768]{0,1:T(8,128)(2,1)} %copy.40), dimensions={1,2} | broadcast | bytes 1966080 | tf_op jit(solution)/shard_map/broadcast_in_dim | solution.py:46
  53.8 4.3 %all-to-all-start.3 = ((bf16[4,256,768]{1,2,0:T(8,128)(2,1)}), bf16[4,256,768]{1,2,0:T(8,128)(2,1)}, u32[]{:S(2)}, u32[]{:S(2)}) async-start(bf16[4,256,768]{1,2,0:T(8,128)(2,1)} %broadcast_in_dim.76), calls=%async_computation.3 | async-start | bytes 3145728 | tf_op jit(solution)/shard_map/all_to_all | solution.py:47
  59.2 3.0 %collective-permute-start.2 = (bf16[2,256,128]{2,1,0:T(8,128)(2,1)S(1)}, bf16[2,256,128]{2,1,0:T(8,128)(2,1)S(1)}, u32[]{:S(2)}, u32[]{:S(2)}) collective-permute-start(bf16[2,256,128]{2,1,0:T(8,128)(2,1)S(1)} %select_reduce_fusion), channel_id=1, source_target_pairs={{0,96},{32,128},{64,160},{96,192},{128,224},{160,256},{192,288},{2... | collective-permute-start | bytes 393224 | tf_op jit(solution)/shard_map/ppermute | solution.py:42
  62.3 2.6 %collective-permute-start.1 = (bf16[2,256,128]{2,1,0:T(8,128)(2,1)S(1)}, bf16[2,256,128]{2,1,0:T(8,128)(2,1)S(1)}, u32[]{:S(2)}, u32[]{:S(2)}) collective-permute-start(bf16[2,256,128]{2,1,0:T(8,128)(2,1)S(1)} %select_reduce_fusion), channel_id=1, source_target_pairs={{0,64},{32,96},{64,128},{96,160},{128,192},{160,224},{192,256},{22... | collective-permute-start | bytes 393224 | tf_op jit(solution)/shard_map/ppermute | solution.py:42
  64.9 2.6 %collective-permute-start = (bf16[2,256,128]{2,1,0:T(8,128)(2,1)S(1)}, bf16[2,256,128]{2,1,0:T(8,128)(2,1)S(1)}, u32[]{:S(2)}, u32[]{:S(2)}) collective-permute-start(bf16[2,256,128]{2,1,0:T(8,128)(2,1)S(1)} %select_reduce_fusion), channel_id=1, source_target_pairs={{0,32},{32,64},{64,96},{96,128},{128,160},{160,192},{192,224},{224... | collective-permute-start | bytes 393224 | tf_op jit(solution)/shard_map/ppermute | solution.py:42
  67.5 7.2 %collective-permute-done.2 = bf16[2,256,128]{2,1,0:T(8,128)(2,1)S(1)} collective-permute-done((bf16[2,256,128]{2,1,0:T(8,128)(2,1)S(1)}, bf16[2,256,128]{2,1,0:T(8,128)(2,1)S(1)}, u32[]{:S(2)}, u32[]{:S(2)}) %collective-permute-start.2) | collective-permute-done | bytes 131104 | tf_op jit(solution)/shard_map/ppermute | solution.py:42
  74.7 5.6 %collective-permute-done.1 = bf16[2,256,128]{2,1,0:T(8,128)(2,1)S(1)} collective-permute-done((bf16[2,256,128]{2,1,0:T(8,128)(2,1)S(1)}, bf16[2,256,128]{2,1,0:T(8,128)(2,1)S(1)}, u32[]{:S(2)}, u32[]{:S(2)}) %collective-permute-start.1) | collective-permute-done | bytes 131104 | tf_op jit(solution)/shard_map/ppermute | solution.py:42
  80.5 5.3 %collective-permute-start.5 = (bf16[2,256,128]{2,1,0:T(8,128)(2,1)S(1)}, bf16[2,256,128]{2,1,0:T(8,128)(2,1)S(1)}, u32[]{:S(2)}, u32[]{:S(2)}) collective-permute-start(bf16[2,256,128]{2,1,0:T(8,128)(2,1)S(1)} %add_add_fusion.1), channel_id=1, source_target_pairs={{0,384},{32,416},{64,448},{96,480},{128,0},{160,32},{192,64},{224,... | collective-permute-start | bytes 393224 | tf_op jit(solution)/shard_map/ppermute | solution.py:42
  85.8 5.3 %collective-permute-start.4 = (bf16[2,256,128]{2,1,0:T(8,128)(2,1)S(1)}, bf16[2,256,128]{2,1,0:T(8,128)(2,1)S(1)}, u32[]{:S(2)}, u32[]{:S(2)}) collective-permute-start(bf16[2,256,128]{2,1,0:T(8,128)(2,1)S(1)} %add_add_fusion.1), channel_id=1, source_target_pairs={{0,256},{32,288},{64,320},{96,352},{128,384},{160,416},{192,448},{... | collective-permute-start | bytes 393224 | tf_op jit(solution)/shard_map/ppermute | solution.py:42
  91.1 4.6 %collective-permute-start.3 = (bf16[2,256,128]{2,1,0:T(8,128)(2,1)S(1)}, bf16[2,256,128]{2,1,0:T(8,128)(2,1)S(1)}, u32[]{:S(2)}, u32[]{:S(2)}) collective-permute-start(bf16[2,256,128]{2,1,0:T(8,128)(2,1)S(1)} %add_add_fusion.1), channel_id=1, source_target_pairs={{0,128},{32,160},{64,192},{96,224},{128,256},{160,288},{192,320},{... | collective-permute-start | bytes 393224 | tf_op jit(solution)/shard_map/ppermute | solution.py:42
  95.7 1.4 collective-permute-done.5
  97.1 5.9 %collective-permute-done.4 = bf16[2,256,128]{2,1,0:T(8,128)(2,1)S(1)} collective-permute-done((bf16[2,256,128]{2,1,0:T(8,128)(2,1)S(1)}, bf16[2,256,128]{2,1,0:T(8,128)(2,1)S(1)}, u32[]{:S(2)}, u32[]{:S(2)}) %collective-permute-start.4) | collective-permute-done | bytes 131104 | tf_op jit(solution)/shard_map/ppermute | solution.py:42
  103.1 16.7 %collective-permute-done.3 = bf16[2,256,128]{2,1,0:T(8,128)(2,1)S(1)} collective-permute-done((bf16[2,256,128]{2,1,0:T(8,128)(2,1)S(1)}, bf16[2,256,128]{2,1,0:T(8,128)(2,1)S(1)}, u32[]{:S(2)}, u32[]{:S(2)}) %collective-permute-start.3) | collective-permute-done | bytes 131104 | tf_op jit(solution)/shard_map/ppermute | solution.py:42
  120.5 2.2 %broadcast_in_dim.75 = bf16[8,2,256,128]{3,2,1,0:T(8,128)(2,1)} broadcast(bf16[2,256,128]{2,1,0:T(8,128)(2,1)} %add_add_fusion), dimensions={1,2,3} | broadcast | bytes 1179648 | tf_op jit(solution)/shard_map/broadcast_in_dim | solution.py:46
  122.6 4.2 %all-to-all-start.2 = ((bf16[8,2,256,128]{3,2,1,0:T(8,128)(2,1)}), bf16[8,2,256,128]{3,2,1,0:T(8,128)(2,1)}, u32[]{:S(2)}, u32[]{:S(2)}) async-start(bf16[8,2,256,128]{3,2,1,0:T(8,128)(2,1)} %broadcast_in_dim.75), calls=%async_computation.2 | async-start | bytes 2097152 | tf_op jit(solution)/shard_map/all_to_all | solution.py:47
  129.3 1.3 multiply_cosine_fusion
  133.8 2.7 %fusion.52 = f32[256,128]{1,0:T(8,128)} fusion(bf16[256,3072]{0,1:T(8,128)(2,1)} %bitcast.8, bf16[3072,128]{1,0:T(8,128)(2,1)S(1)} %copy-done.2), kind=kOutput, calls=%fused_computation.92 | convolution fusion | flops 201326592 | bytes 2490368 | tf_op jit(solution)/shard_map/dot_general | solution.py:128
  136.5 0.9 reshape.367
  137.4 5.4 %all-to-all-done.2 = bf16[8,2,256,128]{3,2,1,0:T(8,128)(2,1)} async-done(((bf16[8,2,256,128]{3,2,1,0:T(8,128)(2,1)}), bf16[8,2,256,128]{3,2,1,0:T(8,128)(2,1)}, u32[]{:S(2)}, u32[]{:S(2)}) %all-to-all-start.2) | async-done | bytes 1048608 | tf_op jit(solution)/shard_map/all_to_all | solution.py:47
  143.5 0.8 constant_dynamic-slice_fusion
  144.7 0.9 broadcast_in_dim.77
  145.6 4.5 %all-to-all-start.4 = ((f32[4,168,256]{2,1,0:T(8,128)}), f32[4,168,256]{2,1,0:T(8,128)S(1)}, u32[]{:S(2)}, u32[]{:S(2)}) async-start(f32[4,168,256]{2,1,0:T(8,128)} %broadcast_in_dim.77), calls=%async_computation.4 | async-start | bytes 1376256 | tf_op jit(solution)/shard_map/all_to_all | solution.py:47
  150.1 0.7 fusion.13
  150.8 2.4 %fusion.53 = f32[256,384]{1,0:T(8,128)S(1)} fusion(bf16[256,3072]{0,1:T(8,128)(2,1)} %bitcast.8, bf16[3072,384]{1,0:T(8,128)(2,1)S(1)} %copy-done), kind=kOutput, calls=%fused_computation.93 | convolution fusion | flops 603979776 | bytes 4325376 | tf_op jit(solution)/shard_map/dot_general | solution.py:151
  154.0 7.1 %all-to-all-done.4 = f32[4,168,256]{2,1,0:T(8,128)S(1)} async-done(((f32[4,168,256]{2,1,0:T(8,128)}), f32[4,168,256]{2,1,0:T(8,128)S(1)}, u32[]{:S(2)}, u32[]{:S(2)}) %all-to-all-start.4) | async-done | bytes 688160 | tf_op jit(solution)/shard_map/all_to_all | solution.py:47
  161.1 1.0 fusion.2
  162.1 1.2 copy.42
  163.3 0.8 fusion.49
  164.1 0.8 slice.77
  164.9 1.9 %reshape.368 = f32[4,256,128]{2,1,0:T(8,128)} reshape(f32[4,128,256]{2,1,0:T(8,128)} %slice.77) | data formatting | bytes 1048576 | tf_op jit(solution)/shard_map/reshape | solution.py:143
  166.8 1.1 fusion.7
  167.9 1.2 fusion.33
  169.2 1.1 copy.53
  170.3 1.1 copy.52
  171.4 1.1 fusion.14
  172.5 1.3 fusion.50
  173.9 1.4 fusion.4
  175.3 0.8 copy.47
  (52 shorter events, 6.7 us)
Async XLA Ops:
  0.0 150.8 %copy-start = (bf16[3072,384]{1,0:T(8,128)(2,1)S(1)}, bf16[3072,384]{1,0:T(8,128)(2,1)}, u32[]{:S(2)}) copy-start(bf16[3072,384]{1,0:T(8,128)(2,1)} %param.10) | copy-start | bytes 7077892
  0.0 41.3 %copy-start.1 = (bf16[256,768]{1,0:T(8,128)(2,1)S(1)}, bf16[256,768]{1,0:T(8,128)(2,1)}, u32[]{:S(2)}) copy-start(bf16[256,768]{1,0:T(8,128)(2,1)} %param.9) | copy-start | bytes 1179652
  3.4 33.5 %all-to-all-start = ((s32[128,1,1]{2,1,0:T(1,128)}), s32[128,1,1]{2,1,0:T(1,128)S(1)}, u32[]{:S(2)}, u32[]{:S(2)}) async-start(s32[128,1,1]{2,1,0:T(1,128)} %broadcast_in_dim.64), calls=%async_computation | async-start | bytes 131072 | tf_op jit(solution)/shard_map/all_to_all | solution.py:47
  37.7 13.8 %all-to-all-start.1 = ((bf16[8,256,128]{2,1,0:T(8,128)(2,1)}), bf16[8,256,128]{2,1,0:T(8,128)(2,1)S(1)}, u32[]{:S(2)}, u32[]{:S(2)}) async-start(bf16[8,256,128]{2,1,0:T(8,128)(2,1)} %broadcast_in_dim.68), calls=%async_computation.1 | async-start | bytes 1048576 | tf_op jit(solution)/shard_map/all_to_all | solution.py:47
  53.8 66.7 %all-to-all-start.3 = ((bf16[4,256,768]{1,2,0:T(8,128)(2,1)}), bf16[4,256,768]{1,2,0:T(8,128)(2,1)}, u32[]{:S(2)}, u32[]{:S(2)}) async-start(bf16[4,256,768]{1,2,0:T(8,128)(2,1)} %broadcast_in_dim.76), calls=%async_computation.3 | async-start | bytes 3145728 | tf_op jit(solution)/shard_map/all_to_all | solution.py:47
  59.2 15.5 %collective-permute-start.2 = (bf16[2,256,128]{2,1,0:T(8,128)(2,1)S(1)}, bf16[2,256,128]{2,1,0:T(8,128)(2,1)S(1)}, u32[]{:S(2)}, u32[]{:S(2)}) collective-permute-start(bf16[2,256,128]{2,1,0:T(8,128)(2,1)S(1)} %select_reduce_fusion), channel_id=1, source_target_pairs={{0,96},{32,128},{64,160},{96,192},{128,224},{160,256},{192,288},{2... | collective-permute-start | bytes 393224 | tf_op jit(solution)/shard_map/ppermute | solution.py:42
  62.3 18.1 %collective-permute-start.1 = (bf16[2,256,128]{2,1,0:T(8,128)(2,1)S(1)}, bf16[2,256,128]{2,1,0:T(8,128)(2,1)S(1)}, u32[]{:S(2)}, u32[]{:S(2)}) collective-permute-start(bf16[2,256,128]{2,1,0:T(8,128)(2,1)S(1)} %select_reduce_fusion), channel_id=1, source_target_pairs={{0,64},{32,96},{64,128},{96,160},{128,192},{160,224},{192,256},{22... | collective-permute-start | bytes 393224 | tf_op jit(solution)/shard_map/ppermute | solution.py:42
  64.9 15.7 %collective-permute-start = (bf16[2,256,128]{2,1,0:T(8,128)(2,1)S(1)}, bf16[2,256,128]{2,1,0:T(8,128)(2,1)S(1)}, u32[]{:S(2)}, u32[]{:S(2)}) collective-permute-start(bf16[2,256,128]{2,1,0:T(8,128)(2,1)S(1)} %select_reduce_fusion), channel_id=1, source_target_pairs={{0,32},{32,64},{64,96},{96,128},{128,160},{160,192},{192,224},{224... | collective-permute-start | bytes 393224 | tf_op jit(solution)/shard_map/ppermute | solution.py:42
  80.5 16.6 %collective-permute-start.5 = (bf16[2,256,128]{2,1,0:T(8,128)(2,1)S(1)}, bf16[2,256,128]{2,1,0:T(8,128)(2,1)S(1)}, u32[]{:S(2)}, u32[]{:S(2)}) collective-permute-start(bf16[2,256,128]{2,1,0:T(8,128)(2,1)S(1)} %add_add_fusion.1), channel_id=1, source_target_pairs={{0,384},{32,416},{64,448},{96,480},{128,0},{160,32},{192,64},{224,... | collective-permute-start | bytes 393224 | tf_op jit(solution)/shard_map/ppermute | solution.py:42
  85.8 17.3 %collective-permute-start.4 = (bf16[2,256,128]{2,1,0:T(8,128)(2,1)S(1)}, bf16[2,256,128]{2,1,0:T(8,128)(2,1)S(1)}, u32[]{:S(2)}, u32[]{:S(2)}) collective-permute-start(bf16[2,256,128]{2,1,0:T(8,128)(2,1)S(1)} %add_add_fusion.1), channel_id=1, source_target_pairs={{0,256},{32,288},{64,320},{96,352},{128,384},{160,416},{192,448},{... | collective-permute-start | bytes 393224 | tf_op jit(solution)/shard_map/ppermute | solution.py:42
  91.1 28.7 %collective-permute-start.3 = (bf16[2,256,128]{2,1,0:T(8,128)(2,1)S(1)}, bf16[2,256,128]{2,1,0:T(8,128)(2,1)S(1)}, u32[]{:S(2)}, u32[]{:S(2)}) collective-permute-start(bf16[2,256,128]{2,1,0:T(8,128)(2,1)S(1)} %add_add_fusion.1), channel_id=1, source_target_pairs={{0,128},{32,160},{64,192},{96,224},{128,256},{160,288},{192,320},{... | collective-permute-start | bytes 393224 | tf_op jit(solution)/shard_map/ppermute | solution.py:42
  120.5 13.3 %copy-start.2 = (bf16[3072,128]{1,0:T(8,128)(2,1)S(1)}, bf16[3072,128]{1,0:T(8,128)(2,1)}, u32[]{:S(2)}) copy-start(bf16[3072,128]{1,0:T(8,128)(2,1)} %param.11) | copy-start | bytes 2359300
  122.6 20.2 %all-to-all-start.2 = ((bf16[8,2,256,128]{3,2,1,0:T(8,128)(2,1)}), bf16[8,2,256,128]{3,2,1,0:T(8,128)(2,1)}, u32[]{:S(2)}, u32[]{:S(2)}) async-start(bf16[8,2,256,128]{3,2,1,0:T(8,128)(2,1)} %broadcast_in_dim.75), calls=%async_computation.2 | async-start | bytes 2097152 | tf_op jit(solution)/shard_map/all_to_all | solution.py:47
  129.3 1.9 %copy-start.6 = (f32[64]{0:T(128)}, f32[64]{0:T(128)S(1)}, u32[]{:S(2)}) copy-start(f32[64]{0:T(128)S(1)} %multiply_power_fusion) | copy-start | bytes 772
  129.3 20.8 %copy-start.8 = (pred[256]{0:T(512)(128)(4,1)}, pred[256]{0:T(512)(128)(4,1)S(1)}, u32[]{:S(2)}) copy-start(pred[256]{0:T(512)(128)(4,1)S(1)} %iota_compare_fusion.3) | copy-start | bytes 772
  129.3 1.8 %copy-start.4 = (f32[256]{0:T(256)}, f32[256]{0:T(256)S(1)}, u32[]{:S(2)}) copy-start(f32[256]{0:T(256)S(1)} %iota_convert_fusion) | copy-start | bytes 3076
  145.6 15.5 %all-to-all-start.4 = ((f32[4,168,256]{2,1,0:T(8,128)}), f32[4,168,256]{2,1,0:T(8,128)S(1)}, u32[]{:S(2)}, u32[]{:S(2)}) async-start(f32[4,168,256]{2,1,0:T(8,128)} %broadcast_in_dim.77), calls=%async_computation.4 | async-start | bytes 1376256 | tf_op jit(solution)/shard_map/all_to_all | solution.py:47
  163.3 4.7 %copy-start.5 = (f32[256]{0:T(256)S(1)}, f32[256]{0:T(256)}, u32[]{:S(2)}) copy-start(f32[256]{0:T(256)} %copy-done.4) | copy-start | bytes 3076
  163.3 4.7 %copy-start.7 = (f32[64]{0:T(128)S(1)}, f32[64]{0:T(128)}, u32[]{:S(2)}) copy-start(f32[64]{0:T(128)} %copy-done.6) | copy-start | bytes 772
  166.8 5.7 %copy-start.3 = (bf16[4,16,128]{2,1,0:T(8,128)(2,1)}, bf16[4,16,128]{2,1,0:T(8,128)(2,1)S(1)}, u32[]{:S(2)}) copy-start(bf16[4,16,128]{2,1,0:T(8,128)(2,1)S(1)} %reshape.369) | copy-start | bytes 49156
  172.5 1.4 copy-start.9

commit v8 on v7

--- a/solution.py
+++ b/solution.py
@@ -115,9 +115,14 @@
         axis=1,
     )
     column = spread_sum(column, "rz", nz)
-    gathered = gather_over(column, "ry", ny)
+    dest_k = prefix[slots_all[plane_req]]
+    held = column[0]
+    for m in range(1, per_column):
+        held = jnp.where((dest_k // ny == m)[:, None, None], column[m], held)
+    send = jnp.where((dest_k % ny == iy)[:, None, None], held, jnp.zeros((), held.dtype))
+    received = lax.all_to_all(send, "ry", 0, 0, tiled=True)
     own_k = prefix[own_slot[0]]
-    picked = gathered[own_k % ny, own_k // ny]
+    picked = received[own_k % ny]
     down_t = picked[:n_down].reshape(down_store.shape[2], down_store.shape[1])
     adapter_query = picked[n_down:n_down + n_query].reshape(query_up_store.shape[1:])
     adapter_pair = picked[n_down + n_query:].reshape(key_value_store.shape[1:])
@@ -129,18 +134,20 @@
 
     rank_part = jnp.einsum("kd,sd->ks", down_t, states, preferred_element_type=jnp.float32)
     n_rank, width = rank_part.shape
-    up_block = adapter_pair.astype(jnp.float32).reshape(-1, width)
-    n_up = up_block.shape[0]
-    bundle = jnp.concatenate([rank_part, up_block, key_value_sum.reshape(-1, width)], axis=0)
+    lanes = key_value_sum.shape[1]
+    rank_rows = rank_part.reshape(-1, lanes)
+    n_mid, n_up = rank_rows.shape[0], adapter_pair.shape[0]
+    bundle = jnp.concatenate(
+        [rank_rows, adapter_pair.astype(jnp.float32), key_value_sum], axis=0
+    )
     arrived = gather_over(bundle, "tp", n_tp)
-    rank_sum = arrived[0, :n_rank]
+    rank_sum = arrived[0, :n_mid]
     for d in range(1, n_tp):
-        rank_sum = rank_sum + arrived[d, :n_rank]
-    rank_mid = rank_sum.astype(jnp.bfloat16)
+        rank_sum = rank_sum + arrived[d, :n_mid]
+    rank_mid = rank_sum.reshape(n_rank, width).astype(jnp.bfloat16)
     rank_cols = rank_mid.shape[0] // 2
-    up_all = arrived[:, n_rank:n_rank + n_up].astype(jnp.bfloat16)
-    up_all = up_all.reshape((n_tp,) + adapter_pair.shape)
-    base_all = arrived[:, n_rank + n_up:].reshape((n_tp,) + key_value_sum.shape)
+    up_all = arrived[:, n_mid:n_mid + n_up].astype(jnp.bfloat16)
+    base_all = arrived[:, n_mid + n_up:]
     kv_heads = (n_tp * kv_cols) // 2 // HEAD_DIM
     group_index = tp_index * heads_here // (HEADS // kv_heads)
     key_up = up_all[group_index]

time: 177 us -> 184 us (1.040)
  waiting for transfers between devices: 67.8 us -> 79.8 us
  other arithmetic: 10.9 us -> 8.83 us
    all_to_all x0 -> x1, waiting for transfers between devices: none -> 10.2 us  [local(): received = lax.all_to_all(send, 'ry', 0, 0, tiled=True)]
    all_to_all x5 -> x4, starting transfers between devices: 35.7 us -> 30.6 us  [gather_over(): return lax.all_to_all(copies, axis, 0, 0, tiled=True)]
    all_to_all x0 -> x1, starting transfers between devices: none -> 4.14 us  [local(): received = lax.all_to_all(send, 'ry', 0, 0, tiled=True)]
    broadcast_in_dim x5 -> x4, local copies, waits for them, and re-layouts: 7.43 us -> 4.27 us  [gather_over(): copies = jnp.broadcast_to(x[None], (n,) + x.shape)]
    all_to_all x5 -> x4, waiting for transfers between devices: 30.8 us -> 33.3 us  [gather_over(): return lax.all_to_all(copies, axis, 0, 0, tiled=True)]
    reshape x3 -> x1, local copies, waits for them, and re-layouts: 2.83 us -> 0.76 us  [local(): rank_rows = rank_part.reshape(-1, lanes)]
  transfers between devices with their start and end apart: 11 -> 11, of which waited for: 10 -> 11; matrix products, arithmetic and copies ran while one was open for 10% -> 10% of each run, Pallas kernels for 0% -> 0%
where the time goes in v8:
time: 184 us; the launch traced here: 183 us
  waiting for transfers between devices  79.8 us (43%)
  starting transfers between devices  58.2 us (32%)
  local copies, waits for them, and re-layouts  20.6 us (11%)
  matrix products  10.1 us (5%)
  other arithmetic  8.83 us (5%)
  between operations  5.5 us (3%)
    ppermute x6, waiting for transfers between devices, shifted(): return lax.ppermute(x, axis, pairs)  36.4 us
    all_to_all x4, waiting for transfers between devices, gather_over(): return lax.all_to_all(copies, axis, 0, 0, tiled=True)  33.3 us
    all_to_all x4, starting transfers between devices, gather_over(): return lax.all_to_all(copies, axis, 0, 0, tiled=True)  30.6 us
    ppermute x6, starting transfers between devices, shifted(): return lax.ppermute(x, axis, pairs)  23.4 us
    all_to_all x1, waiting for transfers between devices, local(): received = lax.all_to_all(send, 'ry', 0, 0, tiled=True)  10.2 us
    broadcast_in_dim x4, local copies, waits for them, and re-layouts, gather_over(): copies = jnp.broadcast_to(x[None], (n,) + x.shape)  4.27 us
    all_to_all x1, starting transfers between devices, local(): received = lax.all_to_all(send, 'ry', 0, 0, tiled=True)  4.14 us
  transfers between devices with their start and end apart: 11, of which 11 were waited for; matrix products, arithmetic and copies ran while one was open for 10% of the time, Pallas kernels for 0%

profile of v8, /device:TPU:32, one launch (start us, length us, event | category | flops | bytes accessed | tf_op | source)
XLA Modules:
  0.0 182.9 jit_solution(15247222714963549916)
XLA Ops:
  0.8 1.3 fusion.46
  2.1 1.2 broadcast_in_dim.94
  3.3 19.2 %all-to-all-start = ((s32[128,1,1]{2,1,0:T(1,128)}), s32[128,1,1]{2,1,0:T(1,128)S(1)}, u32[]{:S(2)}, u32[]{:S(2)}) async-start(s32[128,1,1]{2,1,0:T(1,128)} %broadcast_in_dim.94), calls=%async_computation | async-start | bytes 131072 | tf_op jit(solution)/shard_map/all_to_all | solution.py:47
  22.6 0.7 reshape_squeeze.3
  23.3 0.9 reshape.407
  24.1 0.7 pad_maximum_fusion.1
  24.8 12.0 %all-to-all-done = s32[128,1,1]{2,1,0:T(1,128)S(1)} async-done(((s32[128,1,1]{2,1,0:T(1,128)}), s32[128,1,1]{2,1,0:T(1,128)S(1)}, u32[]{:S(2)}, u32[]{:S(2)}) %all-to-all-start) | async-done | bytes 544 | tf_op jit(solution)/shard_map/all_to_all | solution.py:47
  36.8 0.9 broadcast_in_dim.100
  37.7 3.5 %all-to-all-start.1 = ((bf16[8,256,128]{2,1,0:T(8,128)(2,1)}), bf16[8,256,128]{2,1,0:T(8,128)(2,1)S(1)}, u32[]{:S(2)}, u32[]{:S(2)}) async-start(bf16[8,256,128]{2,1,0:T(8,128)(2,1)} %broadcast_in_dim.100), calls=%async_computation.1 | async-start | bytes 1048576 | tf_op jit(solution)/shard_map/all_to_all | solution.py:47
  41.2 2.4 %reduce.5 = s32[128]{0:T(128)S(1)} reduce(s32[128,1,1]{2,1,0:T(1,128)S(1)} %all-to-all-done, s32[]{:T(128)} %constant.37.clone.1), dimensions={1,2}, to_apply=%all_to_all.16.reduce_sub_computation | reduce | bytes 1028 | tf_op jit(solution)/shard_map/all_to_all | solution.py:47
  43.8 0.7 gather_fusion
  45.8 5.7 %all-to-all-done.1 = bf16[8,256,128]{2,1,0:T(8,128)(2,1)S(1)} async-done(((bf16[8,256,128]{2,1,0:T(8,128)(2,1)}), bf16[8,256,128]{2,1,0:T(8,128)(2,1)S(1)}, u32[]{:S(2)}, u32[]{:S(2)}) %all-to-all-start.1) | async-done | bytes 524320 | tf_op jit(solution)/shard_map/all_to_all | solution.py:47
  51.7 3.0 %collective-permute-start.2 = (bf16[2,256,128]{2,1,0:T(8,128)(2,1)S(1)}, bf16[2,256,128]{2,1,0:T(8,128)(2,1)S(1)}, u32[]{:S(2)}, u32[]{:S(2)}) collective-permute-start(bf16[2,256,128]{2,1,0:T(8,128)(2,1)S(1)} %select_reduce_fusion), channel_id=1, source_target_pairs={{0,96},{32,128},{64,160},{96,192},{128,224},{160,256},{192,288},{2... | collective-permute-start | bytes 393224 | tf_op jit(solution)/shard_map/ppermute | solution.py:42
  54.8 2.6 %collective-permute-start.1 = (bf16[2,256,128]{2,1,0:T(8,128)(2,1)S(1)}, bf16[2,256,128]{2,1,0:T(8,128)(2,1)S(1)}, u32[]{:S(2)}, u32[]{:S(2)}) collective-permute-start(bf16[2,256,128]{2,1,0:T(8,128)(2,1)S(1)} %select_reduce_fusion), channel_id=1, source_target_pairs={{0,64},{32,96},{64,128},{96,160},{128,192},{160,224},{192,256},{22... | collective-permute-start | bytes 393224 | tf_op jit(solution)/shard_map/ppermute | solution.py:42
  57.4 2.6 %collective-permute-start = (bf16[2,256,128]{2,1,0:T(8,128)(2,1)S(1)}, bf16[2,256,128]{2,1,0:T(8,128)(2,1)S(1)}, u32[]{:S(2)}, u32[]{:S(2)}) collective-permute-start(bf16[2,256,128]{2,1,0:T(8,128)(2,1)S(1)} %select_reduce_fusion), channel_id=1, source_target_pairs={{0,32},{32,64},{64,96},{96,128},{128,160},{160,192},{192,224},{224... | collective-permute-start | bytes 393224 | tf_op jit(solution)/shard_map/ppermute | solution.py:42
  60.7 6.6 %collective-permute-done.2 = bf16[2,256,128]{2,1,0:T(8,128)(2,1)S(1)} collective-permute-done((bf16[2,256,128]{2,1,0:T(8,128)(2,1)S(1)}, bf16[2,256,128]{2,1,0:T(8,128)(2,1)S(1)}, u32[]{:S(2)}, u32[]{:S(2)}) %collective-permute-start.2) | collective-permute-done | bytes 131104 | tf_op jit(solution)/shard_map/ppermute | solution.py:42
  67.2 5.6 %collective-permute-done.1 = bf16[2,256,128]{2,1,0:T(8,128)(2,1)S(1)} collective-permute-done((bf16[2,256,128]{2,1,0:T(8,128)(2,1)S(1)}, bf16[2,256,128]{2,1,0:T(8,128)(2,1)S(1)}, u32[]{:S(2)}, u32[]{:S(2)}) %collective-permute-start.1) | collective-permute-done | bytes 131104 | tf_op jit(solution)/shard_map/ppermute | solution.py:42
  73.0 5.3 %collective-permute-start.5 = (bf16[2,256,128]{2,1,0:T(8,128)(2,1)S(1)}, bf16[2,256,128]{2,1,0:T(8,128)(2,1)S(1)}, u32[]{:S(2)}, u32[]{:S(2)}) collective-permute-start(bf16[2,256,128]{2,1,0:T(8,128)(2,1)S(1)} %add_add_fusion.1), channel_id=1, source_target_pairs={{0,384},{32,416},{64,448},{96,480},{128,0},{160,32},{192,64},{224,... | collective-permute-start | bytes 393224 | tf_op jit(solution)/shard_map/ppermute | solution.py:42
  78.3 5.3 %collective-permute-start.4 = (bf16[2,256,128]{2,1,0:T(8,128)(2,1)S(1)}, bf16[2,256,128]{2,1,0:T(8,128)(2,1)S(1)}, u32[]{:S(2)}, u32[]{:S(2)}) collective-permute-start(bf16[2,256,128]{2,1,0:T(8,128)(2,1)S(1)} %add_add_fusion.1), channel_id=1, source_target_pairs={{0,256},{32,288},{64,320},{96,352},{128,384},{160,416},{192,448},{... | collective-permute-start | bytes 393224 | tf_op jit(solution)/shard_map/ppermute | solution.py:42
  83.6 4.6 %collective-permute-start.3 = (bf16[2,256,128]{2,1,0:T(8,128)(2,1)S(1)}, bf16[2,256,128]{2,1,0:T(8,128)(2,1)S(1)}, u32[]{:S(2)}, u32[]{:S(2)}) collective-permute-start(bf16[2,256,128]{2,1,0:T(8,128)(2,1)S(1)} %add_add_fusion.1), channel_id=1, source_target_pairs={{0,128},{32,160},{64,192},{96,224},{128,256},{160,288},{192,320},{... | collective-permute-start | bytes 393224 | tf_op jit(solution)/shard_map/ppermute | solution.py:42
  88.2 1.4 collective-permute-done.5
  89.6 5.9 %collective-permute-done.4 = bf16[2,256,128]{2,1,0:T(8,128)(2,1)S(1)} collective-permute-done((bf16[2,256,128]{2,1,0:T(8,128)(2,1)S(1)}, bf16[2,256,128]{2,1,0:T(8,128)(2,1)S(1)}, u32[]{:S(2)}, u32[]{:S(2)}) %collective-permute-start.4) | collective-permute-done | bytes 131104 | tf_op jit(solution)/shard_map/ppermute | solution.py:42
  95.6 16.7 %collective-permute-done.3 = bf16[2,256,128]{2,1,0:T(8,128)(2,1)S(1)} collective-permute-done((bf16[2,256,128]{2,1,0:T(8,128)(2,1)S(1)}, bf16[2,256,128]{2,1,0:T(8,128)(2,1)S(1)}, u32[]{:S(2)}, u32[]{:S(2)}) %collective-permute-start.3) | collective-permute-done | bytes 131104 | tf_op jit(solution)/shard_map/ppermute | solution.py:42
  112.3 0.9 select_select_fusion
  113.3 4.1 %all-to-all-start.2 = ((bf16[8,256,128]{2,1,0:T(8,128)(2,1)}), bf16[8,256,128]{2,1,0:T(8,128)(2,1)}, u32[]{:S(2)}, u32[]{:S(2)}) async-start(bf16[8,256,128]{2,1,0:T(8,128)(2,1)} %select_select_fusion), calls=%async_computation.2 | async-start | bytes 1048576 | tf_op jit(solution)/shard_map/all_to_all | solution.py:123
  117.6 10.2 %all-to-all-done.2 = bf16[8,256,128]{2,1,0:T(8,128)(2,1)} async-done(((bf16[8,256,128]{2,1,0:T(8,128)(2,1)}), bf16[8,256,128]{2,1,0:T(8,128)(2,1)}, u32[]{:S(2)}, u32[]{:S(2)}) %all-to-all-start.2) | async-done | bytes 524320 | tf_op jit(solution)/shard_map/all_to_all | solution.py:123
  127.7 1.3 broadcast_in_dim.158
  129.0 4.5 %all-to-all-start.3 = ((bf16[4,256,768]{1,2,0:T(8,128)(2,1)}), bf16[4,256,768]{1,2,0:T(8,128)(2,1)}, u32[]{:S(2)}, u32[]{:S(2)}) async-start(bf16[4,256,768]{1,2,0:T(8,128)(2,1)} %broadcast_in_dim.158), calls=%async_computation.3 | async-start | bytes 3145728 | tf_op jit(solution)/shard_map/all_to_all | solution.py:47
  135.9 1.3 multiply_cosine_fusion
  139.7 1.4 constant_dynamic-slice_fusion
  141.1 1.5 reshape.408
  142.6 1.7 fusion.56
  144.3 0.8 reshape.409
  145.0 9.3 %all-to-all-done.3 = bf16[4,256,768]{1,2,0:T(8,128)(2,1)} async-done(((bf16[4,256,768]{1,2,0:T(8,128)(2,1)}), bf16[4,256,768]{1,2,0:T(8,128)(2,1)}, u32[]{:S(2)}, u32[]{:S(2)}) %all-to-all-start.3) | async-done | bytes 1572896 | tf_op jit(solution)/shard_map/all_to_all | solution.py:47
  154.3 2.0 %fusion.57 = f32[256,128]{1,0:T(8,128)S(1)} fusion(bf16[256,3072]{0,1:T(8,128)(2,1)} %bitcast.13, bf16[3072,128]{1,0:T(8,128)(2,1)S(1)} %copy-done.4), kind=kOutput, calls=%fused_computation.107 | convolution fusion | flops 201326592 | bytes 2490368 | tf_op jit(solution)/shard_map/dot_general | solution.py:133
  156.4 0.7 fusion.36
  157.1 0.9 broadcast_in_dim.159
  158.0 3.5 %all-to-all-start.4 = ((f32[4,336,128]{2,1,0:T(8,128)}), f32[4,336,128]{2,1,0:T(8,128)S(1)}, u32[]{:S(2)}, u32[]{:S(2)}) async-start(f32[4,336,128]{2,1,0:T(8,128)} %broadcast_in_dim.159), calls=%async_computation.4 | async-start | bytes 1376256 | tf_op jit(solution)/shard_map/all_to_all | solution.py:47
  161.6 0.7 constant_dynamic-slice_fusion.1
  162.4 3.2 %fusion.58 = f32[256,384]{1,0:T(8,128)} fusion(bf16[256,3072]{0,1:T(8,128)(2,1)} %bitcast.13, bf16[3072,384]{1,0:T(8,128)(2,1)S(1)} %copy-done), kind=kOutput, calls=%fused_computation.108 | convolution fusion | flops 603979776 | bytes 4325376 | tf_op jit(solution)/shard_map/dot_general | solution.py:158
  165.6 6.3 %all-to-all-done.4 = f32[4,336,128]{2,1,0:T(8,128)S(1)} async-done(((f32[4,336,128]{2,1,0:T(8,128)}), f32[4,336,128]{2,1,0:T(8,128)S(1)}, u32[]{:S(2)}, u32[]{:S(2)}) %all-to-all-start.4) | async-done | bytes 688160 | tf_op jit(solution)/shard_map/all_to_all | solution.py:47
  171.9 1.2 fusion.2
  173.2 0.9 copy.43
  174.1 1.8 fusion.53
  175.9 1.1 copy.54
  177.0 1.8 %copy.53 = f32[1,256,3,64]{3,1,2,0:T(8,128)} copy(f32[1,256,3,64]{1,3,2,0:T(8,128)} %get-tuple-element.8) | data formatting | bytes 393216
  180.7 1.4 fusion.4
  182.1 0.8 copy.48
  (52 shorter events, 5.5 us)
Async XLA Ops:
  0.0 162.4 %copy-start = (bf16[3072,384]{1,0:T(8,128)(2,1)S(1)}, bf16[3072,384]{1,0:T(8,128)(2,1)}, u32[]{:S(2)}) copy-start(bf16[3072,384]{1,0:T(8,128)(2,1)} %param.10) | copy-start | bytes 7077892
  3.3 33.5 %all-to-all-start = ((s32[128,1,1]{2,1,0:T(1,128)}), s32[128,1,1]{2,1,0:T(1,128)S(1)}, u32[]{:S(2)}, u32[]{:S(2)}) async-start(s32[128,1,1]{2,1,0:T(1,128)} %broadcast_in_dim.94), calls=%async_computation | async-start | bytes 131072 | tf_op jit(solution)/shard_map/all_to_all | solution.py:47
  37.7 13.8 %all-to-all-start.1 = ((bf16[8,256,128]{2,1,0:T(8,128)(2,1)}), bf16[8,256,128]{2,1,0:T(8,128)(2,1)S(1)}, u32[]{:S(2)}, u32[]{:S(2)}) async-start(bf16[8,256,128]{2,1,0:T(8,128)(2,1)} %broadcast_in_dim.100), calls=%async_computation.1 | async-start | bytes 1048576 | tf_op jit(solution)/shard_map/all_to_all | solution.py:47
  51.7 15.5 %collective-permute-start.2 = (bf16[2,256,128]{2,1,0:T(8,128)(2,1)S(1)}, bf16[2,256,128]{2,1,0:T(8,128)(2,1)S(1)}, u32[]{:S(2)}, u32[]{:S(2)}) collective-permute-start(bf16[2,256,128]{2,1,0:T(8,128)(2,1)S(1)} %select_reduce_fusion), channel_id=1, source_target_pairs={{0,96},{32,128},{64,160},{96,192},{128,224},{160,256},{192,288},{2... | collective-permute-start | bytes 393224 | tf_op jit(solution)/shard_map/ppermute | solution.py:42
  54.8 18.1 %collective-permute-start.1 = (bf16[2,256,128]{2,1,0:T(8,128)(2,1)S(1)}, bf16[2,256,128]{2,1,0:T(8,128)(2,1)S(1)}, u32[]{:S(2)}, u32[]{:S(2)}) collective-permute-start(bf16[2,256,128]{2,1,0:T(8,128)(2,1)S(1)} %select_reduce_fusion), channel_id=1, source_target_pairs={{0,64},{32,96},{64,128},{96,160},{128,192},{160,224},{192,256},{22... | collective-permute-start | bytes 393224 | tf_op jit(solution)/shard_map/ppermute | solution.py:42
  57.4 15.7 %collective-permute-start = (bf16[2,256,128]{2,1,0:T(8,128)(2,1)S(1)}, bf16[2,256,128]{2,1,0:T(8,128)(2,1)S(1)}, u32[]{:S(2)}, u32[]{:S(2)}) collective-permute-start(bf16[2,256,128]{2,1,0:T(8,128)(2,1)S(1)} %select_reduce_fusion), channel_id=1, source_target_pairs={{0,32},{32,64},{64,96},{96,128},{128,160},{160,192},{192,224},{224... | collective-permute-start | bytes 393224 | tf_op jit(solution)/shard_map/ppermute | solution.py:42
  60.7 56.7 %copy-start.1 = (bf16[256,768]{1,0:T(8,128)(2,1)S(1)}, bf16[256,768]{1,0:T(8,128)(2,1)}, u32[]{:S(2)}) copy-start(bf16[256,768]{1,0:T(8,128)(2,1)} %param.9) | copy-start | bytes 1179652
  73.0 16.6 %collective-permute-start.5 = (bf16[2,256,128]{2,1,0:T(8,128)(2,1)S(1)}, bf16[2,256,128]{2,1,0:T(8,128)(2,1)S(1)}, u32[]{:S(2)}, u32[]{:S(2)}) collective-permute-start(bf16[2,256,128]{2,1,0:T(8,128)(2,1)S(1)} %add_add_fusion.1), channel_id=1, source_target_pairs={{0,384},{32,416},{64,448},{96,480},{128,0},{160,32},{192,64},{224,... | collective-permute-start | bytes 393224 | tf_op jit(solution)/shard_map/ppermute | solution.py:42
  78.3 17.3 %collective-permute-start.4 = (bf16[2,256,128]{2,1,0:T(8,128)(2,1)S(1)}, bf16[2,256,128]{2,1,0:T(8,128)(2,1)S(1)}, u32[]{:S(2)}, u32[]{:S(2)}) collective-permute-start(bf16[2,256,128]{2,1,0:T(8,128)(2,1)S(1)} %add_add_fusion.1), channel_id=1, source_target_pairs={{0,256},{32,288},{64,320},{96,352},{128,384},{160,416},{192,448},{... | collective-permute-start | bytes 393224 | tf_op jit(solution)/shard_map/ppermute | solution.py:42
  83.6 28.7 %collective-permute-start.3 = (bf16[2,256,128]{2,1,0:T(8,128)(2,1)S(1)}, bf16[2,256,128]{2,1,0:T(8,128)(2,1)S(1)}, u32[]{:S(2)}, u32[]{:S(2)}) collective-permute-start(bf16[2,256,128]{2,1,0:T(8,128)(2,1)S(1)} %add_add_fusion.1), channel_id=1, source_target_pairs={{0,128},{32,160},{64,192},{96,224},{128,256},{160,288},{192,320},{... | collective-permute-start | bytes 393224 | tf_op jit(solution)/shard_map/ppermute | solution.py:42
  113.3 14.5 %all-to-all-start.2 = ((bf16[8,256,128]{2,1,0:T(8,128)(2,1)}), bf16[8,256,128]{2,1,0:T(8,128)(2,1)}, u32[]{:S(2)}, u32[]{:S(2)}) async-start(bf16[8,256,128]{2,1,0:T(8,128)(2,1)} %select_select_fusion), calls=%async_computation.2 | async-start | bytes 1048576 | tf_op jit(solution)/shard_map/all_to_all | solution.py:123
  129.0 25.3 %copy-start.4 = (bf16[3072,128]{1,0:T(8,128)(2,1)S(1)}, bf16[3072,128]{1,0:T(8,128)(2,1)}, u32[]{:S(2)}) copy-start(bf16[3072,128]{1,0:T(8,128)(2,1)} %param.11) | copy-start | bytes 2359300
  129.0 25.3 %all-to-all-start.3 = ((bf16[4,256,768]{1,2,0:T(8,128)(2,1)}), bf16[4,256,768]{1,2,0:T(8,128)(2,1)}, u32[]{:S(2)}, u32[]{:S(2)}) async-start(bf16[4,256,768]{1,2,0:T(8,128)(2,1)} %broadcast_in_dim.158), calls=%async_computation.3 | async-start | bytes 3145728 | tf_op jit(solution)/shard_map/all_to_all | solution.py:47
  158.0 13.9 %all-to-all-start.4 = ((f32[4,336,128]{2,1,0:T(8,128)}), f32[4,336,128]{2,1,0:T(8,128)S(1)}, u32[]{:S(2)}, u32[]{:S(2)}) async-start(f32[4,336,128]{2,1,0:T(8,128)} %broadcast_in_dim.159), calls=%async_computation.4 | async-start | bytes 1376256 | tf_op jit(solution)/shard_map/all_to_all | solution.py:47
  178.8 1.1 copy-start.2
  178.9 1.2 copy-start.5
  178.9 1.3 copy-start.6
  178.9 0.8 copy-start.3

commit v9 on v8

--- a/solution.py
+++ b/solution.py
@@ -98,6 +98,9 @@
     row = jnp.concatenate([down_rows, query_rows, pair_rows], axis=0)
 
     plane = gather_over(row, "ry", ny)
+    blocks = jnp.stack([states] + [shifted(states, s, n_tp) for s in range(1, n_tp)])
+    source = (tp_index - jnp.arange(n_tp, dtype=jnp.int32)) % n_tp
+    piece = jnp.take(blocks, source, axis=0)
     plane_req = iz * ny + jnp.arange(ny, dtype=jnp.int32)
 
     slot_range = jnp.arange(n_req * store_rows, dtype=jnp.int32)
@@ -127,7 +130,6 @@
     adapter_query = picked[n_down:n_down + n_query].reshape(query_up_store.shape[1:])
     adapter_pair = picked[n_down + n_query:].reshape(key_value_store.shape[1:])
 
-    piece = gather_over(states, "tp", n_tp)
     piece = jnp.transpose(piece, (1, 0, 2)).reshape(rows_total, -1)
 
     key_value_sum = jnp.dot(piece, key_value_weight, preferred_element_type=jnp.float32)

time: 184 us -> 165 us (0.90)
  waiting for transfers between devices: 79.8 us -> 53.4 us
  other arithmetic: 8.83 us -> 13.6 us
  starting transfers between devices: 58.2 us -> 61.6 us
    all_to_all x4 -> x3, waiting for transfers between devices: 33.3 us -> 21 us  [gather_over(): return lax.all_to_all(copies, axis, 0, 0, tiled=True)]
    ppermute x6 -> x9, starting transfers between devices: 23.4 us -> 31.8 us  [shifted(): return lax.ppermute(x, axis, pairs)]
    all_to_all x1, waiting for transfers between devices: 10.2 us -> 2.66 us  [local(): received = lax.all_to_all(send, 'ry', 0, 0, tiled=True)]
    ppermute x6 -> x9, waiting for transfers between devices: 36.4 us -> 29.7 us  [shifted(): return lax.ppermute(x, axis, pairs)]
    all_to_all x4 -> x3, starting transfers between devices: 30.6 us -> 26.3 us  [gather_over(): return lax.all_to_all(copies, axis, 0, 0, tiled=True)]
    gather x0 -> x1, local copies, waits for them, and re-layouts: none -> 3.21 us  [local(): piece = jnp.take(blocks, source, axis=0)]
    select_n x0 -> x2, other arithmetic: none -> 2.79 us  [local(): piece = jnp.take(blocks, source, axis=0)]
    select_n x0 -> x1, local copies, waits for them, and re-layouts: none -> 2.6 us  [local(): piece = jnp.take(blocks, source, axis=0)]
  transfers between devices with their start and end apart: 11 -> 13, of which waited for: 11 -> 9; matrix products, arithmetic and copies ran while one was open for 10% -> 19% of each run, Pallas kernels for 0% -> 0%
where the time goes in v9:
time: 165 us; the launch traced here: 164 us
  starting transfers between devices  61.6 us (37%)
  waiting for transfers between devices  53.4 us (32%)
  local copies, waits for them, and re-layouts  21.3 us (13%)
  other arithmetic  13.6 us (8%)
  matrix products  8.8 us (5%)
  between operations  5.39 us (3%)
    ppermute x9, starting transfers between devices, shifted(): return lax.ppermute(x, axis, pairs)  31.8 us
    ppermute x9, waiting for transfers between devices, shifted(): return lax.ppermute(x, axis, pairs)  29.7 us
    all_to_all x3, starting transfers between devices, gather_over(): return lax.all_to_all(copies, axis, 0, 0, tiled=True)  26.3 us
    all_to_all x3, waiting for transfers between devices, gather_over(): return lax.all_to_all(copies, axis, 0, 0, tiled=True)  21 us
    all_to_all x1, starting transfers between devices, local(): received = lax.all_to_all(send, 'ry', 0, 0, tiled=True)  3.49 us
    unnamed x16, local copies, waits for them, and re-layouts  3.34 us
  transfers between devices with their start and end apart: 13, of which 9 were waited for; matrix products, arithmetic and copies ran while one was open for 19% of the time, Pallas kernels for 0%

profile of v9, /device:TPU:32, one launch (start us, length us, event | category | flops | bytes accessed | tf_op | source)
XLA Modules:
  0.0 164.1 jit_solution(5619363580783874968)
XLA Ops:
  0.0 4.8 %collective-permute-start.8 = (bf16[256,768]{1,0:T(8,128)(2,1)}, bf16[256,768]{1,0:T(8,128)(2,1)}, u32[]{:S(2)}, u32[]{:S(2)}) collective-permute-start(bf16[256,768]{1,0:T(8,128)(2,1)} %param.9), channel_id=1, source_target_pairs={{0,3},{1,0},{2,1},{3,2},{4,7},{5,4},{6,5},{7,6},{8,11},{9,8},{10,9... | collective-permute-start | bytes 1179656 | tf_op jit(solution)/shard_map/ppermute | solution.py:42
  4.8 2.7 %collective-permute-start.7 = (bf16[256,768]{1,0:T(8,128)(2,1)}, bf16[256,768]{1,0:T(8,128)(2,1)}, u32[]{:S(2)}, u32[]{:S(2)}) collective-permute-start(bf16[256,768]{1,0:T(8,128)(2,1)} %param.9), channel_id=1, source_target_pairs={{0,2},{1,3},{2,0},{3,1},{4,6},{5,7},{6,4},{7,5},{8,10},{9,11},{10,... | collective-permute-start | bytes 1179656 | tf_op jit(solution)/shard_map/ppermute | solution.py:42
  7.5 2.8 %collective-permute-start.6 = (bf16[256,768]{1,0:T(8,128)(2,1)}, bf16[256,768]{1,0:T(8,128)(2,1)}, u32[]{:S(2)}, u32[]{:S(2)}) collective-permute-start(bf16[256,768]{1,0:T(8,128)(2,1)} %param.9), channel_id=1, source_target_pairs={{0,1},{1,2},{2,3},{3,0},{4,5},{5,6},{6,7},{7,4},{8,9},{9,10},{10,1... | collective-permute-start | bytes 1179656 | tf_op jit(solution)/shard_map/ppermute | solution.py:42
  11.0 1.3 fusion.46
  12.3 1.2 broadcast_in_dim.102
  13.5 19.2 %all-to-all-start = ((s32[128,1,1]{2,1,0:T(1,128)}), s32[128,1,1]{2,1,0:T(1,128)S(1)}, u32[]{:S(2)}, u32[]{:S(2)}) async-start(s32[128,1,1]{2,1,0:T(1,128)} %broadcast_in_dim.102), calls=%async_computation | async-start | bytes 131072 | tf_op jit(solution)/shard_map/all_to_all | solution.py:47
  32.8 0.7 reshape_squeeze.3
  33.5 0.9 reshape.460
  35.0 1.2 multiply_cosine_fusion
  36.3 0.7 pad_maximum_fusion.2
  38.7 8.3 %all-to-all-done = s32[128,1,1]{2,1,0:T(1,128)S(1)} async-done(((s32[128,1,1]{2,1,0:T(1,128)}), s32[128,1,1]{2,1,0:T(1,128)S(1)}, u32[]{:S(2)}, u32[]{:S(2)}) %all-to-all-start) | async-done | bytes 544 | tf_op jit(solution)/shard_map/all_to_all | solution.py:47
  47.0 0.9 broadcast_in_dim.156
  47.8 3.5 %all-to-all-start.1 = ((bf16[8,256,128]{2,1,0:T(8,128)(2,1)}), bf16[8,256,128]{2,1,0:T(8,128)(2,1)S(1)}, u32[]{:S(2)}, u32[]{:S(2)}) async-start(bf16[8,256,128]{2,1,0:T(8,128)(2,1)} %broadcast_in_dim.156), calls=%async_computation.1 | async-start | bytes 1048576 | tf_op jit(solution)/shard_map/all_to_all | solution.py:47
  51.3 2.4 %reduce.5 = s32[128]{0:T(128)S(1)} reduce(s32[128,1,1]{2,1,0:T(1,128)S(1)} %all-to-all-done, s32[]{:T(128)} %constant.93.clone.1), dimensions={1,2}, to_apply=%all_to_all.13.reduce_sub_computation | reduce | bytes 1028 | tf_op jit(solution)/shard_map/all_to_all | solution.py:47
  53.9 0.7 gather_fusion
  55.2 0.6 gather_fusion.3
  56.0 5.6 %all-to-all-done.1 = bf16[8,256,128]{2,1,0:T(8,128)(2,1)S(1)} async-done(((bf16[8,256,128]{2,1,0:T(8,128)(2,1)}), bf16[8,256,128]{2,1,0:T(8,128)(2,1)S(1)}, u32[]{:S(2)}, u32[]{:S(2)}) %all-to-all-start.1) | async-done | bytes 524320 | tf_op jit(solution)/shard_map/all_to_all | solution.py:47
  61.9 3.0 %collective-permute-start.2 = (bf16[2,256,128]{2,1,0:T(8,128)(2,1)S(1)}, bf16[2,256,128]{2,1,0:T(8,128)(2,1)S(1)}, u32[]{:S(2)}, u32[]{:S(2)}) collective-permute-start(bf16[2,256,128]{2,1,0:T(8,128)(2,1)S(1)} %select_reduce_fusion), channel_id=1, source_target_pairs={{0,96},{32,128},{64,160},{96,192},{128,224},{160,256},{192,288},{2... | collective-permute-start | bytes 393224 | tf_op jit(solution)/shard_map/ppermute | solution.py:42
  68.1 2.6 %collective-permute-start.1 = (bf16[2,256,128]{2,1,0:T(8,128)(2,1)S(1)}, bf16[2,256,128]{2,1,0:T(8,128)(2,1)S(1)}, u32[]{:S(2)}, u32[]{:S(2)}) collective-permute-start(bf16[2,256,128]{2,1,0:T(8,128)(2,1)S(1)} %select_reduce_fusion), channel_id=1, source_target_pairs={{0,64},{32,96},{64,128},{96,160},{128,192},{160,224},{192,256},{22... | collective-permute-start | bytes 393224 | tf_op jit(solution)/shard_map/ppermute | solution.py:42
  70.7 7.3 %collective-permute-done.2 = bf16[2,256,128]{2,1,0:T(8,128)(2,1)S(1)} collective-permute-done((bf16[2,256,128]{2,1,0:T(8,128)(2,1)S(1)}, bf16[2,256,128]{2,1,0:T(8,128)(2,1)S(1)}, u32[]{:S(2)}, u32[]{:S(2)}) %collective-permute-start.2) | collective-permute-done | bytes 131104 | tf_op jit(solution)/shard_map/ppermute | solution.py:42
  78.0 1.9 %collective-permute-start = (bf16[2,256,128]{2,1,0:T(8,128)(2,1)S(1)}, bf16[2,256,128]{2,1,0:T(8,128)(2,1)S(1)}, u32[]{:S(2)}, u32[]{:S(2)}) collective-permute-start(bf16[2,256,128]{2,1,0:T(8,128)(2,1)S(1)} %select_reduce_fusion), channel_id=1, source_target_pairs={{0,32},{32,64},{64,96},{96,128},{128,160},{160,192},{192,224},{224... | collective-permute-start | bytes 393224 | tf_op jit(solution)/shard_map/ppermute | solution.py:42
  79.9 3.2 %collective-permute-done.1 = bf16[2,256,128]{2,1,0:T(8,128)(2,1)S(1)} collective-permute-done((bf16[2,256,128]{2,1,0:T(8,128)(2,1)S(1)}, bf16[2,256,128]{2,1,0:T(8,128)(2,1)S(1)}, u32[]{:S(2)}, u32[]{:S(2)}) %collective-permute-start.1) | collective-permute-done | bytes 131104 | tf_op jit(solution)/shard_map/ppermute | solution.py:42
  83.1 2.3 %collective-permute-done = bf16[2,256,128]{2,1,0:T(8,128)(2,1)S(1)} collective-permute-done((bf16[2,256,128]{2,1,0:T(8,128)(2,1)S(1)}, bf16[2,256,128]{2,1,0:T(8,128)(2,1)S(1)}, u32[]{:S(2)}, u32[]{:S(2)}) %collective-permute-start) | collective-permute-done | bytes 131104 | tf_op jit(solution)/shard_map/ppermute | solution.py:42
  85.5 4.7 %collective-permute-start.5 = (bf16[2,256,128]{2,1,0:T(8,128)(2,1)S(1)}, bf16[2,256,128]{2,1,0:T(8,128)(2,1)S(1)}, u32[]{:S(2)}, u32[]{:S(2)}) collective-permute-start(bf16[2,256,128]{2,1,0:T(8,128)(2,1)S(1)} %add_add_fusion.1), channel_id=1, source_target_pairs={{0,384},{32,416},{64,448},{96,480},{128,0},{160,32},{192,64},{224,... | collective-permute-start | bytes 393224 | tf_op jit(solution)/shard_map/ppermute | solution.py:42
  90.2 6.8 %collective-permute-start.4 = (bf16[2,256,128]{2,1,0:T(8,128)(2,1)S(1)}, bf16[2,256,128]{2,1,0:T(8,128)(2,1)S(1)}, u32[]{:S(2)}, u32[]{:S(2)}) collective-permute-start(bf16[2,256,128]{2,1,0:T(8,128)(2,1)S(1)} %add_add_fusion.1), channel_id=1, source_target_pairs={{0,256},{32,288},{64,320},{96,352},{128,384},{160,416},{192,448},{... | collective-permute-start | bytes 393224 | tf_op jit(solution)/shard_map/ppermute | solution.py:42
  97.0 2.5 %collective-permute-start.3 = (bf16[2,256,128]{2,1,0:T(8,128)(2,1)S(1)}, bf16[2,256,128]{2,1,0:T(8,128)(2,1)S(1)}, u32[]{:S(2)}, u32[]{:S(2)}) collective-permute-start(bf16[2,256,128]{2,1,0:T(8,128)(2,1)S(1)} %add_add_fusion.1), channel_id=1, source_target_pairs={{0,128},{32,160},{64,192},{96,224},{128,256},{160,288},{192,320},{... | collective-permute-start | bytes 393224 | tf_op jit(solution)/shard_map/ppermute | solution.py:42
  99.5 2.6 %pad_maximum_fusion = bf16[4,256,768]{2,1,0:T(8,128)(2,1)} fusion(bf16[1,256,768]{2,1,0:T(8,128)(2,1)} %bitcast.15, bf16[1,256,768]{2,1,0:T(8,128)(2,1)} %bitcast.14, bf16[1,256,768]{2,1,0:T(8,128)(2,1)} %bitcast.13, bf16[1,256,768]{2,1,0:T(8,128)(2,1)S(1)} %bitcast.97), kind=kLoop, calls=%fused_computation.5 | loop fusion | flops 2359296 | bytes 3145728 | tf_op jit(solution)/shard_map/stack | solution.py:101
  102.1 3.2 %gather_fusion.4 = bf16[4,256,768]{2,1,0:T(8,128)(2,1)} fusion(bf16[4,256,768]{2,1,0:T(8,128)(2,1)} %pad_maximum_fusion, s32[1024]{0:T(1024)S(1)} %pad_clamp_fusion), kind=kCustom, calls=%fused_computation.4 | custom fusion | bytes 3145744 | tf_op jit(solution)/shard_map/jit(_take)/gather | solution.py:103
  105.3 5.3 %collective-permute-done.4 = bf16[2,256,128]{2,1,0:T(8,128)(2,1)S(1)} collective-permute-done((bf16[2,256,128]{2,1,0:T(8,128)(2,1)S(1)}, bf16[2,256,128]{2,1,0:T(8,128)(2,1)S(1)}, u32[]{:S(2)}, u32[]{:S(2)}) %collective-permute-start.4) | collective-permute-done | bytes 131104 | tf_op jit(solution)/shard_map/ppermute | solution.py:42
  110.7 11.5 %collective-permute-done.3 = bf16[2,256,128]{2,1,0:T(8,128)(2,1)S(1)} collective-permute-done((bf16[2,256,128]{2,1,0:T(8,128)(2,1)S(1)}, bf16[2,256,128]{2,1,0:T(8,128)(2,1)S(1)}, u32[]{:S(2)}, u32[]{:S(2)}) %collective-permute-start.3) | collective-permute-done | bytes 131104 | tf_op jit(solution)/shard_map/ppermute | solution.py:42
  122.3 1.0 select_select_fusion
  123.2 3.5 %all-to-all-start.2 = ((bf16[8,256,128]{2,1,0:T(8,128)(2,1)}), bf16[8,256,128]{2,1,0:T(8,128)(2,1)S(1)}, u32[]{:S(2)}, u32[]{:S(2)}) async-start(bf16[8,256,128]{2,1,0:T(8,128)(2,1)} %select_select_fusion), calls=%async_computation.2 | async-start | bytes 1048576 | tf_op jit(solution)/shard_map/all_to_all | solution.py:126
  126.7 2.8 %select_bitcast_fusion = bf16[256,4,768]{2,0,1:T(8,128)(2,1)} fusion(bf16[4,256,768]{2,1,0:T(8,128)(2,1)} %gather_fusion.4, pred[4]{0:T(512)(128)(4,1)S(1)} %compare_and_fusion), kind=kLoop, calls=%fused_computation.6 | loop fusion | flops 786432 | bytes 3145732 | tf_op jit(solution)/shard_map/jit(_take)/select_n | solution.py:103
  129.5 2.6 %copy.48 = bf16[256,4,768]{0,2,1:T(8,128)(2,1)} copy(bf16[256,4,768]{2,0,1:T(8,128)(2,1)} %select_bitcast_fusion) | data formatting | bytes 3145728 | tf_op jit(solution)/shard_map/jit(_take)/select_n | solution.py:103
  132.1 2.2 %fusion.60 = f32[256,128]{1,0:T(8,128)S(1)} fusion(bf16[256,3072]{0,1:T(8,128)(2,1)} %bitcast.95, bf16[3072,128]{1,0:T(8,128)(2,1)} %param.11), kind=kOutput, calls=%fused_computation.123 | convolution fusion | flops 201326592 | bytes 2490368 | tf_op jit(solution)/shard_map/dot_general | solution.py:135
  134.3 2.7 %all-to-all-done.2 = bf16[8,256,128]{2,1,0:T(8,128)(2,1)S(1)} async-done(((bf16[8,256,128]{2,1,0:T(8,128)(2,1)}), bf16[8,256,128]{2,1,0:T(8,128)(2,1)S(1)}, u32[]{:S(2)}, u32[]{:S(2)}) %all-to-all-start.2) | async-done | bytes 524320 | tf_op jit(solution)/shard_map/all_to_all | solution.py:126
  137.3 0.9 broadcast_in_dim.164
  138.3 3.6 %all-to-all-start.3 = ((f32[4,336,128]{2,1,0:T(8,128)}), f32[4,336,128]{2,1,0:T(8,128)S(1)}, u32[]{:S(2)}, u32[]{:S(2)}) async-start(f32[4,336,128]{2,1,0:T(8,128)} %broadcast_in_dim.164), calls=%async_computation.3 | async-start | bytes 1376256 | tf_op jit(solution)/shard_map/all_to_all | solution.py:47
  142.0 3.2 %fusion.61 = f32[256,384]{1,0:T(8,128)} fusion(bf16[256,3072]{0,1:T(8,128)(2,1)} %bitcast.96, bf16[3072,384]{1,0:T(8,128)(2,1)S(1)} %copy-done), kind=kOutput, calls=%fused_computation.124 | convolution fusion | flops 603979776 | bytes 4325376 | tf_op jit(solution)/shard_map/dot_general | solution.py:160
  145.2 0.7 constant_dynamic-slice_fusion.1
  145.9 7.1 %all-to-all-done.3 = f32[4,336,128]{2,1,0:T(8,128)S(1)} async-done(((f32[4,336,128]{2,1,0:T(8,128)}), f32[4,336,128]{2,1,0:T(8,128)S(1)}, u32[]{:S(2)}, u32[]{:S(2)}) %all-to-all-start.3) | async-done | bytes 688160 | tf_op jit(solution)/shard_map/all_to_all | solution.py:47
  153.1 1.2 fusion.2
  154.3 0.9 copy.50
  155.3 1.8 %fusion.56 = (f32[1,256,3,64]{1,3,2,0:T(8,128)}, f32[1,256,3,64]{1,3,2,0:T(8,128)}) fusion(f32[1,256,3,128]{1,3,2,0:T(8,128)} %bitcast.98), kind=kLoop, calls=%fused_computation.119 | loop fusion | bytes 786432 | tf_op jit(solution)/shard_map/slice | solution.py:26
  157.1 1.1 copy.61
  158.1 1.8 %copy.60 = f32[1,256,3,64]{3,1,2,0:T(8,128)} copy(f32[1,256,3,64]{1,3,2,0:T(8,128)} %get-tuple-element.8) | data formatting | bytes 393216
  161.9 1.4 fusion.4
  163.2 0.8 copy.55
  (61 shorter events, 5.0 us)
Async XLA Ops:
  0.0 142.0 %copy-start = (bf16[3072,384]{1,0:T(8,128)(2,1)S(1)}, bf16[3072,384]{1,0:T(8,128)(2,1)}, u32[]{:S(2)}) copy-start(bf16[3072,384]{1,0:T(8,128)(2,1)} %param.10) | copy-start | bytes 7077892
  0.0 97.0 %collective-permute-start.8 = (bf16[256,768]{1,0:T(8,128)(2,1)}, bf16[256,768]{1,0:T(8,128)(2,1)}, u32[]{:S(2)}, u32[]{:S(2)}) collective-permute-start(bf16[256,768]{1,0:T(8,128)(2,1)} %param.9), channel_id=1, source_target_pairs={{0,3},{1,0},{2,1},{3,2},{4,7},{5,4},{6,5},{7,6},{8,11},{9,8},{10,9... | collective-permute-start | bytes 1179656 | tf_op jit(solution)/shard_map/ppermute | solution.py:42
  4.8 94.7 %collective-permute-start.7 = (bf16[256,768]{1,0:T(8,128)(2,1)}, bf16[256,768]{1,0:T(8,128)(2,1)}, u32[]{:S(2)}, u32[]{:S(2)}) collective-permute-start(bf16[256,768]{1,0:T(8,128)(2,1)} %param.9), channel_id=1, source_target_pairs={{0,2},{1,3},{2,0},{3,1},{4,6},{5,7},{6,4},{7,5},{8,10},{9,11},{10,... | collective-permute-start | bytes 1179656 | tf_op jit(solution)/shard_map/ppermute | solution.py:42
  7.5 92.0 %collective-permute-start.6 = (bf16[256,768]{1,0:T(8,128)(2,1)}, bf16[256,768]{1,0:T(8,128)(2,1)}, u32[]{:S(2)}, u32[]{:S(2)}) collective-permute-start(bf16[256,768]{1,0:T(8,128)(2,1)} %param.9), channel_id=1, source_target_pairs={{0,1},{1,2},{2,3},{3,0},{4,5},{5,6},{6,7},{7,4},{8,9},{9,10},{10,1... | collective-permute-start | bytes 1179656 | tf_op jit(solution)/shard_map/ppermute | solution.py:42
  13.5 33.5 %all-to-all-start = ((s32[128,1,1]{2,1,0:T(1,128)}), s32[128,1,1]{2,1,0:T(1,128)S(1)}, u32[]{:S(2)}, u32[]{:S(2)}) async-start(s32[128,1,1]{2,1,0:T(1,128)} %broadcast_in_dim.102), calls=%async_computation | async-start | bytes 131072 | tf_op jit(solution)/shard_map/all_to_all | solution.py:47
  47.8 13.8 %all-to-all-start.1 = ((bf16[8,256,128]{2,1,0:T(8,128)(2,1)}), bf16[8,256,128]{2,1,0:T(8,128)(2,1)S(1)}, u32[]{:S(2)}, u32[]{:S(2)}) async-start(bf16[8,256,128]{2,1,0:T(8,128)(2,1)} %broadcast_in_dim.156), calls=%async_computation.1 | async-start | bytes 1048576 | tf_op jit(solution)/shard_map/all_to_all | solution.py:47
  54.6 45.0 %copy-start.1 = (bf16[256,768]{1,0:T(8,128)(2,1)S(1)}, bf16[256,768]{1,0:T(8,128)(2,1)}, u32[]{:S(2)}) copy-start(bf16[256,768]{1,0:T(8,128)(2,1)} %param.9) | copy-start | bytes 1179652
  61.9 16.1 %collective-permute-start.2 = (bf16[2,256,128]{2,1,0:T(8,128)(2,1)S(1)}, bf16[2,256,128]{2,1,0:T(8,128)(2,1)S(1)}, u32[]{:S(2)}, u32[]{:S(2)}) collective-permute-start(bf16[2,256,128]{2,1,0:T(8,128)(2,1)S(1)} %select_reduce_fusion), channel_id=1, source_target_pairs={{0,96},{32,128},{64,160},{96,192},{128,224},{160,256},{192,288},{2... | collective-permute-start | bytes 393224 | tf_op jit(solution)/shard_map/ppermute | solution.py:42
  68.1 15.0 %collective-permute-start.1 = (bf16[2,256,128]{2,1,0:T(8,128)(2,1)S(1)}, bf16[2,256,128]{2,1,0:T(8,128)(2,1)S(1)}, u32[]{:S(2)}, u32[]{:S(2)}) collective-permute-start(bf16[2,256,128]{2,1,0:T(8,128)(2,1)S(1)} %select_reduce_fusion), channel_id=1, source_target_pairs={{0,64},{32,96},{64,128},{96,160},{128,192},{160,224},{192,256},{22... | collective-permute-start | bytes 393224 | tf_op jit(solution)/shard_map/ppermute | solution.py:42
  78.0 7.5 %collective-permute-start = (bf16[2,256,128]{2,1,0:T(8,128)(2,1)S(1)}, bf16[2,256,128]{2,1,0:T(8,128)(2,1)S(1)}, u32[]{:S(2)}, u32[]{:S(2)}) collective-permute-start(bf16[2,256,128]{2,1,0:T(8,128)(2,1)S(1)} %select_reduce_fusion), channel_id=1, source_target_pairs={{0,32},{32,64},{64,96},{96,128},{128,160},{160,192},{192,224},{224... | collective-permute-start | bytes 393224 | tf_op jit(solution)/shard_map/ppermute | solution.py:42
  85.5 19.8 %collective-permute-start.5 = (bf16[2,256,128]{2,1,0:T(8,128)(2,1)S(1)}, bf16[2,256,128]{2,1,0:T(8,128)(2,1)S(1)}, u32[]{:S(2)}, u32[]{:S(2)}) collective-permute-start(bf16[2,256,128]{2,1,0:T(8,128)(2,1)S(1)} %add_add_fusion.1), channel_id=1, source_target_pairs={{0,384},{32,416},{64,448},{96,480},{128,0},{160,32},{192,64},{224,... | collective-permute-start | bytes 393224 | tf_op jit(solution)/shard_map/ppermute | solution.py:42
  90.2 20.5 %collective-permute-start.4 = (bf16[2,256,128]{2,1,0:T(8,128)(2,1)S(1)}, bf16[2,256,128]{2,1,0:T(8,128)(2,1)S(1)}, u32[]{:S(2)}, u32[]{:S(2)}) collective-permute-start(bf16[2,256,128]{2,1,0:T(8,128)(2,1)S(1)} %add_add_fusion.1), channel_id=1, source_target_pairs={{0,256},{32,288},{64,320},{96,352},{128,384},{160,416},{192,448},{... | collective-permute-start | bytes 393224 | tf_op jit(solution)/shard_map/ppermute | solution.py:42
  97.0 25.2 %collective-permute-start.3 = (bf16[2,256,128]{2,1,0:T(8,128)(2,1)S(1)}, bf16[2,256,128]{2,1,0:T(8,128)(2,1)S(1)}, u32[]{:S(2)}, u32[]{:S(2)}) collective-permute-start(bf16[2,256,128]{2,1,0:T(8,128)(2,1)S(1)} %add_add_fusion.1), channel_id=1, source_target_pairs={{0,128},{32,160},{64,192},{96,224},{128,256},{160,288},{192,320},{... | collective-permute-start | bytes 393224 | tf_op jit(solution)/shard_map/ppermute | solution.py:42
  123.2 13.8 %all-to-all-start.2 = ((bf16[8,256,128]{2,1,0:T(8,128)(2,1)}), bf16[8,256,128]{2,1,0:T(8,128)(2,1)S(1)}, u32[]{:S(2)}, u32[]{:S(2)}) async-start(bf16[8,256,128]{2,1,0:T(8,128)(2,1)} %select_select_fusion), calls=%async_computation.2 | async-start | bytes 1048576 | tf_op jit(solution)/shard_map/all_to_all | solution.py:126
  137.0 1.3 copy-start.4
  138.3 14.8 %all-to-all-start.3 = ((f32[4,336,128]{2,1,0:T(8,128)}), f32[4,336,128]{2,1,0:T(8,128)S(1)}, u32[]{:S(2)}, u32[]{:S(2)}) async-start(f32[4,336,128]{2,1,0:T(8,128)} %broadcast_in_dim.164), calls=%async_computation.3 | async-start | bytes 1376256 | tf_op jit(solution)/shard_map/all_to_all | solution.py:47
  160.0 1.1 copy-start.2
  160.0 1.2 copy-start.5
  160.0 1.3 copy-start.6
  160.0 0.8 copy-start.3

commit v10 on v9

--- a/solution.py
+++ b/solution.py
@@ -70,10 +70,11 @@
     key_value_store,
 ):
     tp_index = lax.axis_index("tp")
-    iz = lax.axis_index("rz")
+    n_low = lax.axis_size("zl")
+    iz = lax.axis_index("zh") * n_low + lax.axis_index("zl")
     iy = lax.axis_index("ry")
     n_tp = lax.axis_size("tp")
-    nz = lax.axis_size("rz")
+    nz = lax.axis_size("zh") * n_low
     ny = lax.axis_size("ry")
     n_req = nz * ny
     me = iz * ny + iy
@@ -88,7 +89,7 @@
 
     own_slot = lookup_slots(adapter_ids, adapter_slot)
 
-    slots_all = gather_over(own_slot, ("rz", "ry"), n_req).reshape(n_req)
+    slots_all = gather_over(own_slot, ("zh", "zl", "ry"), n_req).reshape(n_req)
 
     down_rows = down_store[0].T.reshape(-1, 128)
     query_rows = query_up_store[0].reshape(-1, 128)
@@ -117,7 +118,9 @@
         jnp.where(choose[:, :, None, None], plane[None], jnp.zeros((), plane.dtype)),
         axis=1,
     )
-    column = spread_sum(column, "rz", nz)
+    for axis in ("zl", "zh"):
+        copies = gather_over(column, axis, lax.axis_size(axis))
+        column = jnp.sum(copies, axis=0)
     dest_k = prefix[slots_all[plane_req]]
     held = column[0]
     for m in range(1, per_column):
@@ -201,10 +204,12 @@
 def solution(mesh):
     n_req = mesh.shape["req"]
     ny = 8 if n_req % 8 == 0 else 1
+    n_low = 4 if (n_req // ny) % 4 == 0 else 1
     split = jax.sharding.Mesh(
-        mesh.devices.reshape(n_req // ny, ny, mesh.shape["tp"]), ("rz", "ry", "tp")
-    )
-    req = ("rz", "ry")
+        mesh.devices.reshape(n_req // ny // n_low, n_low, ny, mesh.shape["tp"]),
+        ("zh", "zl", "ry", "tp"),
+    )
+    req = ("zh", "zl", "ry")
     return jax.shard_map(
         local,
         mesh=split,

time: 165 us -> 149 us (0.903)
  the two profiles are of different devices: /device:TPU:32 before, /device:TPU:1 now
where the time goes in v10:
time: 149 us; the launch traced here: 148 us
  starting transfers between devices  52.1 us (35%)
  waiting for transfers between devices  45.1 us (30%)
  local copies, waits for them, and re-layouts  23 us (15%)
  other arithmetic  13.7 us (9%)
  matrix products  8.8 us (6%)
  between operations  5.45 us (4%)
    all_to_all x5, waiting for transfers between devices, gather_over(): return lax.all_to_all(copies, axis, 0, 0, tiled=True)  39.5 us
    all_to_all x5, starting transfers between devices, gather_over(): return lax.all_to_all(copies, axis, 0, 0, tiled=True)  38.9 us
    ppermute x3, starting transfers between devices, shifted(): return lax.ppermute(x, axis, pairs)  9.33 us
    broadcast_in_dim x5, local copies, waits for them, and re-layouts, gather_over(): copies = jnp.broadcast_to(x[None], (n,) + x.shape)  4.69 us
    all_to_all x1, starting transfers between devices, local(): received = lax.all_to_all(send, 'ry', 0, 0, tiled=True)  3.89 us
    ppermute x3, waiting for transfers between devices, shifted(): return lax.ppermute(x, axis, pairs)  3.68 us
    unnamed x16, local copies, waits for them, and re-layouts  3.35 us
    gather x1, local copies, waits for them, and re-layouts, local(): piece = jnp.take(blocks, source, axis=0)  3.21 us
  transfers between devices with their start and end apart: 9, of which 7 were waited for; matrix products, arithmetic and copies ran while one was open for 19% of the time, Pallas kernels for 0%

profile of v10, /device:TPU:1, one launch (start us, length us, event | category | flops | bytes accessed | tf_op | source)
XLA Modules:
  0.0 148.1 jit_solution(6689604775397837990)
XLA Ops:
  0.8 1.3 fusion.46
  2.1 1.2 broadcast_in_dim.106
  3.3 20.6 %all-to-all-start = ((s32[128,1,1]{2,1,0:T(1,128)}), s32[128,1,1]{2,1,0:T(1,128)S(1)}, u32[]{:S(2)}, u32[]{:S(2)}) async-start(s32[128,1,1]{2,1,0:T(1,128)} %broadcast_in_dim.106), calls=%async_computation | async-start | bytes 131072 | tf_op jit(solution)/shard_map/all_to_all | solution.py:47
  23.9 0.7 reshape_squeeze.3
  24.6 0.9 reshape.462
  25.5 0.7 pad_maximum_fusion.2
  26.2 12.5 %all-to-all-done = s32[128,1,1]{2,1,0:T(1,128)S(1)} async-done(((s32[128,1,1]{2,1,0:T(1,128)}), s32[128,1,1]{2,1,0:T(1,128)S(1)}, u32[]{:S(2)}, u32[]{:S(2)}) %all-to-all-start) | async-done | bytes 544 | tf_op jit(solution)/shard_map/all_to_all | solution.py:47
  38.7 0.9 broadcast_in_dim.168
  39.6 3.9 %all-to-all-start.1 = ((bf16[8,256,128]{2,1,0:T(8,128)(2,1)}), bf16[8,256,128]{2,1,0:T(8,128)(2,1)S(1)}, u32[]{:S(2)}, u32[]{:S(2)}) async-start(bf16[8,256,128]{2,1,0:T(8,128)(2,1)} %broadcast_in_dim.168), calls=%async_computation.1 | async-start | bytes 1048576 | tf_op jit(solution)/shard_map/all_to_all | solution.py:47
  43.5 2.3 %reduce.7 = s32[128]{0:T(128)S(1)} reduce(s32[128,1,1]{2,1,0:T(1,128)S(1)} %all-to-all-done, s32[]{:T(128)} %constant.97.clone.1), dimensions={1,2}, to_apply=%all_to_all.19.reduce_sub_computation | reduce | bytes 1028 | tf_op jit(solution)/shard_map/all_to_all | solution.py:47
  46.0 0.7 gather_fusion.2
  46.7 0.6 gather_fusion.3
  47.4 5.5 %all-to-all-done.1 = bf16[8,256,128]{2,1,0:T(8,128)(2,1)S(1)} async-done(((bf16[8,256,128]{2,1,0:T(8,128)(2,1)}), bf16[8,256,128]{2,1,0:T(8,128)(2,1)S(1)}, u32[]{:S(2)}, u32[]{:S(2)}) %all-to-all-start.1) | async-done | bytes 524320 | tf_op jit(solution)/shard_map/all_to_all | solution.py:47
  53.2 0.9 broadcast_in_dim.171
  54.1 3.5 %all-to-all-start.2 = ((bf16[4,2,256,128]{3,2,1,0:T(8,128)(2,1)}), bf16[4,2,256,128]{3,2,1,0:T(8,128)(2,1)S(1)}, u32[]{:S(2)}, u32[]{:S(2)}) async-start(bf16[4,2,256,128]{3,2,1,0:T(8,128)(2,1)} %broadcast_in_dim.171), calls=%async_computation.2 | async-start | bytes 1048576 | tf_op jit(solution)/shard_map/all_to_all | solution.py:47
  57.6 4.4 %collective-permute-start.2 = (bf16[256,768]{1,0:T(8,128)(2,1)S(1)}, bf16[256,768]{1,0:T(8,128)(2,1)}, u32[]{:S(2)}, u32[]{:S(2)}) collective-permute-start(bf16[256,768]{1,0:T(8,128)(2,1)S(1)} %copy-done.1), channel_id=1, source_target_pairs={{0,3},{1,0},{2,1},{3,2},{4,7},{5,4},{6,5},{7,6},{8,11},{9,8},{10,9... | collective-permute-start | bytes 1179656 | tf_op jit(solution)/shard_map/ppermute | solution.py:42
  62.0 2.4 %collective-permute-start.1 = (bf16[256,768]{1,0:T(8,128)(2,1)S(1)}, bf16[256,768]{1,0:T(8,128)(2,1)}, u32[]{:S(2)}, u32[]{:S(2)}) collective-permute-start(bf16[256,768]{1,0:T(8,128)(2,1)S(1)} %copy-done.1), channel_id=1, source_target_pairs={{0,2},{1,3},{2,0},{3,1},{4,6},{5,7},{6,4},{7,5},{8,10},{9,11},{10,... | collective-permute-start | bytes 1179656 | tf_op jit(solution)/shard_map/ppermute | solution.py:42
  64.4 2.5 %collective-permute-start = (bf16[256,768]{1,0:T(8,128)(2,1)S(1)}, bf16[256,768]{1,0:T(8,128)(2,1)}, u32[]{:S(2)}, u32[]{:S(2)}) collective-permute-start(bf16[256,768]{1,0:T(8,128)(2,1)S(1)} %copy-done.1), channel_id=1, source_target_pairs={{0,1},{1,2},{2,3},{3,0},{4,5},{5,6},{6,7},{7,4},{8,9},{9,10},{10,1... | collective-permute-start | bytes 1179656 | tf_op jit(solution)/shard_map/ppermute | solution.py:42
  69.3 2.4 %all-to-all-done.2 = bf16[4,2,256,128]{3,2,1,0:T(8,128)(2,1)S(1)} async-done(((bf16[4,2,256,128]{3,2,1,0:T(8,128)(2,1)}), bf16[4,2,256,128]{3,2,1,0:T(8,128)(2,1)S(1)}, u32[]{:S(2)}, u32[]{:S(2)}) %all-to-all-start.2) | async-done | bytes 524320 | tf_op jit(solution)/shard_map/all_to_all | solution.py:47
  71.7 0.9 broadcast_in_dim.172
  72.6 3.5 %all-to-all-start.3 = ((bf16[4,2,256,128]{3,2,1,0:T(8,128)(2,1)}), bf16[4,2,256,128]{3,2,1,0:T(8,128)(2,1)S(1)}, u32[]{:S(2)}, u32[]{:S(2)}) async-start(bf16[4,2,256,128]{3,2,1,0:T(8,128)(2,1)} %broadcast_in_dim.172), calls=%async_computation.3 | async-start | bytes 1048576 | tf_op jit(solution)/shard_map/all_to_all | solution.py:47
  76.1 1.2 multiply_cosine_fusion
  77.4 0.6 gather_fusion
  78.0 0.6 dynamic_slice.18
  80.6 0.6 gather_fusion.1
  81.3 3.7 %collective-permute-done = bf16[256,768]{1,0:T(8,128)(2,1)} collective-permute-done((bf16[256,768]{1,0:T(8,128)(2,1)S(1)}, bf16[256,768]{1,0:T(8,128)(2,1)}, u32[]{:S(2)}, u32[]{:S(2)}) %collective-permute-start) | collective-permute-done | bytes 393248 | tf_op jit(solution)/shard_map/ppermute | solution.py:42
  84.9 2.6 %pad_maximum_fusion = bf16[4,256,768]{2,1,0:T(8,128)(2,1)} fusion(bf16[1,256,768]{2,1,0:T(8,128)(2,1)} %bitcast.15, bf16[1,256,768]{2,1,0:T(8,128)(2,1)} %bitcast.14, bf16[1,256,768]{2,1,0:T(8,128)(2,1)} %bitcast.13, bf16[1,256,768]{2,1,0:T(8,128)(2,1)S(1)} %bitcast.97), kind=kLoop, calls=%fused_computation.5 | loop fusion | flops 2359296 | bytes 3145728 | tf_op jit(solution)/shard_map/stack | solution.py:102
  87.5 3.2 %gather_fusion.4 = bf16[4,256,768]{2,1,0:T(8,128)(2,1)} fusion(bf16[4,256,768]{2,1,0:T(8,128)(2,1)} %pad_maximum_fusion, s32[1024]{0:T(1024)S(1)} %pad_clamp_fusion), kind=kCustom, calls=%fused_computation.4 | custom fusion | bytes 3145744 | tf_op jit(solution)/shard_map/jit(_take)/gather | solution.py:104
  90.8 13.1 %all-to-all-done.3 = bf16[4,2,256,128]{3,2,1,0:T(8,128)(2,1)S(1)} async-done(((bf16[4,2,256,128]{3,2,1,0:T(8,128)(2,1)}), bf16[4,2,256,128]{3,2,1,0:T(8,128)(2,1)S(1)}, u32[]{:S(2)}, u32[]{:S(2)}) %all-to-all-start.3) | async-done | bytes 524320 | tf_op jit(solution)/shard_map/all_to_all | solution.py:47
  103.9 0.9 select_select_fusion
  104.8 3.9 %all-to-all-start.4 = ((bf16[8,256,128]{2,1,0:T(8,128)(2,1)}), bf16[8,256,128]{2,1,0:T(8,128)(2,1)S(1)}, u32[]{:S(2)}, u32[]{:S(2)}) async-start(bf16[8,256,128]{2,1,0:T(8,128)(2,1)} %select_select_fusion), calls=%async_computation.4 | async-start | bytes 1048576 | tf_op jit(solution)/shard_map/all_to_all | solution.py:129
  108.7 2.8 %select_bitcast_fusion = bf16[256,4,768]{2,0,1:T(8,128)(2,1)} fusion(bf16[4,256,768]{2,1,0:T(8,128)(2,1)} %gather_fusion.4, pred[4]{0:T(512)(128)(4,1)S(1)} %compare_and_fusion), kind=kLoop, calls=%fused_computation.6 | loop fusion | flops 786432 | bytes 3145732 | tf_op jit(solution)/shard_map/jit(_take)/select_n | solution.py:104
  111.5 2.6 %copy.48 = bf16[256,4,768]{0,2,1:T(8,128)(2,1)} copy(bf16[256,4,768]{2,0,1:T(8,128)(2,1)} %select_bitcast_fusion) | data formatting | bytes 3145728 | tf_op jit(solution)/shard_map/jit(_take)/select_n | solution.py:104
  114.1 2.2 %fusion.60 = f32[256,128]{1,0:T(8,128)S(1)} fusion(bf16[256,3072]{0,1:T(8,128)(2,1)} %bitcast.95, bf16[3072,128]{1,0:T(8,128)(2,1)} %param.11), kind=kOutput, calls=%fused_computation.121 | convolution fusion | flops 201326592 | bytes 2490368 | tf_op jit(solution)/shard_map/dot_general | solution.py:138
  116.3 1.9 %all-to-all-done.4 = bf16[8,256,128]{2,1,0:T(8,128)(2,1)S(1)} async-done(((bf16[8,256,128]{2,1,0:T(8,128)(2,1)}), bf16[8,256,128]{2,1,0:T(8,128)(2,1)S(1)}, u32[]{:S(2)}, u32[]{:S(2)}) %all-to-all-start.4) | async-done | bytes 524320 | tf_op jit(solution)/shard_map/all_to_all | solution.py:129
  118.6 0.9 broadcast_in_dim.178
  119.5 7.5 %all-to-all-start.5 = ((f32[4,336,128]{2,1,0:T(8,128)}), f32[4,336,128]{2,1,0:T(8,128)S(1)}, u32[]{:S(2)}, u32[]{:S(2)}) async-start(f32[4,336,128]{2,1,0:T(8,128)} %broadcast_in_dim.178), calls=%async_computation.5 | async-start | bytes 1376256 | tf_op jit(solution)/shard_map/all_to_all | solution.py:47
  127.1 3.2 %fusion.61 = f32[256,384]{1,0:T(8,128)} fusion(bf16[256,3072]{0,1:T(8,128)(2,1)} %bitcast.96, bf16[3072,384]{1,0:T(8,128)(2,1)S(1)} %copy-done), kind=kOutput, calls=%fused_computation.122 | convolution fusion | flops 603979776 | bytes 4325376 | tf_op jit(solution)/shard_map/dot_general | solution.py:163
  130.3 0.7 constant_dynamic-slice_fusion.1
  131.0 6.0 %all-to-all-done.5 = f32[4,336,128]{2,1,0:T(8,128)S(1)} async-done(((f32[4,336,128]{2,1,0:T(8,128)}), f32[4,336,128]{2,1,0:T(8,128)S(1)}, u32[]{:S(2)}, u32[]{:S(2)}) %all-to-all-start.5) | async-done | bytes 688160 | tf_op jit(solution)/shard_map/all_to_all | solution.py:47
  137.1 1.2 fusion.2
  138.4 0.9 copy.50
  139.3 1.8 %fusion.56 = (f32[1,256,3,64]{1,3,2,0:T(8,128)}, f32[1,256,3,64]{1,3,2,0:T(8,128)}) fusion(f32[1,256,3,128]{1,3,2,0:T(8,128)} %bitcast.98), kind=kLoop, calls=%fused_computation.117 | loop fusion | bytes 786432 | tf_op jit(solution)/shard_map/slice | solution.py:26
  141.1 1.1 copy.61
  142.2 1.8 %copy.60 = f32[1,256,3,64]{3,1,2,0:T(8,128)} copy(f32[1,256,3,64]{1,3,2,0:T(8,128)} %get-tuple-element.8) | data formatting | bytes 393216
  144.3 0.6 fusion.33
  145.9 1.4 fusion.4
  147.3 0.8 copy.55
  (55 shorter events, 2.6 us)
Async XLA Ops:
  0.0 127.1 %copy-start = (bf16[3072,384]{1,0:T(8,128)(2,1)S(1)}, bf16[3072,384]{1,0:T(8,128)(2,1)}, u32[]{:S(2)}) copy-start(bf16[3072,384]{1,0:T(8,128)(2,1)} %param.10) | copy-start | bytes 7077892
  3.3 35.4 %all-to-all-start = ((s32[128,1,1]{2,1,0:T(1,128)}), s32[128,1,1]{2,1,0:T(1,128)S(1)}, u32[]{:S(2)}, u32[]{:S(2)}) async-start(s32[128,1,1]{2,1,0:T(1,128)} %broadcast_in_dim.106), calls=%async_computation | async-start | bytes 131072 | tf_op jit(solution)/shard_map/all_to_all | solution.py:47
  39.6 13.4 %all-to-all-start.1 = ((bf16[8,256,128]{2,1,0:T(8,128)(2,1)}), bf16[8,256,128]{2,1,0:T(8,128)(2,1)S(1)}, u32[]{:S(2)}, u32[]{:S(2)}) async-start(bf16[8,256,128]{2,1,0:T(8,128)(2,1)} %broadcast_in_dim.168), calls=%async_computation.1 | async-start | bytes 1048576 | tf_op jit(solution)/shard_map/all_to_all | solution.py:47
  46.7 10.9 %copy-start.1 = (bf16[256,768]{1,0:T(8,128)(2,1)S(1)}, bf16[256,768]{1,0:T(8,128)(2,1)}, u32[]{:S(2)}) copy-start(bf16[256,768]{1,0:T(8,128)(2,1)} %param.9) | copy-start | bytes 1179652
  54.1 17.5 %all-to-all-start.2 = ((bf16[4,2,256,128]{3,2,1,0:T(8,128)(2,1)}), bf16[4,2,256,128]{3,2,1,0:T(8,128)(2,1)S(1)}, u32[]{:S(2)}, u32[]{:S(2)}) async-start(bf16[4,2,256,128]{3,2,1,0:T(8,128)(2,1)} %broadcast_in_dim.171), calls=%async_computation.2 | async-start | bytes 1048576 | tf_op jit(solution)/shard_map/all_to_all | solution.py:47
  57.6 23.7 %collective-permute-start.2 = (bf16[256,768]{1,0:T(8,128)(2,1)S(1)}, bf16[256,768]{1,0:T(8,128)(2,1)}, u32[]{:S(2)}, u32[]{:S(2)}) collective-permute-start(bf16[256,768]{1,0:T(8,128)(2,1)S(1)} %copy-done.1), channel_id=1, source_target_pairs={{0,3},{1,0},{2,1},{3,2},{4,7},{5,4},{6,5},{7,6},{8,11},{9,8},{10,9... | collective-permute-start | bytes 1179656 | tf_op jit(solution)/shard_map/ppermute | solution.py:42
  62.0 19.3 %collective-permute-start.1 = (bf16[256,768]{1,0:T(8,128)(2,1)S(1)}, bf16[256,768]{1,0:T(8,128)(2,1)}, u32[]{:S(2)}, u32[]{:S(2)}) collective-permute-start(bf16[256,768]{1,0:T(8,128)(2,1)S(1)} %copy-done.1), channel_id=1, source_target_pairs={{0,2},{1,3},{2,0},{3,1},{4,6},{5,7},{6,4},{7,5},{8,10},{9,11},{10,... | collective-permute-start | bytes 1179656 | tf_op jit(solution)/shard_map/ppermute | solution.py:42
  64.4 20.5 %collective-permute-start = (bf16[256,768]{1,0:T(8,128)(2,1)S(1)}, bf16[256,768]{1,0:T(8,128)(2,1)}, u32[]{:S(2)}, u32[]{:S(2)}) collective-permute-start(bf16[256,768]{1,0:T(8,128)(2,1)S(1)} %copy-done.1), channel_id=1, source_target_pairs={{0,1},{1,2},{2,3},{3,0},{4,5},{5,6},{6,7},{7,4},{8,9},{9,10},{10,1... | collective-permute-start | bytes 1179656 | tf_op jit(solution)/shard_map/ppermute | solution.py:42
  72.6 31.2 %all-to-all-start.3 = ((bf16[4,2,256,128]{3,2,1,0:T(8,128)(2,1)}), bf16[4,2,256,128]{3,2,1,0:T(8,128)(2,1)S(1)}, u32[]{:S(2)}, u32[]{:S(2)}) async-start(bf16[4,2,256,128]{3,2,1,0:T(8,128)(2,1)} %broadcast_in_dim.172), calls=%async_computation.3 | async-start | bytes 1048576 | tf_op jit(solution)/shard_map/all_to_all | solution.py:47
  104.8 13.4 %all-to-all-start.4 = ((bf16[8,256,128]{2,1,0:T(8,128)(2,1)}), bf16[8,256,128]{2,1,0:T(8,128)(2,1)S(1)}, u32[]{:S(2)}, u32[]{:S(2)}) async-start(bf16[8,256,128]{2,1,0:T(8,128)(2,1)} %select_select_fusion), calls=%async_computation.4 | async-start | bytes 1048576 | tf_op jit(solution)/shard_map/all_to_all | solution.py:129
  118.2 1.3 copy-start.4
  119.5 17.6 %all-to-all-start.5 = ((f32[4,336,128]{2,1,0:T(8,128)}), f32[4,336,128]{2,1,0:T(8,128)S(1)}, u32[]{:S(2)}, u32[]{:S(2)}) async-start(f32[4,336,128]{2,1,0:T(8,128)} %broadcast_in_dim.178), calls=%async_computation.5 | async-start | bytes 1376256 | tf_op jit(solution)/shard_map/all_to_all | solution.py:47
  144.1 1.1 copy-start.2
  144.1 1.2 copy-start.5
  144.1 1.3 copy-start.6
  144.1 0.8 copy-start.3

commit v11 on v10

--- a/solution.py
+++ b/solution.py
@@ -89,7 +89,9 @@
 
     own_slot = lookup_slots(adapter_ids, adapter_slot)
 
-    slots_all = gather_over(own_slot, ("zh", "zl", "ry"), n_req).reshape(n_req)
+    column_slots = gather_over(own_slot, "zl", n_low)
+    column_slots = gather_over(column_slots, "zh", nz // n_low).reshape(nz)
+    slots_all = gather_over(column_slots, "ry", ny).T.reshape(n_req)
 
     down_rows = down_store[0].T.reshape(-1, 128)
     query_rows = query_up_store[0].reshape(-1, 128)

time: 149 us -> 161 us (1.081)
  waiting for transfers between devices: 45.1 us -> 52.6 us
  starting transfers between devices: 52.1 us -> 54.3 us
  local copies, waits for them, and re-layouts: 23 us -> 25 us
    all_to_all x5 -> x7, waiting for transfers between devices: 39.5 us -> 47.1 us  [gather_over(): return lax.all_to_all(copies, axis, 0, 0, tiled=True)]
    all_to_all x5 -> x7, starting transfers between devices: 38.9 us -> 41.1 us  [gather_over(): return lax.all_to_all(copies, axis, 0, 0, tiled=True)]
    broadcast_in_dim x5 -> x8, local copies, waits for them, and re-layouts: 4.69 us -> 6 us  [gather_over(): copies = jnp.broadcast_to(x[None], (n,) + x.shape)]
  transfers between devices with their start and end apart: 9 -> 11, of which waited for: 7 -> 9; matrix products, arithmetic and copies ran while one was open for 19% -> 16% of each run, Pallas kernels for 0% -> 0%
where the time goes in v11:
time: 161 us; the launch traced here: 159 us
  starting transfers between devices  54.3 us (34%)
  waiting for transfers between devices  52.6 us (33%)
  local copies, waits for them, and re-layouts  25 us (16%)
  other arithmetic  12.2 us (8%)
  matrix products  8.81 us (5%)
  between operations  5.78 us (4%)
    all_to_all x7, waiting for transfers between devices, gather_over(): return lax.all_to_all(copies, axis, 0, 0, tiled=True)  47.1 us
    all_to_all x7, starting transfers between devices, gather_over(): return lax.all_to_all(copies, axis, 0, 0, tiled=True)  41.1 us
    ppermute x3, starting transfers between devices, shifted(): return lax.ppermute(x, axis, pairs)  9.33 us
    broadcast_in_dim x8, local copies, waits for them, and re-layouts, gather_over(): copies = jnp.broadcast_to(x[None], (n,) + x.shape)  6 us
    all_to_all x1, starting transfers between devices, local(): received = lax.all_to_all(send, 'ry', 0, 0, tiled=True)  3.89 us
    ppermute x3, waiting for transfers between devices, shifted(): return lax.ppermute(x, axis, pairs)  3.68 us
    unnamed x16, local copies, waits for them, and re-layouts  3.35 us
  transfers between devices with their start and end apart: 11, of which 9 were waited for; matrix products, arithmetic and copies ran while one was open for 16% of the time, Pallas kernels for 0%

profile of v11, /device:TPU:1, one launch (start us, length us, event | category | flops | bytes accessed | tf_op | source)
XLA Modules:
  0.0 158.7 jit_solution(11681561679613581800)
XLA Ops:
  0.8 1.4 fusion.46
  2.2 1.2 broadcast_in_dim.114
  3.4 6.4 %all-to-all-start = ((s32[4,1,1]{2,1,0:T(1,128)}), s32[4,1,1]{2,1,0:T(1,128)S(1)}, u32[]{:S(2)}, u32[]{:S(2)}) async-start(s32[4,1,1]{2,1,0:T(1,128)} %broadcast_in_dim.114), calls=%async_computation | async-start | bytes 4096 | tf_op jit(solution)/shard_map/all_to_all | solution.py:47
  9.9 0.7 reshape_squeeze.3
  10.6 0.9 reshape.473
  11.5 0.7 pad_maximum_fusion.2
  12.2 2.0 %all-to-all-done = s32[4,1,1]{2,1,0:T(1,128)S(1)} async-done(((s32[4,1,1]{2,1,0:T(1,128)}), s32[4,1,1]{2,1,0:T(1,128)S(1)}, u32[]{:S(2)}, u32[]{:S(2)}) %all-to-all-start) | async-done | bytes 48 | tf_op jit(solution)/shard_map/all_to_all | solution.py:47
  14.9 12.4 %all-to-all-start.1 = ((s32[4,4,1]{1,2,0:T(1,128)}), s32[4,4,1]{1,2,0:T(1,128)S(1)}, u32[]{:S(2)}, u32[]{:S(2)}) async-start(s32[4,4,1]{1,2,0:T(1,128)} %broadcast_in_dim.116), calls=%async_computation.1 | async-start | bytes 4096 | tf_op jit(solution)/shard_map/all_to_all | solution.py:47
  27.3 11.2 %all-to-all-done.1 = s32[4,4,1]{1,2,0:T(1,128)S(1)} async-done(((s32[4,4,1]{1,2,0:T(1,128)}), s32[4,4,1]{1,2,0:T(1,128)S(1)}, u32[]{:S(2)}, u32[]{:S(2)}) %all-to-all-start.1) | async-done | bytes 96 | tf_op jit(solution)/shard_map/all_to_all | solution.py:47
  39.1 0.7 reduce.11
  40.4 7.7 %all-to-all-start.2 = ((s32[8,1,16]{2,1,0:T(1,128)}), s32[8,1,16]{2,1,0:T(1,128)S(1)}, u32[]{:S(2)}, u32[]{:S(2)}) async-start(s32[8,1,16]{2,1,0:T(1,128)} %broadcast_in_dim.118), calls=%async_computation.2 | async-start | bytes 8192 | tf_op jit(solution)/shard_map/all_to_all | solution.py:47
  48.2 4.5 %all-to-all-done.2 = s32[8,1,16]{2,1,0:T(1,128)S(1)} async-done(((s32[8,1,16]{2,1,0:T(1,128)}), s32[8,1,16]{2,1,0:T(1,128)S(1)}, u32[]{:S(2)}, u32[]{:S(2)}) %all-to-all-start.2) | async-done | bytes 544 | tf_op jit(solution)/shard_map/all_to_all | solution.py:47
  52.6 0.9 broadcast_in_dim.187
  53.5 4.1 %all-to-all-start.3 = ((bf16[8,256,128]{2,1,0:T(8,128)(2,1)}), bf16[8,256,128]{2,1,0:T(8,128)(2,1)S(1)}, u32[]{:S(2)}, u32[]{:S(2)}) async-start(bf16[8,256,128]{2,1,0:T(8,128)(2,1)} %broadcast_in_dim.187), calls=%async_computation.3 | async-start | bytes 1048576 | tf_op jit(solution)/shard_map/all_to_all | solution.py:47
  58.0 0.7 gather_fusion.2
  58.6 0.6 gather_fusion.3
  59.4 7.7 %all-to-all-done.3 = bf16[8,256,128]{2,1,0:T(8,128)(2,1)S(1)} async-done(((bf16[8,256,128]{2,1,0:T(8,128)(2,1)}), bf16[8,256,128]{2,1,0:T(8,128)(2,1)S(1)}, u32[]{:S(2)}, u32[]{:S(2)}) %all-to-all-start.3) | async-done | bytes 524320 | tf_op jit(solution)/shard_map/all_to_all | solution.py:47
  67.4 0.9 broadcast_in_dim.190
  68.2 3.5 %all-to-all-start.4 = ((bf16[4,2,256,128]{3,2,1,0:T(8,128)(2,1)}), bf16[4,2,256,128]{3,2,1,0:T(8,128)(2,1)S(1)}, u32[]{:S(2)}, u32[]{:S(2)}) async-start(bf16[4,2,256,128]{3,2,1,0:T(8,128)(2,1)} %broadcast_in_dim.190), calls=%async_computation.4 | async-start | bytes 1048576 | tf_op jit(solution)/shard_map/all_to_all | solution.py:47
  71.7 4.4 %collective-permute-start.2 = (bf16[256,768]{1,0:T(8,128)(2,1)S(1)}, bf16[256,768]{1,0:T(8,128)(2,1)}, u32[]{:S(2)}, u32[]{:S(2)}) collective-permute-start(bf16[256,768]{1,0:T(8,128)(2,1)S(1)} %copy-done.1), channel_id=1, source_target_pairs={{0,3},{1,0},{2,1},{3,2},{4,7},{5,4},{6,5},{7,6},{8,11},{9,8},{10,9... | collective-permute-start | bytes 1179656 | tf_op jit(solution)/shard_map/ppermute | solution.py:42
  76.1 2.4 %collective-permute-start.1 = (bf16[256,768]{1,0:T(8,128)(2,1)S(1)}, bf16[256,768]{1,0:T(8,128)(2,1)}, u32[]{:S(2)}, u32[]{:S(2)}) collective-permute-start(bf16[256,768]{1,0:T(8,128)(2,1)S(1)} %copy-done.1), channel_id=1, source_target_pairs={{0,2},{1,3},{2,0},{3,1},{4,6},{5,7},{6,4},{7,5},{8,10},{9,11},{10,... | collective-permute-start | bytes 1179656 | tf_op jit(solution)/shard_map/ppermute | solution.py:42
  78.6 2.5 %collective-permute-start = (bf16[256,768]{1,0:T(8,128)(2,1)S(1)}, bf16[256,768]{1,0:T(8,128)(2,1)}, u32[]{:S(2)}, u32[]{:S(2)}) collective-permute-start(bf16[256,768]{1,0:T(8,128)(2,1)S(1)} %copy-done.1), channel_id=1, source_target_pairs={{0,1},{1,2},{2,3},{3,0},{4,5},{5,6},{6,7},{7,4},{8,9},{9,10},{10,1... | collective-permute-start | bytes 1179656 | tf_op jit(solution)/shard_map/ppermute | solution.py:42
  83.8 2.0 %all-to-all-done.4 = bf16[4,2,256,128]{3,2,1,0:T(8,128)(2,1)S(1)} async-done(((bf16[4,2,256,128]{3,2,1,0:T(8,128)(2,1)}), bf16[4,2,256,128]{3,2,1,0:T(8,128)(2,1)S(1)}, u32[]{:S(2)}, u32[]{:S(2)}) %all-to-all-start.4) | async-done | bytes 524320 | tf_op jit(solution)/shard_map/all_to_all | solution.py:47
  85.9 0.9 broadcast_in_dim.191
  86.7 3.5 %all-to-all-start.5 = ((bf16[4,2,256,128]{3,2,1,0:T(8,128)(2,1)}), bf16[4,2,256,128]{3,2,1,0:T(8,128)(2,1)S(1)}, u32[]{:S(2)}, u32[]{:S(2)}) async-start(bf16[4,2,256,128]{3,2,1,0:T(8,128)(2,1)} %broadcast_in_dim.191), calls=%async_computation.5 | async-start | bytes 1048576 | tf_op jit(solution)/shard_map/all_to_all | solution.py:47
  90.3 1.2 multiply_cosine_fusion
  95.4 3.7 %collective-permute-done = bf16[256,768]{1,0:T(8,128)(2,1)} collective-permute-done((bf16[256,768]{1,0:T(8,128)(2,1)S(1)}, bf16[256,768]{1,0:T(8,128)(2,1)}, u32[]{:S(2)}, u32[]{:S(2)}) %collective-permute-start) | collective-permute-done | bytes 393248 | tf_op jit(solution)/shard_map/ppermute | solution.py:42
  99.1 2.6 %pad_maximum_fusion = bf16[4,256,768]{2,1,0:T(8,128)(2,1)} fusion(bf16[1,256,768]{2,1,0:T(8,128)(2,1)} %bitcast.17, bf16[1,256,768]{2,1,0:T(8,128)(2,1)} %bitcast.16, bf16[1,256,768]{2,1,0:T(8,128)(2,1)} %bitcast.15, bf16[1,256,768]{2,1,0:T(8,128)(2,1)S(1)} %bitcast.101), kind=kLoop, calls=%fused_computation.5 | loop fusion | flops 2359296 | bytes 3145728 | tf_op jit(solution)/shard_map/stack | solution.py:104
  101.7 3.2 %gather_fusion.4 = bf16[4,256,768]{2,1,0:T(8,128)(2,1)} fusion(bf16[4,256,768]{2,1,0:T(8,128)(2,1)} %pad_maximum_fusion, s32[1024]{0:T(1024)S(1)} %pad_clamp_fusion), kind=kCustom, calls=%fused_computation.4 | custom fusion | bytes 3145744 | tf_op jit(solution)/shard_map/jit(_take)/gather | solution.py:106
  104.9 13.4 %all-to-all-done.5 = bf16[4,2,256,128]{3,2,1,0:T(8,128)(2,1)S(1)} async-done(((bf16[4,2,256,128]{3,2,1,0:T(8,128)(2,1)}), bf16[4,2,256,128]{3,2,1,0:T(8,128)(2,1)S(1)}, u32[]{:S(2)}, u32[]{:S(2)}) %all-to-all-start.5) | async-done | bytes 524320 | tf_op jit(solution)/shard_map/all_to_all | solution.py:47
  118.4 0.9 select_select_fusion
  119.3 3.9 %all-to-all-start.6 = ((bf16[8,256,128]{2,1,0:T(8,128)(2,1)}), bf16[8,256,128]{2,1,0:T(8,128)(2,1)S(1)}, u32[]{:S(2)}, u32[]{:S(2)}) async-start(bf16[8,256,128]{2,1,0:T(8,128)(2,1)} %select_select_fusion), calls=%async_computation.6 | async-start | bytes 1048576 | tf_op jit(solution)/shard_map/all_to_all | solution.py:131
  123.2 2.8 %select_bitcast_fusion = bf16[256,4,768]{2,0,1:T(8,128)(2,1)} fusion(bf16[4,256,768]{2,1,0:T(8,128)(2,1)} %gather_fusion.4, pred[4]{0:T(512)(128)(4,1)S(1)} %compare_and_fusion), kind=kLoop, calls=%fused_computation.6 | loop fusion | flops 786432 | bytes 3145732 | tf_op jit(solution)/shard_map/jit(_take)/select_n | solution.py:106
  126.0 2.6 %copy.54 = bf16[256,4,768]{0,2,1:T(8,128)(2,1)} copy(bf16[256,4,768]{2,0,1:T(8,128)(2,1)} %select_bitcast_fusion) | data formatting | bytes 3145728 | tf_op jit(solution)/shard_map/jit(_take)/select_n | solution.py:106
  128.6 2.2 %fusion.60 = f32[256,128]{1,0:T(8,128)S(1)} fusion(bf16[256,3072]{0,1:T(8,128)(2,1)} %bitcast.99, bf16[3072,128]{1,0:T(8,128)(2,1)} %param.11), kind=kOutput, calls=%fused_computation.121 | convolution fusion | flops 201326592 | bytes 2490368 | tf_op jit(solution)/shard_map/dot_general | solution.py:140
  130.8 1.9 %all-to-all-done.6 = bf16[8,256,128]{2,1,0:T(8,128)(2,1)S(1)} async-done(((bf16[8,256,128]{2,1,0:T(8,128)(2,1)}), bf16[8,256,128]{2,1,0:T(8,128)(2,1)S(1)}, u32[]{:S(2)}, u32[]{:S(2)}) %all-to-all-start.6) | async-done | bytes 524320 | tf_op jit(solution)/shard_map/all_to_all | solution.py:131
  133.1 0.9 broadcast_in_dim.197
  134.0 3.5 %all-to-all-start.7 = ((f32[4,336,128]{2,1,0:T(8,128)}), f32[4,336,128]{2,1,0:T(8,128)S(1)}, u32[]{:S(2)}, u32[]{:S(2)}) async-start(f32[4,336,128]{2,1,0:T(8,128)} %broadcast_in_dim.197), calls=%async_computation.7 | async-start | bytes 1376256 | tf_op jit(solution)/shard_map/all_to_all | solution.py:47
  137.6 3.2 %fusion.61 = f32[256,384]{1,0:T(8,128)} fusion(bf16[256,3072]{0,1:T(8,128)(2,1)} %bitcast.100, bf16[3072,384]{1,0:T(8,128)(2,1)S(1)} %copy-done), kind=kOutput, calls=%fused_computation.122 | convolution fusion | flops 603979776 | bytes 4325376 | tf_op jit(solution)/shard_map/dot_general | solution.py:165
  140.8 0.7 constant_dynamic-slice_fusion.1
  141.6 6.1 %all-to-all-done.7 = f32[4,336,128]{2,1,0:T(8,128)S(1)} async-done(((f32[4,336,128]{2,1,0:T(8,128)}), f32[4,336,128]{2,1,0:T(8,128)S(1)}, u32[]{:S(2)}, u32[]{:S(2)}) %all-to-all-start.7) | async-done | bytes 688160 | tf_op jit(solution)/shard_map/all_to_all | solution.py:47
  147.7 1.2 fusion.2
  149.0 0.9 copy.56
  149.9 1.8 %fusion.56 = (f32[1,256,3,64]{1,3,2,0:T(8,128)}, f32[1,256,3,64]{1,3,2,0:T(8,128)}) fusion(f32[1,256,3,128]{1,3,2,0:T(8,128)} %bitcast.102), kind=kLoop, calls=%fused_computation.117 | loop fusion | bytes 786432 | tf_op jit(solution)/shard_map/slice | solution.py:26
  151.7 1.1 copy.67
  152.8 1.8 %copy.66 = f32[1,256,3,64]{3,1,2,0:T(8,128)} copy(f32[1,256,3,64]{1,3,2,0:T(8,128)} %get-tuple-element.8) | data formatting | bytes 393216
  156.5 1.4 fusion.4
  157.9 0.8 copy.61
  (66 shorter events, 7.2 us)
Async XLA Ops:
  0.0 137.6 %copy-start = (bf16[3072,384]{1,0:T(8,128)(2,1)S(1)}, bf16[3072,384]{1,0:T(8,128)(2,1)}, u32[]{:S(2)}) copy-start(bf16[3072,384]{1,0:T(8,128)(2,1)} %param.10) | copy-start | bytes 7077892
  3.4 10.8 %all-to-all-start = ((s32[4,1,1]{2,1,0:T(1,128)}), s32[4,1,1]{2,1,0:T(1,128)S(1)}, u32[]{:S(2)}, u32[]{:S(2)}) async-start(s32[4,1,1]{2,1,0:T(1,128)} %broadcast_in_dim.114), calls=%async_computation | async-start | bytes 4096 | tf_op jit(solution)/shard_map/all_to_all | solution.py:47
  14.9 23.6 %all-to-all-start.1 = ((s32[4,4,1]{1,2,0:T(1,128)}), s32[4,4,1]{1,2,0:T(1,128)S(1)}, u32[]{:S(2)}, u32[]{:S(2)}) async-start(s32[4,4,1]{1,2,0:T(1,128)} %broadcast_in_dim.116), calls=%async_computation.1 | async-start | bytes 4096 | tf_op jit(solution)/shard_map/all_to_all | solution.py:47
  40.4 12.2 %all-to-all-start.2 = ((s32[8,1,16]{2,1,0:T(1,128)}), s32[8,1,16]{2,1,0:T(1,128)S(1)}, u32[]{:S(2)}, u32[]{:S(2)}) async-start(s32[8,1,16]{2,1,0:T(1,128)} %broadcast_in_dim.118), calls=%async_computation.2 | async-start | bytes 8192 | tf_op jit(solution)/shard_map/all_to_all | solution.py:47
  53.5 13.6 %all-to-all-start.3 = ((bf16[8,256,128]{2,1,0:T(8,128)(2,1)}), bf16[8,256,128]{2,1,0:T(8,128)(2,1)S(1)}, u32[]{:S(2)}, u32[]{:S(2)}) async-start(bf16[8,256,128]{2,1,0:T(8,128)(2,1)} %broadcast_in_dim.187), calls=%async_computation.3 | async-start | bytes 1048576 | tf_op jit(solution)/shard_map/all_to_all | solution.py:47
  58.6 13.1 %copy-start.1 = (bf16[256,768]{1,0:T(8,128)(2,1)S(1)}, bf16[256,768]{1,0:T(8,128)(2,1)}, u32[]{:S(2)}) copy-start(bf16[256,768]{1,0:T(8,128)(2,1)} %param.9) | copy-start | bytes 1179652
  68.2 17.5 %all-to-all-start.4 = ((bf16[4,2,256,128]{3,2,1,0:T(8,128)(2,1)}), bf16[4,2,256,128]{3,2,1,0:T(8,128)(2,1)S(1)}, u32[]{:S(2)}, u32[]{:S(2)}) async-start(bf16[4,2,256,128]{3,2,1,0:T(8,128)(2,1)} %broadcast_in_dim.190), calls=%async_computation.4 | async-start | bytes 1048576 | tf_op jit(solution)/shard_map/all_to_all | solution.py:47
  71.7 23.7 %collective-permute-start.2 = (bf16[256,768]{1,0:T(8,128)(2,1)S(1)}, bf16[256,768]{1,0:T(8,128)(2,1)}, u32[]{:S(2)}, u32[]{:S(2)}) collective-permute-start(bf16[256,768]{1,0:T(8,128)(2,1)S(1)} %copy-done.1), channel_id=1, source_target_pairs={{0,3},{1,0},{2,1},{3,2},{4,7},{5,4},{6,5},{7,6},{8,11},{9,8},{10,9... | collective-permute-start | bytes 1179656 | tf_op jit(solution)/shard_map/ppermute | solution.py:42
  76.1 19.3 %collective-permute-start.1 = (bf16[256,768]{1,0:T(8,128)(2,1)S(1)}, bf16[256,768]{1,0:T(8,128)(2,1)}, u32[]{:S(2)}, u32[]{:S(2)}) collective-permute-start(bf16[256,768]{1,0:T(8,128)(2,1)S(1)} %copy-done.1), channel_id=1, source_target_pairs={{0,2},{1,3},{2,0},{3,1},{4,6},{5,7},{6,4},{7,5},{8,10},{9,11},{10,... | collective-permute-start | bytes 1179656 | tf_op jit(solution)/shard_map/ppermute | solution.py:42
  78.6 20.5 %collective-permute-start = (bf16[256,768]{1,0:T(8,128)(2,1)S(1)}, bf16[256,768]{1,0:T(8,128)(2,1)}, u32[]{:S(2)}, u32[]{:S(2)}) collective-permute-start(bf16[256,768]{1,0:T(8,128)(2,1)S(1)} %copy-done.1), channel_id=1, source_target_pairs={{0,1},{1,2},{2,3},{3,0},{4,5},{5,6},{6,7},{7,4},{8,9},{9,10},{10,1... | collective-permute-start | bytes 1179656 | tf_op jit(solution)/shard_map/ppermute | solution.py:42
  86.7 31.6 %all-to-all-start.5 = ((bf16[4,2,256,128]{3,2,1,0:T(8,128)(2,1)}), bf16[4,2,256,128]{3,2,1,0:T(8,128)(2,1)S(1)}, u32[]{:S(2)}, u32[]{:S(2)}) async-start(bf16[4,2,256,128]{3,2,1,0:T(8,128)(2,1)} %broadcast_in_dim.191), calls=%async_computation.5 | async-start | bytes 1048576 | tf_op jit(solution)/shard_map/all_to_all | solution.py:47
  119.3 13.4 %all-to-all-start.6 = ((bf16[8,256,128]{2,1,0:T(8,128)(2,1)}), bf16[8,256,128]{2,1,0:T(8,128)(2,1)S(1)}, u32[]{:S(2)}, u32[]{:S(2)}) async-start(bf16[8,256,128]{2,1,0:T(8,128)(2,1)} %select_select_fusion), calls=%async_computation.6 | async-start | bytes 1048576 | tf_op jit(solution)/shard_map/all_to_all | solution.py:131
  132.7 1.3 copy-start.4
  134.0 13.7 %all-to-all-start.7 = ((f32[4,336,128]{2,1,0:T(8,128)}), f32[4,336,128]{2,1,0:T(8,128)S(1)}, u32[]{:S(2)}, u32[]{:S(2)}) async-start(f32[4,336,128]{2,1,0:T(8,128)} %broadcast_in_dim.197), calls=%async_computation.7 | async-start | bytes 1376256 | tf_op jit(solution)/shard_map/all_to_all | solution.py:47
  154.6 1.1 copy-start.2
  154.6 1.2 copy-start.5
  154.6 1.3 copy-start.6
  154.7 0.8 copy-start.3

commit v12 on v10

--- a/solution.py
+++ b/solution.py
@@ -98,11 +98,11 @@
     n_row = n_down + n_query + pair_rows.shape[0]
     row = jnp.concatenate([down_rows, query_rows, pair_rows], axis=0)
 
-    plane = gather_over(row, "ry", ny)
+    plane = jnp.stack([row] + [shifted(row, s, ny, axis="ry") for s in range(1, ny)])
     blocks = jnp.stack([states] + [shifted(states, s, n_tp) for s in range(1, n_tp)])
     source = (tp_index - jnp.arange(n_tp, dtype=jnp.int32)) % n_tp
     piece = jnp.take(blocks, source, axis=0)
-    plane_req = iz * ny + jnp.arange(ny, dtype=jnp.int32)
+    plane_req = iz * ny + (iy - jnp.arange(ny, dtype=jnp.int32)) % ny
 
     slot_range = jnp.arange(n_req * store_rows, dtype=jnp.int32)
     used = jnp.any(slots_all[:, None] == slot_range[None, :], axis=0).astype(jnp.int32)
@@ -121,7 +121,7 @@
     for axis in ("zl", "zh"):
         copies = gather_over(column, axis, lax.axis_size(axis))
         column = jnp.sum(copies, axis=0)
-    dest_k = prefix[slots_all[plane_req]]
+    dest_k = prefix[slots_all[iz * ny + jnp.arange(ny, dtype=jnp.int32)]]
     held = column[0]
     for m in range(1, per_column):
         held = jnp.where((dest_k // ny == m)[:, None, None], column[m], held)

time: 149 us -> 165 us (1.11)
  starting transfers between devices: 52.1 us -> 65.7 us
  waiting for transfers between devices: 45.1 us -> 40.8 us
  local copies, waits for them, and re-layouts: 23 us -> 26.8 us
  other arithmetic: 13.7 us -> 16 us
    ppermute x3 -> x10, starting transfers between devices: 9.33 us -> 34.2 us  [shifted(): return lax.ppermute(x, axis, pairs)]
    all_to_all x5 -> x4, starting transfers between devices: 38.9 us -> 27.6 us  [gather_over(): return lax.all_to_all(copies, axis, 0, 0, tiled=True)]
    unnamed x16 -> x22, local copies, waits for them, and re-layouts: 3.35 us -> 7.11 us
    all_to_all x5 -> x4, waiting for transfers between devices: 39.5 us -> 35.8 us  [gather_over(): return lax.all_to_all(copies, axis, 0, 0, tiled=True)]
    broadcast_in_dim x5 -> x4, local copies, waits for them, and re-layouts: 4.69 us -> 3.95 us  [gather_over(): copies = jnp.broadcast_to(x[None], (n,) + x.shape)]
    ppermute x3 -> x10, waiting for transfers between devices: 3.68 us -> 3.03 us  [shifted(): return lax.ppermute(x, axis, pairs)]
  transfers between devices with their start and end apart: 9 -> 15, of which waited for: 7 -> 6; matrix products, arithmetic and copies ran while one was open for 19% -> 20% of each run, Pallas kernels for 0% -> 0%
where the time goes in v12:
time: 165 us; the launch traced here: 164 us
  starting transfers between devices  65.7 us (40%)
  waiting for transfers between devices  40.8 us (25%)
  local copies, waits for them, and re-layouts  26.8 us (16%)
  other arithmetic  16 us (10%)
  matrix products  8.8 us (5%)
  between operations  5.57 us (3%)
    all_to_all x4, waiting for transfers between devices, gather_over(): return lax.all_to_all(copies, axis, 0, 0, tiled=True)  35.8 us
    ppermute x10, starting transfers between devices, shifted(): return lax.ppermute(x, axis, pairs)  34.2 us
    all_to_all x4, starting transfers between devices, gather_over(): return lax.all_to_all(copies, axis, 0, 0, tiled=True)  27.6 us
    unnamed x22, local copies, waits for them, and re-layouts  7.11 us
    broadcast_in_dim x4, local copies, waits for them, and re-layouts, gather_over(): copies = jnp.broadcast_to(x[None], (n,) + x.shape)  3.95 us
    all_to_all x1, starting transfers between devices, local(): received = lax.all_to_all(send, 'ry', 0, 0, tiled=True)  3.89 us
  transfers between devices with their start and end apart: 15, of which 6 were waited for; matrix products, arithmetic and copies ran while one was open for 20% of the time, Pallas kernels for 0%

profile of v12, /device:TPU:1, one launch (start us, length us, event | category | flops | bytes accessed | tf_op | source)
XLA Modules:
  0.0 163.7 jit_solution(4164308395282189359)
XLA Ops:
  0.0 0.9 reshape_squeeze.3
  0.9 0.9 reshape.513
  1.7 0.7 pad_maximum_fusion.2
  2.4 2.7 %collective-permute-start = (bf16[256,128]{1,0:T(8,128)(2,1)S(1)}, bf16[256,128]{1,0:T(8,128)(2,1)S(1)}, u32[]{:S(2)}, u32[]{:S(2)}) collective-permute-start(bf16[256,128]{1,0:T(8,128)(2,1)S(1)} %pad_maximum_fusion.2), channel_id=1, source_target_pairs={{0,4},{4,8},{8,12},{12,16},{16,20},{20,24},{24,28},{28,0},{1,5},{5... | collective-permute-start | bytes 196616 | tf_op jit(solution)/shard_map/ppermute | solution.py:42
  5.1 3.2 %collective-permute-start.1 = (bf16[256,128]{1,0:T(8,128)(2,1)S(1)}, bf16[256,128]{1,0:T(8,128)(2,1)S(1)}, u32[]{:S(2)}, u32[]{:S(2)}) collective-permute-start(bf16[256,128]{1,0:T(8,128)(2,1)S(1)} %pad_maximum_fusion.2), channel_id=1, source_target_pairs={{0,8},{4,12},{8,16},{12,20},{16,24},{20,28},{24,0},{28,4},{1,9},{5... | collective-permute-start | bytes 196616 | tf_op jit(solution)/shard_map/ppermute | solution.py:42
  8.3 3.5 %collective-permute-start.2 = (bf16[256,128]{1,0:T(8,128)(2,1)S(1)}, bf16[256,128]{1,0:T(8,128)(2,1)S(1)}, u32[]{:S(2)}, u32[]{:S(2)}) collective-permute-start(bf16[256,128]{1,0:T(8,128)(2,1)S(1)} %pad_maximum_fusion.2), channel_id=1, source_target_pairs={{0,12},{4,16},{8,20},{12,24},{16,28},{20,0},{24,4},{28,8},{1,13},{... | collective-permute-start | bytes 196616 | tf_op jit(solution)/shard_map/ppermute | solution.py:42
  11.8 7.0 %collective-permute-start.3 = (bf16[256,128]{1,0:T(8,128)(2,1)S(1)}, bf16[256,128]{1,0:T(8,128)(2,1)S(1)}, u32[]{:S(2)}, u32[]{:S(2)}) collective-permute-start(bf16[256,128]{1,0:T(8,128)(2,1)S(1)} %pad_maximum_fusion.2), channel_id=1, source_target_pairs={{0,16},{4,20},{8,24},{12,28},{16,0},{20,4},{24,8},{28,12},{1,17},{... | collective-permute-start | bytes 196616 | tf_op jit(solution)/shard_map/ppermute | solution.py:42
  18.8 4.5 %collective-permute-start.4 = (bf16[256,128]{1,0:T(8,128)(2,1)S(1)}, bf16[256,128]{1,0:T(8,128)(2,1)S(1)}, u32[]{:S(2)}, u32[]{:S(2)}) collective-permute-start(bf16[256,128]{1,0:T(8,128)(2,1)S(1)} %pad_maximum_fusion.2), channel_id=1, source_target_pairs={{0,20},{4,24},{8,28},{12,0},{16,4},{20,8},{24,12},{28,16},{1,21},{... | collective-permute-start | bytes 196616 | tf_op jit(solution)/shard_map/ppermute | solution.py:42
  24.0 1.3 fusion.46
  25.3 1.3 broadcast_in_dim.104
  26.6 12.9 %all-to-all-start = ((s32[128,1,1]{2,1,0:T(1,128)}), s32[128,1,1]{2,1,0:T(1,128)S(1)}, u32[]{:S(2)}, u32[]{:S(2)}) async-start(s32[128,1,1]{2,1,0:T(1,128)} %broadcast_in_dim.104), calls=%async_computation | async-start | bytes 131072 | tf_op jit(solution)/shard_map/all_to_all | solution.py:47
  39.5 1.3 bitcast_dynamic-update-slice_fusion.7
  40.9 13.5 %all-to-all-done = s32[128,1,1]{2,1,0:T(1,128)S(1)} async-done(((s32[128,1,1]{2,1,0:T(1,128)}), s32[128,1,1]{2,1,0:T(1,128)S(1)}, u32[]{:S(2)}, u32[]{:S(2)}) %all-to-all-start) | async-done | bytes 544 | tf_op jit(solution)/shard_map/all_to_all | solution.py:47
  54.4 2.3 %reduce.7 = s32[128]{0:T(128)S(1)} reduce(s32[128,1,1]{2,1,0:T(1,128)S(1)} %all-to-all-done, s32[]{:T(128)} %constant.102.clone.1), dimensions={1,2}, to_apply=%all_to_all.16.reduce_sub_computation | reduce | bytes 1028 | tf_op jit(solution)/shard_map/all_to_all | solution.py:47
  58.3 3.1 %collective-permute-start.5 = (bf16[256,128]{1,0:T(8,128)(2,1)S(1)}, bf16[256,128]{1,0:T(8,128)(2,1)S(1)}, u32[]{:S(2)}, u32[]{:S(2)}) collective-permute-start(bf16[256,128]{1,0:T(8,128)(2,1)S(1)} %pad_maximum_fusion.2), channel_id=1, source_target_pairs={{0,24},{4,28},{8,0},{12,4},{16,8},{20,12},{24,16},{28,20},{1,25},{... | collective-permute-start | bytes 196616 | tf_op jit(solution)/shard_map/ppermute | solution.py:42
  62.0 0.9 collective-permute-start.6
  66.7 1.3 select_reduce_fusion
  68.0 0.9 broadcast_in_dim.164
  68.9 3.5 %all-to-all-start.1 = ((bf16[4,2,256,128]{3,2,1,0:T(8,128)(2,1)}), bf16[4,2,256,128]{3,2,1,0:T(8,128)(2,1)S(1)}, u32[]{:S(2)}, u32[]{:S(2)}) async-start(bf16[4,2,256,128]{3,2,1,0:T(8,128)(2,1)} %broadcast_in_dim.164), calls=%async_computation.1 | async-start | bytes 1048576 | tf_op jit(solution)/shard_map/all_to_all | solution.py:47
  72.4 4.4 %collective-permute-start.9 = (bf16[256,768]{1,0:T(8,128)(2,1)S(1)}, bf16[256,768]{1,0:T(8,128)(2,1)}, u32[]{:S(2)}, u32[]{:S(2)}) collective-permute-start(bf16[256,768]{1,0:T(8,128)(2,1)S(1)} %copy-done.1), channel_id=1, source_target_pairs={{0,3},{1,0},{2,1},{3,2},{4,7},{5,4},{6,5},{7,6},{8,11},{9,8},{10,9... | collective-permute-start | bytes 1179656 | tf_op jit(solution)/shard_map/ppermute | solution.py:42
  76.8 2.4 %collective-permute-start.8 = (bf16[256,768]{1,0:T(8,128)(2,1)S(1)}, bf16[256,768]{1,0:T(8,128)(2,1)}, u32[]{:S(2)}, u32[]{:S(2)}) collective-permute-start(bf16[256,768]{1,0:T(8,128)(2,1)S(1)} %copy-done.1), channel_id=1, source_target_pairs={{0,2},{1,3},{2,0},{3,1},{4,6},{5,7},{6,4},{7,5},{8,10},{9,11},{10,... | collective-permute-start | bytes 1179656 | tf_op jit(solution)/shard_map/ppermute | solution.py:42
  79.2 2.5 %collective-permute-start.7 = (bf16[256,768]{1,0:T(8,128)(2,1)S(1)}, bf16[256,768]{1,0:T(8,128)(2,1)}, u32[]{:S(2)}, u32[]{:S(2)}) collective-permute-start(bf16[256,768]{1,0:T(8,128)(2,1)S(1)} %copy-done.1), channel_id=1, source_target_pairs={{0,1},{1,2},{2,3},{3,0},{4,5},{5,6},{6,7},{7,4},{8,9},{9,10},{10,1... | collective-permute-start | bytes 1179656 | tf_op jit(solution)/shard_map/ppermute | solution.py:42
  84.3 2.8 %all-to-all-done.1 = bf16[4,2,256,128]{3,2,1,0:T(8,128)(2,1)S(1)} async-done(((bf16[4,2,256,128]{3,2,1,0:T(8,128)(2,1)}), bf16[4,2,256,128]{3,2,1,0:T(8,128)(2,1)S(1)}, u32[]{:S(2)}, u32[]{:S(2)}) %all-to-all-start.1) | async-done | bytes 524320 | tf_op jit(solution)/shard_map/all_to_all | solution.py:47
  87.2 0.9 broadcast_in_dim.165
  88.1 3.5 %all-to-all-start.2 = ((bf16[4,2,256,128]{3,2,1,0:T(8,128)(2,1)}), bf16[4,2,256,128]{3,2,1,0:T(8,128)(2,1)S(1)}, u32[]{:S(2)}, u32[]{:S(2)}) async-start(bf16[4,2,256,128]{3,2,1,0:T(8,128)(2,1)} %broadcast_in_dim.165), calls=%async_computation.2 | async-start | bytes 1048576 | tf_op jit(solution)/shard_map/all_to_all | solution.py:47
  91.6 1.2 multiply_cosine_fusion
  96.8 3.0 %collective-permute-done.7 = bf16[256,768]{1,0:T(8,128)(2,1)} collective-permute-done((bf16[256,768]{1,0:T(8,128)(2,1)S(1)}, bf16[256,768]{1,0:T(8,128)(2,1)}, u32[]{:S(2)}, u32[]{:S(2)}) %collective-permute-start.7) | collective-permute-done | bytes 393248 | tf_op jit(solution)/shard_map/ppermute | solution.py:42
  99.8 2.6 %pad_maximum_fusion = bf16[4,256,768]{2,1,0:T(8,128)(2,1)} fusion(bf16[1,256,768]{2,1,0:T(8,128)(2,1)} %bitcast.24, bf16[1,256,768]{2,1,0:T(8,128)(2,1)} %bitcast.23, bf16[1,256,768]{2,1,0:T(8,128)(2,1)} %bitcast.22, bf16[1,256,768]{2,1,0:T(8,128)(2,1)S(1)} %bitcast.115), kind=kLoop, calls=%fused_computation.5 | loop fusion | flops 2359296 | bytes 3145728 | tf_op jit(solution)/shard_map/stack | solution.py:102
  102.3 3.2 %gather_fusion.4 = bf16[4,256,768]{2,1,0:T(8,128)(2,1)} fusion(bf16[4,256,768]{2,1,0:T(8,128)(2,1)} %pad_maximum_fusion, s32[1024]{0:T(1024)S(1)} %pad_clamp_fusion), kind=kCustom, calls=%fused_computation.4 | custom fusion | bytes 3145744 | tf_op jit(solution)/shard_map/jit(_take)/gather | solution.py:104
  105.5 13.5 %all-to-all-done.2 = bf16[4,2,256,128]{3,2,1,0:T(8,128)(2,1)S(1)} async-done(((bf16[4,2,256,128]{3,2,1,0:T(8,128)(2,1)}), bf16[4,2,256,128]{3,2,1,0:T(8,128)(2,1)S(1)}, u32[]{:S(2)}, u32[]{:S(2)}) %all-to-all-start.2) | async-done | bytes 524320 | tf_op jit(solution)/shard_map/all_to_all | solution.py:47
  119.2 0.9 select_select_fusion
  120.1 3.9 %all-to-all-start.3 = ((bf16[8,256,128]{2,1,0:T(8,128)(2,1)}), bf16[8,256,128]{2,1,0:T(8,128)(2,1)S(1)}, u32[]{:S(2)}, u32[]{:S(2)}) async-start(bf16[8,256,128]{2,1,0:T(8,128)(2,1)} %select_select_fusion), calls=%async_computation.3 | async-start | bytes 1048576 | tf_op jit(solution)/shard_map/all_to_all | solution.py:129
  124.0 2.8 %select_bitcast_fusion = bf16[256,4,768]{2,0,1:T(8,128)(2,1)} fusion(bf16[4,256,768]{2,1,0:T(8,128)(2,1)} %gather_fusion.4, pred[4]{0:T(512)(128)(4,1)S(1)} %compare_and_fusion), kind=kLoop, calls=%fused_computation.6 | loop fusion | flops 786432 | bytes 3145732 | tf_op jit(solution)/shard_map/jit(_take)/select_n | solution.py:104
  126.7 2.6 %copy.48 = bf16[256,4,768]{0,2,1:T(8,128)(2,1)} copy(bf16[256,4,768]{2,0,1:T(8,128)(2,1)} %select_bitcast_fusion) | data formatting | bytes 3145728 | tf_op jit(solution)/shard_map/jit(_take)/select_n | solution.py:104
  129.3 2.2 %fusion.63 = f32[256,128]{1,0:T(8,128)S(1)} fusion(bf16[256,3072]{0,1:T(8,128)(2,1)} %bitcast.113, bf16[3072,128]{1,0:T(8,128)(2,1)} %param.11), kind=kOutput, calls=%fused_computation.137 | convolution fusion | flops 201326592 | bytes 2490368 | tf_op jit(solution)/shard_map/dot_general | solution.py:138
  131.6 1.9 %all-to-all-done.3 = bf16[8,256,128]{2,1,0:T(8,128)(2,1)S(1)} async-done(((bf16[8,256,128]{2,1,0:T(8,128)(2,1)}), bf16[8,256,128]{2,1,0:T(8,128)(2,1)S(1)}, u32[]{:S(2)}, u32[]{:S(2)}) %all-to-all-start.3) | async-done | bytes 524320 | tf_op jit(solution)/shard_map/all_to_all | solution.py:129
  133.8 0.9 broadcast_in_dim.171
  134.8 7.8 %all-to-all-start.4 = ((f32[4,336,128]{2,1,0:T(8,128)}), f32[4,336,128]{2,1,0:T(8,128)S(1)}, u32[]{:S(2)}, u32[]{:S(2)}) async-start(f32[4,336,128]{2,1,0:T(8,128)} %broadcast_in_dim.171), calls=%async_computation.4 | async-start | bytes 1376256 | tf_op jit(solution)/shard_map/all_to_all | solution.py:47
  142.7 3.2 %fusion.64 = f32[256,384]{1,0:T(8,128)} fusion(bf16[256,3072]{0,1:T(8,128)(2,1)} %bitcast.114, bf16[3072,384]{1,0:T(8,128)(2,1)S(1)} %copy-done), kind=kOutput, calls=%fused_computation.138 | convolution fusion | flops 603979776 | bytes 4325376 | tf_op jit(solution)/shard_map/dot_general | solution.py:163
  145.9 0.7 constant_dynamic-slice_fusion.1
  146.6 6.1 %all-to-all-done.4 = f32[4,336,128]{2,1,0:T(8,128)S(1)} async-done(((f32[4,336,128]{2,1,0:T(8,128)}), f32[4,336,128]{2,1,0:T(8,128)S(1)}, u32[]{:S(2)}, u32[]{:S(2)}) %all-to-all-start.4) | async-done | bytes 688160 | tf_op jit(solution)/shard_map/all_to_all | solution.py:47
  152.7 1.2 fusion.2
  154.0 0.9 copy.50
  154.9 1.8 %fusion.59 = (f32[1,256,3,64]{1,3,2,0:T(8,128)}, f32[1,256,3,64]{1,3,2,0:T(8,128)}) fusion(f32[1,256,3,128]{1,3,2,0:T(8,128)} %bitcast.116), kind=kLoop, calls=%fused_computation.133 | loop fusion | bytes 786432 | tf_op jit(solution)/shard_map/slice | solution.py:26
  156.7 1.1 copy.61
  157.8 1.8 %copy.60 = f32[1,256,3,64]{3,1,2,0:T(8,128)} copy(f32[1,256,3,64]{1,3,2,0:T(8,128)} %get-tuple-element.8) | data formatting | bytes 393216
  161.5 1.4 fusion.4
  162.9 0.8 copy.55
  (75 shorter events, 10.5 us)
Async XLA Ops:
  0.0 142.7 %copy-start = (bf16[3072,384]{1,0:T(8,128)(2,1)S(1)}, bf16[3072,384]{1,0:T(8,128)(2,1)}, u32[]{:S(2)}) copy-start(bf16[3072,384]{1,0:T(8,128)(2,1)} %param.10) | copy-start | bytes 7077892
  2.4 55.9 %collective-permute-start = (bf16[256,128]{1,0:T(8,128)(2,1)S(1)}, bf16[256,128]{1,0:T(8,128)(2,1)S(1)}, u32[]{:S(2)}, u32[]{:S(2)}) collective-permute-start(bf16[256,128]{1,0:T(8,128)(2,1)S(1)} %pad_maximum_fusion.2), channel_id=1, source_target_pairs={{0,4},{4,8},{8,12},{12,16},{16,20},{20,24},{24,28},{28,0},{1,5},{5... | collective-permute-start | bytes 196616 | tf_op jit(solution)/shard_map/ppermute | solution.py:42
  5.1 56.9 %collective-permute-start.1 = (bf16[256,128]{1,0:T(8,128)(2,1)S(1)}, bf16[256,128]{1,0:T(8,128)(2,1)S(1)}, u32[]{:S(2)}, u32[]{:S(2)}) collective-permute-start(bf16[256,128]{1,0:T(8,128)(2,1)S(1)} %pad_maximum_fusion.2), channel_id=1, source_target_pairs={{0,8},{4,12},{8,16},{12,20},{16,24},{20,28},{24,0},{28,4},{1,9},{5... | collective-permute-start | bytes 196616 | tf_op jit(solution)/shard_map/ppermute | solution.py:42
  8.3 55.3 %collective-permute-start.2 = (bf16[256,128]{1,0:T(8,128)(2,1)S(1)}, bf16[256,128]{1,0:T(8,128)(2,1)S(1)}, u32[]{:S(2)}, u32[]{:S(2)}) collective-permute-start(bf16[256,128]{1,0:T(8,128)(2,1)S(1)} %pad_maximum_fusion.2), channel_id=1, source_target_pairs={{0,12},{4,16},{8,20},{12,24},{16,28},{20,0},{24,4},{28,8},{1,13},{... | collective-permute-start | bytes 196616 | tf_op jit(solution)/shard_map/ppermute | solution.py:42
  11.8 52.4 %collective-permute-start.3 = (bf16[256,128]{1,0:T(8,128)(2,1)S(1)}, bf16[256,128]{1,0:T(8,128)(2,1)S(1)}, u32[]{:S(2)}, u32[]{:S(2)}) collective-permute-start(bf16[256,128]{1,0:T(8,128)(2,1)S(1)} %pad_maximum_fusion.2), channel_id=1, source_target_pairs={{0,16},{4,20},{8,24},{12,28},{16,0},{20,4},{24,8},{28,12},{1,17},{... | collective-permute-start | bytes 196616 | tf_op jit(solution)/shard_map/ppermute | solution.py:42
  18.8 46.1 %collective-permute-start.4 = (bf16[256,128]{1,0:T(8,128)(2,1)S(1)}, bf16[256,128]{1,0:T(8,128)(2,1)S(1)}, u32[]{:S(2)}, u32[]{:S(2)}) collective-permute-start(bf16[256,128]{1,0:T(8,128)(2,1)S(1)} %pad_maximum_fusion.2), channel_id=1, source_target_pairs={{0,20},{4,24},{8,28},{12,0},{16,4},{20,8},{24,12},{28,16},{1,21},{... | collective-permute-start | bytes 196616 | tf_op jit(solution)/shard_map/ppermute | solution.py:42
  26.6 27.7 %all-to-all-start = ((s32[128,1,1]{2,1,0:T(1,128)}), s32[128,1,1]{2,1,0:T(1,128)S(1)}, u32[]{:S(2)}, u32[]{:S(2)}) async-start(s32[128,1,1]{2,1,0:T(1,128)} %broadcast_in_dim.104), calls=%async_computation | async-start | bytes 131072 | tf_op jit(solution)/shard_map/all_to_all | solution.py:47
  58.3 7.2 %collective-permute-start.5 = (bf16[256,128]{1,0:T(8,128)(2,1)S(1)}, bf16[256,128]{1,0:T(8,128)(2,1)S(1)}, u32[]{:S(2)}, u32[]{:S(2)}) collective-permute-start(bf16[256,128]{1,0:T(8,128)(2,1)S(1)} %pad_maximum_fusion.2), channel_id=1, source_target_pairs={{0,24},{4,28},{8,0},{12,4},{16,8},{20,12},{24,16},{28,20},{1,25},{... | collective-permute-start | bytes 196616 | tf_op jit(solution)/shard_map/ppermute | solution.py:42
  62.0 10.4 %copy-start.1 = (bf16[256,768]{1,0:T(8,128)(2,1)S(1)}, bf16[256,768]{1,0:T(8,128)(2,1)}, u32[]{:S(2)}) copy-start(bf16[256,768]{1,0:T(8,128)(2,1)} %param.9) | copy-start | bytes 1179652
  62.0 4.1 %collective-permute-start.6 = (bf16[256,128]{1,0:T(8,128)(2,1)S(1)}, bf16[256,128]{1,0:T(8,128)(2,1)S(1)}, u32[]{:S(2)}, u32[]{:S(2)}) collective-permute-start(bf16[256,128]{1,0:T(8,128)(2,1)S(1)} %pad_maximum_fusion.2), channel_id=1, source_target_pairs={{0,28},{4,0},{8,4},{12,8},{16,12},{20,16},{24,20},{28,24},{1,29},{... | collective-permute-start | bytes 196616 | tf_op jit(solution)/shard_map/ppermute | solution.py:42
  68.9 18.2 %all-to-all-start.1 = ((bf16[4,2,256,128]{3,2,1,0:T(8,128)(2,1)}), bf16[4,2,256,128]{3,2,1,0:T(8,128)(2,1)S(1)}, u32[]{:S(2)}, u32[]{:S(2)}) async-start(bf16[4,2,256,128]{3,2,1,0:T(8,128)(2,1)} %broadcast_in_dim.164), calls=%async_computation.1 | async-start | bytes 1048576 | tf_op jit(solution)/shard_map/all_to_all | solution.py:47
  72.4 24.3 %collective-permute-start.9 = (bf16[256,768]{1,0:T(8,128)(2,1)S(1)}, bf16[256,768]{1,0:T(8,128)(2,1)}, u32[]{:S(2)}, u32[]{:S(2)}) collective-permute-start(bf16[256,768]{1,0:T(8,128)(2,1)S(1)} %copy-done.1), channel_id=1, source_target_pairs={{0,3},{1,0},{2,1},{3,2},{4,7},{5,4},{6,5},{7,6},{8,11},{9,8},{10,9... | collective-permute-start | bytes 1179656 | tf_op jit(solution)/shard_map/ppermute | solution.py:42
  76.8 19.9 %collective-permute-start.8 = (bf16[256,768]{1,0:T(8,128)(2,1)S(1)}, bf16[256,768]{1,0:T(8,128)(2,1)}, u32[]{:S(2)}, u32[]{:S(2)}) collective-permute-start(bf16[256,768]{1,0:T(8,128)(2,1)S(1)} %copy-done.1), channel_id=1, source_target_pairs={{0,2},{1,3},{2,0},{3,1},{4,6},{5,7},{6,4},{7,5},{8,10},{9,11},{10,... | collective-permute-start | bytes 1179656 | tf_op jit(solution)/shard_map/ppermute | solution.py:42
  79.2 20.5 %collective-permute-start.7 = (bf16[256,768]{1,0:T(8,128)(2,1)S(1)}, bf16[256,768]{1,0:T(8,128)(2,1)}, u32[]{:S(2)}, u32[]{:S(2)}) collective-permute-start(bf16[256,768]{1,0:T(8,128)(2,1)S(1)} %copy-done.1), channel_id=1, source_target_pairs={{0,1},{1,2},{2,3},{3,0},{4,5},{5,6},{6,7},{7,4},{8,9},{9,10},{10,1... | collective-permute-start | bytes 1179656 | tf_op jit(solution)/shard_map/ppermute | solution.py:42
  88.1 31.0 %all-to-all-start.2 = ((bf16[4,2,256,128]{3,2,1,0:T(8,128)(2,1)}), bf16[4,2,256,128]{3,2,1,0:T(8,128)(2,1)S(1)}, u32[]{:S(2)}, u32[]{:S(2)}) async-start(bf16[4,2,256,128]{3,2,1,0:T(8,128)(2,1)} %broadcast_in_dim.165), calls=%async_computation.2 | async-start | bytes 1048576 | tf_op jit(solution)/shard_map/all_to_all | solution.py:47
  120.1 13.4 %all-to-all-start.3 = ((bf16[8,256,128]{2,1,0:T(8,128)(2,1)}), bf16[8,256,128]{2,1,0:T(8,128)(2,1)S(1)}, u32[]{:S(2)}, u32[]{:S(2)}) async-start(bf16[8,256,128]{2,1,0:T(8,128)(2,1)} %select_select_fusion), calls=%async_computation.3 | async-start | bytes 1048576 | tf_op jit(solution)/shard_map/all_to_all | solution.py:129
  133.5 1.3 copy-start.4
  134.8 17.9 %all-to-all-start.4 = ((f32[4,336,128]{2,1,0:T(8,128)}), f32[4,336,128]{2,1,0:T(8,128)S(1)}, u32[]{:S(2)}, u32[]{:S(2)}) async-start(f32[4,336,128]{2,1,0:T(8,128)} %broadcast_in_dim.171), calls=%async_computation.4 | async-start | bytes 1376256 | tf_op jit(solution)/shard_map/all_to_all | solution.py:47
  159.6 1.1 copy-start.2
  159.6 1.2 copy-start.5
  159.6 1.3 copy-start.6
  159.6 0.8 copy-start.3

commit v13 on v10

--- a/solution.py
+++ b/solution.py
@@ -136,6 +136,15 @@
     piece = jnp.transpose(piece, (1, 0, 2)).reshape(rows_total, -1)
 
     key_value_sum = jnp.dot(piece, key_value_weight, preferred_element_type=jnp.float32)
+    from_left = shifted(key_value_sum, 1, n_tp, [(0, 1), (1, 2)])
+    from_right = shifted(key_value_sum, -1, n_tp, [(2, 1), (3, 2)])
+    from_far = shifted(key_value_sum, 2, n_tp, [(1, 3), (2, 0)])
+    key_sum = jnp.where(
+        tp_index == 0, key_value_sum, jnp.where(tp_index == 3, from_far, from_left)
+    )
+    value_sum = jnp.where(
+        tp_index == 3, key_value_sum, jnp.where(tp_index == 0, from_far, from_right)
+    )
 
     rank_part = jnp.einsum("kd,sd->ks", down_t, states, preferred_element_type=jnp.float32)
     n_rank, width = rank_part.shape
@@ -143,7 +152,7 @@
     rank_rows = rank_part.reshape(-1, lanes)
     n_mid, n_up = rank_rows.shape[0], adapter_pair.shape[0]
     bundle = jnp.concatenate(
-        [rank_rows, adapter_pair.astype(jnp.float32), key_value_sum], axis=0
+        [rank_rows, adapter_pair.astype(jnp.float32)], axis=0
     )
     arrived = gather_over(bundle, "tp", n_tp)
     rank_sum = arrived[0, :n_mid]
@@ -152,13 +161,10 @@
     rank_mid = rank_sum.reshape(n_rank, width).astype(jnp.bfloat16)
     rank_cols = rank_mid.shape[0] // 2
     up_all = arrived[:, n_mid:n_mid + n_up].astype(jnp.bfloat16)
-    base_all = arrived[:, n_mid + n_up:]
     kv_heads = (n_tp * kv_cols) // 2 // HEAD_DIM
     group_index = tp_index * heads_here // (HEADS // kv_heads)
     key_up = up_all[group_index]
     value_up = up_all[kv_heads + group_index]
-    key_sum = base_all[group_index]
-    value_sum = base_all[kv_heads + group_index]
 
     query_total = jnp.dot(piece, query_weight, preferred_element_type=jnp.float32)
     query_addition = jnp.einsum(

time: 149 us -> 147 us (0.987)
  starting transfers between devices: 52.1 us -> 59.4 us
  waiting for transfers between devices: 45.1 us -> 39.1 us
  local copies, waits for them, and re-layouts: 23 us -> 18 us
    ppermute x3 -> x6, starting transfers between devices: 9.33 us -> 20.7 us  [shifted(): return lax.ppermute(x, axis, pairs)]
    all_to_all x5, starting transfers between devices: 38.9 us -> 34.7 us  [gather_over(): return lax.all_to_all(copies, axis, 0, 0, tiled=True)]
    all_to_all x5, waiting for transfers between devices: 39.5 us -> 36.1 us  [gather_over(): return lax.all_to_all(copies, axis, 0, 0, tiled=True)]
    unnamed x16 -> x14, local copies, waits for them, and re-layouts: 3.35 us -> 0.98 us
    all_to_all x1, waiting for transfers between devices: 1.92 us -> 0.01 us  [local(): received = lax.all_to_all(send, 'ry', 0, 0, tiled=True)]
    slice x1, local copies, waits for them, and re-layouts: 1.79 us -> 0.03 us  [rotate(): second_half = field[..., half:]]
    ppermute x3 -> x6, waiting for transfers between devices: 3.68 us -> 2.97 us  [shifted(): return lax.ppermute(x, axis, pairs)]
  transfers between devices with their start and end apart: 9 -> 12, of which waited for: 7 -> 6; matrix products, arithmetic and copies ran while one was open for 19% -> 23% of each run, Pallas kernels for 0% -> 0%
where the time goes in v13:
time: 147 us; the launch traced here: 146 us
  starting transfers between devices  59.4 us (40%)
  waiting for transfers between devices  39.1 us (27%)
  local copies, waits for them, and re-layouts  18 us (12%)
  other arithmetic  15 us (10%)
  matrix products  8.48 us (6%)
  between operations  5.88 us (4%)
    all_to_all x5, waiting for transfers between devices, gather_over(): return lax.all_to_all(copies, axis, 0, 0, tiled=True)  36.1 us
    all_to_all x5, starting transfers between devices, gather_over(): return lax.all_to_all(copies, axis, 0, 0, tiled=True)  34.7 us
    ppermute x6, starting transfers between devices, shifted(): return lax.ppermute(x, axis, pairs)  20.7 us
    broadcast_in_dim x5, local copies, waits for them, and re-layouts, gather_over(): copies = jnp.broadcast_to(x[None], (n,) + x.shape)  4.59 us
    all_to_all x1, starting transfers between devices, local(): received = lax.all_to_all(send, 'ry', 0, 0, tiled=True)  3.89 us
    gather x1, local copies, waits for them, and re-layouts, local(): piece = jnp.take(blocks, source, axis=0)  3.2 us
    ppermute x6, waiting for transfers between devices, shifted(): return lax.ppermute(x, axis, pairs)  2.97 us
  transfers between devices with their start and end apart: 12, of which 6 were waited for; matrix products, arithmetic and copies ran while one was open for 23% of the time, Pallas kernels for 0%

profile of v13, /device:TPU:1, one launch (start us, length us, event | category | flops | bytes accessed | tf_op | source)
XLA Modules:
  0.0 145.9 jit_solution(7210536549181207018)
XLA Ops:
  0.8 1.4 fusion.42
  2.2 1.3 broadcast_in_dim.108
  3.5 20.6 %all-to-all-start = ((s32[128,1,1]{2,1,0:T(1,128)}), s32[128,1,1]{2,1,0:T(1,128)S(1)}, u32[]{:S(2)}, u32[]{:S(2)}) async-start(s32[128,1,1]{2,1,0:T(1,128)} %broadcast_in_dim.108), calls=%async_computation | async-start | bytes 131072 | tf_op jit(solution)/shard_map/all_to_all | solution.py:47
  24.1 0.7 reshape_squeeze.3
  24.8 0.9 reshape.463
  25.7 0.7 pad_maximum_fusion.1
  26.4 12.5 %all-to-all-done = s32[128,1,1]{2,1,0:T(1,128)S(1)} async-done(((s32[128,1,1]{2,1,0:T(1,128)}), s32[128,1,1]{2,1,0:T(1,128)S(1)}, u32[]{:S(2)}, u32[]{:S(2)}) %all-to-all-start) | async-done | bytes 544 | tf_op jit(solution)/shard_map/all_to_all | solution.py:47
  38.9 0.9 broadcast_in_dim.170
  39.8 3.9 %all-to-all-start.1 = ((bf16[8,256,128]{2,1,0:T(8,128)(2,1)}), bf16[8,256,128]{2,1,0:T(8,128)(2,1)S(1)}, u32[]{:S(2)}, u32[]{:S(2)}) async-start(bf16[8,256,128]{2,1,0:T(8,128)(2,1)} %broadcast_in_dim.170), calls=%async_computation.1 | async-start | bytes 1048576 | tf_op jit(solution)/shard_map/all_to_all | solution.py:47
  43.7 2.3 %reduce.7 = s32[128]{0:T(128)S(1)} reduce(s32[128,1,1]{2,1,0:T(1,128)S(1)} %all-to-all-done, s32[]{:T(128)} %constant.99.clone.1), dimensions={1,2}, to_apply=%all_to_all.19.reduce_sub_computation | reduce | bytes 1028 | tf_op jit(solution)/shard_map/all_to_all | solution.py:47
  46.2 0.7 gather_fusion.3
  46.9 0.6 gather_fusion.4
  47.6 5.5 %all-to-all-done.1 = bf16[8,256,128]{2,1,0:T(8,128)(2,1)S(1)} async-done(((bf16[8,256,128]{2,1,0:T(8,128)(2,1)}), bf16[8,256,128]{2,1,0:T(8,128)(2,1)S(1)}, u32[]{:S(2)}, u32[]{:S(2)}) %all-to-all-start.1) | async-done | bytes 524320 | tf_op jit(solution)/shard_map/all_to_all | solution.py:47
  53.4 0.9 broadcast_in_dim.173
  54.3 3.5 %all-to-all-start.2 = ((bf16[4,2,256,128]{3,2,1,0:T(8,128)(2,1)}), bf16[4,2,256,128]{3,2,1,0:T(8,128)(2,1)S(1)}, u32[]{:S(2)}, u32[]{:S(2)}) async-start(bf16[4,2,256,128]{3,2,1,0:T(8,128)(2,1)} %broadcast_in_dim.173), calls=%async_computation.2 | async-start | bytes 1048576 | tf_op jit(solution)/shard_map/all_to_all | solution.py:47
  57.8 4.4 %collective-permute-start.2 = (bf16[256,768]{1,0:T(8,128)(2,1)S(1)}, bf16[256,768]{1,0:T(8,128)(2,1)}, u32[]{:S(2)}, u32[]{:S(2)}) collective-permute-start(bf16[256,768]{1,0:T(8,128)(2,1)S(1)} %copy-done.1), channel_id=1, source_target_pairs={{0,3},{1,0},{2,1},{3,2},{4,7},{5,4},{6,5},{7,6},{8,11},{9,8},{10,9... | collective-permute-start | bytes 1179656 | tf_op jit(solution)/shard_map/ppermute | solution.py:42
  62.2 2.4 %collective-permute-start.1 = (bf16[256,768]{1,0:T(8,128)(2,1)S(1)}, bf16[256,768]{1,0:T(8,128)(2,1)}, u32[]{:S(2)}, u32[]{:S(2)}) collective-permute-start(bf16[256,768]{1,0:T(8,128)(2,1)S(1)} %copy-done.1), channel_id=1, source_target_pairs={{0,2},{1,3},{2,0},{3,1},{4,6},{5,7},{6,4},{7,5},{8,10},{9,11},{10,... | collective-permute-start | bytes 1179656 | tf_op jit(solution)/shard_map/ppermute | solution.py:42
  64.6 2.5 %collective-permute-start = (bf16[256,768]{1,0:T(8,128)(2,1)S(1)}, bf16[256,768]{1,0:T(8,128)(2,1)}, u32[]{:S(2)}, u32[]{:S(2)}) collective-permute-start(bf16[256,768]{1,0:T(8,128)(2,1)S(1)} %copy-done.1), channel_id=1, source_target_pairs={{0,1},{1,2},{2,3},{3,0},{4,5},{5,6},{6,7},{7,4},{8,9},{9,10},{10,1... | collective-permute-start | bytes 1179656 | tf_op jit(solution)/shard_map/ppermute | solution.py:42
  69.9 1.9 %all-to-all-done.2 = bf16[4,2,256,128]{3,2,1,0:T(8,128)(2,1)S(1)} async-done(((bf16[4,2,256,128]{3,2,1,0:T(8,128)(2,1)}), bf16[4,2,256,128]{3,2,1,0:T(8,128)(2,1)S(1)}, u32[]{:S(2)}, u32[]{:S(2)}) %all-to-all-start.2) | async-done | bytes 524320 | tf_op jit(solution)/shard_map/all_to_all | solution.py:47
  71.9 0.9 broadcast_in_dim.174
  72.8 3.5 %all-to-all-start.3 = ((bf16[4,2,256,128]{3,2,1,0:T(8,128)(2,1)}), bf16[4,2,256,128]{3,2,1,0:T(8,128)(2,1)S(1)}, u32[]{:S(2)}, u32[]{:S(2)}) async-start(bf16[4,2,256,128]{3,2,1,0:T(8,128)(2,1)} %broadcast_in_dim.174), calls=%async_computation.3 | async-start | bytes 1048576 | tf_op jit(solution)/shard_map/all_to_all | solution.py:47
  76.3 0.7 fusion.7
  77.0 1.2 multiply_cosine_fusion
  78.3 0.6 gather_fusion.1
  78.9 0.6 dynamic_slice.12
  81.5 0.6 gather_fusion.2
  82.2 3.0 %collective-permute-done = bf16[256,768]{1,0:T(8,128)(2,1)} collective-permute-done((bf16[256,768]{1,0:T(8,128)(2,1)S(1)}, bf16[256,768]{1,0:T(8,128)(2,1)}, u32[]{:S(2)}, u32[]{:S(2)}) %collective-permute-start) | collective-permute-done | bytes 393248 | tf_op jit(solution)/shard_map/ppermute | solution.py:42
  85.1 2.6 %pad_maximum_fusion = bf16[4,256,768]{2,1,0:T(8,128)(2,1)} fusion(bf16[1,256,768]{2,1,0:T(8,128)(2,1)} %bitcast.4, bf16[1,256,768]{2,1,0:T(8,128)(2,1)} %bitcast.3, bf16[1,256,768]{2,1,0:T(8,128)(2,1)} %bitcast.2, bf16[1,256,768]{2,1,0:T(8,128)(2,1)S(1)} %bitcast.89), kind=kLoop, calls=%fused_computation.5 | loop fusion | flops 2359296 | bytes 3145728 | tf_op jit(solution)/shard_map/stack | solution.py:102
  87.7 3.2 %gather_fusion = bf16[4,256,768]{2,1,0:T(8,128)(2,1)} fusion(bf16[4,256,768]{2,1,0:T(8,128)(2,1)} %pad_maximum_fusion, s32[1024]{0:T(1024)S(1)} %pad_clamp_fusion.2), kind=kCustom, calls=%fused_computation | custom fusion | bytes 3145744 | tf_op jit(solution)/shard_map/jit(_take)/gather | solution.py:104
  90.9 13.6 %all-to-all-done.3 = bf16[4,2,256,128]{3,2,1,0:T(8,128)(2,1)S(1)} async-done(((bf16[4,2,256,128]{3,2,1,0:T(8,128)(2,1)}), bf16[4,2,256,128]{3,2,1,0:T(8,128)(2,1)S(1)}, u32[]{:S(2)}, u32[]{:S(2)}) %all-to-all-start.3) | async-done | bytes 524320 | tf_op jit(solution)/shard_map/all_to_all | solution.py:47
  104.6 0.9 select_select_fusion
  105.5 3.9 %all-to-all-start.4 = ((bf16[8,256,128]{2,1,0:T(8,128)(2,1)}), bf16[8,256,128]{2,1,0:T(8,128)(2,1)S(1)}, u32[]{:S(2)}, u32[]{:S(2)}) async-start(bf16[8,256,128]{2,1,0:T(8,128)(2,1)} %select_select_fusion), calls=%async_computation.4 | async-start | bytes 1048576 | tf_op jit(solution)/shard_map/all_to_all | solution.py:129
  109.4 2.8 %select_bitcast_fusion = bf16[256,4,768]{2,0,1:T(8,128)(2,1)} fusion(bf16[4,256,768]{2,1,0:T(8,128)(2,1)} %gather_fusion, pred[4]{0:T(512)(128)(4,1)S(1)} %compare_and_fusion.1), kind=kLoop, calls=%fused_computation.6 | loop fusion | flops 786432 | bytes 3145732 | tf_op jit(solution)/shard_map/jit(_take)/select_n | solution.py:104
  112.2 2.6 %copy.45 = bf16[256,4,768]{0,2,1:T(8,128)(2,1)} copy(bf16[256,4,768]{2,0,1:T(8,128)(2,1)} %select_bitcast_fusion) | data formatting | bytes 3145728 | tf_op jit(solution)/shard_map/jit(_take)/select_n | solution.py:104
  114.8 2.7 %fusion.55 = f32[256,128]{0,1:T(8,128)} fusion(bf16[256,3072]{0,1:T(8,128)(2,1)} %bitcast.87, bf16[3072,128]{1,0:T(8,128)(2,1)} %param.11), kind=kOutput, calls=%fused_computation.117 | convolution fusion | flops 201326592 | bytes 2490368 | tf_op jit(solution)/shard_map/dot_general | solution.py:138
  117.5 1.3 collective-permute-start.3
  118.8 8.8 %collective-permute-start.5 = (f32[256,128]{0,1:T(8,128)}, f32[256,128]{0,1:T(8,128)}, u32[]{:S(2)}, u32[]{:S(2)}) collective-permute-start(f32[256,128]{0,1:T(8,128)} %fusion.55), channel_id=1, source_target_pairs={{0,1},{1,2},{4,5},{5,6},{8,9},{9,10},{12,13},{13,14},{16,17},{17,1... | collective-permute-start | bytes 393224 | tf_op jit(solution)/shard_map/ppermute | solution.py:42
  127.6 1.3 collective-permute-start.4
  129.2 0.7 broadcast_in_dim.178
  129.9 3.3 %all-to-all-start.5 = ((f32[4,80,128]{2,1,0:T(8,128)}), f32[4,80,128]{2,1,0:T(8,128)S(1)}, u32[]{:S(2)}, u32[]{:S(2)}) async-start(f32[4,80,128]{2,1,0:T(8,128)} %broadcast_in_dim.178), calls=%async_computation.5 | async-start | bytes 327680 | tf_op jit(solution)/shard_map/all_to_all | solution.py:47
  133.3 2.4 %fusion.57 = f32[256,384]{1,0:T(8,128)S(1)} fusion(bf16[256,3072]{0,1:T(8,128)(2,1)} %bitcast.88, bf16[3072,384]{1,0:T(8,128)(2,1)S(1)} %copy-done), kind=kOutput, calls=%fused_computation.119 | convolution fusion | flops 603979776 | bytes 4325376 | tf_op jit(solution)/shard_map/dot_general | solution.py:169
  135.7 2.6 %all-to-all-done.5 = f32[4,80,128]{2,1,0:T(8,128)S(1)} async-done(((f32[4,80,128]{2,1,0:T(8,128)}), f32[4,80,128]{2,1,0:T(8,128)S(1)}, u32[]{:S(2)}, u32[]{:S(2)}) %all-to-all-start.5) | async-done | bytes 163872 | tf_op jit(solution)/shard_map/all_to_all | solution.py:47
  138.3 0.6 copy-done.2
  139.8 0.8 slice.125
  140.6 1.2 reduce-precision_bitcast_fusion
  142.1 1.1 fusion.8
  143.7 1.3 fusion.4
  145.0 0.8 copy.52
  (58 shorter events, 2.9 us)
Async XLA Ops:
  0.0 133.3 %copy-start = (bf16[3072,384]{1,0:T(8,128)(2,1)S(1)}, bf16[3072,384]{1,0:T(8,128)(2,1)}, u32[]{:S(2)}) copy-start(bf16[3072,384]{1,0:T(8,128)(2,1)} %param.10) | copy-start | bytes 7077892
  3.5 35.4 %all-to-all-start = ((s32[128,1,1]{2,1,0:T(1,128)}), s32[128,1,1]{2,1,0:T(1,128)S(1)}, u32[]{:S(2)}, u32[]{:S(2)}) async-start(s32[128,1,1]{2,1,0:T(1,128)} %broadcast_in_dim.108), calls=%async_computation | async-start | bytes 131072 | tf_op jit(solution)/shard_map/all_to_all | solution.py:47
  39.8 13.4 %all-to-all-start.1 = ((bf16[8,256,128]{2,1,0:T(8,128)(2,1)}), bf16[8,256,128]{2,1,0:T(8,128)(2,1)S(1)}, u32[]{:S(2)}, u32[]{:S(2)}) async-start(bf16[8,256,128]{2,1,0:T(8,128)(2,1)} %broadcast_in_dim.170), calls=%async_computation.1 | async-start | bytes 1048576 | tf_op jit(solution)/shard_map/all_to_all | solution.py:47
  46.9 10.9 %copy-start.1 = (bf16[256,768]{1,0:T(8,128)(2,1)S(1)}, bf16[256,768]{1,0:T(8,128)(2,1)}, u32[]{:S(2)}) copy-start(bf16[256,768]{1,0:T(8,128)(2,1)} %param.9) | copy-start | bytes 1179652
  54.3 17.5 %all-to-all-start.2 = ((bf16[4,2,256,128]{3,2,1,0:T(8,128)(2,1)}), bf16[4,2,256,128]{3,2,1,0:T(8,128)(2,1)S(1)}, u32[]{:S(2)}, u32[]{:S(2)}) async-start(bf16[4,2,256,128]{3,2,1,0:T(8,128)(2,1)} %broadcast_in_dim.173), calls=%async_computation.2 | async-start | bytes 1048576 | tf_op jit(solution)/shard_map/all_to_all | solution.py:47
  57.8 24.4 %collective-permute-start.2 = (bf16[256,768]{1,0:T(8,128)(2,1)S(1)}, bf16[256,768]{1,0:T(8,128)(2,1)}, u32[]{:S(2)}, u32[]{:S(2)}) collective-permute-start(bf16[256,768]{1,0:T(8,128)(2,1)S(1)} %copy-done.1), channel_id=1, source_target_pairs={{0,3},{1,0},{2,1},{3,2},{4,7},{5,4},{6,5},{7,6},{8,11},{9,8},{10,9... | collective-permute-start | bytes 1179656 | tf_op jit(solution)/shard_map/ppermute | solution.py:42
  62.2 20.0 %collective-permute-start.1 = (bf16[256,768]{1,0:T(8,128)(2,1)S(1)}, bf16[256,768]{1,0:T(8,128)(2,1)}, u32[]{:S(2)}, u32[]{:S(2)}) collective-permute-start(bf16[256,768]{1,0:T(8,128)(2,1)S(1)} %copy-done.1), channel_id=1, source_target_pairs={{0,2},{1,3},{2,0},{3,1},{4,6},{5,7},{6,4},{7,5},{8,10},{9,11},{10,... | collective-permute-start | bytes 1179656 | tf_op jit(solution)/shard_map/ppermute | solution.py:42
  64.6 20.5 %collective-permute-start = (bf16[256,768]{1,0:T(8,128)(2,1)S(1)}, bf16[256,768]{1,0:T(8,128)(2,1)}, u32[]{:S(2)}, u32[]{:S(2)}) collective-permute-start(bf16[256,768]{1,0:T(8,128)(2,1)S(1)} %copy-done.1), channel_id=1, source_target_pairs={{0,1},{1,2},{2,3},{3,0},{4,5},{5,6},{6,7},{7,4},{8,9},{9,10},{10,1... | collective-permute-start | bytes 1179656 | tf_op jit(solution)/shard_map/ppermute | solution.py:42
  72.8 31.7 %all-to-all-start.3 = ((bf16[4,2,256,128]{3,2,1,0:T(8,128)(2,1)}), bf16[4,2,256,128]{3,2,1,0:T(8,128)(2,1)S(1)}, u32[]{:S(2)}, u32[]{:S(2)}) async-start(bf16[4,2,256,128]{3,2,1,0:T(8,128)(2,1)} %broadcast_in_dim.174), calls=%async_computation.3 | async-start | bytes 1048576 | tf_op jit(solution)/shard_map/all_to_all | solution.py:47
  76.3 5.2 %copy-start.4 = (pred[256]{0:T(512)(128)(4,1)}, pred[256]{0:T(512)(128)(4,1)S(1)}, u32[]{:S(2)}) copy-start(pred[256]{0:T(512)(128)(4,1)S(1)} %iota_compare_fusion.3) | copy-start | bytes 772
  105.5 23.3 %all-to-all-start.4 = ((bf16[8,256,128]{2,1,0:T(8,128)(2,1)}), bf16[8,256,128]{2,1,0:T(8,128)(2,1)S(1)}, u32[]{:S(2)}, u32[]{:S(2)}) async-start(bf16[8,256,128]{2,1,0:T(8,128)(2,1)} %select_select_fusion), calls=%async_computation.4 | async-start | bytes 1048576 | tf_op jit(solution)/shard_map/all_to_all | solution.py:129
  117.5 23.1 %collective-permute-start.3 = (f32[256,128]{0,1:T(8,128)}, f32[256,128]{0,1:T(8,128)}, u32[]{:S(2)}, u32[]{:S(2)}) collective-permute-start(f32[256,128]{0,1:T(8,128)} %fusion.55), channel_id=1, source_target_pairs={{1,3},{2,0},{5,7},{6,4},{9,11},{10,8},{13,15},{14,12},{17,19},{18,... | collective-permute-start | bytes 393224 | tf_op jit(solution)/shard_map/ppermute | solution.py:42
  118.8 21.8 %collective-permute-start.5 = (f32[256,128]{0,1:T(8,128)}, f32[256,128]{0,1:T(8,128)}, u32[]{:S(2)}, u32[]{:S(2)}) collective-permute-start(f32[256,128]{0,1:T(8,128)} %fusion.55), channel_id=1, source_target_pairs={{0,1},{1,2},{4,5},{5,6},{8,9},{9,10},{12,13},{13,14},{16,17},{17,1... | collective-permute-start | bytes 393224 | tf_op jit(solution)/shard_map/ppermute | solution.py:42
  127.6 16.2 %collective-permute-start.4 = (f32[256,128]{0,1:T(8,128)}, f32[256,128]{0,1:T(8,128)}, u32[]{:S(2)}, u32[]{:S(2)}) collective-permute-start(f32[256,128]{0,1:T(8,128)} %fusion.55), channel_id=1, source_target_pairs={{2,1},{3,2},{6,5},{7,6},{10,9},{11,10},{14,13},{15,14},{18,17},{19... | collective-permute-start | bytes 393224 | tf_op jit(solution)/shard_map/ppermute | solution.py:42
  129.9 8.4 %all-to-all-start.5 = ((f32[4,80,128]{2,1,0:T(8,128)}), f32[4,80,128]{2,1,0:T(8,128)S(1)}, u32[]{:S(2)}, u32[]{:S(2)}) async-start(f32[4,80,128]{2,1,0:T(8,128)} %broadcast_in_dim.178), calls=%async_computation.5 | async-start | bytes 327680 | tf_op jit(solution)/shard_map/all_to_all | solution.py:47
  138.3 0.7 copy-start.2
  139.6 3.6 %copy-start.3 = (pred[256,256]{0,1:T(8,128)(4,1)S(1)}, pred[256,256]{0,1:T(8,128)(4,1)}, u32[]{:S(2)}) copy-start(pred[256,256]{0,1:T(8,128)(4,1)} %fusion.7) | copy-start | bytes 196612
  142.1 1.6 %copy-start.5 = (pred[256]{0:T(512)(128)(4,1)S(1)}, pred[256]{0:T(512)(128)(4,1)}, u32[]{:S(2)}) copy-start(pred[256]{0:T(512)(128)(4,1)} %copy-done.4) | copy-start | bytes 772

commit v14 on v13

--- a/solution.py
+++ b/solution.py
@@ -118,7 +118,7 @@
         jnp.where(choose[:, :, None, None], plane[None], jnp.zeros((), plane.dtype)),
         axis=1,
     )
-    for axis in ("zl", "zh"):
+    for axis in ("zh", "zl"):
         copies = gather_over(column, axis, lax.axis_size(axis))
         column = jnp.sum(copies, axis=0)
     dest_k = prefix[slots_all[plane_req]]

time: 147 us -> 148 us (level)
  waiting for transfers between devices: 39.1 us -> 34.2 us
  starting transfers between devices: 59.4 us -> 64 us
    all_to_all x1, starting transfers between devices: 3.89 us -> 7.55 us  [local(): received = lax.all_to_all(send, 'ry', 0, 0, tiled=True)]
    ppermute x6, waiting for transfers between devices: 2.97 us -> 0.02 us  [shifted(): return lax.ppermute(x, axis, pairs)]
    all_to_all x5, starting transfers between devices: 34.7 us -> 37.7 us  [gather_over(): return lax.all_to_all(copies, axis, 0, 0, tiled=True)]
    ppermute x6, starting transfers between devices: 20.7 us -> 18.8 us  [shifted(): return lax.ppermute(x, axis, pairs)]
    all_to_all x5, waiting for transfers between devices: 36.1 us -> 34.2 us  [gather_over(): return lax.all_to_all(copies, axis, 0, 0, tiled=True)]
  transfers between devices with their start and end apart: 12 -> 12, of which waited for: 6 -> 4; matrix products, arithmetic and copies ran while one was open for 23% -> 23% of each run, Pallas kernels for 0% -> 0%
where the time goes in v14:
time: 148 us; the launch traced here: 146 us
  starting transfers between devices  64 us (43%)
  waiting for transfers between devices  34.2 us (23%)
  local copies, waits for them, and re-layouts  18 us (12%)
  other arithmetic  15.1 us (10%)
  matrix products  8.47 us (6%)
  between operations  5.88 us (4%)
    all_to_all x5, starting transfers between devices, gather_over(): return lax.all_to_all(copies, axis, 0, 0, tiled=True)  37.7 us
    all_to_all x5, waiting for transfers between devices, gather_over(): return lax.all_to_all(copies, axis, 0, 0, tiled=True)  34.2 us
    ppermute x6, starting transfers between devices, shifted(): return lax.ppermute(x, axis, pairs)  18.8 us
    all_to_all x1, starting transfers between devices, local(): received = lax.all_to_all(send, 'ry', 0, 0, tiled=True)  7.55 us
    broadcast_in_dim x5, local copies, waits for them, and re-layouts, gather_over(): copies = jnp.broadcast_to(x[None], (n,) + x.shape)  4.59 us
    gather x1, local copies, waits for them, and re-layouts, local(): piece = jnp.take(blocks, source, axis=0)  3.2 us
  transfers between devices with their start and end apart: 12, of which 4 were waited for; matrix products, arithmetic and copies ran while one was open for 23% of the time, Pallas kernels for 0%

profile of v14, /device:TPU:1, one launch (start us, length us, event | category | flops | bytes accessed | tf_op | source)
XLA Modules:
  0.0 145.7 jit_solution(16488346873395856530)
XLA Ops:
  0.8 1.4 fusion.42
  2.2 1.3 broadcast_in_dim.108
  3.5 20.6 %all-to-all-start = ((s32[128,1,1]{2,1,0:T(1,128)}), s32[128,1,1]{2,1,0:T(1,128)S(1)}, u32[]{:S(2)}, u32[]{:S(2)}) async-start(s32[128,1,1]{2,1,0:T(1,128)} %broadcast_in_dim.108), calls=%async_computation | async-start | bytes 131072 | tf_op jit(solution)/shard_map/all_to_all | solution.py:47
  24.1 0.7 reshape_squeeze.3
  24.8 0.9 reshape.463
  25.7 0.7 pad_maximum_fusion.1
  26.4 12.5 %all-to-all-done = s32[128,1,1]{2,1,0:T(1,128)S(1)} async-done(((s32[128,1,1]{2,1,0:T(1,128)}), s32[128,1,1]{2,1,0:T(1,128)S(1)}, u32[]{:S(2)}, u32[]{:S(2)}) %all-to-all-start) | async-done | bytes 544 | tf_op jit(solution)/shard_map/all_to_all | solution.py:47
  38.9 0.9 broadcast_in_dim.170
  39.8 3.9 %all-to-all-start.1 = ((bf16[8,256,128]{2,1,0:T(8,128)(2,1)}), bf16[8,256,128]{2,1,0:T(8,128)(2,1)S(1)}, u32[]{:S(2)}, u32[]{:S(2)}) async-start(bf16[8,256,128]{2,1,0:T(8,128)(2,1)} %broadcast_in_dim.170), calls=%async_computation.1 | async-start | bytes 1048576 | tf_op jit(solution)/shard_map/all_to_all | solution.py:47
  43.7 2.3 %reduce.7 = s32[128]{0:T(128)S(1)} reduce(s32[128,1,1]{2,1,0:T(1,128)S(1)} %all-to-all-done, s32[]{:T(128)} %constant.99.clone.1), dimensions={1,2}, to_apply=%all_to_all.19.reduce_sub_computation | reduce | bytes 1028 | tf_op jit(solution)/shard_map/all_to_all | solution.py:47
  46.2 0.7 gather_fusion.3
  46.9 0.6 gather_fusion.4
  47.6 5.5 %all-to-all-done.1 = bf16[8,256,128]{2,1,0:T(8,128)(2,1)S(1)} async-done(((bf16[8,256,128]{2,1,0:T(8,128)(2,1)}), bf16[8,256,128]{2,1,0:T(8,128)(2,1)S(1)}, u32[]{:S(2)}, u32[]{:S(2)}) %all-to-all-start.1) | async-done | bytes 524320 | tf_op jit(solution)/shard_map/all_to_all | solution.py:47
  53.4 0.9 broadcast_in_dim.173
  54.3 3.5 %all-to-all-start.2 = ((bf16[4,2,256,128]{3,2,1,0:T(8,128)(2,1)}), bf16[4,2,256,128]{3,2,1,0:T(8,128)(2,1)S(1)}, u32[]{:S(2)}, u32[]{:S(2)}) async-start(bf16[4,2,256,128]{3,2,1,0:T(8,128)(2,1)} %broadcast_in_dim.173), calls=%async_computation.2 | async-start | bytes 1048576 | tf_op jit(solution)/shard_map/all_to_all | solution.py:47
  57.8 4.4 %collective-permute-start.2 = (bf16[256,768]{1,0:T(8,128)(2,1)S(1)}, bf16[256,768]{1,0:T(8,128)(2,1)}, u32[]{:S(2)}, u32[]{:S(2)}) collective-permute-start(bf16[256,768]{1,0:T(8,128)(2,1)S(1)} %copy-done.1), channel_id=1, source_target_pairs={{0,3},{1,0},{2,1},{3,2},{4,7},{5,4},{6,5},{7,6},{8,11},{9,8},{10,9... | collective-permute-start | bytes 1179656 | tf_op jit(solution)/shard_map/ppermute | solution.py:42
  62.2 2.4 %collective-permute-start.1 = (bf16[256,768]{1,0:T(8,128)(2,1)S(1)}, bf16[256,768]{1,0:T(8,128)(2,1)}, u32[]{:S(2)}, u32[]{:S(2)}) collective-permute-start(bf16[256,768]{1,0:T(8,128)(2,1)S(1)} %copy-done.1), channel_id=1, source_target_pairs={{0,2},{1,3},{2,0},{3,1},{4,6},{5,7},{6,4},{7,5},{8,10},{9,11},{10,... | collective-permute-start | bytes 1179656 | tf_op jit(solution)/shard_map/ppermute | solution.py:42
  64.6 2.5 %collective-permute-start = (bf16[256,768]{1,0:T(8,128)(2,1)S(1)}, bf16[256,768]{1,0:T(8,128)(2,1)}, u32[]{:S(2)}, u32[]{:S(2)}) collective-permute-start(bf16[256,768]{1,0:T(8,128)(2,1)S(1)} %copy-done.1), channel_id=1, source_target_pairs={{0,1},{1,2},{2,3},{3,0},{4,5},{5,6},{6,7},{7,4},{8,9},{9,10},{10,1... | collective-permute-start | bytes 1179656 | tf_op jit(solution)/shard_map/ppermute | solution.py:42
  69.9 13.7 %all-to-all-done.2 = bf16[4,2,256,128]{3,2,1,0:T(8,128)(2,1)S(1)} async-done(((bf16[4,2,256,128]{3,2,1,0:T(8,128)(2,1)}), bf16[4,2,256,128]{3,2,1,0:T(8,128)(2,1)S(1)}, u32[]{:S(2)}, u32[]{:S(2)}) %all-to-all-start.2) | async-done | bytes 524320 | tf_op jit(solution)/shard_map/all_to_all | solution.py:47
  83.7 0.9 broadcast_in_dim.174
  84.5 6.4 %all-to-all-start.3 = ((bf16[4,2,256,128]{3,2,1,0:T(8,128)(2,1)}), bf16[4,2,256,128]{3,2,1,0:T(8,128)(2,1)S(1)}, u32[]{:S(2)}, u32[]{:S(2)}) async-start(bf16[4,2,256,128]{3,2,1,0:T(8,128)(2,1)} %broadcast_in_dim.174), calls=%async_computation.3 | async-start | bytes 1048576 | tf_op jit(solution)/shard_map/all_to_all | solution.py:47
  91.0 0.7 fusion.7
  91.7 1.2 multiply_cosine_fusion
  92.9 0.6 gather_fusion.1
  93.6 0.6 dynamic_slice.12
  96.2 0.6 gather_fusion.2
  96.9 2.6 %pad_maximum_fusion = bf16[4,256,768]{2,1,0:T(8,128)(2,1)} fusion(bf16[1,256,768]{2,1,0:T(8,128)(2,1)} %bitcast.4, bf16[1,256,768]{2,1,0:T(8,128)(2,1)} %bitcast.3, bf16[1,256,768]{2,1,0:T(8,128)(2,1)} %bitcast.2, bf16[1,256,768]{2,1,0:T(8,128)(2,1)S(1)} %bitcast.89), kind=kLoop, calls=%fused_computation.5 | loop fusion | flops 2359296 | bytes 3145728 | tf_op jit(solution)/shard_map/stack | solution.py:102
  99.4 3.2 %gather_fusion = bf16[4,256,768]{2,1,0:T(8,128)(2,1)} fusion(bf16[4,256,768]{2,1,0:T(8,128)(2,1)} %pad_maximum_fusion, s32[1024]{0:T(1024)S(1)} %pad_clamp_fusion.2), kind=kCustom, calls=%fused_computation | custom fusion | bytes 3145744 | tf_op jit(solution)/shard_map/jit(_take)/gather | solution.py:104
  102.8 0.9 select_select_fusion
  103.7 7.5 %all-to-all-start.4 = ((bf16[8,256,128]{2,1,0:T(8,128)(2,1)}), bf16[8,256,128]{2,1,0:T(8,128)(2,1)S(1)}, u32[]{:S(2)}, u32[]{:S(2)}) async-start(bf16[8,256,128]{2,1,0:T(8,128)(2,1)} %select_select_fusion), calls=%async_computation.4 | async-start | bytes 1048576 | tf_op jit(solution)/shard_map/all_to_all | solution.py:129
  111.2 2.8 %select_bitcast_fusion = bf16[256,4,768]{2,0,1:T(8,128)(2,1)} fusion(bf16[4,256,768]{2,1,0:T(8,128)(2,1)} %gather_fusion, pred[4]{0:T(512)(128)(4,1)S(1)} %compare_and_fusion.1), kind=kLoop, calls=%fused_computation.6 | loop fusion | flops 786432 | bytes 3145732 | tf_op jit(solution)/shard_map/jit(_take)/select_n | solution.py:104
  114.0 2.6 %copy.45 = bf16[256,4,768]{0,2,1:T(8,128)(2,1)} copy(bf16[256,4,768]{2,0,1:T(8,128)(2,1)} %select_bitcast_fusion) | data formatting | bytes 3145728 | tf_op jit(solution)/shard_map/jit(_take)/select_n | solution.py:104
  116.6 2.7 %fusion.55 = f32[256,128]{0,1:T(8,128)} fusion(bf16[256,3072]{0,1:T(8,128)(2,1)} %bitcast.87, bf16[3072,128]{1,0:T(8,128)(2,1)} %param.11), kind=kOutput, calls=%fused_computation.117 | convolution fusion | flops 201326592 | bytes 2490368 | tf_op jit(solution)/shard_map/dot_general | solution.py:138
  119.3 1.3 collective-permute-start.3
  120.6 6.9 %collective-permute-start.5 = (f32[256,128]{0,1:T(8,128)}, f32[256,128]{0,1:T(8,128)}, u32[]{:S(2)}, u32[]{:S(2)}) collective-permute-start(f32[256,128]{0,1:T(8,128)} %fusion.55), channel_id=1, source_target_pairs={{0,1},{1,2},{4,5},{5,6},{8,9},{9,10},{12,13},{13,14},{16,17},{17,1... | collective-permute-start | bytes 393224 | tf_op jit(solution)/shard_map/ppermute | solution.py:42
  127.5 1.3 collective-permute-start.4
  129.1 0.7 broadcast_in_dim.178
  129.8 3.3 %all-to-all-start.5 = ((f32[4,80,128]{2,1,0:T(8,128)}), f32[4,80,128]{2,1,0:T(8,128)S(1)}, u32[]{:S(2)}, u32[]{:S(2)}) async-start(f32[4,80,128]{2,1,0:T(8,128)} %broadcast_in_dim.178), calls=%async_computation.5 | async-start | bytes 327680 | tf_op jit(solution)/shard_map/all_to_all | solution.py:47
  133.2 2.4 %fusion.57 = f32[256,384]{1,0:T(8,128)S(1)} fusion(bf16[256,3072]{0,1:T(8,128)(2,1)} %bitcast.88, bf16[3072,384]{1,0:T(8,128)(2,1)S(1)} %copy-done), kind=kOutput, calls=%fused_computation.119 | convolution fusion | flops 603979776 | bytes 4325376 | tf_op jit(solution)/shard_map/dot_general | solution.py:169
  135.6 2.5 %all-to-all-done.5 = f32[4,80,128]{2,1,0:T(8,128)S(1)} async-done(((f32[4,80,128]{2,1,0:T(8,128)}), f32[4,80,128]{2,1,0:T(8,128)S(1)}, u32[]{:S(2)}, u32[]{:S(2)}) %all-to-all-start.5) | async-done | bytes 163872 | tf_op jit(solution)/shard_map/all_to_all | solution.py:47
  138.2 0.6 copy-done.2
  139.6 0.8 slice.125
  140.4 1.2 reduce-precision_bitcast_fusion
  141.6 0.3 fusion.31
  141.9 1.1 fusion.8
  143.0 0.4 fusion.54
  143.6 1.3 fusion.4
  144.9 0.8 copy.52
  (58 shorter events, 2.2 us)
Async XLA Ops:
  0.0 133.2 %copy-start = (bf16[3072,384]{1,0:T(8,128)(2,1)S(1)}, bf16[3072,384]{1,0:T(8,128)(2,1)}, u32[]{:S(2)}) copy-start(bf16[3072,384]{1,0:T(8,128)(2,1)} %param.10) | copy-start | bytes 7077892
  3.5 35.4 %all-to-all-start = ((s32[128,1,1]{2,1,0:T(1,128)}), s32[128,1,1]{2,1,0:T(1,128)S(1)}, u32[]{:S(2)}, u32[]{:S(2)}) async-start(s32[128,1,1]{2,1,0:T(1,128)} %broadcast_in_dim.108), calls=%async_computation | async-start | bytes 131072 | tf_op jit(solution)/shard_map/all_to_all | solution.py:47
  39.8 13.4 %all-to-all-start.1 = ((bf16[8,256,128]{2,1,0:T(8,128)(2,1)}), bf16[8,256,128]{2,1,0:T(8,128)(2,1)S(1)}, u32[]{:S(2)}, u32[]{:S(2)}) async-start(bf16[8,256,128]{2,1,0:T(8,128)(2,1)} %broadcast_in_dim.170), calls=%async_computation.1 | async-start | bytes 1048576 | tf_op jit(solution)/shard_map/all_to_all | solution.py:47
  46.9 10.9 %copy-start.1 = (bf16[256,768]{1,0:T(8,128)(2,1)S(1)}, bf16[256,768]{1,0:T(8,128)(2,1)}, u32[]{:S(2)}) copy-start(bf16[256,768]{1,0:T(8,128)(2,1)} %param.9) | copy-start | bytes 1179652
  54.3 29.3 %all-to-all-start.2 = ((bf16[4,2,256,128]{3,2,1,0:T(8,128)(2,1)}), bf16[4,2,256,128]{3,2,1,0:T(8,128)(2,1)S(1)}, u32[]{:S(2)}, u32[]{:S(2)}) async-start(bf16[4,2,256,128]{3,2,1,0:T(8,128)(2,1)} %broadcast_in_dim.173), calls=%async_computation.2 | async-start | bytes 1048576 | tf_op jit(solution)/shard_map/all_to_all | solution.py:47
  57.8 39.1 %collective-permute-start.2 = (bf16[256,768]{1,0:T(8,128)(2,1)S(1)}, bf16[256,768]{1,0:T(8,128)(2,1)}, u32[]{:S(2)}, u32[]{:S(2)}) collective-permute-start(bf16[256,768]{1,0:T(8,128)(2,1)S(1)} %copy-done.1), channel_id=1, source_target_pairs={{0,3},{1,0},{2,1},{3,2},{4,7},{5,4},{6,5},{7,6},{8,11},{9,8},{10,9... | collective-permute-start | bytes 1179656 | tf_op jit(solution)/shard_map/ppermute | solution.py:42
  62.2 34.7 %collective-permute-start.1 = (bf16[256,768]{1,0:T(8,128)(2,1)S(1)}, bf16[256,768]{1,0:T(8,128)(2,1)}, u32[]{:S(2)}, u32[]{:S(2)}) collective-permute-start(bf16[256,768]{1,0:T(8,128)(2,1)S(1)} %copy-done.1), channel_id=1, source_target_pairs={{0,2},{1,3},{2,0},{3,1},{4,6},{5,7},{6,4},{7,5},{8,10},{9,11},{10,... | collective-permute-start | bytes 1179656 | tf_op jit(solution)/shard_map/ppermute | solution.py:42
  64.6 32.2 %collective-permute-start = (bf16[256,768]{1,0:T(8,128)(2,1)S(1)}, bf16[256,768]{1,0:T(8,128)(2,1)}, u32[]{:S(2)}, u32[]{:S(2)}) collective-permute-start(bf16[256,768]{1,0:T(8,128)(2,1)S(1)} %copy-done.1), channel_id=1, source_target_pairs={{0,1},{1,2},{2,3},{3,0},{4,5},{5,6},{6,7},{7,4},{8,9},{9,10},{10,1... | collective-permute-start | bytes 1179656 | tf_op jit(solution)/shard_map/ppermute | solution.py:42
  84.5 18.1 %all-to-all-start.3 = ((bf16[4,2,256,128]{3,2,1,0:T(8,128)(2,1)}), bf16[4,2,256,128]{3,2,1,0:T(8,128)(2,1)S(1)}, u32[]{:S(2)}, u32[]{:S(2)}) async-start(bf16[4,2,256,128]{3,2,1,0:T(8,128)(2,1)} %broadcast_in_dim.174), calls=%async_computation.3 | async-start | bytes 1048576 | tf_op jit(solution)/shard_map/all_to_all | solution.py:47
  91.0 5.2 %copy-start.4 = (pred[256]{0:T(512)(128)(4,1)}, pred[256]{0:T(512)(128)(4,1)S(1)}, u32[]{:S(2)}) copy-start(pred[256]{0:T(512)(128)(4,1)S(1)} %iota_compare_fusion.3) | copy-start | bytes 772
  103.7 25.1 %all-to-all-start.4 = ((bf16[8,256,128]{2,1,0:T(8,128)(2,1)}), bf16[8,256,128]{2,1,0:T(8,128)(2,1)S(1)}, u32[]{:S(2)}, u32[]{:S(2)}) async-start(bf16[8,256,128]{2,1,0:T(8,128)(2,1)} %select_select_fusion), calls=%async_computation.4 | async-start | bytes 1048576 | tf_op jit(solution)/shard_map/all_to_all | solution.py:129
  119.3 21.1 %collective-permute-start.3 = (f32[256,128]{0,1:T(8,128)}, f32[256,128]{0,1:T(8,128)}, u32[]{:S(2)}, u32[]{:S(2)}) collective-permute-start(f32[256,128]{0,1:T(8,128)} %fusion.55), channel_id=1, source_target_pairs={{1,3},{2,0},{5,7},{6,4},{9,11},{10,8},{13,15},{14,12},{17,19},{18,... | collective-permute-start | bytes 393224 | tf_op jit(solution)/shard_map/ppermute | solution.py:42
  120.6 19.8 %collective-permute-start.5 = (f32[256,128]{0,1:T(8,128)}, f32[256,128]{0,1:T(8,128)}, u32[]{:S(2)}, u32[]{:S(2)}) collective-permute-start(f32[256,128]{0,1:T(8,128)} %fusion.55), channel_id=1, source_target_pairs={{0,1},{1,2},{4,5},{5,6},{8,9},{9,10},{12,13},{13,14},{16,17},{17,1... | collective-permute-start | bytes 393224 | tf_op jit(solution)/shard_map/ppermute | solution.py:42
  127.5 16.1 %collective-permute-start.4 = (f32[256,128]{0,1:T(8,128)}, f32[256,128]{0,1:T(8,128)}, u32[]{:S(2)}, u32[]{:S(2)}) collective-permute-start(f32[256,128]{0,1:T(8,128)} %fusion.55), channel_id=1, source_target_pairs={{2,1},{3,2},{6,5},{7,6},{10,9},{11,10},{14,13},{15,14},{18,17},{19... | collective-permute-start | bytes 393224 | tf_op jit(solution)/shard_map/ppermute | solution.py:42
  129.8 8.3 %all-to-all-start.5 = ((f32[4,80,128]{2,1,0:T(8,128)}), f32[4,80,128]{2,1,0:T(8,128)S(1)}, u32[]{:S(2)}, u32[]{:S(2)}) async-start(f32[4,80,128]{2,1,0:T(8,128)} %broadcast_in_dim.178), calls=%async_computation.5 | async-start | bytes 327680 | tf_op jit(solution)/shard_map/all_to_all | solution.py:47
  138.1 0.7 copy-start.2
  139.4 3.6 %copy-start.3 = (pred[256,256]{0,1:T(8,128)(4,1)S(1)}, pred[256,256]{0,1:T(8,128)(4,1)}, u32[]{:S(2)}) copy-start(pred[256,256]{0,1:T(8,128)(4,1)} %fusion.7) | copy-start | bytes 196612
  141.9 1.6 %copy-start.5 = (pred[256]{0:T(512)(128)(4,1)S(1)}, pred[256]{0:T(512)(128)(4,1)}, u32[]{:S(2)}) copy-start(pred[256]{0:T(512)(128)(4,1)} %copy-done.4) | copy-start | bytes 772

commit v15 on v14

--- a/solution.py
+++ b/solution.py
@@ -89,7 +89,6 @@
 
     own_slot = lookup_slots(adapter_ids, adapter_slot)
 
-    slots_all = gather_over(own_slot, ("zh", "zl", "ry"), n_req).reshape(n_req)
 
     down_rows = down_store[0].T.reshape(-1, 128)
     query_rows = query_up_store[0].reshape(-1, 128)
@@ -99,6 +98,8 @@
     row = jnp.concatenate([down_rows, query_rows, pair_rows], axis=0)
 
     plane = gather_over(row, "ry", ny)
+    own_slot, plane = lax.optimization_barrier((own_slot, plane))
+    slots_all = gather_over(own_slot, ("zh", "zl", "ry"), n_req).reshape(n_req)
     blocks = jnp.stack([states] + [shifted(states, s, n_tp) for s in range(1, n_tp)])
     source = (tp_index - jnp.arange(n_tp, dtype=jnp.int32)) % n_tp
     piece = jnp.take(blocks, source, axis=0)

time: 148 us -> 155 us (1.047)
  waiting for transfers between devices: 34.2 us -> 42.9 us
    all_to_all x5, waiting for transfers between devices: 34.2 us -> 42.9 us  [gather_over(): return lax.all_to_all(copies, axis, 0, 0, tiled=True)]
  transfers between devices with their start and end apart: 12 -> 12, of which waited for: 4 -> 5; matrix products, arithmetic and copies ran while one was open for 23% -> 18% of each run, Pallas kernels for 0% -> 0%
where the time goes in v15:
time: 155 us; the launch traced here: 153 us
  starting transfers between devices  63.7 us (41%)
  waiting for transfers between devices  42.9 us (28%)
  local copies, waits for them, and re-layouts  18.2 us (12%)
  other arithmetic  14.4 us (9%)
  matrix products  8.49 us (5%)
  between operations  5.67 us (4%)
    all_to_all x5, waiting for transfers between devices, gather_over(): return lax.all_to_all(copies, axis, 0, 0, tiled=True)  42.9 us
    all_to_all x5, starting transfers between devices, gather_over(): return lax.all_to_all(copies, axis, 0, 0, tiled=True)  36.9 us
    ppermute x6, starting transfers between devices, shifted(): return lax.ppermute(x, axis, pairs)  18.8 us
    all_to_all x1, starting transfers between devices, local(): received = lax.all_to_all(send, 'ry', 0, 0, tiled=True)  7.97 us
    broadcast_in_dim x5, local copies, waits for them, and re-layouts, gather_over(): copies = jnp.broadcast_to(x[None], (n,) + x.shape)  4.59 us
    gather x1, local copies, waits for them, and re-layouts, local(): piece = jnp.take(blocks, source, axis=0)  3.21 us
  transfers between devices with their start and end apart: 12, of which 5 were waited for; matrix products, arithmetic and copies ran while one was open for 18% of the time, Pallas kernels for 0%

profile of v15, /device:TPU:1, one launch (start us, length us, event | category | flops | bytes accessed | tf_op | source)
XLA Modules:
  0.0 153.4 jit_solution(1080149695621453217)
XLA Ops:
  0.0 0.9 reshape_squeeze.3
  0.9 0.9 reshape.461
  1.8 0.7 pad_maximum_fusion.1
  2.5 0.9 broadcast_in_dim.110
  3.3 10.3 %all-to-all-start = ((bf16[8,256,128]{2,1,0:T(8,128)(2,1)}), bf16[8,256,128]{2,1,0:T(8,128)(2,1)S(1)}, u32[]{:S(2)}, u32[]{:S(2)}) async-start(bf16[8,256,128]{2,1,0:T(8,128)(2,1)} %broadcast_in_dim.110), calls=%async_computation | async-start | bytes 1048576 | tf_op jit(solution)/shard_map/all_to_all | solution.py:47
  14.3 0.7 fusion.42
  15.0 8.1 %all-to-all-done = bf16[8,256,128]{2,1,0:T(8,128)(2,1)S(1)} async-done(((bf16[8,256,128]{2,1,0:T(8,128)(2,1)}), bf16[8,256,128]{2,1,0:T(8,128)(2,1)S(1)}, u32[]{:S(2)}, u32[]{:S(2)}) %all-to-all-start) | async-done | bytes 524320 | tf_op jit(solution)/shard_map/all_to_all | solution.py:47
  23.1 1.3 broadcast_in_dim.168
  24.4 13.6 %all-to-all-start.1 = ((s32[128,1,1]{2,1,0:T(1,128)}), s32[128,1,1]{2,1,0:T(1,128)S(1)}, u32[]{:S(2)}, u32[]{:S(2)}) async-start(s32[128,1,1]{2,1,0:T(1,128)} %broadcast_in_dim.168), calls=%async_computation.1 | async-start | bytes 131072 | tf_op jit(solution)/shard_map/all_to_all | solution.py:47
  38.0 14.8 %all-to-all-done.1 = s32[128,1,1]{2,1,0:T(1,128)S(1)} async-done(((s32[128,1,1]{2,1,0:T(1,128)}), s32[128,1,1]{2,1,0:T(1,128)S(1)}, u32[]{:S(2)}, u32[]{:S(2)}) %all-to-all-start.1) | async-done | bytes 544 | tf_op jit(solution)/shard_map/all_to_all | solution.py:47
  52.8 2.3 %reduce.7 = s32[128]{0:T(128)S(1)} reduce(s32[128,1,1]{2,1,0:T(1,128)S(1)} %all-to-all-done.1, s32[]{:T(128)} %constant.99.clone.1), dimensions={1,2}, to_apply=%all_to_all.20.reduce_sub_computation | reduce | bytes 1028 | tf_op jit(solution)/shard_map/all_to_all | solution.py:47
  55.4 0.7 gather_fusion.3
  56.1 0.6 gather_fusion.4
  57.1 0.9 broadcast_in_dim.176
  58.0 3.5 %all-to-all-start.2 = ((bf16[4,2,256,128]{3,2,1,0:T(8,128)(2,1)}), bf16[4,2,256,128]{3,2,1,0:T(8,128)(2,1)S(1)}, u32[]{:S(2)}, u32[]{:S(2)}) async-start(bf16[4,2,256,128]{3,2,1,0:T(8,128)(2,1)} %broadcast_in_dim.176), calls=%async_computation.2 | async-start | bytes 1048576 | tf_op jit(solution)/shard_map/all_to_all | solution.py:47
  61.4 4.4 %collective-permute-start.2 = (bf16[256,768]{1,0:T(8,128)(2,1)S(1)}, bf16[256,768]{1,0:T(8,128)(2,1)}, u32[]{:S(2)}, u32[]{:S(2)}) collective-permute-start(bf16[256,768]{1,0:T(8,128)(2,1)S(1)} %copy-done.1), channel_id=1, source_target_pairs={{0,3},{1,0},{2,1},{3,2},{4,7},{5,4},{6,5},{7,6},{8,11},{9,8},{10,9... | collective-permute-start | bytes 1179656 | tf_op jit(solution)/shard_map/ppermute | solution.py:42
  65.8 2.4 %collective-permute-start.1 = (bf16[256,768]{1,0:T(8,128)(2,1)S(1)}, bf16[256,768]{1,0:T(8,128)(2,1)}, u32[]{:S(2)}, u32[]{:S(2)}) collective-permute-start(bf16[256,768]{1,0:T(8,128)(2,1)S(1)} %copy-done.1), channel_id=1, source_target_pairs={{0,2},{1,3},{2,0},{3,1},{4,6},{5,7},{6,4},{7,5},{8,10},{9,11},{10,... | collective-permute-start | bytes 1179656 | tf_op jit(solution)/shard_map/ppermute | solution.py:42
  68.3 2.5 %collective-permute-start = (bf16[256,768]{1,0:T(8,128)(2,1)S(1)}, bf16[256,768]{1,0:T(8,128)(2,1)}, u32[]{:S(2)}, u32[]{:S(2)}) collective-permute-start(bf16[256,768]{1,0:T(8,128)(2,1)S(1)} %copy-done.1), channel_id=1, source_target_pairs={{0,1},{1,2},{2,3},{3,0},{4,5},{5,6},{6,7},{7,4},{8,9},{9,10},{10,1... | collective-permute-start | bytes 1179656 | tf_op jit(solution)/shard_map/ppermute | solution.py:42
  71.5 15.8 %all-to-all-done.2 = bf16[4,2,256,128]{3,2,1,0:T(8,128)(2,1)S(1)} async-done(((bf16[4,2,256,128]{3,2,1,0:T(8,128)(2,1)}), bf16[4,2,256,128]{3,2,1,0:T(8,128)(2,1)S(1)}, u32[]{:S(2)}, u32[]{:S(2)}) %all-to-all-start.2) | async-done | bytes 524320 | tf_op jit(solution)/shard_map/all_to_all | solution.py:47
  87.4 0.9 broadcast_in_dim.177
  88.2 6.2 %all-to-all-start.3 = ((bf16[4,2,256,128]{3,2,1,0:T(8,128)(2,1)}), bf16[4,2,256,128]{3,2,1,0:T(8,128)(2,1)S(1)}, u32[]{:S(2)}, u32[]{:S(2)}) async-start(bf16[4,2,256,128]{3,2,1,0:T(8,128)(2,1)} %broadcast_in_dim.177), calls=%async_computation.3 | async-start | bytes 1048576 | tf_op jit(solution)/shard_map/all_to_all | solution.py:47
  94.5 0.7 fusion.7
  95.2 1.2 multiply_cosine_fusion
  96.5 2.6 %pad_maximum_fusion = bf16[4,256,768]{2,1,0:T(8,128)(2,1)} fusion(bf16[1,256,768]{2,1,0:T(8,128)(2,1)} %bitcast.4, bf16[1,256,768]{2,1,0:T(8,128)(2,1)} %bitcast.3, bf16[1,256,768]{2,1,0:T(8,128)(2,1)} %bitcast.2, bf16[1,256,768]{2,1,0:T(8,128)(2,1)S(1)} %bitcast.91), kind=kLoop, calls=%fused_computation.5 | loop fusion | flops 2359296 | bytes 3145728 | tf_op jit(solution)/shard_map/stack | solution.py:103
  99.1 3.2 %gather_fusion = bf16[4,256,768]{2,1,0:T(8,128)(2,1)} fusion(bf16[4,256,768]{2,1,0:T(8,128)(2,1)} %pad_maximum_fusion, s32[1024]{0:T(1024)S(1)} %pad_clamp_fusion.2), kind=kCustom, calls=%fused_computation | custom fusion | bytes 3145744 | tf_op jit(solution)/shard_map/jit(_take)/gather | solution.py:105
  102.3 0.6 gather_fusion.1
  103.0 0.6 gather_fusion.2
  103.6 1.7 %all-to-all-done.3 = bf16[4,2,256,128]{3,2,1,0:T(8,128)(2,1)S(1)} async-done(((bf16[4,2,256,128]{3,2,1,0:T(8,128)(2,1)}), bf16[4,2,256,128]{3,2,1,0:T(8,128)(2,1)S(1)}, u32[]{:S(2)}, u32[]{:S(2)}) %all-to-all-start.3) | async-done | bytes 524320 | tf_op jit(solution)/shard_map/all_to_all | solution.py:47
  105.4 0.9 select_select_fusion
  106.4 8.0 %all-to-all-start.4 = ((bf16[8,256,128]{2,1,0:T(8,128)(2,1)}), bf16[8,256,128]{2,1,0:T(8,128)(2,1)S(1)}, u32[]{:S(2)}, u32[]{:S(2)}) async-start(bf16[8,256,128]{2,1,0:T(8,128)(2,1)} %select_select_fusion), calls=%async_computation.4 | async-start | bytes 1048576 | tf_op jit(solution)/shard_map/all_to_all | solution.py:130
  114.3 2.8 %select_bitcast_fusion = bf16[256,4,768]{2,0,1:T(8,128)(2,1)} fusion(bf16[4,256,768]{2,1,0:T(8,128)(2,1)} %gather_fusion, pred[4]{0:T(512)(128)(4,1)S(1)} %compare_and_fusion.1), kind=kLoop, calls=%fused_computation.6 | loop fusion | flops 786432 | bytes 3145732 | tf_op jit(solution)/shard_map/jit(_take)/select_n | solution.py:105
  117.1 2.6 %copy.45 = bf16[256,4,768]{0,2,1:T(8,128)(2,1)} copy(bf16[256,4,768]{2,0,1:T(8,128)(2,1)} %select_bitcast_fusion) | data formatting | bytes 3145728 | tf_op jit(solution)/shard_map/jit(_take)/select_n | solution.py:105
  119.7 2.7 %fusion.55 = f32[256,128]{0,1:T(8,128)} fusion(bf16[256,3072]{0,1:T(8,128)(2,1)} %bitcast.89, bf16[3072,128]{1,0:T(8,128)(2,1)} %param.11), kind=kOutput, calls=%fused_computation.117 | convolution fusion | flops 201326592 | bytes 2490368 | tf_op jit(solution)/shard_map/dot_general | solution.py:139
  122.4 1.3 collective-permute-start.3
  123.7 6.9 %collective-permute-start.5 = (f32[256,128]{0,1:T(8,128)}, f32[256,128]{0,1:T(8,128)}, u32[]{:S(2)}, u32[]{:S(2)}) collective-permute-start(f32[256,128]{0,1:T(8,128)} %fusion.55), channel_id=1, source_target_pairs={{0,1},{1,2},{4,5},{5,6},{8,9},{9,10},{12,13},{13,14},{16,17},{17,1... | collective-permute-start | bytes 393224 | tf_op jit(solution)/shard_map/ppermute | solution.py:42
  130.6 1.3 collective-permute-start.4
  134.0 0.6 dynamic_slice.12
  136.9 0.7 broadcast_in_dim.181
  137.6 3.3 %all-to-all-start.5 = ((f32[4,80,128]{2,1,0:T(8,128)}), f32[4,80,128]{2,1,0:T(8,128)S(1)}, u32[]{:S(2)}, u32[]{:S(2)}) async-start(f32[4,80,128]{2,1,0:T(8,128)} %broadcast_in_dim.181), calls=%async_computation.5 | async-start | bytes 327680 | tf_op jit(solution)/shard_map/all_to_all | solution.py:47
  140.9 2.4 %fusion.57 = f32[256,384]{1,0:T(8,128)S(1)} fusion(bf16[256,3072]{0,1:T(8,128)(2,1)} %bitcast.90, bf16[3072,384]{1,0:T(8,128)(2,1)S(1)} %copy-done), kind=kOutput, calls=%fused_computation.119 | convolution fusion | flops 603979776 | bytes 4325376 | tf_op jit(solution)/shard_map/dot_general | solution.py:170
  143.4 2.5 %all-to-all-done.5 = f32[4,80,128]{2,1,0:T(8,128)S(1)} async-done(((f32[4,80,128]{2,1,0:T(8,128)}), f32[4,80,128]{2,1,0:T(8,128)S(1)}, u32[]{:S(2)}, u32[]{:S(2)}) %all-to-all-start.5) | async-done | bytes 163872 | tf_op jit(solution)/shard_map/all_to_all | solution.py:47
  145.9 0.6 copy-done.2
  147.4 0.8 slice.125
  148.2 1.2 reduce-precision_bitcast_fusion
  149.7 1.1 fusion.8
  150.8 0.4 fusion.54
  151.3 1.3 fusion.4
  152.6 0.8 copy.52
  (60 shorter events, 2.5 us)
Async XLA Ops:
  0.0 140.9 %copy-start = (bf16[3072,384]{1,0:T(8,128)(2,1)S(1)}, bf16[3072,384]{1,0:T(8,128)(2,1)}, u32[]{:S(2)}) copy-start(bf16[3072,384]{1,0:T(8,128)(2,1)} %param.10) | copy-start | bytes 7077892
  0.0 14.3 %copy-start.6 = (s32[64]{0:T(128)S(1)}, s32[64]{0:T(128)}, u32[]{:S(2)}) copy-start(s32[64]{0:T(128)} %param.14) | copy-start | bytes 772
  3.3 19.8 %all-to-all-start = ((bf16[8,256,128]{2,1,0:T(8,128)(2,1)}), bf16[8,256,128]{2,1,0:T(8,128)(2,1)S(1)}, u32[]{:S(2)}, u32[]{:S(2)}) async-start(bf16[8,256,128]{2,1,0:T(8,128)(2,1)} %broadcast_in_dim.110), calls=%async_computation | async-start | bytes 1048576 | tf_op jit(solution)/shard_map/all_to_all | solution.py:47
  24.4 28.4 %all-to-all-start.1 = ((s32[128,1,1]{2,1,0:T(1,128)}), s32[128,1,1]{2,1,0:T(1,128)S(1)}, u32[]{:S(2)}, u32[]{:S(2)}) async-start(s32[128,1,1]{2,1,0:T(1,128)} %broadcast_in_dim.168), calls=%async_computation.1 | async-start | bytes 131072 | tf_op jit(solution)/shard_map/all_to_all | solution.py:47
  56.1 5.4 %copy-start.1 = (bf16[256,768]{1,0:T(8,128)(2,1)S(1)}, bf16[256,768]{1,0:T(8,128)(2,1)}, u32[]{:S(2)}) copy-start(bf16[256,768]{1,0:T(8,128)(2,1)} %param.9) | copy-start | bytes 1179652
  58.0 29.3 %all-to-all-start.2 = ((bf16[4,2,256,128]{3,2,1,0:T(8,128)(2,1)}), bf16[4,2,256,128]{3,2,1,0:T(8,128)(2,1)S(1)}, u32[]{:S(2)}, u32[]{:S(2)}) async-start(bf16[4,2,256,128]{3,2,1,0:T(8,128)(2,1)} %broadcast_in_dim.176), calls=%async_computation.2 | async-start | bytes 1048576 | tf_op jit(solution)/shard_map/all_to_all | solution.py:47
  61.4 35.0 %collective-permute-start.2 = (bf16[256,768]{1,0:T(8,128)(2,1)S(1)}, bf16[256,768]{1,0:T(8,128)(2,1)}, u32[]{:S(2)}, u32[]{:S(2)}) collective-permute-start(bf16[256,768]{1,0:T(8,128)(2,1)S(1)} %copy-done.1), channel_id=1, source_target_pairs={{0,3},{1,0},{2,1},{3,2},{4,7},{5,4},{6,5},{7,6},{8,11},{9,8},{10,9... | collective-permute-start | bytes 1179656 | tf_op jit(solution)/shard_map/ppermute | solution.py:42
  65.8 30.7 %collective-permute-start.1 = (bf16[256,768]{1,0:T(8,128)(2,1)S(1)}, bf16[256,768]{1,0:T(8,128)(2,1)}, u32[]{:S(2)}, u32[]{:S(2)}) collective-permute-start(bf16[256,768]{1,0:T(8,128)(2,1)S(1)} %copy-done.1), channel_id=1, source_target_pairs={{0,2},{1,3},{2,0},{3,1},{4,6},{5,7},{6,4},{7,5},{8,10},{9,11},{10,... | collective-permute-start | bytes 1179656 | tf_op jit(solution)/shard_map/ppermute | solution.py:42
  68.3 28.2 %collective-permute-start = (bf16[256,768]{1,0:T(8,128)(2,1)S(1)}, bf16[256,768]{1,0:T(8,128)(2,1)}, u32[]{:S(2)}, u32[]{:S(2)}) collective-permute-start(bf16[256,768]{1,0:T(8,128)(2,1)S(1)} %copy-done.1), channel_id=1, source_target_pairs={{0,1},{1,2},{2,3},{3,0},{4,5},{5,6},{6,7},{7,4},{8,9},{9,10},{10,1... | collective-permute-start | bytes 1179656 | tf_op jit(solution)/shard_map/ppermute | solution.py:42
  88.2 17.1 %all-to-all-start.3 = ((bf16[4,2,256,128]{3,2,1,0:T(8,128)(2,1)}), bf16[4,2,256,128]{3,2,1,0:T(8,128)(2,1)S(1)}, u32[]{:S(2)}, u32[]{:S(2)}) async-start(bf16[4,2,256,128]{3,2,1,0:T(8,128)(2,1)} %broadcast_in_dim.177), calls=%async_computation.3 | async-start | bytes 1048576 | tf_op jit(solution)/shard_map/all_to_all | solution.py:47
  94.5 4.6 %copy-start.4 = (pred[256]{0:T(512)(128)(4,1)}, pred[256]{0:T(512)(128)(4,1)S(1)}, u32[]{:S(2)}) copy-start(pred[256]{0:T(512)(128)(4,1)S(1)} %iota_compare_fusion.3) | copy-start | bytes 772
  106.4 30.1 %all-to-all-start.4 = ((bf16[8,256,128]{2,1,0:T(8,128)(2,1)}), bf16[8,256,128]{2,1,0:T(8,128)(2,1)S(1)}, u32[]{:S(2)}, u32[]{:S(2)}) async-start(bf16[8,256,128]{2,1,0:T(8,128)(2,1)} %select_select_fusion), calls=%async_computation.4 | async-start | bytes 1048576 | tf_op jit(solution)/shard_map/all_to_all | solution.py:130
  122.4 25.7 %collective-permute-start.3 = (f32[256,128]{0,1:T(8,128)}, f32[256,128]{0,1:T(8,128)}, u32[]{:S(2)}, u32[]{:S(2)}) collective-permute-start(f32[256,128]{0,1:T(8,128)} %fusion.55), channel_id=1, source_target_pairs={{1,3},{2,0},{5,7},{6,4},{9,11},{10,8},{13,15},{14,12},{17,19},{18,... | collective-permute-start | bytes 393224 | tf_op jit(solution)/shard_map/ppermute | solution.py:42
  123.7 24.5 %collective-permute-start.5 = (f32[256,128]{0,1:T(8,128)}, f32[256,128]{0,1:T(8,128)}, u32[]{:S(2)}, u32[]{:S(2)}) collective-permute-start(f32[256,128]{0,1:T(8,128)} %fusion.55), channel_id=1, source_target_pairs={{0,1},{1,2},{4,5},{5,6},{8,9},{9,10},{12,13},{13,14},{16,17},{17,1... | collective-permute-start | bytes 393224 | tf_op jit(solution)/shard_map/ppermute | solution.py:42
  130.6 20.7 %collective-permute-start.4 = (f32[256,128]{0,1:T(8,128)}, f32[256,128]{0,1:T(8,128)}, u32[]{:S(2)}, u32[]{:S(2)}) collective-permute-start(f32[256,128]{0,1:T(8,128)} %fusion.55), channel_id=1, source_target_pairs={{2,1},{3,2},{6,5},{7,6},{10,9},{11,10},{14,13},{15,14},{18,17},{19... | collective-permute-start | bytes 393224 | tf_op jit(solution)/shard_map/ppermute | solution.py:42
  137.6 8.3 %all-to-all-start.5 = ((f32[4,80,128]{2,1,0:T(8,128)}), f32[4,80,128]{2,1,0:T(8,128)S(1)}, u32[]{:S(2)}, u32[]{:S(2)}) async-start(f32[4,80,128]{2,1,0:T(8,128)} %broadcast_in_dim.181), calls=%async_computation.5 | async-start | bytes 327680 | tf_op jit(solution)/shard_map/all_to_all | solution.py:47
  145.9 0.7 copy-start.2
  147.2 3.6 %copy-start.3 = (pred[256,256]{0,1:T(8,128)(4,1)S(1)}, pred[256,256]{0,1:T(8,128)(4,1)}, u32[]{:S(2)}) copy-start(pred[256,256]{0,1:T(8,128)(4,1)} %fusion.7) | copy-start | bytes 196612
  149.7 1.6 %copy-start.5 = (pred[256]{0:T(512)(128)(4,1)S(1)}, pred[256]{0:T(512)(128)(4,1)}, u32[]{:S(2)}) copy-start(pred[256]{0:T(512)(128)(4,1)} %copy-done.4) | copy-start | bytes 772

commit v16 on v14

--- a/solution.py
+++ b/solution.py
@@ -210,7 +210,7 @@
 def solution(mesh):
     n_req = mesh.shape["req"]
     ny = 8 if n_req % 8 == 0 else 1
-    n_low = 4 if (n_req // ny) % 4 == 0 else 1
+    n_low = 2 if (n_req // ny) % 2 == 0 else 1
     split = jax.sharding.Mesh(
         mesh.devices.reshape(n_req // ny // n_low, n_low, ny, mesh.shape["tp"]),
         ("zh", "zl", "ry", "tp"),

time: 148 us -> 169 us (1.14)
  waiting for transfers between devices: 34.2 us -> 48.5 us
  starting transfers between devices: 64 us -> 67.7 us
  matrix products: 8.47 us -> 10.9 us
  other arithmetic: 15.1 us -> 16.8 us
    all_to_all x5, waiting for transfers between devices: 34.2 us -> 48.4 us  [gather_over(): return lax.all_to_all(copies, axis, 0, 0, tiled=True)]
    all_to_all x1, starting transfers between devices: 7.55 us -> 11.9 us  [local(): received = lax.all_to_all(send, 'ry', 0, 0, tiled=True)]
  transfers between devices with their start and end apart: 12 -> 12, of which waited for: 4 -> 4; matrix products, arithmetic and copies ran while one was open for 23% -> 22% of each run, Pallas kernels for 0% -> 0%
where the time goes in v16:
time: 169 us; the launch traced here: 167 us
  starting transfers between devices  67.7 us (40%)
  waiting for transfers between devices  48.5 us (29%)
  local copies, waits for them, and re-layouts  17.2 us (10%)
  other arithmetic  16.8 us (10%)
  matrix products  10.9 us (6%)
  between operations  5.38 us (3%)
    all_to_all x5, waiting for transfers between devices, gather_over(): return lax.all_to_all(copies, axis, 0, 0, tiled=True)  48.4 us
    all_to_all x5, starting transfers between devices, gather_over(): return lax.all_to_all(copies, axis, 0, 0, tiled=True)  38.3 us
    ppermute x6, starting transfers between devices, shifted(): return lax.ppermute(x, axis, pairs)  17.5 us
    all_to_all x1, starting transfers between devices, local(): received = lax.all_to_all(send, 'ry', 0, 0, tiled=True)  11.9 us
    broadcast_in_dim x5, local copies, waits for them, and re-layouts, gather_over(): copies = jnp.broadcast_to(x[None], (n,) + x.shape)  4.71 us
  transfers between devices with their start and end apart: 12, of which 4 were waited for; matrix products, arithmetic and copies ran while one was open for 22% of the time, Pallas kernels for 0%

profile of v16, /device:TPU:1, one launch (start us, length us, event | category | flops | bytes accessed | tf_op | source)
XLA Modules:
  0.0 166.5 jit_solution(17050452666778322328)
XLA Ops:
  0.8 1.3 fusion.42
  2.1 1.3 broadcast_in_dim.108
  3.4 20.6 %all-to-all-start = ((s32[128,1,1]{2,1,0:T(1,128)}), s32[128,1,1]{2,1,0:T(1,128)S(1)}, u32[]{:S(2)}, u32[]{:S(2)}) async-start(s32[128,1,1]{2,1,0:T(1,128)} %broadcast_in_dim.108), calls=%async_computation | async-start | bytes 131072 | tf_op jit(solution)/shard_map/all_to_all | solution.py:47
  24.0 0.7 reshape_squeeze.3
  24.7 0.9 reshape.463
  25.6 0.7 pad_maximum_fusion.1
  26.3 12.5 %all-to-all-done = s32[128,1,1]{2,1,0:T(1,128)S(1)} async-done(((s32[128,1,1]{2,1,0:T(1,128)}), s32[128,1,1]{2,1,0:T(1,128)S(1)}, u32[]{:S(2)}, u32[]{:S(2)}) %all-to-all-start) | async-done | bytes 544 | tf_op jit(solution)/shard_map/all_to_all | solution.py:47
  38.8 0.9 broadcast_in_dim.170
  39.7 3.9 %all-to-all-start.1 = ((bf16[8,256,128]{2,1,0:T(8,128)(2,1)}), bf16[8,256,128]{2,1,0:T(8,128)(2,1)S(1)}, u32[]{:S(2)}, u32[]{:S(2)}) async-start(bf16[8,256,128]{2,1,0:T(8,128)(2,1)} %broadcast_in_dim.170), calls=%async_computation.1 | async-start | bytes 1048576 | tf_op jit(solution)/shard_map/all_to_all | solution.py:47
  43.6 2.3 %reduce.7 = s32[128]{0:T(128)S(1)} reduce(s32[128,1,1]{2,1,0:T(1,128)S(1)} %all-to-all-done, s32[]{:T(128)} %constant.100.clone.1), dimensions={1,2}, to_apply=%all_to_all.19.reduce_sub_computation | reduce | bytes 1028 | tf_op jit(solution)/shard_map/all_to_all | solution.py:47
  46.1 0.7 gather_fusion.3
  46.8 0.6 gather_fusion.4
  47.5 5.5 %all-to-all-done.1 = bf16[8,256,128]{2,1,0:T(8,128)(2,1)S(1)} async-done(((bf16[8,256,128]{2,1,0:T(8,128)(2,1)}), bf16[8,256,128]{2,1,0:T(8,128)(2,1)S(1)}, u32[]{:S(2)}, u32[]{:S(2)}) %all-to-all-start.1) | async-done | bytes 524320 | tf_op jit(solution)/shard_map/all_to_all | solution.py:47
  53.3 1.2 broadcast_in_dim.173
  54.5 3.6 %all-to-all-start.2 = ((bf16[8,2,256,128]{3,2,1,0:T(8,128)(2,1)}), bf16[8,2,256,128]{3,2,1,0:T(8,128)(2,1)S(1)}, u32[]{:S(2)}, u32[]{:S(2)}) async-start(bf16[8,2,256,128]{3,2,1,0:T(8,128)(2,1)} %broadcast_in_dim.173), calls=%async_computation.2 | async-start | bytes 2097152 | tf_op jit(solution)/shard_map/all_to_all | solution.py:47
  58.1 4.7 %collective-permute-start.1 = (bf16[256,768]{1,0:T(8,128)(2,1)}, bf16[256,768]{1,0:T(8,128)(2,1)}, u32[]{:S(2)}, u32[]{:S(2)}) collective-permute-start(bf16[256,768]{1,0:T(8,128)(2,1)} %param.9), channel_id=1, source_target_pairs={{0,2},{1,3},{2,0},{3,1},{4,6},{5,7},{6,4},{7,5},{8,10},{9,11},{10,... | collective-permute-start | bytes 1179656 | tf_op jit(solution)/shard_map/ppermute | solution.py:42
  62.7 2.2 %collective-permute-start = (bf16[256,768]{1,0:T(8,128)(2,1)}, bf16[256,768]{1,0:T(8,128)(2,1)}, u32[]{:S(2)}, u32[]{:S(2)}) collective-permute-start(bf16[256,768]{1,0:T(8,128)(2,1)} %param.9), channel_id=1, source_target_pairs={{0,1},{1,2},{2,3},{3,0},{4,5},{5,6},{6,7},{7,4},{8,9},{9,10},{10,1... | collective-permute-start | bytes 1179656 | tf_op jit(solution)/shard_map/ppermute | solution.py:42
  65.0 4.3 %collective-permute-start.2 = (bf16[256,768]{1,0:T(8,128)(2,1)}, bf16[256,768]{1,0:T(8,128)(2,1)}, u32[]{:S(2)}, u32[]{:S(2)}) collective-permute-start(bf16[256,768]{1,0:T(8,128)(2,1)} %param.9), channel_id=1, source_target_pairs={{0,3},{1,0},{2,1},{3,2},{4,7},{5,4},{6,5},{7,6},{8,11},{9,8},{10,9... | collective-permute-start | bytes 1179656 | tf_op jit(solution)/shard_map/ppermute | solution.py:42
  72.3 0.7 fusion.7
  73.1 1.2 multiply_cosine_fusion
  74.3 1.1 gather_fusion.1
  75.4 28.6 %all-to-all-done.2 = bf16[8,2,256,128]{3,2,1,0:T(8,128)(2,1)S(1)} async-done(((bf16[8,2,256,128]{3,2,1,0:T(8,128)(2,1)}), bf16[8,2,256,128]{3,2,1,0:T(8,128)(2,1)S(1)}, u32[]{:S(2)}, u32[]{:S(2)}) %all-to-all-start.2) | async-done | bytes 1048608 | tf_op jit(solution)/shard_map/all_to_all | solution.py:47
  104.2 0.7 broadcast_in_dim.174
  104.9 5.4 %all-to-all-start.3 = ((bf16[2,2,256,128]{3,2,1,0:T(8,128)(2,1)}), bf16[2,2,256,128]{3,2,1,0:T(8,128)(2,1)S(1)}, u32[]{:S(2)}, u32[]{:S(2)}) async-start(bf16[2,2,256,128]{3,2,1,0:T(8,128)(2,1)} %broadcast_in_dim.174), calls=%async_computation.3 | async-start | bytes 524288 | tf_op jit(solution)/shard_map/all_to_all | solution.py:47
  110.4 0.6 fusion.48
  110.9 0.5 dynamic_slice.12
  113.1 0.6 gather_fusion.2
  113.8 2.6 %pad_maximum_fusion = bf16[4,256,768]{2,1,0:T(8,128)(2,1)} fusion(bf16[1,256,768]{2,1,0:T(8,128)(2,1)} %bitcast.4, bf16[1,256,768]{2,1,0:T(8,128)(2,1)} %bitcast.3, bf16[1,256,768]{2,1,0:T(8,128)(2,1)} %bitcast.2, bf16[1,256,768]{2,1,0:T(8,128)(2,1)S(1)} %bitcast.89), kind=kLoop, calls=%fused_computation.5 | loop fusion | flops 2359296 | bytes 3145728 | tf_op jit(solution)/shard_map/stack | solution.py:102
  116.4 3.2 %gather_fusion = bf16[4,256,768]{2,1,0:T(8,128)(2,1)} fusion(bf16[4,256,768]{2,1,0:T(8,128)(2,1)} %pad_maximum_fusion, s32[1024]{0:T(1024)S(1)} %pad_clamp_fusion.2), kind=kCustom, calls=%fused_computation | custom fusion | bytes 3145744 | tf_op jit(solution)/shard_map/jit(_take)/gather | solution.py:104
  119.7 0.9 select_select_fusion
  120.6 11.9 %all-to-all-start.4 = ((bf16[8,256,128]{2,1,0:T(8,128)(2,1)}), bf16[8,256,128]{2,1,0:T(8,128)(2,1)S(1)}, u32[]{:S(2)}, u32[]{:S(2)}) async-start(bf16[8,256,128]{2,1,0:T(8,128)(2,1)} %select_select_fusion), calls=%async_computation.4 | async-start | bytes 1048576 | tf_op jit(solution)/shard_map/all_to_all | solution.py:129
  132.6 2.8 %select_bitcast_fusion = bf16[256,4,768]{2,0,1:T(8,128)(2,1)} fusion(bf16[4,256,768]{2,1,0:T(8,128)(2,1)} %gather_fusion, pred[4]{0:T(512)(128)(4,1)S(1)} %copy-done.9), kind=kLoop, calls=%fused_computation.6 | loop fusion | flops 786432 | bytes 3145732 | tf_op jit(solution)/shard_map/jit(_take)/select_n | solution.py:104
  135.3 2.6 %copy.45 = bf16[256,4,768]{0,2,1:T(8,128)(2,1)} copy(bf16[256,4,768]{2,0,1:T(8,128)(2,1)} %select_bitcast_fusion) | data formatting | bytes 3145728 | tf_op jit(solution)/shard_map/jit(_take)/select_n | solution.py:104
  137.9 2.7 %fusion.55 = f32[256,128]{0,1:T(8,128)} fusion(bf16[256,3072]{0,1:T(8,128)(2,1)} %bitcast.87, bf16[3072,128]{1,0:T(8,128)(2,1)} %param.11), kind=kOutput, calls=%fused_computation.117 | convolution fusion | flops 201326592 | bytes 2490368 | tf_op jit(solution)/shard_map/dot_general | solution.py:138
  140.6 3.8 %collective-permute-start.5 = (f32[256,128]{0,1:T(8,128)}, f32[256,128]{0,1:T(8,128)}, u32[]{:S(2)}, u32[]{:S(2)}) collective-permute-start(f32[256,128]{0,1:T(8,128)} %fusion.55), channel_id=1, source_target_pairs={{0,1},{1,2},{4,5},{5,6},{8,9},{9,10},{12,13},{13,14},{16,17},{17,1... | collective-permute-start | bytes 393224 | tf_op jit(solution)/shard_map/ppermute | solution.py:42
  144.4 1.3 collective-permute-start.4
  145.7 1.3 collective-permute-start.3
  147.4 0.7 broadcast_in_dim.178
  148.1 4.9 %all-to-all-start.5 = ((f32[4,80,128]{2,1,0:T(8,128)}), f32[4,80,128]{2,1,0:T(8,128)S(1)}, u32[]{:S(2)}, u32[]{:S(2)}) async-start(f32[4,80,128]{2,1,0:T(8,128)} %broadcast_in_dim.178), calls=%async_computation.5 | async-start | bytes 327680 | tf_op jit(solution)/shard_map/all_to_all | solution.py:47
  152.9 3.2 %fusion.57 = f32[256,384]{1,0:T(8,128)} fusion(bf16[256,3072]{0,1:T(8,128)(2,1)} %bitcast.88, bf16[3072,384]{1,0:T(8,128)(2,1)S(1)} %copy-done), kind=kOutput, calls=%fused_computation.119 | convolution fusion | flops 603979776 | bytes 4325376 | tf_op jit(solution)/shard_map/dot_general | solution.py:169
  156.1 1.8 %all-to-all-done.5 = f32[4,80,128]{2,1,0:T(8,128)S(1)} async-done(((f32[4,80,128]{2,1,0:T(8,128)}), f32[4,80,128]{2,1,0:T(8,128)S(1)}, u32[]{:S(2)}, u32[]{:S(2)}) %all-to-all-start.5) | async-done | bytes 163872 | tf_op jit(solution)/shard_map/all_to_all | solution.py:47
  158.0 1.2 reduce-precision_bitcast_fusion
  159.3 1.0 fusion.31
  160.2 1.2 fusion.2
  162.1 1.1 fusion.8
  163.2 1.3 fusion.54
  164.6 1.1 fusion.4
  165.7 0.8 copy.52
  (66 shorter events, 2.5 us)
Async XLA Ops:
  0.0 152.9 %copy-start = (bf16[3072,384]{1,0:T(8,128)(2,1)S(1)}, bf16[3072,384]{1,0:T(8,128)(2,1)}, u32[]{:S(2)}) copy-start(bf16[3072,384]{1,0:T(8,128)(2,1)} %param.10) | copy-start | bytes 7077892
  3.4 35.4 %all-to-all-start = ((s32[128,1,1]{2,1,0:T(1,128)}), s32[128,1,1]{2,1,0:T(1,128)S(1)}, u32[]{:S(2)}, u32[]{:S(2)}) async-start(s32[128,1,1]{2,1,0:T(1,128)} %broadcast_in_dim.108), calls=%async_computation | async-start | bytes 131072 | tf_op jit(solution)/shard_map/all_to_all | solution.py:47
  39.7 13.4 %all-to-all-start.1 = ((bf16[8,256,128]{2,1,0:T(8,128)(2,1)}), bf16[8,256,128]{2,1,0:T(8,128)(2,1)S(1)}, u32[]{:S(2)}, u32[]{:S(2)}) async-start(bf16[8,256,128]{2,1,0:T(8,128)(2,1)} %broadcast_in_dim.170), calls=%async_computation.1 | async-start | bytes 1048576 | tf_op jit(solution)/shard_map/all_to_all | solution.py:47
  54.5 49.5 %all-to-all-start.2 = ((bf16[8,2,256,128]{3,2,1,0:T(8,128)(2,1)}), bf16[8,2,256,128]{3,2,1,0:T(8,128)(2,1)S(1)}, u32[]{:S(2)}, u32[]{:S(2)}) async-start(bf16[8,2,256,128]{3,2,1,0:T(8,128)(2,1)} %broadcast_in_dim.173), calls=%async_computation.2 | async-start | bytes 2097152 | tf_op jit(solution)/shard_map/all_to_all | solution.py:47
  58.1 55.8 %collective-permute-start.1 = (bf16[256,768]{1,0:T(8,128)(2,1)}, bf16[256,768]{1,0:T(8,128)(2,1)}, u32[]{:S(2)}, u32[]{:S(2)}) collective-permute-start(bf16[256,768]{1,0:T(8,128)(2,1)} %param.9), channel_id=1, source_target_pairs={{0,2},{1,3},{2,0},{3,1},{4,6},{5,7},{6,4},{7,5},{8,10},{9,11},{10,... | collective-permute-start | bytes 1179656 | tf_op jit(solution)/shard_map/ppermute | solution.py:42
  62.7 51.1 %collective-permute-start = (bf16[256,768]{1,0:T(8,128)(2,1)}, bf16[256,768]{1,0:T(8,128)(2,1)}, u32[]{:S(2)}, u32[]{:S(2)}) collective-permute-start(bf16[256,768]{1,0:T(8,128)(2,1)} %param.9), channel_id=1, source_target_pairs={{0,1},{1,2},{2,3},{3,0},{4,5},{5,6},{6,7},{7,4},{8,9},{9,10},{10,1... | collective-permute-start | bytes 1179656 | tf_op jit(solution)/shard_map/ppermute | solution.py:42
  65.0 48.9 %collective-permute-start.2 = (bf16[256,768]{1,0:T(8,128)(2,1)}, bf16[256,768]{1,0:T(8,128)(2,1)}, u32[]{:S(2)}, u32[]{:S(2)}) collective-permute-start(bf16[256,768]{1,0:T(8,128)(2,1)} %param.9), channel_id=1, source_target_pairs={{0,3},{1,0},{2,1},{3,2},{4,7},{5,4},{6,5},{7,6},{8,11},{9,8},{10,9... | collective-permute-start | bytes 1179656 | tf_op jit(solution)/shard_map/ppermute | solution.py:42
  71.8 3.7 %copy-start.5 = (f32[64]{0:T(128)}, f32[64]{0:T(128)S(1)}, u32[]{:S(2)}) copy-start(f32[64]{0:T(128)S(1)} %multiply_power_fusion) | copy-start | bytes 772
  72.3 3.1 %copy-start.7 = (pred[256]{0:T(512)(128)(4,1)}, pred[256]{0:T(512)(128)(4,1)S(1)}, u32[]{:S(2)}) copy-start(pred[256]{0:T(512)(128)(4,1)S(1)} %iota_compare_fusion.3) | copy-start | bytes 772
  104.2 9.7 %copy-start.1 = (bf16[256,768]{1,0:T(8,128)(2,1)S(1)}, bf16[256,768]{1,0:T(8,128)(2,1)}, u32[]{:S(2)}) copy-start(bf16[256,768]{1,0:T(8,128)(2,1)} %param.9) | copy-start | bytes 1179652
  104.9 14.7 %all-to-all-start.3 = ((bf16[2,2,256,128]{3,2,1,0:T(8,128)(2,1)}), bf16[2,2,256,128]{3,2,1,0:T(8,128)(2,1)S(1)}, u32[]{:S(2)}, u32[]{:S(2)}) async-start(bf16[2,2,256,128]{3,2,1,0:T(8,128)(2,1)} %broadcast_in_dim.174), calls=%async_computation.3 | async-start | bytes 524288 | tf_op jit(solution)/shard_map/all_to_all | solution.py:47
  119.6 12.9 %copy-start.9 = (pred[4]{0:T(512)(128)(4,1)S(1)}, pred[4]{0:T(512)(128)(4,1)}, u32[]{:S(2)}) copy-start(pred[4]{0:T(512)(128)(4,1)} %compare_and_fusion.1) | copy-start | bytes 16
  120.6 26.4 %all-to-all-start.4 = ((bf16[8,256,128]{2,1,0:T(8,128)(2,1)}), bf16[8,256,128]{2,1,0:T(8,128)(2,1)S(1)}, u32[]{:S(2)}, u32[]{:S(2)}) async-start(bf16[8,256,128]{2,1,0:T(8,128)(2,1)} %select_select_fusion), calls=%async_computation.4 | async-start | bytes 1048576 | tf_op jit(solution)/shard_map/all_to_all | solution.py:129
  140.6 17.4 %collective-permute-start.5 = (f32[256,128]{0,1:T(8,128)}, f32[256,128]{0,1:T(8,128)}, u32[]{:S(2)}, u32[]{:S(2)}) collective-permute-start(f32[256,128]{0,1:T(8,128)} %fusion.55), channel_id=1, source_target_pairs={{0,1},{1,2},{4,5},{5,6},{8,9},{9,10},{12,13},{13,14},{16,17},{17,1... | collective-permute-start | bytes 393224 | tf_op jit(solution)/shard_map/ppermute | solution.py:42
  144.4 20.2 %collective-permute-start.4 = (f32[256,128]{0,1:T(8,128)}, f32[256,128]{0,1:T(8,128)}, u32[]{:S(2)}, u32[]{:S(2)}) collective-permute-start(f32[256,128]{0,1:T(8,128)} %fusion.55), channel_id=1, source_target_pairs={{2,1},{3,2},{6,5},{7,6},{10,9},{11,10},{14,13},{15,14},{18,17},{19... | collective-permute-start | bytes 393224 | tf_op jit(solution)/shard_map/ppermute | solution.py:42
  145.7 12.3 %collective-permute-start.3 = (f32[256,128]{0,1:T(8,128)}, f32[256,128]{0,1:T(8,128)S(1)}, u32[]{:S(2)}, u32[]{:S(2)}) collective-permute-start(f32[256,128]{0,1:T(8,128)} %fusion.55), channel_id=1, source_target_pairs={{1,3},{2,0},{5,7},{6,4},{9,11},{10,8},{13,15},{14,12},{17,19},{18,... | collective-permute-start | bytes 393224 | tf_op jit(solution)/shard_map/ppermute | solution.py:42
  148.1 9.9 %all-to-all-start.5 = ((f32[4,80,128]{2,1,0:T(8,128)}), f32[4,80,128]{2,1,0:T(8,128)S(1)}, u32[]{:S(2)}, u32[]{:S(2)}) async-start(f32[4,80,128]{2,1,0:T(8,128)} %broadcast_in_dim.178), calls=%async_computation.5 | async-start | bytes 327680 | tf_op jit(solution)/shard_map/all_to_all | solution.py:47
  152.9 6.4 %copy-start.6 = (f32[64]{0:T(128)S(1)}, f32[64]{0:T(128)}, u32[]{:S(2)}) copy-start(f32[64]{0:T(128)} %copy-done.5) | copy-start | bytes 772
  158.0 3.7 %copy-start.4 = (bf16[4,16,128]{2,1,0:T(8,128)(2,1)}, bf16[4,16,128]{2,1,0:T(8,128)(2,1)S(1)}, u32[]{:S(2)}) copy-start(bf16[4,16,128]{2,1,0:T(8,128)(2,1)S(1)} %slice.125) | copy-start | bytes 49156
  158.0 3.7 %copy-start.2 = (f32[256,128]{0,1:T(8,128)}, f32[256,128]{0,1:T(8,128)S(1)}, u32[]{:S(2)}) copy-start(f32[256,128]{0,1:T(8,128)S(1)} %collective-permute-done.3) | copy-start | bytes 393220
  162.1 2.6 %copy-start.3 = (f32[256,128]{0,1:T(8,128)S(1)}, f32[256,128]{0,1:T(8,128)}, u32[]{:S(2)}) copy-start(f32[256,128]{0,1:T(8,128)} %copy-done.2) | copy-start | bytes 393220
  162.1 2.6 %copy-start.8 = (pred[256]{0:T(512)(128)(4,1)S(1)}, pred[256]{0:T(512)(128)(4,1)}, u32[]{:S(2)}) copy-start(pred[256]{0:T(512)(128)(4,1)} %copy-done.7) | copy-start | bytes 772

commit v17 on v14

--- a/solution.py
+++ b/solution.py
@@ -118,17 +118,18 @@
         jnp.where(choose[:, :, None, None], plane[None], jnp.zeros((), plane.dtype)),
         axis=1,
     )
-    for axis in ("zh", "zl"):
-        copies = gather_over(column, axis, lax.axis_size(axis))
-        column = jnp.sum(copies, axis=0)
-    dest_k = prefix[slots_all[plane_req]]
+    copies = gather_over(column, "zh", nz // n_low)
+    column = jnp.sum(copies, axis=0)
+    group = n_low * ny
+    dest_req = lax.axis_index("zh") * group + jnp.arange(group, dtype=jnp.int32)
+    dest_k = prefix[slots_all[dest_req]]
     held = column[0]
     for m in range(1, per_column):
         held = jnp.where((dest_k // ny == m)[:, None, None], column[m], held)
     send = jnp.where((dest_k % ny == iy)[:, None, None], held, jnp.zeros((), held.dtype))
-    received = lax.all_to_all(send, "ry", 0, 0, tiled=True)
+    received = lax.all_to_all(send, ("zl", "ry"), 0, 0, tiled=True)
     own_k = prefix[own_slot[0]]
-    picked = received[own_k % ny]
+    picked = jnp.sum(received, axis=0)
     down_t = picked[:n_down].reshape(down_store.shape[2], down_store.shape[1])
     adapter_query = picked[n_down:n_down + n_query].reshape(query_up_store.shape[1:])
     adapter_pair = picked[n_down + n_query:].reshape(key_value_store.shape[1:])

time: 148 us -> 166 us (1.12)
  waiting for transfers between devices: 34.2 us -> 56.7 us
  between operations: 5.88 us -> 1.86 us
  other arithmetic: 15.1 us -> 18.6 us
  local copies, waits for them, and re-layouts: 18 us -> 15.5 us
    all_to_all x5 -> x4, waiting for transfers between devices: 34.2 us -> 44.9 us  [gather_over(): return lax.all_to_all(copies, axis, 0, 0, tiled=True)]
    ppermute x6, waiting for transfers between devices: 0.02 us -> 10.5 us  [shifted(): return lax.ppermute(x, axis, pairs)]
    all_to_all x5 -> x4, starting transfers between devices: 37.7 us -> 31.9 us  [gather_over(): return lax.all_to_all(copies, axis, 0, 0, tiled=True)]
    all_to_all x1, starting transfers between devices: 7.55 us -> 11.5 us  [local(): received = lax.all_to_all(send, ('zl', 'ry'), 0, 0, tiled=True)]
    reduce_sum x0 -> x1, other arithmetic: none -> 1.88 us  [local(): picked = jnp.sum(received, axis=0)]
    broadcast_in_dim x5 -> x4, local copies, waits for them, and re-layouts: 4.59 us -> 3.76 us  [gather_over(): copies = jnp.broadcast_to(x[None], (n,) + x.shape)]
  transfers between devices with their start and end apart: 12 -> 11, of which waited for: 4 -> 7; matrix products, arithmetic and copies ran while one was open for 23% -> 21% of each run, Pallas kernels for 0% -> 0%
where the time goes in v17:
time: 166 us; the launch traced here: 164 us
  starting transfers between devices  63 us (38%)
  waiting for transfers between devices  56.7 us (34%)
  other arithmetic  18.6 us (11%)
  local copies, waits for them, and re-layouts  15.5 us (9%)
  matrix products  8.91 us (5%)
  between operations  1.86 us (1%)
    all_to_all x4, waiting for transfers between devices, gather_over(): return lax.all_to_all(copies, axis, 0, 0, tiled=True)  44.9 us
    all_to_all x4, starting transfers between devices, gather_over(): return lax.all_to_all(copies, axis, 0, 0, tiled=True)  31.9 us
    ppermute x6, starting transfers between devices, shifted(): return lax.ppermute(x, axis, pairs)  19.6 us
    all_to_all x1, starting transfers between devices, local(): received = lax.all_to_all(send, ('zl', 'ry'), 0, 0, tiled=True)  11.5 us
    ppermute x6, waiting for transfers between devices, shifted(): return lax.ppermute(x, axis, pairs)  10.5 us
    broadcast_in_dim x4, local copies, waits for them, and re-layouts, gather_over(): copies = jnp.broadcast_to(x[None], (n,) + x.shape)  3.76 us
  transfers between devices with their start and end apart: 11, of which 7 were waited for; matrix products, arithmetic and copies ran while one was open for 21% of the time, Pallas kernels for 0%

profile of v17, /device:TPU:1, one launch (start us, length us, event | category | flops | bytes accessed | tf_op | source)
XLA Modules:
  0.0 164.5 jit_solution(10296478764316420684)
XLA Ops:
  0.8 1.4 fusion.38
  2.2 1.4 broadcast_in_dim.106
  3.5 20.6 %all-to-all-start = ((s32[128,1,1]{2,1,0:T(1,128)}), s32[128,1,1]{2,1,0:T(1,128)S(1)}, u32[]{:S(2)}, u32[]{:S(2)}) async-start(s32[128,1,1]{2,1,0:T(1,128)} %broadcast_in_dim.106), calls=%async_computation | async-start | bytes 131072 | tf_op jit(solution)/shard_map/all_to_all | solution.py:47
  24.1 0.9 reshape.470
  25.0 0.7 reshape_squeeze.3
  25.7 0.7 pad_maximum_fusion.1
  26.4 12.5 %all-to-all-done = s32[128,1,1]{2,1,0:T(1,128)S(1)} async-done(((s32[128,1,1]{2,1,0:T(1,128)}), s32[128,1,1]{2,1,0:T(1,128)S(1)}, u32[]{:S(2)}, u32[]{:S(2)}) %all-to-all-start) | async-done | bytes 544 | tf_op jit(solution)/shard_map/all_to_all | solution.py:47
  38.9 0.9 broadcast_in_dim.164
  39.8 3.9 %all-to-all-start.1 = ((bf16[8,256,128]{2,1,0:T(8,128)(2,1)}), bf16[8,256,128]{2,1,0:T(8,128)(2,1)S(1)}, u32[]{:S(2)}, u32[]{:S(2)}) async-start(bf16[8,256,128]{2,1,0:T(8,128)(2,1)} %broadcast_in_dim.164), calls=%async_computation.1 | async-start | bytes 1048576 | tf_op jit(solution)/shard_map/all_to_all | solution.py:47
  43.7 2.3 %reduce.7 = s32[128]{0:T(128)S(1)} reduce(s32[128,1,1]{2,1,0:T(1,128)S(1)} %all-to-all-done, s32[]{:T(128)} %constant.95.clone.1), dimensions={1,2}, to_apply=%all_to_all.16.reduce_sub_computation | reduce | bytes 1028 | tf_op jit(solution)/shard_map/all_to_all | solution.py:47
  46.3 0.7 gather_fusion.3
  46.9 0.6 gather_fusion.4
  47.6 5.5 %all-to-all-done.1 = bf16[8,256,128]{2,1,0:T(8,128)(2,1)S(1)} async-done(((bf16[8,256,128]{2,1,0:T(8,128)(2,1)}), bf16[8,256,128]{2,1,0:T(8,128)(2,1)S(1)}, u32[]{:S(2)}, u32[]{:S(2)}) %all-to-all-start.1) | async-done | bytes 524320 | tf_op jit(solution)/shard_map/all_to_all | solution.py:47
  53.5 0.9 broadcast_in_dim.167
  54.3 3.5 %all-to-all-start.2 = ((bf16[4,2,256,128]{3,2,1,0:T(8,128)(2,1)}), bf16[4,2,256,128]{3,2,1,0:T(8,128)(2,1)S(1)}, u32[]{:S(2)}, u32[]{:S(2)}) async-start(bf16[4,2,256,128]{3,2,1,0:T(8,128)(2,1)} %broadcast_in_dim.167), calls=%async_computation.2 | async-start | bytes 1048576 | tf_op jit(solution)/shard_map/all_to_all | solution.py:47
  57.8 0.7 gather_fusion.1
  58.5 0.7 gather_fusion.2
  59.3 24.4 %all-to-all-done.2 = bf16[4,2,256,128]{3,2,1,0:T(8,128)(2,1)S(1)} async-done(((bf16[4,2,256,128]{3,2,1,0:T(8,128)(2,1)}), bf16[4,2,256,128]{3,2,1,0:T(8,128)(2,1)S(1)}, u32[]{:S(2)}, u32[]{:S(2)}) %all-to-all-start.2) | async-done | bytes 524320 | tf_op jit(solution)/shard_map/all_to_all | solution.py:47
  83.7 1.6 select_select_fusion
  85.3 11.5 %all-to-all-start.3 = ((bf16[32,256,128]{2,1,0:T(8,128)(2,1)}), bf16[32,256,128]{2,1,0:T(8,128)(2,1)}, u32[]{:S(2)}, u32[]{:S(2)}) async-start(bf16[32,256,128]{2,1,0:T(8,128)(2,1)} %select_select_fusion), calls=%async_computation.3 | async-start | bytes 4194304 | tf_op jit(solution)/shard_map/all_to_all | solution.py:130
  96.9 3.1 %collective-permute-start = (bf16[256,768]{1,0:T(8,128)(2,1)S(1)}, bf16[256,768]{1,0:T(8,128)(2,1)S(1)}, u32[]{:S(2)}, u32[]{:S(2)}) collective-permute-start(bf16[256,768]{1,0:T(8,128)(2,1)S(1)} %copy-done.1), channel_id=1, source_target_pairs={{0,1},{1,2},{2,3},{3,0},{4,5},{5,6},{6,7},{7,4},{8,9},{9,10},{10,1... | collective-permute-start | bytes 1179656 | tf_op jit(solution)/shard_map/ppermute | solution.py:42
  100.0 4.4 %collective-permute-start.1 = (bf16[256,768]{1,0:T(8,128)(2,1)S(1)}, bf16[256,768]{1,0:T(8,128)(2,1)S(1)}, u32[]{:S(2)}, u32[]{:S(2)}) collective-permute-start(bf16[256,768]{1,0:T(8,128)(2,1)S(1)} %copy-done.1), channel_id=1, source_target_pairs={{0,2},{1,3},{2,0},{3,1},{4,6},{5,7},{6,4},{7,5},{8,10},{9,11},{10,... | collective-permute-start | bytes 1179656 | tf_op jit(solution)/shard_map/ppermute | solution.py:42
  104.3 3.1 %collective-permute-start.2 = (bf16[256,768]{1,0:T(8,128)(2,1)S(1)}, bf16[256,768]{1,0:T(8,128)(2,1)}, u32[]{:S(2)}, u32[]{:S(2)}) collective-permute-start(bf16[256,768]{1,0:T(8,128)(2,1)S(1)} %copy-done.1), channel_id=1, source_target_pairs={{0,3},{1,0},{2,1},{3,2},{4,7},{5,4},{6,5},{7,6},{8,11},{9,8},{10,9... | collective-permute-start | bytes 1179656 | tf_op jit(solution)/shard_map/ppermute | solution.py:42
  108.1 0.5 compare_and_fusion.1
  108.6 0.7 fusion.7
  109.4 1.2 multiply_cosine_fusion
  110.6 9.2 %collective-permute-done.1 = bf16[256,768]{1,0:T(8,128)(2,1)S(1)} collective-permute-done((bf16[256,768]{1,0:T(8,128)(2,1)S(1)}, bf16[256,768]{1,0:T(8,128)(2,1)S(1)}, u32[]{:S(2)}, u32[]{:S(2)}) %collective-permute-start.1) | collective-permute-done | bytes 393248 | tf_op jit(solution)/shard_map/ppermute | solution.py:42
  119.9 1.2 collective-permute-done.2
  121.1 2.4 %pad_maximum_fusion = bf16[4,256,768]{2,1,0:T(8,128)(2,1)} fusion(bf16[1,256,768]{2,1,0:T(8,128)(2,1)} %bitcast.4, bf16[1,256,768]{2,1,0:T(8,128)(2,1)S(1)} %bitcast.88, bf16[1,256,768]{2,1,0:T(8,128)(2,1)S(1)} %bitcast.87, bf16[1,256,768]{2,1,0:T(8,128)(2,1)S(1)} %bitcast.85), kind=kLoop, calls=%fused_computation.6 | loop fusion | flops 2359296 | bytes 3145728 | tf_op jit(solution)/shard_map/stack | solution.py:102
  123.5 3.2 %gather_fusion = bf16[4,256,768]{2,1,0:T(8,128)(2,1)} fusion(bf16[4,256,768]{2,1,0:T(8,128)(2,1)} %pad_maximum_fusion, s32[1024]{0:T(1024)S(1)} %pad_clamp_fusion.3), kind=kCustom, calls=%fused_computation | custom fusion | bytes 3145744 | tf_op jit(solution)/shard_map/jit(_take)/gather | solution.py:104
  126.7 2.8 %select_bitcast_fusion = bf16[256,4,768]{2,0,1:T(8,128)(2,1)} fusion(bf16[4,256,768]{2,1,0:T(8,128)(2,1)} %gather_fusion, pred[4]{0:T(512)(128)(4,1)S(1)} %copy-done.7), kind=kLoop, calls=%fused_computation.7 | loop fusion | flops 786432 | bytes 3145732 | tf_op jit(solution)/shard_map/jit(_take)/select_n | solution.py:104
  129.5 2.7 %copy.45 = bf16[256,4,768]{0,2,1:T(8,128)(2,1)} copy(bf16[256,4,768]{2,0,1:T(8,128)(2,1)} %select_bitcast_fusion) | data formatting | bytes 3145728 | tf_op jit(solution)/shard_map/jit(_take)/select_n | solution.py:104
  132.2 2.5 %fusion.55 = f32[256,128]{0,1:T(8,128)} fusion(bf16[256,3072]{0,1:T(8,128)(2,1)} %bitcast.83, bf16[3072,128]{1,0:T(8,128)(2,1)S(1)} %copy-done.8), kind=kOutput, calls=%fused_computation.117 | convolution fusion | flops 201326592 | bytes 2490368 | tf_op jit(solution)/shard_map/dot_general | solution.py:139
  134.7 1.3 collective-permute-start.3
  136.0 6.4 %collective-permute-start.5 = (f32[256,128]{0,1:T(8,128)}, f32[256,128]{0,1:T(8,128)S(1)}, u32[]{:S(2)}, u32[]{:S(2)}) collective-permute-start(f32[256,128]{0,1:T(8,128)} %fusion.55), channel_id=1, source_target_pairs={{0,1},{1,2},{4,5},{5,6},{8,9},{9,10},{12,13},{13,14},{16,17},{17,1... | collective-permute-start | bytes 393224 | tf_op jit(solution)/shard_map/ppermute | solution.py:42
  142.4 1.3 collective-permute-start.4
  143.8 1.3 all-to-all-done.3
  145.0 1.9 %reduce_sum.67 = bf16[256,128]{1,0:T(8,128)(2,1)S(1)} reduce(bf16[32,256,128]{2,1,0:T(8,128)(2,1)} %all-to-all-done.3, bf16[]{:T(256)} %constant.108.clone.1), dimensions={0}, to_apply=%region_5.6 | reduce | flops 1015808 | bytes 2162690 | tf_op jit(solution)/shard_map/reduce_sum | solution.py:132
  147.3 0.7 broadcast_in_dim.171
  148.0 4.0 %all-to-all-start.4 = ((f32[4,80,128]{2,1,0:T(8,128)}), f32[4,80,128]{2,1,0:T(8,128)S(1)}, u32[]{:S(2)}, u32[]{:S(2)}) async-start(f32[4,80,128]{2,1,0:T(8,128)} %broadcast_in_dim.171), calls=%async_computation.4 | async-start | bytes 327680 | tf_op jit(solution)/shard_map/all_to_all | solution.py:47
  152.0 2.4 %fusion.57 = f32[256,384]{1,0:T(8,128)S(1)} fusion(bf16[256,3072]{0,1:T(8,128)(2,1)} %bitcast.84, bf16[3072,384]{1,0:T(8,128)(2,1)S(1)} %copy-done), kind=kOutput, calls=%fused_computation.119 | convolution fusion | flops 603979776 | bytes 4325376 | tf_op jit(solution)/shard_map/dot_general | solution.py:170
  154.4 2.5 %all-to-all-done.4 = f32[4,80,128]{2,1,0:T(8,128)S(1)} async-done(((f32[4,80,128]{2,1,0:T(8,128)}), f32[4,80,128]{2,1,0:T(8,128)S(1)}, u32[]{:S(2)}, u32[]{:S(2)}) %all-to-all-start.4) | async-done | bytes 163872 | tf_op jit(solution)/shard_map/all_to_all | solution.py:47
  157.1 1.2 reduce-precision_bitcast_fusion
  158.3 0.9 fusion.31
  160.1 1.1 fusion.8
  161.2 1.3 fusion.54
  162.6 1.1 fusion.4
  163.7 0.8 copy.52
  (62 shorter events, 2.1 us)
Async XLA Ops:
  0.0 152.0 %copy-start = (bf16[3072,384]{1,0:T(8,128)(2,1)S(1)}, bf16[3072,384]{1,0:T(8,128)(2,1)}, u32[]{:S(2)}) copy-start(bf16[3072,384]{1,0:T(8,128)(2,1)} %param.10) | copy-start | bytes 7077892
  3.5 35.4 %all-to-all-start = ((s32[128,1,1]{2,1,0:T(1,128)}), s32[128,1,1]{2,1,0:T(1,128)S(1)}, u32[]{:S(2)}, u32[]{:S(2)}) async-start(s32[128,1,1]{2,1,0:T(1,128)} %broadcast_in_dim.106), calls=%async_computation | async-start | bytes 131072 | tf_op jit(solution)/shard_map/all_to_all | solution.py:47
  39.8 13.4 %all-to-all-start.1 = ((bf16[8,256,128]{2,1,0:T(8,128)(2,1)}), bf16[8,256,128]{2,1,0:T(8,128)(2,1)S(1)}, u32[]{:S(2)}, u32[]{:S(2)}) async-start(bf16[8,256,128]{2,1,0:T(8,128)(2,1)} %broadcast_in_dim.164), calls=%async_computation.1 | async-start | bytes 1048576 | tf_op jit(solution)/shard_map/all_to_all | solution.py:47
  54.3 29.3 %all-to-all-start.2 = ((bf16[4,2,256,128]{3,2,1,0:T(8,128)(2,1)}), bf16[4,2,256,128]{3,2,1,0:T(8,128)(2,1)S(1)}, u32[]{:S(2)}, u32[]{:S(2)}) async-start(bf16[4,2,256,128]{3,2,1,0:T(8,128)(2,1)} %broadcast_in_dim.167), calls=%async_computation.2 | async-start | bytes 1048576 | tf_op jit(solution)/shard_map/all_to_all | solution.py:47
  85.3 11.5 %copy-start.1 = (bf16[256,768]{1,0:T(8,128)(2,1)S(1)}, bf16[256,768]{1,0:T(8,128)(2,1)}, u32[]{:S(2)}) copy-start(bf16[256,768]{1,0:T(8,128)(2,1)} %param.9) | copy-start | bytes 1179652
  85.3 59.7 %all-to-all-start.3 = ((bf16[32,256,128]{2,1,0:T(8,128)(2,1)}), bf16[32,256,128]{2,1,0:T(8,128)(2,1)}, u32[]{:S(2)}, u32[]{:S(2)}) async-start(bf16[32,256,128]{2,1,0:T(8,128)(2,1)} %select_select_fusion), calls=%async_computation.3 | async-start | bytes 4194304 | tf_op jit(solution)/shard_map/all_to_all | solution.py:130
  96.9 13.8 %collective-permute-start = (bf16[256,768]{1,0:T(8,128)(2,1)S(1)}, bf16[256,768]{1,0:T(8,128)(2,1)S(1)}, u32[]{:S(2)}, u32[]{:S(2)}) collective-permute-start(bf16[256,768]{1,0:T(8,128)(2,1)S(1)} %copy-done.1), channel_id=1, source_target_pairs={{0,1},{1,2},{2,3},{3,0},{4,5},{5,6},{6,7},{7,4},{8,9},{9,10},{10,1... | collective-permute-start | bytes 1179656 | tf_op jit(solution)/shard_map/ppermute | solution.py:42
  100.0 19.9 %collective-permute-start.1 = (bf16[256,768]{1,0:T(8,128)(2,1)S(1)}, bf16[256,768]{1,0:T(8,128)(2,1)S(1)}, u32[]{:S(2)}, u32[]{:S(2)}) collective-permute-start(bf16[256,768]{1,0:T(8,128)(2,1)S(1)} %copy-done.1), channel_id=1, source_target_pairs={{0,2},{1,3},{2,0},{3,1},{4,6},{5,7},{6,4},{7,5},{8,10},{9,11},{10,... | collective-permute-start | bytes 1179656 | tf_op jit(solution)/shard_map/ppermute | solution.py:42
  104.3 16.8 %collective-permute-start.2 = (bf16[256,768]{1,0:T(8,128)(2,1)S(1)}, bf16[256,768]{1,0:T(8,128)(2,1)}, u32[]{:S(2)}, u32[]{:S(2)}) collective-permute-start(bf16[256,768]{1,0:T(8,128)(2,1)S(1)} %copy-done.1), channel_id=1, source_target_pairs={{0,3},{1,0},{2,1},{3,2},{4,7},{5,4},{6,5},{7,6},{8,11},{9,8},{10,9... | collective-permute-start | bytes 1179656 | tf_op jit(solution)/shard_map/ppermute | solution.py:42
  108.6 0.7 copy-start.5
  123.5 3.2 %copy-start.7 = (pred[4]{0:T(512)(128)(4,1)S(1)}, pred[4]{0:T(512)(128)(4,1)}, u32[]{:S(2)}) copy-start(pred[4]{0:T(512)(128)(4,1)} %compare_and_fusion.1) | copy-start | bytes 16
  129.5 2.7 %copy-start.8 = (bf16[3072,128]{1,0:T(8,128)(2,1)S(1)}, bf16[3072,128]{1,0:T(8,128)(2,1)}, u32[]{:S(2)}) copy-start(bf16[3072,128]{1,0:T(8,128)(2,1)} %param.11) | copy-start | bytes 2359300
  134.7 22.3 %collective-permute-start.3 = (f32[256,128]{0,1:T(8,128)}, f32[256,128]{0,1:T(8,128)S(1)}, u32[]{:S(2)}, u32[]{:S(2)}) collective-permute-start(f32[256,128]{0,1:T(8,128)} %fusion.55), channel_id=1, source_target_pairs={{1,3},{2,0},{5,7},{6,4},{9,11},{10,8},{13,15},{14,12},{17,19},{18,... | collective-permute-start | bytes 393224 | tf_op jit(solution)/shard_map/ppermute | solution.py:42
  136.0 21.1 %collective-permute-start.5 = (f32[256,128]{0,1:T(8,128)}, f32[256,128]{0,1:T(8,128)S(1)}, u32[]{:S(2)}, u32[]{:S(2)}) collective-permute-start(f32[256,128]{0,1:T(8,128)} %fusion.55), channel_id=1, source_target_pairs={{0,1},{1,2},{4,5},{5,6},{8,9},{9,10},{12,13},{13,14},{16,17},{17,1... | collective-permute-start | bytes 393224 | tf_op jit(solution)/shard_map/ppermute | solution.py:42
  142.4 20.2 %collective-permute-start.4 = (f32[256,128]{0,1:T(8,128)}, f32[256,128]{0,1:T(8,128)}, u32[]{:S(2)}, u32[]{:S(2)}) collective-permute-start(f32[256,128]{0,1:T(8,128)} %fusion.55), channel_id=1, source_target_pairs={{2,1},{3,2},{6,5},{7,6},{10,9},{11,10},{14,13},{15,14},{18,17},{19... | collective-permute-start | bytes 393224 | tf_op jit(solution)/shard_map/ppermute | solution.py:42
  148.0 9.0 %all-to-all-start.4 = ((f32[4,80,128]{2,1,0:T(8,128)}), f32[4,80,128]{2,1,0:T(8,128)S(1)}, u32[]{:S(2)}, u32[]{:S(2)}) async-start(f32[4,80,128]{2,1,0:T(8,128)} %broadcast_in_dim.171), calls=%async_computation.4 | async-start | bytes 327680 | tf_op jit(solution)/shard_map/all_to_all | solution.py:47
  157.0 2.2 %copy-start.4 = (bf16[4,16,128]{2,1,0:T(8,128)(2,1)}, bf16[4,16,128]{2,1,0:T(8,128)(2,1)S(1)}, u32[]{:S(2)}) copy-start(bf16[4,16,128]{2,1,0:T(8,128)(2,1)S(1)} %slice.126) | copy-start | bytes 49156
  157.1 2.6 %copy-start.2 = (f32[256,128]{0,1:T(8,128)}, f32[256,128]{0,1:T(8,128)S(1)}, u32[]{:S(2)}) copy-start(f32[256,128]{0,1:T(8,128)S(1)} %collective-permute-done.3) | copy-start | bytes 393220
  160.0 2.6 %copy-start.3 = (f32[256,128]{0,1:T(8,128)S(1)}, f32[256,128]{0,1:T(8,128)}, u32[]{:S(2)}) copy-start(f32[256,128]{0,1:T(8,128)} %copy-done.2) | copy-start | bytes 393220
  160.0 2.6 %copy-start.6 = (pred[256]{0:T(512)(128)(4,1)S(1)}, pred[256]{0:T(512)(128)(4,1)}, u32[]{:S(2)}) copy-start(pred[256]{0:T(512)(128)(4,1)} %copy-done.5) | copy-start | bytes 772
